TPU v7x, 32 devices: a whole 2x2x4 slice. The times are simulated.
32 devices in a mesh: req: 16 (over z, y, x), tp: 2 (over core).
Axes of the slice: x: 2, y: 2, z: 4, core: 2. Of those that a mesh axis runs over, the one named last changes fastest.
Arguments:
- new_queries: bfloat16 [4096, 2048], P('req', 'tp'), may hold values from -9 to 9
- new_keys: bfloat16 [4096, 2048], P('req', 'tp'), may hold values from -9 to 9
- new_values: bfloat16 [4096, 2048], P('req', 'tp'), may hold values from -5 to 5
- kv_pages: bfloat16 [256, 2, 128, 2048], P('req', None, None, 'tp'), may hold values from -5.5 to 5.5
- page_table: int32 [16, 16], replicated, may hold values from -1 to 255, as said below
- cache_len: int32 [16], replicated, may hold values from 1 to 2048, as said below
- w_out: bfloat16 [2048, 4096], P('tp'), may hold values from -0.25 to 0.25
- out_bias: bfloat16 [4096], P('tp'), may hold values from -3 to 3
Outputs:
- projected: bfloat16 [4096, 4096], P('req', 'tp')
Inputs may be any that keep to these rules, and one draw needn't show every extreme that they name: page_table[r, s] is the page holding cached positions s * 128 to (s + 1) * 128 - 1 of request r, for s below ceil(cache_len[r] / 128), and -1 after; page p is held by index p // 16 of req; the pages of one request lie on distinct indices of req; every page belongs to exactly one request. `cache_len`: some request has exactly 2048 cached positions.
All inputs are finite; a program needn't handle non-finite values.
Results may differ from a plain program's by a relative error of at most 0.0053.
Values may be sent and summed in bfloat16 or wider, within the bound.
No kernel may reach another device: no remote copies, remote signals or barrier semaphores. Data moves between devices by JAX's collectives and lax.ppermute only.
A program may use at most 192 MiB of HBM per device.

v0:
```python
import math

import jax
import jax.numpy as jnp
from jax import lax
from jax.sharding import PartitionSpec as P

HEAD_DIM = 128
ROT = 32


NEG_FILL = -1e30


def rotate_rows(block, positions):
    row_count = block.shape[0]
    shaped = block.astype(jnp.float32).reshape(row_count, -1, HEAD_DIM)
    half_rot = ROT // 2
    frequency = 10000.0 ** (-2.0 * jnp.arange(half_rot, dtype=jnp.float32) / ROT)
    angles = positions.astype(jnp.float32)[:, None] * frequency[None, :]
    cosine = jnp.cos(angles)[:, None, :]
    sines = jnp.sin(angles)[:, None, :]
    first_half = shaped[:, :, :half_rot]
    second_half = shaped[:, :, half_rot:ROT]
    turned = jnp.concatenate(
        [
            first_half * cosine - second_half * sines,
            second_half * cosine + first_half * sines,
            shaped[:, :, ROT:],
        ],
        axis=2,
    )
    return turned.reshape(row_count, -1).astype(jnp.bfloat16)


def head_partials(query_heads, key_blocks, value_blocks, usable):
    head_count = key_blocks.shape[2]
    score_scale = 1.0 / math.sqrt(HEAD_DIM)

    def one_head(head_index):
        keys_h = lax.dynamic_index_in_dim(key_blocks, head_index, 2, keepdims=False)
        values_h = lax.dynamic_index_in_dim(value_blocks, head_index, 2, keepdims=False)
        query_h = lax.dynamic_index_in_dim(query_heads, head_index, 1, keepdims=False)
        scores = jnp.einsum("ce,bke->bck", query_h, keys_h, preferred_element_type=jnp.float32)
        scores = jnp.where(usable, scores * score_scale, NEG_FILL)
        maxima = jnp.max(scores, axis=2)
        weights = jnp.where(usable, jnp.exp(scores - maxima[:, :, None]), 0.0)
        totals = jnp.sum(weights, axis=2)
        weighted = jnp.einsum(
            "bck,bke->bce",
            weights.astype(jnp.bfloat16),
            values_h,
            preferred_element_type=jnp.float32,
        )
        return (maxima, totals, weighted)

    return lax.map(one_head, jnp.arange(head_count, dtype=jnp.int32))


def block_partials(query_heads, key_blocks, value_blocks, usable):
    block_count = key_blocks.shape[0]
    group = max((d for d in range(1, 9) if block_count % d == 0))
    rounds = block_count // group
    usable_g = usable.reshape((rounds, group) + usable.shape[1:])
    keys_g = key_blocks.reshape((rounds, group) + key_blocks.shape[1:])
    values_g = value_blocks.reshape((rounds, group) + value_blocks.shape[1:])

    def one_round(index):
        keys_r = lax.dynamic_index_in_dim(keys_g, index, 0, keepdims=False)
        values_r = lax.dynamic_index_in_dim(values_g, index, 0, keepdims=False)
        usable_r = lax.dynamic_index_in_dim(usable_g, index, 0, keepdims=False)
        return head_partials(query_heads, keys_r, values_r, usable_r)

    maxima, totals, weighted = lax.map(one_round, jnp.arange(rounds, dtype=jnp.int32))
    head_count = maxima.shape[1]
    span_len = maxima.shape[3]
    maxima = jnp.transpose(maxima, (1, 0, 2, 3)).reshape(head_count, block_count, span_len)
    totals = jnp.transpose(totals, (1, 0, 2, 3)).reshape(head_count, block_count, span_len)
    weighted = jnp.transpose(weighted, (1, 0, 2, 3, 4)).reshape(
        head_count, block_count, span_len, weighted.shape[4]
    )
    return (maxima, totals, weighted)


def combine(maxima, totals, weighted):
    peak_score = jnp.max(maxima, axis=1, keepdims=True)
    factor = jnp.exp(maxima - peak_score)
    numerator = jnp.sum(factor[..., None] * weighted, axis=1)
    denominator = jnp.sum(factor * totals, axis=1)
    return numerator / denominator[..., None]


def on_device(new_queries, new_keys, new_values, kv_pages, page_table, cache_len, w_out, out_bias):
    own_index = lax.axis_index("req")
    span_len = new_queries.shape[0]
    head_count = new_queries.shape[1] // HEAD_DIM
    page_count = kv_pages.shape[0]
    page_size = kv_pages.shape[2]
    request_count = page_table.shape[0]
    slot_count = page_table.shape[1]
    own_length = lax.dynamic_index_in_dim(cache_len, own_index, 0, keepdims=False)
    positions = own_length + jnp.arange(span_len, dtype=jnp.int32)
    query_rot = rotate_rows(new_queries, positions)
    key_rot = rotate_rows(new_keys, positions)
    query_heads = query_rot.reshape(span_len, head_count, HEAD_DIM)
    causal = (
        jnp.arange(span_len, dtype=jnp.int32)[:, None]
        >= jnp.arange(span_len, dtype=jnp.int32)[None, :]
    )[None]
    local_parts = block_partials(
        query_heads,
        key_rot.reshape(1, span_len, head_count, HEAD_DIM),
        new_values.reshape(1, span_len, head_count, HEAD_DIM),
        causal,
    )
    slot_ids = jnp.arange(slot_count, dtype=jnp.int32)
    within_page = jnp.arange(page_size, dtype=jnp.int32)
    request_ids = jnp.arange(request_count, dtype=jnp.int32)
    owners = jnp.where(page_table >= 0, page_table // page_count, -1)
    held_here = owners == own_index
    local_page = jnp.sum(jnp.where(held_here, page_table - own_index * page_count, 0), axis=1)
    outgoing = jnp.take(kv_pages, local_page, axis=0)
    incoming = lax.all_to_all(outgoing, "req", split_axis=0, concat_axis=0, tiled=True)
    own_row = lax.dynamic_index_in_dim(page_table, own_index, 0, keepdims=False)
    row_owner = jnp.where(own_row >= 0, own_row // page_count, -1)
    matches = row_owner[None, :] == request_ids[:, None]
    present = jnp.any(matches, axis=1)
    slot_of = jnp.sum(jnp.where(matches, slot_ids[None, :], 0), axis=1)
    key_place = slot_of[:, None] * page_size + within_page[None, :]
    usable = (present[:, None] & (key_place < own_length))[:, None, :]
    remote_parts = block_partials(
        query_heads,
        incoming[:, 0].reshape(request_count, page_size, head_count, HEAD_DIM),
        incoming[:, 1].reshape(request_count, page_size, head_count, HEAD_DIM),
        usable,
    )
    maxima_all = jnp.concatenate([local_parts[0], remote_parts[0]], axis=1)
    totals_all = jnp.concatenate([local_parts[1], remote_parts[1]], axis=1)
    weighted_all = jnp.concatenate([local_parts[2], remote_parts[2]], axis=1)
    merged = combine(maxima_all, totals_all, weighted_all)
    attended = (
        jnp.transpose(merged, (1, 0, 2))
        .reshape(span_len, head_count * HEAD_DIM)
        .astype(jnp.bfloat16)
    )
    partial_terms = jnp.dot(attended, w_out, preferred_element_type=jnp.float32)
    summed = lax.psum_scatter(partial_terms, "tp", scatter_dimension=1, tiled=True)
    return (summed + out_bias.astype(jnp.float32)).astype(jnp.bfloat16)


def solution(mesh):
    return jax.shard_map(
        on_device,
        mesh=mesh,
        in_specs=(
            P("req", "tp"),
            P("req", "tp"),
            P("req", "tp"),
            P("req", None, None, "tp"),
            P(),
            P(),
            P("tp", None),
            P("tp"),
        ),
        out_specs=P("req", "tp"),
        check_vma=False,
    )
```

profile of v0, /device:TPU:11, one launch (start us, length us, event | category | flops | bytes accessed | tf_op | source)
XLA Modules:
  0.0 421.4 jit_solution(2045228802590445701)
XLA Ops:
  7.4 8.1 %gather_fusion = bf16[16,2,128,1024]{3,2,1,0:T(8,128)(2,1)} fusion(bf16[16,2,128,1024]{3,2,1,0:T(8,128)(2,1)} %param.17, s32[1024]{0:T(1024)S(1)} %pad_clamp_fusion), kind=kCustom, calls=%fused_computation | custom fusion | bytes 16777280 | tf_op jit(solution)/shard_map/jit(_take)/gather | solution.py:122
  15.5 7.5 %broadcast_select_fusion = bf16[16,2,128,1024]{3,2,1,0:T(8,128)(2,1)} fusion(bf16[16,2,128,1024]{3,2,1,0:T(8,128)(2,1)} %gather_fusion, pred[16]{0:T(512)(128)(4,1)S(1)} %compare_and_fusion), kind=kLoop, calls=%fused_computation.55 | loop fusion | flops 4194304 | bytes 16777232 | tf_op jit(solution)/shard_map/jit(_take)/select_n | solution.py:122
  23.0 6.8 %all-to-all-start = ((bf16[16,2,128,1024]{3,2,1,0:T(8,128)(2,1)}), bf16[16,2,128,1024]{3,2,1,0:T(8,128)(2,1)}, u32[]{:S(2)}, u32[]{:S(2)}) async-start(bf16[16,2,128,1024]{3,2,1,0:T(8,128)(2,1)} %broadcast_select_fusion), calls=%async_computation | async-start | bytes 16777216 | tf_op jit(solution)/shard_map/all_to_all | solution.py:123
  34.4 29.4 %while.57 = (s32[]{:T(128)}, f32[8,1,256]{2,1,0:T(1,128)S(1)}, f32[8,1,256]{2,1,0:T(1,128)S(1)}, f32[8,1,256,128]{3,2,1,0:T(8,128)}, s32[8]{0:T(128)S(1)}, /*ind...) while((s32[]{:T(128)}, f32[8,1,256]{2,1,0:T(1,128)S(1)}, ...), condition=%wide.region_3.4_spmd.clone.clone, body=%wide.region_0.3_spmd.clone.clone.sunk | while | flops 34340356 | bytes 1123503 | solution.py:57
  63.8 153.6 %all-to-all-done = bf16[16,2,128,1024]{3,2,1,0:T(8,128)(2,1)} async-done(((bf16[16,2,128,1024]{3,2,1,0:T(8,128)(2,1)}), bf16[16,2,128,1024]{3,2,1,0:T(8,128)(2,1)}, u32[]{:S(2)}, u32[]{:S(2)}) %all-to-all-start) | async-done | bytes 8388640 | tf_op jit(solution)/shard_map/all_to_all | solution.py:123
  217.3 6.1 %fusion.55 = (bf16[16,1,128,1024]{3,2,1,0:T(8,128)(2,1)}, bf16[16,1,128,1024]{3,2,1,0:T(8,128)(2,1)}) fusion(bf16[16,2,128,1024]{3,2,1,0:T(8,128)(2,1)} %all-to-all-done), kind=kLoop, calls=%fused_computation.108 | loop fusion | bytes 16777216 | tf_op jit(solution)/shard_map/slice | solution.py:134
  223.5 6.4 %copy.39 = bf16[16,1,128,1024]{2,3,0,1:T(8,128)(2,1)} copy(bf16[16,1,128,1024]{3,2,1,0:T(8,128)(2,1)} %get-tuple-element.340) | data formatting | bytes 8388608 | tf_op jit(solution)/shard_map/slice | solution.py:133
  229.9 6.4 %copy.40 = bf16[16,1,128,1024]{2,3,0,1:T(8,128)(2,1)} copy(bf16[16,1,128,1024]{3,2,1,0:T(8,128)(2,1)} %get-tuple-element.339) | data formatting | bytes 8388608 | tf_op jit(solution)/shard_map/slice | solution.py:134
  236.3 143.3 %while.56 = (s32[]{:T(128)}, f32[2,8,8,256]{3,2,0,1:T(8,128)S(1)}, f32[2,8,8,256]{3,2,0,1:T(8,128)S(1)}, f32[2,8,8,256,128]{4,3,2,0,1:T(8,128)}, s32[2]{0:T(128)...) while((s32[]{:T(128)}, f32[2,8,8,256]{3,2,0,1:T(8,128)S(1)}, ...), condition=%wide.region_12.13_spmd, body=%wide.region_7.12_spmd.sunk | while | flops 136572928 | bytes 38672916 | solution.py:74
  240.7 2.6 copy.66
  245.0 2.6 copy.67
  247.7 52.6 %while.58 = (s32[]{:T(128)}, f32[8,8,256]{2,1,0:T(8,128)S(1)}, f32[8,8,256]{2,1,0:T(8,128)S(1)}, f32[8,8,256,128]{3,2,1,0:T(8,128)}, pred[8,1,128]{2,0,1:T(8,128...) while((s32[]{:T(128)}, f32[8,8,256]{2,1,0:T(8,128)S(1)}, ...), condition=%wide.region_11.11_spmd, body=%wide.region_8.10_spmd.sunk | while | flops 136572928 | bytes 4853943 | solution.py:57
  251.7 2.5 fusion.78
  258.3 2.6 fusion.78
  264.9 2.5 fusion.78
  271.5 2.5 fusion.78
  284.6 2.5 fusion.78
  291.2 2.5 fusion.78
  300.3 7.6 %bitcast_dynamic-update-slice_fusion.9 = f32[2,8,8,256,128]{4,3,2,0,1:T(8,128)} fusion(f32[2,8,8,256,128]{4,3,2,0,1:T(8,128)} %get-tuple-element.609, s32[]{:T(128)S(6)} %copy.93, f32[8,8,256,128]{3,2,1,0:T(8,128)} %get-tuple-element.526), kind=kLoop, calls=%fused_computation.24.clone.1 | loop fusion | bytes 16777220 | tf_op jit(solution)/shard_map/while/body/jit(dynamic_update_index_in_dim)/dynamic_update_slice | solution.py:74
  312.4 2.6 copy.66
  316.7 2.6 copy.67
  319.4 52.6 %while.58 = (s32[]{:T(128)}, f32[8,8,256]{2,1,0:T(8,128)S(1)}, f32[8,8,256]{2,1,0:T(8,128)S(1)}, f32[8,8,256,128]{3,2,1,0:T(8,128)}, pred[8,1,128]{2,0,1:T(8,128...) while((s32[]{:T(128)}, f32[8,8,256]{2,1,0:T(8,128)S(1)}, ...), condition=%wide.region_11.11_spmd, body=%wide.region_8.10_spmd.sunk | while | flops 136572928 | bytes 4853943 | solution.py:57
  323.4 2.5 fusion.78
  330.0 2.6 fusion.78
  336.6 2.5 fusion.78
  356.3 2.5 fusion.78
  362.9 2.5 fusion.78
  372.0 7.6 %bitcast_dynamic-update-slice_fusion.9 = f32[2,8,8,256,128]{4,3,2,0,1:T(8,128)} fusion(f32[2,8,8,256,128]{4,3,2,0,1:T(8,128)} %get-tuple-element.609, s32[]{:T(128)S(6)} %copy.93, f32[8,8,256,128]{3,2,1,0:T(8,128)} %get-tuple-element.526), kind=kLoop, calls=%fused_computation.24.clone.1 | loop fusion | bytes 16777220 | tf_op jit(solution)/shard_map/while/body/jit(dynamic_update_index_in_dim)/dynamic_update_slice | solution.py:74
  379.7 7.8 %fusion.39 = f32[8,256,128]{2,1,0:T(8,128)S(1)} fusion(f32[8,16,256,128]{3,2,1,0:T(8,128)} %bitcast.159, f32[8,1,256,128]{3,2,1,0:T(8,128)} %get-tuple-element.181, f32[8,17,256]{2,1,0:T(8,128)S(1)} %get-tuple-element.346), kind=kLoop, calls=%fused_computation.54 | loop fusion | flops 13107200 | bytes 19013632 | tf_op jit(solution)/shard_map/reduce_sum | solution.py:88
  388.1 7.7 %fusion.56 = f32[256,4096]{1,0:T(8,128)} fusion(bf16[256,1024]{0,1:T(8,128)(2,1)S(1)} %bitcast.167, bf16[1024,4096]{1,0:T(8,128)(2,1)} %param.20), kind=kOutput, calls=%fused_computation.109 | convolution fusion | flops 2147483648 | bytes 13107200 | tf_op jit(solution)/shard_map/dot_general | solution.py:146
  395.9 16.0 %reduce-scatter.2.cloned.1.call-done = f32[256,2048]{1,0:T(8,128)} async-done(((f32[256,4096]{1,0:T(8,128)}), f32[256,2048]{1,0:T(8,128)}) %reduce-scatter.2.cloned.1.call-update) | async-done | bytes 2097168 | tf_op jit(solution)/shard_map/reduce_scatter | solution.py:147
  411.8 2.8 add_convert_fusion
  (180 shorter events, 75.7 us)
Async XLA Ops:
  23.0 6.9 %copy-start = (bf16[256,1024]{1,0:T(8,128)(2,1)S(1)}, bf16[256,1024]{1,0:T(8,128)(2,1)}, u32[]{:S(2)}) copy-start(bf16[256,1024]{1,0:T(8,128)(2,1)} %param.14) | copy-start | bytes 1572868
  23.0 7.2 %copy-start.4 = (s32[16]{0:T(128)S(1)}, s32[16]{0:T(128)}, u32[]{:S(2)}) copy-start(s32[16]{0:T(128)} %param.19) | copy-start | bytes 196
  23.0 9.0 %copy-start.1 = (bf16[256,1024]{1,0:T(8,128)(2,1)S(1)}, bf16[256,1024]{1,0:T(8,128)(2,1)}, u32[]{:S(2)}) copy-start(bf16[256,1024]{1,0:T(8,128)(2,1)} %param.15) | copy-start | bytes 1572868
  23.0 194.4 %all-to-all-start = ((bf16[16,2,128,1024]{3,2,1,0:T(8,128)(2,1)}), bf16[16,2,128,1024]{3,2,1,0:T(8,128)(2,1)}, u32[]{:S(2)}, u32[]{:S(2)}) async-start(bf16[16,2,128,1024]{3,2,1,0:T(8,128)(2,1)} %broadcast_select_fusion), calls=%async_computation | async-start | bytes 16777216 | tf_op jit(solution)/shard_map/all_to_all | solution.py:123
  29.7 3.7 copy-start.2
  29.8 382.1 %reduce-scatter.2.cloned.1.call-start = ((), (), s32[]{:S(2)}) async-start(), calls=%async_computation.2 | async-start | bytes 6291456 | tf_op jit(solution)/shard_map/reduce_scatter | solution.py:147
  388.1 7.7 %copy-start.3 = (bf16[2048]{0:T(1024)(128)(2,1)S(1)}, bf16[2048]{0:T(1024)(128)(2,1)}, u32[]{:S(2)}) copy-start(bf16[2048]{0:T(1024)(128)(2,1)} %param.21) | copy-start | bytes 12292
Sparse Core Ops, SparseCore 0:
  396.0 15.8 reduce-scatter.1
where the time goes:
time: 425 us; the launch traced here: 421 us
  waiting for transfers between devices  170 us (40%)
  local copies, waits for them, and re-layouts  77.8 us (18%)
  matrix products  77.7 us (18%)
  loops' own time  49.5 us (12%)
  other arithmetic  26.4 us (6%)
  between operations  13.7 us (3%)
  starting transfers between devices  6.81 us (2%)
    all_to_all x1, waiting for transfers between devices, on_device(): lax.all_to_all(outgoing, 'req', split_axis=0, concat_axis=0, tiled=True)  154 us
    dot_general x24, matrix products, one_head(): jnp.einsum('bck,bke->bce', weights.astype(jnp.bfloat16), values_h, prefer...  47.4 us
    another operation x3, loops' own time, head_partials(): return lax.map(one_head, jnp.arange(head_count, dtype=jnp.int32))  45.4 us
    dot_general x24, matrix products, one_head(): jnp.einsum('ce,bke->bck', query_h, keys_h, preferred_element_type=jnp.flo...  22.5 us
    reduce_scatter x1, waiting for transfers between devices, on_device(): lax.psum_scatter(partial_terms, 'tp', scatter_dimension=1, tiled=True)  16 us
    dynamic_update_slice x4, local copies, waits for them, and re-layouts, block_partials(): lax.map(one_round, jnp.arange(rounds, dtype=jnp.int32))  15.2 us
    dynamic_slice x24, local copies, waits for them, and re-layouts, head_partials(): return lax.map(one_head, jnp.arange(head_count, dtype=jnp.int32))  14.6 us
    slice x2, local copies, waits for them, and re-layouts, on_device(): incoming[:, 1].reshape(request_count, page_size, head_count, HEAD_DIM)  12.5 us
  transfers between devices with their start and end apart: 2, of which 2 were waited for; matrix products, arithmetic and copies ran while one was open for 5% of the time, Pallas kernels for 0%

commit v1 on v0

v1 whole, which is shorter than its diff:
```python
import math
from functools import partial

import jax
import jax.numpy as jnp
from jax import lax
from jax.experimental import pallas as pl
from jax.experimental.pallas import tpu as pltpu
from jax.sharding import PartitionSpec as P

HEAD_DIM = 128
ROT = 32


NEG_FILL = -1e30


def rotate_rows(block, positions):
    row_count = block.shape[0]
    shaped = block.astype(jnp.float32).reshape(row_count, -1, HEAD_DIM)
    half_rot = ROT // 2
    frequency = 10000.0 ** (-2.0 * jnp.arange(half_rot, dtype=jnp.float32) / ROT)
    angles = positions.astype(jnp.float32)[:, None] * frequency[None, :]
    cosine = jnp.cos(angles)[:, None, :]
    sines = jnp.sin(angles)[:, None, :]
    first_half = shaped[:, :, :half_rot]
    second_half = shaped[:, :, half_rot:ROT]
    turned = jnp.concatenate(
        [
            first_half * cosine - second_half * sines,
            second_half * cosine + first_half * sines,
            shaped[:, :, ROT:],
        ],
        axis=2,
    )
    return turned.reshape(row_count, -1).astype(jnp.bfloat16)


def attention_kernel(nvalid_ref, q_ref, kl_ref, vl_ref, kp_ref, vp_ref, o_ref):
    score_scale = 1.0 / math.sqrt(HEAD_DIM)
    dims = (((1,), (1,)), ((), ()))
    q = q_ref[...]
    span = q.shape[0]
    page_size = kp_ref.shape[1]
    block_count = kp_ref.shape[0]

    s = lax.dot_general(q, kl_ref[...], dims, preferred_element_type=jnp.float32) * score_scale
    row = lax.broadcasted_iota(jnp.int32, (span, span), 0)
    col = lax.broadcasted_iota(jnp.int32, (span, span), 1)
    causal = row >= col
    s = jnp.where(causal, s, NEG_FILL)
    m = jnp.max(s, axis=1, keepdims=True)
    p = jnp.where(causal, jnp.exp(s - m), 0.0)
    l = jnp.sum(p, axis=1, keepdims=True)
    acc = jnp.dot(p.astype(jnp.bfloat16), vl_ref[...], preferred_element_type=jnp.float32)

    page_col = lax.broadcasted_iota(jnp.int32, (span, page_size), 1)

    def body(j, carry):
        m, l, acc = carry
        n = nvalid_ref[j]
        usable = page_col < n
        s = lax.dot_general(q, kp_ref[j], dims, preferred_element_type=jnp.float32) * score_scale
        s = jnp.where(usable, s, NEG_FILL)
        m_b = jnp.max(s, axis=1, keepdims=True)
        p = jnp.where(usable, jnp.exp(s - m_b), 0.0)
        l_b = jnp.sum(p, axis=1, keepdims=True)
        o_b = jnp.dot(p.astype(jnp.bfloat16), vp_ref[j], preferred_element_type=jnp.float32)
        m_new = jnp.maximum(m, m_b)
        a = jnp.exp(m - m_new)
        b = jnp.exp(m_b - m_new)
        return (m_new, l * a + l_b * b, acc * a + o_b * b)

    m, l, acc = lax.fori_loop(0, block_count, body, (m, l, acc))
    o_ref[...] = (acc / l).astype(o_ref.dtype)


def attend(nvalid, query_rot, key_rot, values, incoming):
    span, width = query_rot.shape
    head_count = width // HEAD_DIM
    block_count, _, page_size, _ = incoming.shape
    grid_spec = pltpu.PrefetchScalarGridSpec(
        num_scalar_prefetch=1,
        grid=(head_count,),
        in_specs=[
            pl.BlockSpec((span, HEAD_DIM), lambda h, nv: (0, h)),
            pl.BlockSpec((span, HEAD_DIM), lambda h, nv: (0, h)),
            pl.BlockSpec((span, HEAD_DIM), lambda h, nv: (0, h)),
            pl.BlockSpec((block_count, None, page_size, HEAD_DIM), lambda h, nv: (0, 0, 0, h)),
            pl.BlockSpec((block_count, None, page_size, HEAD_DIM), lambda h, nv: (0, 1, 0, h)),
        ],
        out_specs=pl.BlockSpec((span, HEAD_DIM), lambda h, nv: (0, h)),
    )
    return pl.pallas_call(
        attention_kernel,
        grid_spec=grid_spec,
        out_shape=jax.ShapeDtypeStruct((span, width), jnp.bfloat16),
    )(nvalid, query_rot, key_rot, values, incoming, incoming)


def on_device(new_queries, new_keys, new_values, kv_pages, page_table, cache_len, w_out, out_bias):
    own_index = lax.axis_index("req")
    tp_index = lax.axis_index("tp")
    tp_count = lax.axis_size("tp")
    span_len = new_queries.shape[0]
    page_count = kv_pages.shape[0]
    page_size = kv_pages.shape[2]
    request_count = page_table.shape[0]
    slot_count = page_table.shape[1]
    out_cols = w_out.shape[1] // tp_count

    w_recv = []
    for shift in range(1, tp_count):
        target = (tp_index + shift) % tp_count
        piece = lax.dynamic_slice_in_dim(w_out, target * out_cols, out_cols, axis=1)
        perm = [(i, (i + shift) % tp_count) for i in range(tp_count)]
        w_recv.append(lax.ppermute(piece, "tp", perm))
    w_mine = lax.dynamic_slice_in_dim(w_out, tp_index * out_cols, out_cols, axis=1)

    slot_ids = jnp.arange(slot_count, dtype=jnp.int32)
    request_ids = jnp.arange(request_count, dtype=jnp.int32)
    owners = jnp.where(page_table >= 0, page_table // page_count, -1)
    held_here = owners == own_index
    local_page = jnp.sum(jnp.where(held_here, page_table - own_index * page_count, 0), axis=1)
    outgoing = jnp.take(kv_pages, local_page, axis=0)
    incoming = lax.all_to_all(outgoing, "req", split_axis=0, concat_axis=0, tiled=True)

    own_length = lax.dynamic_index_in_dim(cache_len, own_index, 0, keepdims=False)
    positions = own_length + jnp.arange(span_len, dtype=jnp.int32)
    query_rot = rotate_rows(new_queries, positions)
    key_rot = rotate_rows(new_keys, positions)

    own_row = lax.dynamic_index_in_dim(page_table, own_index, 0, keepdims=False)
    row_owner = jnp.where(own_row >= 0, own_row // page_count, -1)
    matches = row_owner[None, :] == request_ids[:, None]
    present = jnp.any(matches, axis=1)
    slot_of = jnp.sum(jnp.where(matches, slot_ids[None, :], 0), axis=1)
    nvalid = jnp.where(present, jnp.clip(own_length - slot_of * page_size, 0, page_size), 0)
    nvalid = nvalid.astype(jnp.int32)

    attended = attend(nvalid, query_rot, key_rot, new_values, incoming)

    summed = jnp.dot(attended, w_mine, preferred_element_type=jnp.float32)
    for shift in range(1, tp_count):
        perm = [(i, (i + shift) % tp_count) for i in range(tp_count)]
        other = lax.ppermute(attended, "tp", perm)
        summed = summed + jnp.dot(other, w_recv[shift - 1], preferred_element_type=jnp.float32)
    return (summed + out_bias.astype(jnp.float32)).astype(jnp.bfloat16)


def solution(mesh):
    return jax.shard_map(
        on_device,
        mesh=mesh,
        in_specs=(
            P("req", "tp"),
            P("req", "tp"),
            P("req", "tp"),
            P("req", None, None, "tp"),
            P(),
            P(),
            P("tp", None),
            P("tp"),
        ),
        out_specs=P("req", "tp"),
        check_vma=False,
    )
```

time: 425 us -> 282 us (0.66)
  matrix products: 77.7 us -> 8.09 us
  local copies, waits for them, and re-layouts: 77.8 us -> 16.2 us
  Pallas kernels: 0 us -> 58.8 us
  loops' own time: 49.5 us -> 0 us
  between operations: 13.7 us -> 0.15 us
  other arithmetic: 26.4 us -> 12.9 us
    dot_general x49 -> x2, matrix products: 77.7 us -> 8.09 us  [the longest x1 4.49 us: on_device(): jnp.dot(other, w_recv[shift - 1], preferred_element_type=jnp.float32)]
    pallas_call x0 -> x1, Pallas kernels: none -> 58.8 us  [attend(): pl.pallas_call(attention_kernel, grid_spec=grid_spec, out_shape=jax.Shape...]
    another operation x4 -> x0, loops' own time: 49.5 us -> none  [the longest x3 45.4 us: head_partials(): return lax.map(one_head, jnp.arange(head_count, dtype=jnp.int32))]
    dynamic_slice x34 -> x1, local copies, waits for them, and re-layouts: 33.3 us -> 4.84 us  [on_device(): piece = lax.dynamic_slice_in_dim(w_out, target * out_cols, out_cols, axis=1)]
    all_to_all x1, waiting for transfers between devices: 154 us -> 174 us  [on_device(): lax.all_to_all(outgoing, 'req', split_axis=0, concat_axis=0, tiled=True)]
    slice x3 -> x0, local copies, waits for them, and re-layouts: 18.9 us -> none  [the longest x2 12.5 us: on_device(): incoming[:, 1].reshape(request_count, page_size, head_count, HEAD_DIM)]
    reduce_scatter x1 -> x0, waiting for transfers between devices: 16 us -> none  [on_device(): lax.psum_scatter(partial_terms, 'tp', scatter_dimension=1, tiled=True)]
    dynamic_update_slice x28 -> x0, local copies, waits for them, and re-layouts: 15.5 us -> none  [the longest x4 15.2 us: block_partials(): lax.map(one_round, jnp.arange(rounds, dtype=jnp.int32))]
  transfers between devices with their start and end apart: 2 -> 3, of which waited for: 2 -> 1; matrix products, arithmetic and copies ran while one was open for 5% -> 6% of each run, Pallas kernels for 0% -> 21%
where the time goes in v1:
time: 282 us; the launch traced here: 280 us
  waiting for transfers between devices  174 us (62%)
  Pallas kernels  58.8 us (21%)
  local copies, waits for them, and re-layouts  16.2 us (6%)
  other arithmetic  12.9 us (5%)
  starting transfers between devices  9.73 us (3%)
  matrix products  8.09 us (3%)
    all_to_all x1, waiting for transfers between devices, on_device(): lax.all_to_all(outgoing, 'req', split_axis=0, concat_axis=0, tiled=True)  174 us
    pallas_call x1, Pallas kernels, attend(): pl.pallas_call(attention_kernel, grid_spec=grid_spec, out_shape=jax.Shape...  58.8 us
    gather x1, local copies, waits for them, and re-layouts, on_device(): outgoing = jnp.take(kv_pages, local_page, axis=0)  8.15 us
    select_n x2, other arithmetic, on_device(): outgoing = jnp.take(kv_pages, local_page, axis=0)  7.48 us
    all_to_all x1, starting transfers between devices, on_device(): lax.all_to_all(outgoing, 'req', split_axis=0, concat_axis=0, tiled=True)  6.64 us
  transfers between devices with their start and end apart: 3, of which 1 were waited for; matrix products, arithmetic and copies ran while one was open for 6% of the time, Pallas kernels for 21%

profile of v1, /device:TPU:11, one launch (start us, length us, event | category | flops | bytes accessed | tf_op | source)
XLA Modules:
  0.0 279.6 jit_solution(10566051142785661171)
XLA Ops:
  0.0 0.8 select_reduce_fusion
  0.8 8.2 %gather_fusion = bf16[16,2,128,1024]{3,2,1,0:T(8,128)(2,1)} fusion(bf16[16,2,128,1024]{3,2,1,0:T(8,128)(2,1)} %param.11, s32[1024]{0:T(1024)S(1)} %pad_clamp_fusion), kind=kCustom, calls=%fused_computation | custom fusion | bytes 16777280 | tf_op jit(solution)/shard_map/jit(_take)/gather | solution.py:125
  9.0 7.5 %broadcast_select_fusion = bf16[16,2,128,1024]{3,2,1,0:T(8,128)(2,1)} fusion(bf16[16,2,128,1024]{3,2,1,0:T(8,128)(2,1)} %gather_fusion, pred[16]{0:T(512)(128)(4,1)S(1)} %compare_and_fusion), kind=kLoop, calls=%fused_computation.1 | loop fusion | flops 4194304 | bytes 16777232 | tf_op jit(solution)/shard_map/jit(_take)/select_n | solution.py:125
  16.5 6.6 %all-to-all-start = ((bf16[16,2,128,1024]{3,2,1,0:T(8,128)(2,1)}), bf16[16,2,128,1024]{3,2,1,0:T(8,128)(2,1)}, u32[]{:S(2)}, u32[]{:S(2)}) async-start(bf16[16,2,128,1024]{3,2,1,0:T(8,128)(2,1)} %broadcast_select_fusion), calls=%async_computation | async-start | bytes 16777216 | tf_op jit(solution)/shard_map/all_to_all | solution.py:126
  23.1 0.0 copy-start
  23.1 0.0 copy-start.1
  23.1 4.8 %constant_dynamic-slice_fusion = bf16[1024,2048]{1,0:T(8,128)(2,1)} fusion(bf16[1024,4096]{1,0:T(8,128)(2,1)} %param.14, s32[]{:T(128)S(6)} %select_n.81), kind=kLoop, calls=%fused_computation.41 | loop fusion | bytes 8388612 | tf_op jit(solution)/shard_map/dynamic_slice | solution.py:115
  28.0 1.2 collective-permute-start.1
  29.2 0.6 dynamic_slice.15
  29.8 0.6 add_convert_fusion.2
  30.3 0.1 multiply_cosine_fusion
  30.5 0.1 copy.10
  30.6 0.1 copy.9
  30.7 0.1 copy.13
  30.8 0.1 copy.11
  30.9 0.2 slice.30
  31.1 0.2 slice.33
  31.3 0.1 bitcast_convert_fusion
  31.4 0.1 bitcast_convert_fusion.1
  31.6 0.7 subtract_convert_fusion
  32.3 1.0 pad_maximum_fusion
  33.3 1.0 copy.17
  34.2 0.9 copy.18
  35.1 0.7 fusion.11
  35.8 0.1 fusion.7
  35.9 0.1 select_reduce_fusion.1
  36.0 1.1 clamp_select_fusion.nvalid_ref
  37.1 173.6 %all-to-all-done.kp_ref.vp_ref = bf16[16,2,128,1024]{3,2,1,0:T(8,128)(2,1)} async-done(((bf16[16,2,128,1024]{3,2,1,0:T(8,128)(2,1)}), bf16[16,2,128,1024]{3,2,1,0:T(8,128)(2,1)}, u32[]{:S(2)}, u32[]{:S(2)}) %all-to-all-start) | async-done | bytes 8388640 | tf_op jit(solution)/shard_map/all_to_all | solution.py:126
  210.7 58.8 %shard_map.82 = bf16[256,1024]{1,0:T(8,128)(2,1)} custom-call(s32[16]{0:T(128)} %clamp_select_fusion.nvalid_ref, bf16[256,1024]{1,0:T(8,128)(2,1)} %bitcast.27, bf16[256,1024]{1,0:T(8,128)(2,1)} %bitcast.26, bf16[256,1024]{1,0:T(8,128)(2,1)} %vl_ref.1, bf16[16,2,128,1024]{3,2,1,0:T(8,128)(2,1)} %all-to-all-done.kp_ref.vp_ref, ...), custom_call_target="tpu_custom_call" | custom-call | tf_op jit(solution)/shard_map/pallas_call | solution.py:94
  269.6 1.9 collective-permute-start
  271.4 3.6 %fusion = f32[256,2048]{1,0:T(8,128)S(1)} fusion(bf16[256,1024]{1,0:T(8,128)(2,1)} %shard_map.82, bf16[1024,4096]{1,0:T(8,128)(2,1)} %param.14, s32[]{:T(128)S(6)} %select_n.79), kind=kOutput, calls=%fused_computation.2 | convolution fusion | flops 1073741824 | bytes 6815748 | tf_op jit(solution)/shard_map/dot_general | solution.py:143
  275.1 4.5 %fusion.3 = bf16[256,2048]{1,0:T(8,128)(2,1)} fusion(f32[256,2048]{1,0:T(8,128)S(1)} %fusion, bf16[256,1024]{1,0:T(8,128)(2,1)S(1)} %collective-permute-done, bf16[1024,2048]{1,0:T(8,128)(2,1)} %collective-permute-done.1, f32[2048]{0:T(1024)S(1)} %convert_element_type.25), kind=kOutput, calls=%fused_computation.6 | convolution fusion | flops 1075314688 | bytes 7872512 | tf_op jit(solution)/shard_map/dot_general | solution.py:147
  (13 shorter events, 0.0 us)
Async XLA Ops:
  16.5 194.2 %all-to-all-start = ((bf16[16,2,128,1024]{3,2,1,0:T(8,128)(2,1)}), bf16[16,2,128,1024]{3,2,1,0:T(8,128)(2,1)}, u32[]{:S(2)}, u32[]{:S(2)}) async-start(bf16[16,2,128,1024]{3,2,1,0:T(8,128)(2,1)} %broadcast_select_fusion), calls=%async_computation | async-start | bytes 16777216 | tf_op jit(solution)/shard_map/all_to_all | solution.py:126
  23.1 6.1 %copy-start.3 = (s32[16]{0:T(128)S(1)}, s32[16]{0:T(128)}, u32[]{:S(2)}) copy-start(s32[16]{0:T(128)} %param.13) | copy-start | bytes 196
  23.1 7.6 %copy-start = (bf16[256,1024]{1,0:T(8,128)(2,1)S(1)}, bf16[256,1024]{1,0:T(8,128)(2,1)}, u32[]{:S(2)}) copy-start(bf16[256,1024]{1,0:T(8,128)(2,1)} %param.9) | copy-start | bytes 1572868
  23.1 7.7 %copy-start.1 = (bf16[256,1024]{1,0:T(8,128)(2,1)S(1)}, bf16[256,1024]{1,0:T(8,128)(2,1)}, u32[]{:S(2)}) copy-start(bf16[256,1024]{1,0:T(8,128)(2,1)} %param.8) | copy-start | bytes 1572868
  28.0 247.1 %collective-permute-start.1 = (bf16[1024,2048]{1,0:T(8,128)(2,1)}, bf16[1024,2048]{1,0:T(8,128)(2,1)}, u32[]{:S(2)}, u32[]{:S(2)}) collective-permute-start(bf16[1024,2048]{1,0:T(8,128)(2,1)} %constant_dynamic-slice_fusion), channel_id=1, source_target_pairs={{0,1},{1,0},{2,3},{3,2},{4,5},{5,4},{6,7},{7,6},{8,9},{9,8},{10,11... | collective-permute-start | bytes 12582920 | tf_op jit(solution)/shard_map/ppermute | solution.py:117
  210.7 60.7 %copy-start.2 = (bf16[2048]{0:T(1024)(128)(2,1)S(1)}, bf16[2048]{0:T(1024)(128)(2,1)}, u32[]{:S(2)}) copy-start(bf16[2048]{0:T(1024)(128)(2,1)} %param.15) | copy-start | bytes 12292
  269.6 5.5 %collective-permute-start = (bf16[256,1024]{1,0:T(8,128)(2,1)}, bf16[256,1024]{1,0:T(8,128)(2,1)S(1)}, u32[]{:S(2)}, u32[]{:S(2)}) collective-permute-start(bf16[256,1024]{1,0:T(8,128)(2,1)} %shard_map.82), channel_id=1, source_target_pairs={{0,1},{1,0},{2,3},{3,2},{4,5},{5,4},{6,7},{7,6},{8,9},{9,8},{10,11... | collective-permute-start | bytes 1572872 | tf_op jit(solution)/shard_map/ppermute | solution.py:146

commit v2 on v1

--- a/solution.py
+++ b/solution.py
@@ -36,66 +36,48 @@
     return turned.reshape(row_count, -1).astype(jnp.bfloat16)
 
 
-def attention_kernel(nvalid_ref, q_ref, kl_ref, vl_ref, kp_ref, vp_ref, o_ref):
+def attention_kernel(q_ref, kl_ref, vl_ref, kp_ref, vp_ref, ok_ref, o_ref):
     score_scale = 1.0 / math.sqrt(HEAD_DIM)
     dims = (((1,), (1,)), ((), ()))
     q = q_ref[...]
     span = q.shape[0]
-    page_size = kp_ref.shape[1]
-    block_count = kp_ref.shape[0]
+    block_count, page_size, _ = kp_ref.shape
+    keys_p = kp_ref[...].reshape(block_count * page_size, HEAD_DIM)
+    values_p = vp_ref[...].reshape(block_count * page_size, HEAD_DIM)
 
-    s = lax.dot_general(q, kl_ref[...], dims, preferred_element_type=jnp.float32) * score_scale
+    s_loc = lax.dot_general(q, kl_ref[...], dims, preferred_element_type=jnp.float32) * score_scale
     row = lax.broadcasted_iota(jnp.int32, (span, span), 0)
     col = lax.broadcasted_iota(jnp.int32, (span, span), 1)
-    causal = row >= col
-    s = jnp.where(causal, s, NEG_FILL)
-    m = jnp.max(s, axis=1, keepdims=True)
-    p = jnp.where(causal, jnp.exp(s - m), 0.0)
-    l = jnp.sum(p, axis=1, keepdims=True)
-    acc = jnp.dot(p.astype(jnp.bfloat16), vl_ref[...], preferred_element_type=jnp.float32)
-
-    page_col = lax.broadcasted_iota(jnp.int32, (span, page_size), 1)
-
-    def body(j, carry):
-        m, l, acc = carry
-        n = nvalid_ref[j]
-        usable = page_col < n
-        s = lax.dot_general(q, kp_ref[j], dims, preferred_element_type=jnp.float32) * score_scale
-        s = jnp.where(usable, s, NEG_FILL)
-        m_b = jnp.max(s, axis=1, keepdims=True)
-        p = jnp.where(usable, jnp.exp(s - m_b), 0.0)
-        l_b = jnp.sum(p, axis=1, keepdims=True)
-        o_b = jnp.dot(p.astype(jnp.bfloat16), vp_ref[j], preferred_element_type=jnp.float32)
-        m_new = jnp.maximum(m, m_b)
-        a = jnp.exp(m - m_new)
-        b = jnp.exp(m_b - m_new)
-        return (m_new, l * a + l_b * b, acc * a + o_b * b)
-
-    m, l, acc = lax.fori_loop(0, block_count, body, (m, l, acc))
+    s_loc = jnp.where(row >= col, s_loc, NEG_FILL)
+    s_pg = lax.dot_general(q, keys_p, dims, preferred_element_type=jnp.float32) * score_scale
+    s_pg = jnp.where(ok_ref[...] > 0, s_pg, NEG_FILL)
+    m = jnp.maximum(jnp.max(s_loc, axis=1, keepdims=True), jnp.max(s_pg, axis=1, keepdims=True))
+    p_loc = jnp.exp(s_loc - m)
+    p_pg = jnp.exp(s_pg - m)
+    l = jnp.sum(p_loc, axis=1, keepdims=True) + jnp.sum(p_pg, axis=1, keepdims=True)
+    acc = jnp.dot(p_loc.astype(jnp.bfloat16), vl_ref[...], preferred_element_type=jnp.float32)
+    acc = acc + jnp.dot(p_pg.astype(jnp.bfloat16), values_p, preferred_element_type=jnp.float32)
     o_ref[...] = (acc / l).astype(o_ref.dtype)
 
 
-def attend(nvalid, query_rot, key_rot, values, incoming):
+def attend(key_ok, query_rot, key_rot, values, incoming):
     span, width = query_rot.shape
     head_count = width // HEAD_DIM
     block_count, _, page_size, _ = incoming.shape
-    grid_spec = pltpu.PrefetchScalarGridSpec(
-        num_scalar_prefetch=1,
+    return pl.pallas_call(
+        attention_kernel,
         grid=(head_count,),
         in_specs=[
-            pl.BlockSpec((span, HEAD_DIM), lambda h, nv: (0, h)),
-            pl.BlockSpec((span, HEAD_DIM), lambda h, nv: (0, h)),
-            pl.BlockSpec((span, HEAD_DIM), lambda h, nv: (0, h)),
-            pl.BlockSpec((block_count, None, page_size, HEAD_DIM), lambda h, nv: (0, 0, 0, h)),
-            pl.BlockSpec((block_count, None, page_size, HEAD_DIM), lambda h, nv: (0, 1, 0, h)),
+            pl.BlockSpec((span, HEAD_DIM), lambda h: (0, h)),
+            pl.BlockSpec((span, HEAD_DIM), lambda h: (0, h)),
+            pl.BlockSpec((span, HEAD_DIM), lambda h: (0, h)),
+            pl.BlockSpec((block_count, None, page_size, HEAD_DIM), lambda h: (0, 0, 0, h)),
+            pl.BlockSpec((block_count, None, page_size, HEAD_DIM), lambda h: (0, 1, 0, h)),
+            pl.BlockSpec((1, block_count * page_size), lambda h: (0, 0)),
         ],
-        out_specs=pl.BlockSpec((span, HEAD_DIM), lambda h, nv: (0, h)),
-    )
-    return pl.pallas_call(
-        attention_kernel,
-        grid_spec=grid_spec,
+        out_specs=pl.BlockSpec((span, HEAD_DIM), lambda h: (0, h)),
         out_shape=jax.ShapeDtypeStruct((span, width), jnp.bfloat16),
-    )(nvalid, query_rot, key_rot, values, incoming, incoming)
+    )(query_rot, key_rot, values, incoming, incoming, key_ok)
 
 
 def on_device(new_queries, new_keys, new_values, kv_pages, page_table, cache_len, w_out, out_bias):
@@ -122,7 +104,7 @@
     owners = jnp.where(page_table >= 0, page_table // page_count, -1)
     held_here = owners == own_index
     local_page = jnp.sum(jnp.where(held_here, page_table - own_index * page_count, 0), axis=1)
-    outgoing = jnp.take(kv_pages, local_page, axis=0)
+    outgoing = jnp.take(kv_pages, local_page, axis=0, mode="clip")
     incoming = lax.all_to_all(outgoing, "req", split_axis=0, concat_axis=0, tiled=True)
 
     own_length = lax.dynamic_index_in_dim(cache_len, own_index, 0, keepdims=False)
@@ -136,9 +118,10 @@
     present = jnp.any(matches, axis=1)
     slot_of = jnp.sum(jnp.where(matches, slot_ids[None, :], 0), axis=1)
     nvalid = jnp.where(present, jnp.clip(own_length - slot_of * page_size, 0, page_size), 0)
-    nvalid = nvalid.astype(jnp.int32)
+    within = jnp.arange(page_size, dtype=jnp.int32)
+    key_ok = (within[None, :] < nvalid[:, None]).astype(jnp.int32).reshape(1, request_count * page_size)
 
-    attended = attend(nvalid, query_rot, key_rot, new_values, incoming)
+    attended = attend(key_ok, query_rot, key_rot, new_values, incoming)
 
     summed = jnp.dot(attended, w_mine, preferred_element_type=jnp.float32)
     for shift in range(1, tp_count):

time: 282 us -> 229 us (0.81)
  Pallas kernels: 58.8 us -> 13.1 us
  other arithmetic: 12.9 us -> 5.64 us
    pallas_call x1, Pallas kernels: 58.8 us -> 13.1 us  [attend(): pl.pallas_call(attention_kernel, grid=(head_count,), in_specs=[pl.BlockSp...]
    select_n x2 -> x0, other arithmetic: 7.48 us -> none  [on_device(): outgoing = jnp.take(kv_pages, local_page, axis=0)]
  transfers between devices with their start and end apart: 3 -> 3, of which waited for: 1 -> 1; matrix products, arithmetic and copies ran while one was open for 6% -> 7% of each run, Pallas kernels for 21% -> 6%
where the time goes in v2:
time: 229 us; the launch traced here: 226 us
  waiting for transfers between devices  173 us (76%)
  local copies, waits for them, and re-layouts  16.3 us (7%)
  Pallas kernels  13.1 us (6%)
  starting transfers between devices  9.73 us (4%)
  matrix products  8.09 us (4%)
  other arithmetic  5.64 us (2%)
    all_to_all x1, waiting for transfers between devices, on_device(): lax.all_to_all(outgoing, 'req', split_axis=0, concat_axis=0, tiled=True)  173 us
    pallas_call x1, Pallas kernels, attend(): pl.pallas_call(attention_kernel, grid=(head_count,), in_specs=[pl.BlockSp...  13.1 us
    gather x1, local copies, waits for them, and re-layouts, on_device(): outgoing = jnp.take(kv_pages, local_page, axis=0, mode='clip')  8.15 us
    all_to_all x1, starting transfers between devices, on_device(): lax.all_to_all(outgoing, 'req', split_axis=0, concat_axis=0, tiled=True)  6.64 us
    dynamic_slice x1, local copies, waits for them, and re-layouts, on_device(): piece = lax.dynamic_slice_in_dim(w_out, target * out_cols, out_cols, axis=1)  4.83 us
  transfers between devices with their start and end apart: 3, of which 1 were waited for; matrix products, arithmetic and copies ran while one was open for 7% of the time, Pallas kernels for 6%

profile of v2, /device:TPU:11, one launch (start us, length us, event | category | flops | bytes accessed | tf_op | source)
XLA Modules:
  0.0 226.3 jit_solution(5714485620796228838)
XLA Ops:
  0.0 0.8 select_reduce_fusion.1
  0.8 8.2 %gather_fusion = bf16[16,2,128,1024]{3,2,1,0:T(8,128)(2,1)} fusion(bf16[16,2,128,1024]{3,2,1,0:T(8,128)(2,1)} %param.11, s32[1024]{0:T(1024)S(1)} %pad_clamp_fusion), kind=kCustom, calls=%fused_computation | custom fusion | bytes 16777280 | tf_op jit(solution)/shard_map/jit(_take)/gather | solution.py:107
  9.0 6.6 %all-to-all-start = ((bf16[16,2,128,1024]{3,2,1,0:T(8,128)(2,1)}), bf16[16,2,128,1024]{3,2,1,0:T(8,128)(2,1)}, u32[]{:S(2)}, u32[]{:S(2)}) async-start(bf16[16,2,128,1024]{3,2,1,0:T(8,128)(2,1)} %gather_fusion), calls=%async_computation | async-start | bytes 16777216 | tf_op jit(solution)/shard_map/all_to_all | solution.py:108
  15.6 0.0 copy-start.1
  15.6 0.0 copy-start.3
  15.6 4.8 %constant_dynamic-slice_fusion.1 = bf16[1024,2048]{1,0:T(8,128)(2,1)} fusion(bf16[1024,4096]{1,0:T(8,128)(2,1)} %param.14, s32[]{:T(128)S(6)} %select_n.63), kind=kLoop, calls=%fused_computation.40 | loop fusion | bytes 8388612 | tf_op jit(solution)/shard_map/dynamic_slice | solution.py:97
  20.5 1.2 collective-permute-start.1
  21.7 0.1 copy.11
  21.8 0.2 slice.30
  22.0 0.1 copy.13
  22.2 0.6 dynamic_slice.14
  22.8 0.6 add_convert_fusion.2
  23.3 0.1 multiply_cosine_fusion
  23.5 0.1 copy.10
  23.6 0.1 copy.9
  23.7 0.2 slice.33
  23.9 0.1 bitcast_convert_fusion
  24.0 0.1 bitcast_convert_fusion.1
  24.1 0.7 subtract_convert_fusion
  24.9 1.0 pad_maximum_fusion
  25.8 0.9 copy.18
  26.7 1.0 copy.17
  27.7 0.7 fusion.11
  28.4 0.1 fusion.7
  28.5 0.1 select_reduce_fusion
  28.6 0.6 clamp_select_fusion
  29.2 0.7 fusion.9
  29.9 173.3 %all-to-all-done.kp_ref.vp_ref = bf16[16,2,128,1024]{3,2,1,0:T(8,128)(2,1)} async-done(((bf16[16,2,128,1024]{3,2,1,0:T(8,128)(2,1)}), bf16[16,2,128,1024]{3,2,1,0:T(8,128)(2,1)}, u32[]{:S(2)}, u32[]{:S(2)}) %all-to-all-start) | async-done | bytes 8388640 | tf_op jit(solution)/shard_map/all_to_all | solution.py:108
  203.2 13.1 %shard_map.82 = bf16[256,1024]{1,0:T(8,128)(2,1)} custom-call(bf16[256,1024]{1,0:T(8,128)(2,1)} %bitcast.23, bf16[256,1024]{1,0:T(8,128)(2,1)} %bitcast.24, bf16[256,1024]{1,0:T(8,128)(2,1)} %vl_ref.1, bf16[16,2,128,1024]{3,2,1,0:T(8,128)(2,1)} %all-to-all-done.kp_ref.vp_ref, bf16[16,2,128,1024]{3,2,1,0:T(8,128)(2,1)} %all-to-all-done.kp_ref.vp_ref, ...), custom_call_target="tpu_custom_call" | custom-call | tf_op jit(solution)/shard_map/pallas_call | solution.py:67
  216.3 1.9 collective-permute-start
  218.2 3.6 %fusion = f32[256,2048]{1,0:T(8,128)S(1)} fusion(bf16[256,1024]{1,0:T(8,128)(2,1)} %shard_map.82, bf16[1024,4096]{1,0:T(8,128)(2,1)} %param.14, s32[]{:T(128)S(6)} %select_n.61), kind=kOutput, calls=%fused_computation.1 | convolution fusion | flops 1073741824 | bytes 6815748 | tf_op jit(solution)/shard_map/dot_general | solution.py:126
  221.8 4.5 %fusion.3 = bf16[256,2048]{1,0:T(8,128)(2,1)} fusion(f32[256,2048]{1,0:T(8,128)S(1)} %fusion, bf16[256,1024]{1,0:T(8,128)(2,1)S(1)} %collective-permute-done, bf16[1024,2048]{1,0:T(8,128)(2,1)} %collective-permute-done.1, f32[2048]{0:T(1024)S(1)} %convert_element_type.40), kind=kOutput, calls=%fused_computation.5 | convolution fusion | flops 1075314688 | bytes 7872512 | tf_op jit(solution)/shard_map/dot_general | solution.py:130
  (11 shorter events, 0.0 us)
Async XLA Ops:
  9.0 194.2 %all-to-all-start = ((bf16[16,2,128,1024]{3,2,1,0:T(8,128)(2,1)}), bf16[16,2,128,1024]{3,2,1,0:T(8,128)(2,1)}, u32[]{:S(2)}, u32[]{:S(2)}) async-start(bf16[16,2,128,1024]{3,2,1,0:T(8,128)(2,1)} %gather_fusion), calls=%async_computation | async-start | bytes 16777216 | tf_op jit(solution)/shard_map/all_to_all | solution.py:108
  15.6 6.1 %copy-start = (bf16[256,1024]{1,0:T(8,128)(2,1)S(1)}, bf16[256,1024]{1,0:T(8,128)(2,1)}, u32[]{:S(2)}) copy-start(bf16[256,1024]{1,0:T(8,128)(2,1)} %param.8) | copy-start | bytes 1572868
  15.6 6.4 %copy-start.1 = (bf16[256,1024]{1,0:T(8,128)(2,1)S(1)}, bf16[256,1024]{1,0:T(8,128)(2,1)}, u32[]{:S(2)}) copy-start(bf16[256,1024]{1,0:T(8,128)(2,1)} %param.9) | copy-start | bytes 1572868
  15.6 6.5 %copy-start.3 = (s32[16]{0:T(128)S(1)}, s32[16]{0:T(128)}, u32[]{:S(2)}) copy-start(s32[16]{0:T(128)} %param.13) | copy-start | bytes 196
  20.5 201.3 %collective-permute-start.1 = (bf16[1024,2048]{1,0:T(8,128)(2,1)}, bf16[1024,2048]{1,0:T(8,128)(2,1)}, u32[]{:S(2)}, u32[]{:S(2)}) collective-permute-start(bf16[1024,2048]{1,0:T(8,128)(2,1)} %constant_dynamic-slice_fusion.1), channel_id=1, source_target_pairs={{0,1},{1,0},{2,3},{3,2},{4,5},{5,4},{6,7},{7,6},{8,9},{9,8},{10,11... | collective-permute-start | bytes 12582920 | tf_op jit(solution)/shard_map/ppermute | solution.py:99
  203.2 15.0 %copy-start.2 = (bf16[2048]{0:T(1024)(128)(2,1)S(1)}, bf16[2048]{0:T(1024)(128)(2,1)}, u32[]{:S(2)}) copy-start(bf16[2048]{0:T(1024)(128)(2,1)} %param.15) | copy-start | bytes 12292
  216.3 5.5 %collective-permute-start = (bf16[256,1024]{1,0:T(8,128)(2,1)}, bf16[256,1024]{1,0:T(8,128)(2,1)S(1)}, u32[]{:S(2)}, u32[]{:S(2)}) collective-permute-start(bf16[256,1024]{1,0:T(8,128)(2,1)} %shard_map.82), channel_id=1, source_target_pairs={{0,1},{1,0},{2,3},{3,2},{4,5},{5,4},{6,7},{7,6},{8,9},{9,8},{10,11... | collective-permute-start | bytes 1572872 | tf_op jit(solution)/shard_map/ppermute | solution.py:129

commit v3 on v2

v3 whole, which is shorter than its diff:
```python
import math
from functools import partial

import jax
import jax.numpy as jnp
from jax import lax
from jax.experimental import pallas as pl
from jax.experimental.pallas import tpu as pltpu
from jax.sharding import PartitionSpec as P

HEAD_DIM = 128
ROT = 32


NEG_FILL = -1e30


def rotate_rows(block, positions):
    row_count = block.shape[0]
    shaped = block.astype(jnp.float32).reshape(row_count, -1, HEAD_DIM)
    half_rot = ROT // 2
    frequency = 10000.0 ** (-2.0 * jnp.arange(half_rot, dtype=jnp.float32) / ROT)
    angles = positions.astype(jnp.float32)[:, None] * frequency[None, :]
    cosine = jnp.cos(angles)[:, None, :]
    sines = jnp.sin(angles)[:, None, :]
    first_half = shaped[:, :, :half_rot]
    second_half = shaped[:, :, half_rot:ROT]
    turned = jnp.concatenate(
        [
            first_half * cosine - second_half * sines,
            second_half * cosine + first_half * sines,
            shaped[:, :, ROT:],
        ],
        axis=2,
    )
    return turned.reshape(row_count, -1).astype(jnp.bfloat16)


def attention_kernel(*refs, with_local):
    if with_local:
        q_ref, kl_ref, vl_ref, kp_ref, vp_ref, ok_ref, o_ref, m_ref, l_ref = refs
    else:
        q_ref, kp_ref, vp_ref, ok_ref, o_ref, m_ref, l_ref = refs
    score_scale = 1.0 / math.sqrt(HEAD_DIM)
    dims = (((1,), (1,)), ((), ()))
    q = q_ref[...]
    span = q.shape[0]
    block_count, page_size, _ = kp_ref.shape
    keys_p = kp_ref[...].reshape(block_count * page_size, HEAD_DIM)
    values_p = vp_ref[...].reshape(block_count * page_size, HEAD_DIM)

    s_pg = lax.dot_general(q, keys_p, dims, preferred_element_type=jnp.float32) * score_scale
    s_pg = jnp.where(ok_ref[...] > 0, s_pg, NEG_FILL)
    m = jnp.max(s_pg, axis=1, keepdims=True)
    if with_local:
        s_loc = lax.dot_general(q, kl_ref[...], dims, preferred_element_type=jnp.float32) * score_scale
        row = lax.broadcasted_iota(jnp.int32, (span, span), 0)
        col = lax.broadcasted_iota(jnp.int32, (span, span), 1)
        s_loc = jnp.where(row >= col, s_loc, NEG_FILL)
        m = jnp.maximum(m, jnp.max(s_loc, axis=1, keepdims=True))
    p_pg = jnp.exp(s_pg - m)
    l = jnp.sum(p_pg, axis=1, keepdims=True)
    acc = jnp.dot(p_pg.astype(jnp.bfloat16), values_p, preferred_element_type=jnp.float32)
    if with_local:
        p_loc = jnp.exp(s_loc - m)
        l = l + jnp.sum(p_loc, axis=1, keepdims=True)
        acc = acc + jnp.dot(p_loc.astype(jnp.bfloat16), vl_ref[...], preferred_element_type=jnp.float32)
    o_ref[...] = (acc / l).astype(o_ref.dtype)
    m_ref[...] = m
    l_ref[...] = l


def attend(key_ok, query_rot, incoming, which, out_dtype, local=None):
    span, width = query_rot.shape
    head_count = width // HEAD_DIM
    block_count = incoming.shape[0]
    page_size = incoming.shape[3]
    col_spec = pl.BlockSpec((span, HEAD_DIM), lambda h: (0, h))
    page_specs = [
        pl.BlockSpec((block_count, None, None, page_size, HEAD_DIM), lambda h: (0, which, 0, 0, h)),
        pl.BlockSpec((block_count, None, None, page_size, HEAD_DIM), lambda h: (0, which, 1, 0, h)),
        pl.BlockSpec((1, block_count * page_size), lambda h: (0, 0)),
    ]
    stat_spec = pl.BlockSpec((None, span, 1), lambda h: (h, 0, 0))
    if local is None:
        in_specs = [col_spec] + page_specs
        operands = (query_rot, incoming, incoming, key_ok)
    else:
        in_specs = [col_spec, col_spec, col_spec] + page_specs
        operands = (query_rot, local[0], local[1], incoming, incoming, key_ok)
    return pl.pallas_call(
        partial(attention_kernel, with_local=local is not None),
        grid=(head_count,),
        in_specs=in_specs,
        out_specs=[col_spec, stat_spec, stat_spec],
        out_shape=[
            jax.ShapeDtypeStruct((span, width), out_dtype),
            jax.ShapeDtypeStruct((head_count, span, 1), jnp.float32),
            jax.ShapeDtypeStruct((head_count, span, 1), jnp.float32),
        ],
    )(*operands)


def usable_keys(page_table, request, length, source_base, source_count, page_count, page_size):
    row = lax.dynamic_index_in_dim(page_table, request, 0, keepdims=False)
    row_owner = jnp.where(row >= 0, row // page_count, -1)
    sources = source_base + jnp.arange(source_count, dtype=jnp.int32)
    slot_ids = jnp.arange(row.shape[0], dtype=jnp.int32)
    matches = row_owner[None, :] == sources[:, None]
    present = jnp.any(matches, axis=1)
    slot_of = jnp.sum(jnp.where(matches, slot_ids[None, :], 0), axis=1)
    nvalid = jnp.where(present, jnp.clip(length - slot_of * page_size, 0, page_size), 0)
    within = jnp.arange(page_size, dtype=jnp.int32)
    return (within[None, :] < nvalid[:, None]).astype(jnp.int32).reshape(1, source_count * page_size)


def by_rows(stat):
    return jnp.transpose(stat, (1, 0, 2))


def on_device(new_queries, new_keys, new_values, kv_pages, page_table, cache_len, w_out, out_bias):
    half = lax.axis_index("half")
    sub = lax.axis_index("sub")
    sub_count = lax.axis_size("sub")
    tp_index = lax.axis_index("tp")
    tp_count = lax.axis_size("tp")
    own_index = half * sub_count + sub
    partner = (1 - half) * sub_count + sub
    span_len = new_queries.shape[0]
    width = new_queries.shape[1]
    head_count = width // HEAD_DIM
    page_count = kv_pages.shape[0]
    page_size = kv_pages.shape[2]
    out_cols = w_out.shape[1] // tp_count
    swap = [(0, 1), (1, 0)]

    w_recv = []
    for shift in range(1, tp_count):
        target = (tp_index + shift) % tp_count
        piece = lax.dynamic_slice_in_dim(w_out, target * out_cols, out_cols, axis=1)
        perm = [(i, (i + shift) % tp_count) for i in range(tp_count)]
        w_recv.append(lax.ppermute(piece, "tp", perm))
    w_mine = lax.dynamic_slice_in_dim(w_out, tp_index * out_cols, out_cols, axis=1)

    owners = jnp.where(page_table >= 0, page_table // page_count, -1)
    held_here = owners == own_index
    local_page = jnp.sum(jnp.where(held_here, page_table - own_index * page_count, 0), axis=1)
    dest = jnp.arange(sub_count, dtype=jnp.int32)
    wanted = jnp.stack([half * sub_count + dest, (1 - half) * sub_count + dest], axis=1).reshape(-1)
    outgoing = jnp.take(kv_pages, jnp.take(local_page, wanted), axis=0, mode="clip")
    outgoing = outgoing.reshape((sub_count, 2) + kv_pages.shape[1:])
    incoming = lax.all_to_all(outgoing, "sub", split_axis=0, concat_axis=0, tiled=True)

    own_length = lax.dynamic_index_in_dim(cache_len, own_index, 0, keepdims=False)
    partner_length = lax.dynamic_index_in_dim(cache_len, partner, 0, keepdims=False)
    positions = own_length + jnp.arange(span_len, dtype=jnp.int32)
    query_rot = rotate_rows(new_queries, positions)
    key_rot = rotate_rows(new_keys, positions)
    partner_query = lax.ppermute(query_rot, "half", swap)

    source_base = half * sub_count
    ok_own = usable_keys(page_table, own_index, own_length, source_base, sub_count, page_count, page_size)
    ok_partner = usable_keys(page_table, partner, partner_length, source_base, sub_count, page_count, page_size)

    far_out, far_max, far_sum = attend(ok_partner, partner_query, incoming, 1, jnp.bfloat16)
    far_stats = jnp.concatenate([far_max, far_sum], axis=2)
    back_out = lax.ppermute(far_out, "half", swap)
    back_stats = lax.ppermute(far_stats, "half", swap)
    near_out, near_max, near_sum = attend(
        ok_own, query_rot, incoming, 0, jnp.float32, local=(key_rot, new_values)
    )

    near_max = by_rows(near_max)
    near_sum = by_rows(near_sum)
    back_stats = by_rows(back_stats)
    back_max = back_stats[:, :, 0:1]
    back_sum = back_stats[:, :, 1:2]
    peak = jnp.maximum(near_max, back_max)
    near_w = jnp.exp(near_max - peak) * near_sum
    back_w = jnp.exp(back_max - peak) * back_sum
    near3 = near_out.reshape(span_len, head_count, HEAD_DIM)
    back3 = back_out.astype(jnp.float32).reshape(span_len, head_count, HEAD_DIM)
    merged = (near3 * near_w + back3 * back_w) / (near_w + back_w)
    attended = merged.reshape(span_len, width).astype(jnp.bfloat16)

    summed = jnp.dot(attended, w_mine, preferred_element_type=jnp.float32)
    for shift in range(1, tp_count):
        perm = [(i, (i + shift) % tp_count) for i in range(tp_count)]
        other = lax.ppermute(attended, "tp", perm)
        summed = summed + jnp.dot(other, w_recv[shift - 1], preferred_element_type=jnp.float32)
    return (summed + out_bias.astype(jnp.float32)).astype(jnp.bfloat16)


def solution(mesh):
    req_count = mesh.shape["req"]
    tp_count = mesh.shape["tp"]
    assert tuple(mesh.axis_names) == ("req", "tp")
    devices = mesh.devices.reshape(2, req_count // 2, tp_count)
    split_mesh = jax.sharding.Mesh(devices, ("half", "sub", "tp"))
    rows = ("half", "sub")
    return jax.shard_map(
        on_device,
        mesh=split_mesh,
        in_specs=(
            P(rows, "tp"),
            P(rows, "tp"),
            P(rows, "tp"),
            P(rows, None, None, "tp"),
            P(),
            P(),
            P("tp", None),
            P("tp"),
        ),
        out_specs=P(rows, "tp"),
        check_vma=False,
    )
```

time: 229 us -> 182 us (0.79)
  waiting for transfers between devices: 173 us -> 100 us
  local copies, waits for them, and re-layouts: 16.3 us -> 27.6 us
  other arithmetic: 5.64 us -> 12 us
  Pallas kernels: 13.1 us -> 18.5 us
  starting transfers between devices: 9.73 us -> 12.8 us
    all_to_all x1, waiting for transfers between devices: 173 us -> 0.01 us  [on_device(): lax.all_to_all(outgoing, 'sub', split_axis=0, concat_axis=0, tiled=True)]
    ppermute x0 -> x3, waiting for transfers between devices: none -> 100 us  [the longest x1 100 us: on_device(): partner_query = lax.ppermute(query_rot, 'half', swap)]
    pallas_call x1 -> x2, Pallas kernels: 13.1 us -> 18.5 us  [attend(): pl.pallas_call(partial(attention_kernel, with_local=local is not None), g...]
    mul x0 -> x4, local copies, waits for them, and re-layouts: none -> 5.14 us  [on_device(): merged = (near3 * near_w + back3 * back_w) / (near_w + back_w)]
    ppermute x0 -> x3, starting transfers between devices: none -> 4.88 us  [the longest x1 2.48 us: on_device(): partner_query = lax.ppermute(query_rot, 'half', swap)]
    pallas_call x0 -> x2, local copies, waits for them, and re-layouts: none -> 3.1 us  [attend(): pl.pallas_call(partial(attention_kernel, with_local=local is not None), g...]
    add x0 -> x3, other arithmetic: none -> 3 us  [the longest x1 3 us: on_device(): merged = (near3 * near_w + back3 * back_w) / (near_w + back_w)]
    convert_element_type x1 -> x3, other arithmetic: 0.67 us -> 3.11 us  [the longest x1 1.78 us: on_device(): attended = merged.reshape(span_len, width).astype(jnp.bfloat16)]
  transfers between devices with their start and end apart: 3 -> 6, of which waited for: 1 -> 1; matrix products, arithmetic and copies ran while one was open for 7% -> 18% of each run, Pallas kernels for 6% -> 10%
where the time goes in v3:
time: 182 us; the launch traced here: 179 us
  waiting for transfers between devices  100 us (55%)
  local copies, waits for them, and re-layouts  27.6 us (15%)
  Pallas kernels  18.5 us (10%)
  starting transfers between devices  12.8 us (7%)
  other arithmetic  12 us (7%)
  matrix products  7.92 us (4%)
    ppermute x1, waiting for transfers between devices, on_device(): partner_query = lax.ppermute(query_rot, 'half', swap)  100 us
    pallas_call x2, Pallas kernels, attend(): pl.pallas_call(partial(attention_kernel, with_local=local is not None), g...  18.5 us
    gather x1, local copies, waits for them, and re-layouts, on_device(): jnp.take(kv_pages, jnp.take(local_page, wanted), axis=0, mode='clip')  8.16 us
    mul x4, local copies, waits for them, and re-layouts, on_device(): merged = (near3 * near_w + back3 * back_w) / (near_w + back_w)  5.14 us
    all_to_all x1, starting transfers between devices, on_device(): lax.all_to_all(outgoing, 'sub', split_axis=0, concat_axis=0, tiled=True)  4.92 us
    dynamic_slice x1, local copies, waits for them, and re-layouts, on_device(): piece = lax.dynamic_slice_in_dim(w_out, target * out_cols, out_cols, axis=1)  4.81 us
    dot_general x1, matrix products, on_device(): jnp.dot(other, w_recv[shift - 1], preferred_element_type=jnp.float32)  4.49 us
  transfers between devices with their start and end apart: 6, of which 1 were waited for; matrix products, arithmetic and copies ran while one was open for 18% of the time, Pallas kernels for 10%

profile of v3, /device:TPU:11, one launch (start us, length us, event | category | flops | bytes accessed | tf_op | source)
XLA Modules:
  0.0 179.4 jit_solution(12780248132609630479)
XLA Ops:
  0.2 0.8 select_reduce_fusion
  1.0 0.7 gather_fusion
  1.7 8.2 %gather_fusion.1 = bf16[16,2,128,1024]{3,2,1,0:T(8,128)(2,1)} fusion(bf16[16,2,128,1024]{3,2,1,0:T(8,128)(2,1)} %param.11, s32[1024]{0:T(1024)S(1)} %pad_clamp_fusion), kind=kCustom, calls=%fused_computation.1 | custom fusion | bytes 16777280 | tf_op jit(solution)/shard_map/jit(_take)/gather | solution.py:150
  9.9 4.9 %all-to-all-start = ((bf16[8,2,2,128,1024]{4,3,2,1,0:T(8,128)(2,1)}), bf16[8,2,2,128,1024]{4,3,2,1,0:T(8,128)(2,1)}, u32[]{:S(2)}, u32[]{:S(2)}) async-start(bf16[8,2,2,128,1024]{4,3,2,1,0:T(8,128)(2,1)} %bitcast.63), calls=%async_computation | async-start | bytes 16777216 | tf_op jit(solution)/shard_map/all_to_all | solution.py:152
  14.8 4.8 %constant_dynamic-slice_fusion.1 = bf16[1024,2048]{1,0:T(8,128)(2,1)} fusion(bf16[1024,4096]{1,0:T(8,128)(2,1)} %param.14, s32[]{:T(128)S(6)} %select_n.121), kind=kLoop, calls=%fused_computation.67 | loop fusion | bytes 8388612 | tf_op jit(solution)/shard_map/dynamic_slice | solution.py:140
  19.7 0.9 collective-permute-start.4
  20.5 0.6 fusion.26
  21.2 0.6 add_convert_fusion.2
  23.0 0.7 subtract_convert_fusion
  23.7 1.0 pad_maximum_fusion
  24.8 2.5 %collective-permute-start = (bf16[256,1024]{1,0:T(8,128)(2,1)S(1)}, bf16[256,1024]{1,0:T(8,128)(2,1)S(1)}, u32[]{:S(2)}, u32[]{:S(2)}) collective-permute-start(bf16[256,1024]{1,0:T(8,128)(2,1)S(1)} %bitcast.70), channel_id=1, source_target_pairs={{0,16},{16,0},{1,17},{17,1},{2,18},{18,2},{3,19},{19,3},{4,20},{20... | collective-permute-start | bytes 1572872 | tf_op jit(solution)/shard_map/ppermute | solution.py:159
  27.3 0.7 fusion.20
  28.4 1.3 clamp_select_fusion
  29.6 0.7 fusion.17
  30.3 100.4 %collective-permute-done.refs_0_ = bf16[256,1024]{1,0:T(8,128)(2,1)S(1)} collective-permute-done((bf16[256,1024]{1,0:T(8,128)(2,1)S(1)}, bf16[256,1024]{1,0:T(8,128)(2,1)S(1)}, u32[]{:S(2)}, u32[]{:S(2)}) %collective-permute-start) | collective-permute-done | bytes 524320 | tf_op jit(solution)/shard_map/ppermute | solution.py:159
  130.7 0.8 copy-done.2
  131.5 8.5 %shard_map.83 = (bf16[256,1024]{1,0:T(8,128)(2,1)}, f32[8,256,1]{2,1,0:T(8,128)}, f32[8,256,1]{2,1,0:T(8,128)}) custom-call(bf16[256,1024]{1,0:T(8,128)(2,1)} %copy-done.2, bf16[8,2,2,128,1024]{4,3,2,1,0:T(8,128)(2,1)} %all-to-all-done.refs_3_.refs_4_.refs_1_.refs_2_, bf16[8,2,2,128,1024]{4,3,2,1,0:T(8,128)(2,1)} %all-to-all-done.refs_3_.refs_4_.refs_1_.refs_2_, ...), custom_call_target="tpu_custom_call" | custom-call | tf_op jit(solution)/shard_map/pallas_call | solution.py:91
  140.1 1.5 copy.32
  141.6 1.6 copy.33
  143.2 2.4 %collective-permute-start.2 = (bf16[256,1024]{1,0:T(8,128)(2,1)}, bf16[256,1024]{1,0:T(8,128)(2,1)}, u32[]{:S(2)}, u32[]{:S(2)}) collective-permute-start(bf16[256,1024]{1,0:T(8,128)(2,1)} %get-tuple-element.16), channel_id=1, source_target_pairs={{0,16},{16,0},{1,17},{17,1},{2,18},{18,2},{3,19},{19,3},{4,20},{20... | collective-permute-start | bytes 1572872 | tf_op jit(solution)/shard_map/ppermute | solution.py:167
  145.6 0.7 fusion.16
  146.3 0.9 copy.53
  147.2 9.9 %shard_map.82 = (f32[256,1024]{1,0:T(8,128)}, f32[8,256,1]{2,1,0:T(8,128)}, f32[8,256,1]{2,1,0:T(8,128)}) custom-call(bf16[256,1024]{1,0:T(8,128)(2,1)} %bitcast.71, bf16[256,1024]{1,0:T(8,128)(2,1)} %bitcast.72, bf16[256,1024]{1,0:T(8,128)(2,1)} %refs_2_.1, bf16[8,2,2,128,1024]{4,3,2,1,0:T(8,128)(2,1)} %all-to-all-done.refs_3_.refs_4_.refs_1_.refs_2_, ...), custom_call_target="tpu_custom_call" | custom-call | tf_op jit(solution)/shard_map/pallas_call | solution.py:91
  157.1 0.4 copy.34
  157.5 3.0 %fusion.23 = (f32[256,8,1]{2,0,1:T(8,128)S(1)}, f32[256,8,1]{2,0,1:T(8,128)S(1)}, f32[256,8,1]{2,0,1:T(8,128)}) fusion(f32[256,8,2]{2,0,1:T(8,128)S(1)} %bitcast.64, f32[8,256,1]{2,1,0:T(8,128)} %get-tuple-element.12, f32[8,256,1]{2,1,0:T(8,128)} %get-tuple-element.15), kind=kLoop, calls=%fused_computation.81 | loop fusion | flops 12288 | bytes 57344 | tf_op jit(solution)/shard_map/add | solution.py:183
  160.5 2.9 %copy.38 = f32[256,8,1]{1,0,2:T(8,128)S(1)} copy(f32[256,8,1]{2,0,1:T(8,128)} %get-tuple-element.23) | data formatting | bytes 16384 | tf_op jit(solution)/shard_map/mul | solution.py:183
  163.3 1.6 copy.39
  164.9 1.6 copy.40
  167.6 1.8 fusion.8
  169.3 2.1 %collective-permute-start.3 = (bf16[256,1024]{1,0:T(8,128)(2,1)S(1)}, bf16[256,1024]{1,0:T(8,128)(2,1)S(1)}, u32[]{:S(2)}, u32[]{:S(2)}) collective-permute-start(bf16[256,1024]{1,0:T(8,128)(2,1)S(1)} %fusion.8), channel_id=1, source_target_pairs={{0,1},{1,0},{2,3},{3,2},{4,5},{5,4},{6,7},{7,6},{8,9},{9,8},{10,11... | collective-permute-start | bytes 1572872 | tf_op jit(solution)/shard_map/ppermute | solution.py:189
  171.5 3.4 %fusion = f32[256,2048]{1,0:T(8,128)S(1)} fusion(bf16[256,1024]{1,0:T(8,128)(2,1)S(1)} %fusion.8, bf16[1024,4096]{1,0:T(8,128)(2,1)} %param.14, s32[]{:T(128)S(6)} %select_n.119), kind=kOutput, calls=%fused_computation.2 | convolution fusion | flops 1073741824 | bytes 6815748 | tf_op jit(solution)/shard_map/dot_general | solution.py:186
  174.9 4.5 %fusion.3 = bf16[256,2048]{1,0:T(8,128)(2,1)} fusion(f32[256,2048]{1,0:T(8,128)S(1)} %fusion, bf16[256,1024]{1,0:T(8,128)(2,1)S(1)} %collective-permute-done.3, bf16[1024,2048]{1,0:T(8,128)(2,1)} %collective-permute-done.4, f32[2048]{0:T(1024)S(1)} %convert_element_type.63), kind=kOutput, calls=%fused_computation.6 | convolution fusion | flops 1075314688 | bytes 7872512 | tf_op jit(solution)/shard_map/dot_general | solution.py:190
  (46 shorter events, 2.9 us)
Async XLA Ops:
  9.9 120.8 %all-to-all-start = ((bf16[8,2,2,128,1024]{4,3,2,1,0:T(8,128)(2,1)}), bf16[8,2,2,128,1024]{4,3,2,1,0:T(8,128)(2,1)}, u32[]{:S(2)}, u32[]{:S(2)}) async-start(bf16[8,2,2,128,1024]{4,3,2,1,0:T(8,128)(2,1)} %bitcast.63), calls=%async_computation | async-start | bytes 16777216 | tf_op jit(solution)/shard_map/all_to_all | solution.py:152
  14.8 5.7 %copy-start.6 = (s32[16]{0:T(128)S(1)}, s32[16]{0:T(128)}, u32[]{:S(2)}) copy-start(s32[16]{0:T(128)} %param.13) | copy-start | bytes 196
  14.8 7.3 %copy-start.3 = (bf16[256,1024]{1,0:T(8,128)(2,1)S(1)}, bf16[256,1024]{1,0:T(8,128)(2,1)}, u32[]{:S(2)}) copy-start(bf16[256,1024]{1,0:T(8,128)(2,1)} %param.9) | copy-start | bytes 1572868
  14.8 7.4 %copy-start.4 = (bf16[256,1024]{1,0:T(8,128)(2,1)S(1)}, bf16[256,1024]{1,0:T(8,128)(2,1)}, u32[]{:S(2)}) copy-start(bf16[256,1024]{1,0:T(8,128)(2,1)} %param.8) | copy-start | bytes 1572868
  19.7 155.3 %collective-permute-start.4 = (bf16[1024,2048]{1,0:T(8,128)(2,1)}, bf16[1024,2048]{1,0:T(8,128)(2,1)}, u32[]{:S(2)}, u32[]{:S(2)}) collective-permute-start(bf16[1024,2048]{1,0:T(8,128)(2,1)} %constant_dynamic-slice_fusion.1), channel_id=1, source_target_pairs={{0,1},{1,0},{2,3},{3,2},{4,5},{5,4},{6,7},{7,6},{8,9},{9,8},{10,11... | collective-permute-start | bytes 12582920 | tf_op jit(solution)/shard_map/ppermute | solution.py:142
  24.8 115.3 %copy-start = (bf16[32,8,8,128]{3,1,2,0:T(8,128)(2,1)}, bf16[32,8,8,128]{3,1,2,0:T(8,128)(2,1)S(1)}, u32[]{:S(2)}) copy-start(bf16[32,8,8,128]{3,1,2,0:T(8,128)(2,1)S(1)} %copy.54) | copy-start | bytes 1572868
  24.8 105.9 %collective-permute-start = (bf16[256,1024]{1,0:T(8,128)(2,1)S(1)}, bf16[256,1024]{1,0:T(8,128)(2,1)S(1)}, u32[]{:S(2)}, u32[]{:S(2)}) collective-permute-start(bf16[256,1024]{1,0:T(8,128)(2,1)S(1)} %bitcast.70), channel_id=1, source_target_pairs={{0,16},{16,0},{1,17},{17,1},{2,18},{18,2},{3,19},{19,3},{4,20},{20... | collective-permute-start | bytes 1572872 | tf_op jit(solution)/shard_map/ppermute | solution.py:159
  130.7 0.8 copy-start.2
  143.2 13.9 %collective-permute-start.1 = (f32[8,256,2]{1,0,2:T(8,128)S(1)}, f32[8,256,2]{1,0,2:T(8,128)S(1)}, u32[]{:S(2)}, u32[]{:S(2)}) collective-permute-start(f32[8,256,2]{1,0,2:T(8,128)S(1)} %pad_maximum_fusion.2), channel_id=1, source_target_pairs={{0,16},{16,0},{1,17},{17,1},{2,18},{18,2},{3,19},{19,3},{4,20},{20... | collective-permute-start | bytes 49160 | tf_op jit(solution)/shard_map/ppermute | solution.py:168
  143.2 23.3 %collective-permute-start.2 = (bf16[256,1024]{1,0:T(8,128)(2,1)}, bf16[256,1024]{1,0:T(8,128)(2,1)}, u32[]{:S(2)}, u32[]{:S(2)}) collective-permute-start(bf16[256,1024]{1,0:T(8,128)(2,1)} %get-tuple-element.16), channel_id=1, source_target_pairs={{0,16},{16,0},{1,17},{17,1},{2,18},{18,2},{3,19},{19,3},{4,20},{20... | collective-permute-start | bytes 1572872 | tf_op jit(solution)/shard_map/ppermute | solution.py:167
  160.5 7.1 %copy-start.1 = (f32[256,1024]{1,0:T(8,128)S(1)}, f32[256,1024]{1,0:T(8,128)}, u32[]{:S(2)}) copy-start(f32[256,1024]{1,0:T(8,128)} %get-tuple-element.11) | copy-start | bytes 3145732
  166.5 4.9 %copy-start.5 = (bf16[2048]{0:T(1024)(128)(2,1)S(1)}, bf16[2048]{0:T(1024)(128)(2,1)}, u32[]{:S(2)}) copy-start(bf16[2048]{0:T(1024)(128)(2,1)} %param.15) | copy-start | bytes 12292
  169.3 5.6 %collective-permute-start.3 = (bf16[256,1024]{1,0:T(8,128)(2,1)S(1)}, bf16[256,1024]{1,0:T(8,128)(2,1)S(1)}, u32[]{:S(2)}, u32[]{:S(2)}) collective-permute-start(bf16[256,1024]{1,0:T(8,128)(2,1)S(1)} %fusion.8), channel_id=1, source_target_pairs={{0,1},{1,0},{2,3},{3,2},{4,5},{5,4},{6,7},{7,6},{8,9},{9,8},{10,11... | collective-permute-start | bytes 1572872 | tf_op jit(solution)/shard_map/ppermute | solution.py:189

commit v4 on v3

--- a/solution.py
+++ b/solution.py
@@ -70,15 +70,15 @@
     l_ref[...] = l
 
 
-def attend(key_ok, query_rot, incoming, which, out_dtype, local=None):
+def attend(key_ok, query_rot, incoming, out_dtype, local=None):
     span, width = query_rot.shape
     head_count = width // HEAD_DIM
     block_count = incoming.shape[0]
-    page_size = incoming.shape[3]
+    page_size = incoming.shape[2]
     col_spec = pl.BlockSpec((span, HEAD_DIM), lambda h: (0, h))
     page_specs = [
-        pl.BlockSpec((block_count, None, None, page_size, HEAD_DIM), lambda h: (0, which, 0, 0, h)),
-        pl.BlockSpec((block_count, None, None, page_size, HEAD_DIM), lambda h: (0, which, 1, 0, h)),
+        pl.BlockSpec((block_count, None, page_size, HEAD_DIM), lambda h: (0, 0, 0, h)),
+        pl.BlockSpec((block_count, None, page_size, HEAD_DIM), lambda h: (0, 1, 0, h)),
         pl.BlockSpec((1, block_count * page_size), lambda h: (0, 0)),
     ]
     stat_spec = pl.BlockSpec((None, span, 1), lambda h: (h, 0, 0))
@@ -146,10 +146,10 @@
     held_here = owners == own_index
     local_page = jnp.sum(jnp.where(held_here, page_table - own_index * page_count, 0), axis=1)
     dest = jnp.arange(sub_count, dtype=jnp.int32)
-    wanted = jnp.stack([half * sub_count + dest, (1 - half) * sub_count + dest], axis=1).reshape(-1)
-    outgoing = jnp.take(kv_pages, jnp.take(local_page, wanted), axis=0, mode="clip")
-    outgoing = outgoing.reshape((sub_count, 2) + kv_pages.shape[1:])
-    incoming = lax.all_to_all(outgoing, "sub", split_axis=0, concat_axis=0, tiled=True)
+    far_pages = jnp.take(kv_pages, jnp.take(local_page, (1 - half) * sub_count + dest), axis=0, mode="clip")
+    far_incoming = lax.all_to_all(far_pages, "sub", split_axis=0, concat_axis=0, tiled=True)
+    near_pages = jnp.take(kv_pages, jnp.take(local_page, half * sub_count + dest), axis=0, mode="clip")
+    near_incoming = lax.all_to_all(near_pages, "sub", split_axis=0, concat_axis=0, tiled=True)
 
     own_length = lax.dynamic_index_in_dim(cache_len, own_index, 0, keepdims=False)
     partner_length = lax.dynamic_index_in_dim(cache_len, partner, 0, keepdims=False)
@@ -162,12 +162,12 @@
     ok_own = usable_keys(page_table, own_index, own_length, source_base, sub_count, page_count, page_size)
     ok_partner = usable_keys(page_table, partner, partner_length, source_base, sub_count, page_count, page_size)
 
-    far_out, far_max, far_sum = attend(ok_partner, partner_query, incoming, 1, jnp.bfloat16)
+    far_out, far_max, far_sum = attend(ok_partner, partner_query, far_incoming, jnp.bfloat16)
     far_stats = jnp.concatenate([far_max, far_sum], axis=2)
     back_out = lax.ppermute(far_out, "half", swap)
     back_stats = lax.ppermute(far_stats, "half", swap)
     near_out, near_max, near_sum = attend(
-        ok_own, query_rot, incoming, 0, jnp.float32, local=(key_rot, new_values)
+        ok_own, query_rot, near_incoming, jnp.float32, local=(key_rot, new_values)
     )
 
     near_max = by_rows(near_max)

time: 182 us -> 185 us (1.016)
  waiting for transfers between devices: 100 us -> 92.8 us
  starting transfers between devices: 12.8 us -> 18.7 us
  local copies, waits for them, and re-layouts: 27.6 us -> 32.2 us
    ppermute x1, waiting for transfers between devices: 100 us -> 46.4 us  [on_device(): partner_query = lax.ppermute(query_rot, 'half', swap)]
    all_to_all x1 -> x2, waiting for transfers between devices: 0.01 us -> 44.8 us  [the longest x1 44.7 us: on_device(): lax.all_to_all(far_pages, 'sub', split_axis=0, concat_axis=0, tiled=True)]
    gather x2 -> x4, local copies, waits for them, and re-layouts: 8.82 us -> 13.6 us  [the longest x1 6.15 us: on_device(): jnp.take(kv_pages, jnp.take(local_page, (1 - half) * sub_count + dest), a...]
    all_to_all x1 -> x2, starting transfers between devices: 4.92 us -> 9.45 us  [the longest x1 4.85 us: on_device(): lax.all_to_all(near_pages, 'sub', split_axis=0, concat_axis=0, tiled=True)]
  transfers between devices with their start and end apart: 6 -> 7, of which waited for: 1 -> 3; matrix products, arithmetic and copies ran while one was open for 18% -> 22% of each run, Pallas kernels for 10% -> 10%
where the time goes in v4:
time: 185 us; the launch traced here: 182 us
  waiting for transfers between devices  92.8 us (50%)
  local copies, waits for them, and re-layouts  32.2 us (17%)
  starting transfers between devices  18.7 us (10%)
  Pallas kernels  18.5 us (10%)
  other arithmetic  12.2 us (7%)
  matrix products  7.92 us (4%)
    ppermute x1, waiting for transfers between devices, on_device(): partner_query = lax.ppermute(query_rot, 'half', swap)  46.4 us
    all_to_all x1, waiting for transfers between devices, on_device(): lax.all_to_all(far_pages, 'sub', split_axis=0, concat_axis=0, tiled=True)  44.7 us
    pallas_call x2, Pallas kernels, attend(): pl.pallas_call(partial(attention_kernel, with_local=local is not None), g...  18.5 us
    gather x1, local copies, waits for them, and re-layouts, on_device(): jnp.take(kv_pages, jnp.take(local_page, (1 - half) * sub_count + dest), a...  6.15 us
    gather x1, local copies, waits for them, and re-layouts, on_device(): jnp.take(kv_pages, jnp.take(local_page, half * sub_count + dest), axis=0,...  6.12 us
    all_to_all x1, starting transfers between devices, on_device(): lax.all_to_all(near_pages, 'sub', split_axis=0, concat_axis=0, tiled=True)  4.85 us
    dynamic_slice x1, local copies, waits for them, and re-layouts, on_device(): piece = lax.dynamic_slice_in_dim(w_out, target * out_cols, out_cols, axis=1)  4.82 us
    all_to_all x1, starting transfers between devices, on_device(): lax.all_to_all(far_pages, 'sub', split_axis=0, concat_axis=0, tiled=True)  4.59 us
  transfers between devices with their start and end apart: 7, of which 3 were waited for; matrix products, arithmetic and copies ran while one was open for 22% of the time, Pallas kernels for 10%

profile of v4, /device:TPU:11, one launch (start us, length us, event | category | flops | bytes accessed | tf_op | source)
XLA Modules:
  0.0 182.4 jit_solution(14743767873447028550)
XLA Ops:
  0.0 0.8 select_reduce_fusion
  1.5 6.1 %gather_fusion.1 = bf16[8,2,128,1024]{3,2,1,0:T(8,128)(2,1)} fusion(bf16[16,2,128,1024]{3,2,1,0:T(8,128)(2,1)} %param.13, s32[1024]{0:T(1024)S(1)} %pad_clamp_fusion), kind=kCustom, calls=%fused_computation.3 | custom fusion | bytes 8388640 | tf_op jit(solution)/shard_map/jit(_take)/gather | solution.py:149
  7.7 4.6 %all-to-all-start.1 = ((bf16[8,2,128,1024]{3,2,1,0:T(8,128)(2,1)}), bf16[8,2,128,1024]{3,2,1,0:T(8,128)(2,1)}, u32[]{:S(2)}, u32[]{:S(2)}) async-start(bf16[8,2,128,1024]{3,2,1,0:T(8,128)(2,1)} %gather_fusion.1), calls=%async_computation.1 | async-start | bytes 8388608 | tf_op jit(solution)/shard_map/all_to_all | solution.py:150
  12.9 6.1 %gather_fusion = bf16[8,2,128,1024]{3,2,1,0:T(8,128)(2,1)} fusion(bf16[16,2,128,1024]{3,2,1,0:T(8,128)(2,1)} %param.13, s32[1024]{0:T(1024)S(1)} %pad_clamp_fusion.2), kind=kCustom, calls=%fused_computation.2 | custom fusion | bytes 8388640 | tf_op jit(solution)/shard_map/jit(_take)/gather | solution.py:151
  19.0 44.7 %all-to-all-done.1.refs_1_.refs_2_ = bf16[8,2,128,1024]{3,2,1,0:T(8,128)(2,1)} async-done(((bf16[8,2,128,1024]{3,2,1,0:T(8,128)(2,1)}), bf16[8,2,128,1024]{3,2,1,0:T(8,128)(2,1)}, u32[]{:S(2)}, u32[]{:S(2)}) %all-to-all-start.1) | async-done | bytes 4194336 | tf_op jit(solution)/shard_map/all_to_all | solution.py:150
  63.8 4.9 %all-to-all-start = ((bf16[8,2,128,1024]{3,2,1,0:T(8,128)(2,1)}), bf16[8,2,128,1024]{3,2,1,0:T(8,128)(2,1)}, u32[]{:S(2)}, u32[]{:S(2)}) async-start(bf16[8,2,128,1024]{3,2,1,0:T(8,128)(2,1)} %gather_fusion), calls=%async_computation | async-start | bytes 8388608 | tf_op jit(solution)/shard_map/all_to_all | solution.py:152
  68.7 4.8 %constant_dynamic-slice_fusion.2 = bf16[1024,2048]{1,0:T(8,128)(2,1)} fusion(bf16[1024,4096]{1,0:T(8,128)(2,1)} %param.16, s32[]{:T(128)S(6)} %select_n.98), kind=kLoop, calls=%fused_computation.73 | loop fusion | bytes 8388612 | tf_op jit(solution)/shard_map/dynamic_slice | solution.py:140
  73.5 2.4 %collective-permute-start.4 = (bf16[1024,2048]{1,0:T(8,128)(2,1)}, bf16[1024,2048]{1,0:T(8,128)(2,1)}, u32[]{:S(2)}, u32[]{:S(2)}) collective-permute-start(bf16[1024,2048]{1,0:T(8,128)(2,1)} %constant_dynamic-slice_fusion.2), channel_id=1, source_target_pairs={{0,1},{1,0},{2,3},{3,2},{4,5},{5,4},{6,7},{7,6},{8,9},{9,8},{10,11... | collective-permute-start | bytes 12582920 | tf_op jit(solution)/shard_map/ppermute | solution.py:142
  77.0 0.7 add_convert_fusion.2
  78.4 0.7 subtract_convert_fusion
  79.2 1.0 pad_maximum_fusion
  80.2 2.4 %collective-permute-start = (bf16[256,1024]{1,0:T(8,128)(2,1)S(1)}, bf16[256,1024]{1,0:T(8,128)(2,1)S(1)}, u32[]{:S(2)}, u32[]{:S(2)}) collective-permute-start(bf16[256,1024]{1,0:T(8,128)(2,1)S(1)} %bitcast.60), channel_id=1, source_target_pairs={{0,16},{16,0},{1,17},{17,1},{2,18},{18,2},{3,19},{19,3},{4,20},{20... | collective-permute-start | bytes 1572872 | tf_op jit(solution)/shard_map/ppermute | solution.py:159
  82.6 0.7 fusion.19
  83.7 0.7 clamp_select_fusion.1
  85.1 0.7 fusion.17
  85.7 46.4 %collective-permute-done.refs_0_ = bf16[256,1024]{1,0:T(8,128)(2,1)S(1)} collective-permute-done((bf16[256,1024]{1,0:T(8,128)(2,1)S(1)}, bf16[256,1024]{1,0:T(8,128)(2,1)S(1)}, u32[]{:S(2)}, u32[]{:S(2)}) %collective-permute-start) | collective-permute-done | bytes 524320 | tf_op jit(solution)/shard_map/ppermute | solution.py:159
  132.2 0.8 copy-done.2
  133.0 8.6 %shard_map.83 = (bf16[256,1024]{1,0:T(8,128)(2,1)}, f32[8,256,1]{2,1,0:T(8,128)}, f32[8,256,1]{2,1,0:T(8,128)}) custom-call(bf16[256,1024]{1,0:T(8,128)(2,1)} %copy-done.2, bf16[8,2,128,1024]{3,2,1,0:T(8,128)(2,1)} %all-to-all-done.1.refs_1_.refs_2_, bf16[8,2,128,1024]{3,2,1,0:T(8,128)(2,1)} %all-to-all-done.1.refs_1_.refs_2_, s32[1,1024]{1,0:T(1,128)} %bitcast.71), custom_call_target="tpu_custom_call" | custom-call | tf_op jit(solution)/shard_map/pallas_call | solution.py:91
  141.5 1.5 copy.30
  143.1 1.6 copy.29
  144.7 2.4 %collective-permute-start.2 = (bf16[256,1024]{1,0:T(8,128)(2,1)}, bf16[256,1024]{1,0:T(8,128)(2,1)}, u32[]{:S(2)}, u32[]{:S(2)}) collective-permute-start(bf16[256,1024]{1,0:T(8,128)(2,1)} %get-tuple-element.17), channel_id=1, source_target_pairs={{0,16},{16,0},{1,17},{17,1},{2,18},{18,2},{3,19},{19,3},{4,20},{20... | collective-permute-start | bytes 1572872 | tf_op jit(solution)/shard_map/ppermute | solution.py:167
  147.7 0.9 copy.50
  148.6 9.9 %shard_map.82 = (f32[256,1024]{1,0:T(8,128)}, f32[8,256,1]{2,1,0:T(8,128)}, f32[8,256,1]{2,1,0:T(8,128)}) custom-call(bf16[256,1024]{1,0:T(8,128)(2,1)} %bitcast.61, bf16[256,1024]{1,0:T(8,128)(2,1)} %bitcast.62, bf16[256,1024]{1,0:T(8,128)(2,1)} %refs_2_.1, bf16[8,2,128,1024]{3,2,1,0:T(8,128)(2,1)} %all-to-all-done.refs_3_.refs_4_, ...), custom_call_target="tpu_custom_call" | custom-call | tf_op jit(solution)/shard_map/pallas_call | solution.py:91
  158.9 3.1 %fusion.21 = (f32[256,8,1]{2,0,1:T(8,128)}, f32[256,8,1]{2,0,1:T(8,128)S(1)}, f32[256,8,1]{2,0,1:T(8,128)S(1)}) fusion(f32[256,8,2]{2,0,1:T(8,128)S(1)} %bitcast.54, f32[8,256,1]{2,1,0:T(8,128)} %get-tuple-element.13, f32[8,256,1]{2,1,0:T(8,128)} %get-tuple-element.16), kind=kLoop, calls=%fused_computation.82 | loop fusion | flops 12288 | bytes 57344 | tf_op jit(solution)/shard_map/add | solution.py:183
  162.0 2.9 %copy.37 = f32[256,8,1]{1,0,2:T(8,128)S(1)} copy(f32[256,8,1]{2,0,1:T(8,128)} %get-tuple-element.22) | data formatting | bytes 16384 | tf_op jit(solution)/shard_map/div | solution.py:183
  164.9 1.6 copy.36
  166.5 1.6 copy.35
  168.1 1.6 collective-permute-done.2
  170.7 1.8 fusion.8
  172.4 2.0 %collective-permute-start.3 = (bf16[256,1024]{1,0:T(8,128)(2,1)S(1)}, bf16[256,1024]{1,0:T(8,128)(2,1)S(1)}, u32[]{:S(2)}, u32[]{:S(2)}) collective-permute-start(bf16[256,1024]{1,0:T(8,128)(2,1)S(1)} %fusion.8), channel_id=1, source_target_pairs={{0,1},{1,0},{2,3},{3,2},{4,5},{5,4},{6,7},{7,6},{8,9},{9,8},{10,11... | collective-permute-start | bytes 1572872 | tf_op jit(solution)/shard_map/ppermute | solution.py:189
  174.5 3.4 %fusion = f32[256,2048]{1,0:T(8,128)S(1)} fusion(bf16[256,1024]{1,0:T(8,128)(2,1)S(1)} %fusion.8, bf16[1024,4096]{1,0:T(8,128)(2,1)} %param.16, s32[]{:T(128)S(6)} %select_n.96), kind=kOutput, calls=%fused_computation.4 | convolution fusion | flops 1073741824 | bytes 6815748 | tf_op jit(solution)/shard_map/dot_general | solution.py:186
  177.9 4.5 %fusion.3 = bf16[256,2048]{1,0:T(8,128)(2,1)} fusion(f32[256,2048]{1,0:T(8,128)S(1)} %fusion, bf16[256,1024]{1,0:T(8,128)(2,1)S(1)} %collective-permute-done.3, bf16[1024,2048]{1,0:T(8,128)(2,1)} %collective-permute-done.4, f32[2048]{0:T(1024)S(1)} %convert_element_type.63), kind=kOutput, calls=%fused_computation.8 | convolution fusion | flops 1075314688 | bytes 7872512 | tf_op jit(solution)/shard_map/dot_general | solution.py:190
  (50 shorter events, 6.4 us)
Async XLA Ops:
  7.7 56.1 %all-to-all-start.1 = ((bf16[8,2,128,1024]{3,2,1,0:T(8,128)(2,1)}), bf16[8,2,128,1024]{3,2,1,0:T(8,128)(2,1)}, u32[]{:S(2)}, u32[]{:S(2)}) async-start(bf16[8,2,128,1024]{3,2,1,0:T(8,128)(2,1)} %gather_fusion.1), calls=%async_computation.1 | async-start | bytes 8388608 | tf_op jit(solution)/shard_map/all_to_all | solution.py:150
  63.8 84.8 %all-to-all-start = ((bf16[8,2,128,1024]{3,2,1,0:T(8,128)(2,1)}), bf16[8,2,128,1024]{3,2,1,0:T(8,128)(2,1)}, u32[]{:S(2)}, u32[]{:S(2)}) async-start(bf16[8,2,128,1024]{3,2,1,0:T(8,128)(2,1)} %gather_fusion), calls=%async_computation | async-start | bytes 8388608 | tf_op jit(solution)/shard_map/all_to_all | solution.py:152
  68.6 7.2 %copy-start.3 = (bf16[256,1024]{1,0:T(8,128)(2,1)S(1)}, bf16[256,1024]{1,0:T(8,128)(2,1)}, u32[]{:S(2)}) copy-start(bf16[256,1024]{1,0:T(8,128)(2,1)} %param.10) | copy-start | bytes 1572868
  68.6 7.5 %copy-start.4 = (bf16[256,1024]{1,0:T(8,128)(2,1)S(1)}, bf16[256,1024]{1,0:T(8,128)(2,1)}, u32[]{:S(2)}) copy-start(bf16[256,1024]{1,0:T(8,128)(2,1)} %param.11) | copy-start | bytes 1572868
  68.7 7.6 %copy-start.6 = (s32[16]{0:T(128)S(1)}, s32[16]{0:T(128)}, u32[]{:S(2)}) copy-start(s32[16]{0:T(128)} %param.15) | copy-start | bytes 196
  73.5 104.4 %collective-permute-start.4 = (bf16[1024,2048]{1,0:T(8,128)(2,1)}, bf16[1024,2048]{1,0:T(8,128)(2,1)}, u32[]{:S(2)}, u32[]{:S(2)}) collective-permute-start(bf16[1024,2048]{1,0:T(8,128)(2,1)} %constant_dynamic-slice_fusion.2), channel_id=1, source_target_pairs={{0,1},{1,0},{2,3},{3,2},{4,5},{5,4},{6,7},{7,6},{8,9},{9,8},{10,11... | collective-permute-start | bytes 12582920 | tf_op jit(solution)/shard_map/ppermute | solution.py:142
  80.2 61.3 %copy-start = (bf16[32,8,8,128]{3,1,2,0:T(8,128)(2,1)}, bf16[32,8,8,128]{3,1,2,0:T(8,128)(2,1)S(1)}, u32[]{:S(2)}) copy-start(bf16[32,8,8,128]{3,1,2,0:T(8,128)(2,1)S(1)} %copy.51) | copy-start | bytes 1572868
  80.2 51.9 %collective-permute-start = (bf16[256,1024]{1,0:T(8,128)(2,1)S(1)}, bf16[256,1024]{1,0:T(8,128)(2,1)S(1)}, u32[]{:S(2)}, u32[]{:S(2)}) collective-permute-start(bf16[256,1024]{1,0:T(8,128)(2,1)S(1)} %bitcast.60), channel_id=1, source_target_pairs={{0,16},{16,0},{1,17},{17,1},{2,18},{18,2},{3,19},{19,3},{4,20},{20... | collective-permute-start | bytes 1572872 | tf_op jit(solution)/shard_map/ppermute | solution.py:159
  132.2 0.8 copy-start.2
  144.7 13.9 %collective-permute-start.1 = (f32[8,256,2]{1,0,2:T(8,128)S(1)}, f32[8,256,2]{1,0,2:T(8,128)S(1)}, u32[]{:S(2)}, u32[]{:S(2)}) collective-permute-start(f32[8,256,2]{1,0,2:T(8,128)S(1)} %pad_maximum_fusion.2), channel_id=1, source_target_pairs={{0,16},{16,0},{1,17},{17,1},{2,18},{18,2},{3,19},{19,3},{4,20},{20... | collective-permute-start | bytes 49160 | tf_op jit(solution)/shard_map/ppermute | solution.py:168
  144.7 24.9 %collective-permute-start.2 = (bf16[256,1024]{1,0:T(8,128)(2,1)}, bf16[256,1024]{1,0:T(8,128)(2,1)}, u32[]{:S(2)}, u32[]{:S(2)}) collective-permute-start(bf16[256,1024]{1,0:T(8,128)(2,1)} %get-tuple-element.17), channel_id=1, source_target_pairs={{0,16},{16,0},{1,17},{17,1},{2,18},{18,2},{3,19},{19,3},{4,20},{20... | collective-permute-start | bytes 1572872 | tf_op jit(solution)/shard_map/ppermute | solution.py:167
  162.0 8.6 %copy-start.1 = (f32[256,1024]{1,0:T(8,128)S(1)}, f32[256,1024]{1,0:T(8,128)}, u32[]{:S(2)}) copy-start(f32[256,1024]{1,0:T(8,128)} %get-tuple-element.12) | copy-start | bytes 3145732
  169.6 4.8 %copy-start.5 = (bf16[2048]{0:T(1024)(128)(2,1)S(1)}, bf16[2048]{0:T(1024)(128)(2,1)}, u32[]{:S(2)}) copy-start(bf16[2048]{0:T(1024)(128)(2,1)} %param.17) | copy-start | bytes 12292
  172.4 5.5 %collective-permute-start.3 = (bf16[256,1024]{1,0:T(8,128)(2,1)S(1)}, bf16[256,1024]{1,0:T(8,128)(2,1)S(1)}, u32[]{:S(2)}, u32[]{:S(2)}) collective-permute-start(bf16[256,1024]{1,0:T(8,128)(2,1)S(1)} %fusion.8), channel_id=1, source_target_pairs={{0,1},{1,0},{2,3},{3,2},{4,5},{5,4},{6,7},{7,6},{8,9},{9,8},{10,11... | collective-permute-start | bytes 1572872 | tf_op jit(solution)/shard_map/ppermute | solution.py:189

commit v5 on v4

--- a/solution.py
+++ b/solution.py
@@ -146,17 +146,18 @@
     held_here = owners == own_index
     local_page = jnp.sum(jnp.where(held_here, page_table - own_index * page_count, 0), axis=1)
     dest = jnp.arange(sub_count, dtype=jnp.int32)
-    far_pages = jnp.take(kv_pages, jnp.take(local_page, (1 - half) * sub_count + dest), axis=0, mode="clip")
-    far_incoming = lax.all_to_all(far_pages, "sub", split_axis=0, concat_axis=0, tiled=True)
-    near_pages = jnp.take(kv_pages, jnp.take(local_page, half * sub_count + dest), axis=0, mode="clip")
-    near_incoming = lax.all_to_all(near_pages, "sub", split_axis=0, concat_axis=0, tiled=True)
-
     own_length = lax.dynamic_index_in_dim(cache_len, own_index, 0, keepdims=False)
     partner_length = lax.dynamic_index_in_dim(cache_len, partner, 0, keepdims=False)
     positions = own_length + jnp.arange(span_len, dtype=jnp.int32)
     query_rot = rotate_rows(new_queries, positions)
+    partner_query = lax.ppermute(query_rot, "half", swap)
+
+    far_pages = jnp.take(kv_pages, jnp.take(local_page, (1 - half) * sub_count + dest), axis=0, mode="clip")
+    partner_query, far_pages = lax.optimization_barrier((partner_query, far_pages))
+    far_incoming = lax.all_to_all(far_pages, "sub", split_axis=0, concat_axis=0, tiled=True)
+    near_pages = jnp.take(kv_pages, jnp.take(local_page, half * sub_count + dest), axis=0, mode="clip")
+    near_incoming = lax.all_to_all(near_pages, "sub", split_axis=0, concat_axis=0, tiled=True)
     key_rot = rotate_rows(new_keys, positions)
-    partner_query = lax.ppermute(query_rot, "half", swap)
 
     source_base = half * sub_count
     ok_own = usable_keys(page_table, own_index, own_length, source_base, sub_count, page_count, page_size)

time: 185 us -> 189 us (1.022)
  starting transfers between devices: 18.7 us -> 20.9 us
    all_to_all x1, waiting for transfers between devices: 0.01 us -> 33.8 us  [on_device(): lax.all_to_all(near_pages, 'sub', split_axis=0, concat_axis=0, tiled=True)]
    ppermute x1, waiting for transfers between devices: 46.4 us -> 15.8 us  [on_device(): partner_query = lax.ppermute(query_rot, 'half', swap)]
    ppermute x1, starting transfers between devices: 0.05 us -> 2.98 us  [on_device(): back_stats = lax.ppermute(far_stats, 'half', swap)]
    ppermute x1, starting transfers between devices: 2.35 us -> 0.06 us  [on_device(): back_out = lax.ppermute(far_out, 'half', swap)]
where the time goes in v5:
time: 189 us; the launch traced here: 186 us
  waiting for transfers between devices  94.1 us (50%)
  local copies, waits for them, and re-layouts  33.3 us (18%)
  starting transfers between devices  20.9 us (11%)
  Pallas kernels  18.5 us (10%)
  other arithmetic  10.6 us (6%)
  matrix products  7.93 us (4%)
    all_to_all x1, waiting for transfers between devices, on_device(): lax.all_to_all(far_pages, 'sub', split_axis=0, concat_axis=0, tiled=True)  44.6 us
    all_to_all x1, waiting for transfers between devices, on_device(): lax.all_to_all(near_pages, 'sub', split_axis=0, concat_axis=0, tiled=True)  33.8 us
    pallas_call x2, Pallas kernels, attend(): pl.pallas_call(partial(attention_kernel, with_local=local is not None), g...  18.5 us
    ppermute x1, waiting for transfers between devices, on_device(): partner_query = lax.ppermute(query_rot, 'half', swap)  15.8 us
    gather x1, local copies, waits for them, and re-layouts, on_device(): jnp.take(kv_pages, jnp.take(local_page, (1 - half) * sub_count + dest), a...  6.15 us
    gather x1, local copies, waits for them, and re-layouts, on_device(): jnp.take(kv_pages, jnp.take(local_page, half * sub_count + dest), axis=0,...  6.12 us
    all_to_all x1, starting transfers between devices, on_device(): lax.all_to_all(near_pages, 'sub', split_axis=0, concat_axis=0, tiled=True)  4.76 us
    dynamic_slice x1, local copies, waits for them, and re-layouts, on_device(): piece = lax.dynamic_slice_in_dim(w_out, target * out_cols, out_cols, axis=1)  4.73 us
  transfers between devices with their start and end apart: 7, of which 3 were waited for; matrix products, arithmetic and copies ran while one was open for 22% of the time, Pallas kernels for 10%

profile of v5, /device:TPU:11, one launch (start us, length us, event | category | flops | bytes accessed | tf_op | source)
XLA Modules:
  0.0 185.6 jit_solution(6967697280760387907)
XLA Ops:
  0.0 1.1 copy.38
  1.5 1.1 copy.40
  4.5 0.7 subtract_convert_fusion
  5.2 1.0 pad_maximum_fusion
  6.3 2.4 %collective-permute-start = (bf16[256,1024]{1,0:T(8,128)(2,1)S(1)}, bf16[256,1024]{1,0:T(8,128)(2,1)S(1)}, u32[]{:S(2)}, u32[]{:S(2)}) collective-permute-start(bf16[256,1024]{1,0:T(8,128)(2,1)S(1)} %bitcast.60), channel_id=1, source_target_pairs={{0,16},{16,0},{1,17},{17,1},{2,18},{18,2},{3,19},{19,3},{4,20},{20... | collective-permute-start | bytes 1572872 | tf_op jit(solution)/shard_map/ppermute | solution.py:153
  8.8 0.6 gather_fusion.3
  9.5 6.2 %gather_fusion.1 = bf16[8,2,128,1024]{3,2,1,0:T(8,128)(2,1)} fusion(bf16[16,2,128,1024]{3,2,1,0:T(8,128)(2,1)} %param.13, s32[1024]{0:T(1024)S(1)} %pad_clamp_fusion), kind=kCustom, calls=%fused_computation.3 | custom fusion | bytes 8388640 | tf_op jit(solution)/shard_map/jit(_take)/gather | solution.py:155
  15.7 15.8 %collective-permute-done.refs_0_ = bf16[256,1024]{1,0:T(8,128)(2,1)S(1)} collective-permute-done((bf16[256,1024]{1,0:T(8,128)(2,1)S(1)}, bf16[256,1024]{1,0:T(8,128)(2,1)S(1)}, u32[]{:S(2)}, u32[]{:S(2)}) %collective-permute-start) | collective-permute-done | bytes 524320 | tf_op jit(solution)/shard_map/ppermute | solution.py:153
  31.5 4.7 %all-to-all-start.1 = ((bf16[8,2,128,1024]{3,2,1,0:T(8,128)(2,1)}), bf16[8,2,128,1024]{3,2,1,0:T(8,128)(2,1)}, u32[]{:S(2)}, u32[]{:S(2)}) async-start(bf16[8,2,128,1024]{3,2,1,0:T(8,128)(2,1)} %gather_fusion.1), calls=%async_computation.1 | async-start | bytes 8388608 | tf_op jit(solution)/shard_map/all_to_all | solution.py:157
  36.9 6.1 %gather_fusion = bf16[8,2,128,1024]{3,2,1,0:T(8,128)(2,1)} fusion(bf16[16,2,128,1024]{3,2,1,0:T(8,128)(2,1)} %param.13, s32[1024]{0:T(1024)S(1)} %pad_clamp_fusion.2), kind=kCustom, calls=%fused_computation.2 | custom fusion | bytes 8388640 | tf_op jit(solution)/shard_map/jit(_take)/gather | solution.py:158
  43.0 44.6 %all-to-all-done.1.refs_1_.refs_2_ = bf16[8,2,128,1024]{3,2,1,0:T(8,128)(2,1)} async-done(((bf16[8,2,128,1024]{3,2,1,0:T(8,128)(2,1)}), bf16[8,2,128,1024]{3,2,1,0:T(8,128)(2,1)}, u32[]{:S(2)}, u32[]{:S(2)}) %all-to-all-start.1) | async-done | bytes 4194336 | tf_op jit(solution)/shard_map/all_to_all | solution.py:157
  87.6 4.8 %all-to-all-start = ((bf16[8,2,128,1024]{3,2,1,0:T(8,128)(2,1)}), bf16[8,2,128,1024]{3,2,1,0:T(8,128)(2,1)}, u32[]{:S(2)}, u32[]{:S(2)}) async-start(bf16[8,2,128,1024]{3,2,1,0:T(8,128)(2,1)} %gather_fusion), calls=%async_computation | async-start | bytes 8388608 | tf_op jit(solution)/shard_map/all_to_all | solution.py:159
  92.3 4.7 %constant_dynamic-slice_fusion.2 = bf16[1024,2048]{1,0:T(8,128)(2,1)} fusion(bf16[1024,4096]{1,0:T(8,128)(2,1)} %param.16, s32[]{:T(128)S(6)} %select_n.98), kind=kLoop, calls=%fused_computation.73 | loop fusion | bytes 8388612 | tf_op jit(solution)/shard_map/dynamic_slice | solution.py:140
  97.1 2.7 %collective-permute-start.4 = (bf16[1024,2048]{1,0:T(8,128)(2,1)}, bf16[1024,2048]{1,0:T(8,128)(2,1)}, u32[]{:S(2)}, u32[]{:S(2)}) collective-permute-start(bf16[1024,2048]{1,0:T(8,128)(2,1)} %constant_dynamic-slice_fusion.2), channel_id=1, source_target_pairs={{0,1},{1,0},{2,3},{3,2},{4,5},{5,4},{6,7},{7,6},{8,9},{9,8},{10,11... | collective-permute-start | bytes 12582920 | tf_op jit(solution)/shard_map/ppermute | solution.py:142
  100.7 0.7 clamp_select_fusion
  101.4 0.7 fusion.17
  102.0 8.6 %shard_map.83 = (bf16[256,1024]{1,0:T(8,128)(2,1)}, f32[8,256,1]{2,1,0:T(8,128)}, f32[8,256,1]{2,1,0:T(8,128)}) custom-call(bf16[256,1024]{1,0:T(8,128)(2,1)} %copy-done.2, bf16[8,2,128,1024]{3,2,1,0:T(8,128)(2,1)} %all-to-all-done.1.refs_1_.refs_2_, bf16[8,2,128,1024]{3,2,1,0:T(8,128)(2,1)} %all-to-all-done.1.refs_1_.refs_2_, s32[1,1024]{1,0:T(1,128)} %bitcast.71), custom_call_target="tpu_custom_call" | custom-call | tf_op jit(solution)/shard_map/pallas_call | solution.py:91
  110.6 1.5 copy.30
  112.1 1.6 copy.29
  113.7 3.0 %collective-permute-start.1 = (f32[8,256,2]{1,0,2:T(8,128)S(1)}, f32[8,256,2]{1,0,2:T(8,128)S(1)}, u32[]{:S(2)}, u32[]{:S(2)}) collective-permute-start(f32[8,256,2]{1,0,2:T(8,128)S(1)} %pad_maximum_fusion.2), channel_id=1, source_target_pairs={{0,16},{16,0},{1,17},{17,1},{2,18},{18,2},{3,19},{19,3},{4,20},{20... | collective-permute-start | bytes 49160 | tf_op jit(solution)/shard_map/ppermute | solution.py:169
  116.7 0.7 fusion.16
  117.4 0.9 copy.50
  118.3 33.8 %all-to-all-done.refs_3_.refs_4_ = bf16[8,2,128,1024]{3,2,1,0:T(8,128)(2,1)} async-done(((bf16[8,2,128,1024]{3,2,1,0:T(8,128)(2,1)}), bf16[8,2,128,1024]{3,2,1,0:T(8,128)(2,1)}, u32[]{:S(2)}, u32[]{:S(2)}) %all-to-all-start) | async-done | bytes 4194336 | tf_op jit(solution)/shard_map/all_to_all | solution.py:159
  152.0 9.9 %shard_map.82 = (f32[256,1024]{1,0:T(8,128)}, f32[8,256,1]{2,1,0:T(8,128)}, f32[8,256,1]{2,1,0:T(8,128)}) custom-call(bf16[256,1024]{1,0:T(8,128)(2,1)} %bitcast.61, bf16[256,1024]{1,0:T(8,128)(2,1)} %bitcast.62, bf16[256,1024]{1,0:T(8,128)(2,1)} %refs_2_.1, bf16[8,2,128,1024]{3,2,1,0:T(8,128)(2,1)} %all-to-all-done.refs_3_.refs_4_, ...), custom_call_target="tpu_custom_call" | custom-call | tf_op jit(solution)/shard_map/pallas_call | solution.py:91
  162.3 3.1 %fusion.21 = (f32[256,8,1]{2,0,1:T(8,128)}, f32[256,8,1]{2,0,1:T(8,128)S(1)}, f32[256,8,1]{2,0,1:T(8,128)S(1)}) fusion(f32[256,8,2]{2,0,1:T(8,128)S(1)} %bitcast.54, f32[8,256,1]{2,1,0:T(8,128)} %get-tuple-element.15, f32[8,256,1]{2,1,0:T(8,128)} %get-tuple-element.20), kind=kLoop, calls=%fused_computation.82 | loop fusion | flops 12288 | bytes 57344 | tf_op jit(solution)/shard_map/add | solution.py:184
  165.4 2.9 %copy.37 = f32[256,8,1]{1,0,2:T(8,128)S(1)} copy(f32[256,8,1]{2,0,1:T(8,128)} %get-tuple-element.26) | data formatting | bytes 16384 | tf_op jit(solution)/shard_map/div | solution.py:184
  168.3 1.6 copy.36
  169.9 1.6 copy.35
  172.5 1.8 fusion.8
  174.3 3.3 %collective-permute-start.3 = (bf16[256,1024]{1,0:T(8,128)(2,1)S(1)}, bf16[256,1024]{1,0:T(8,128)(2,1)S(1)}, u32[]{:S(2)}, u32[]{:S(2)}) collective-permute-start(bf16[256,1024]{1,0:T(8,128)(2,1)S(1)} %fusion.8), channel_id=1, source_target_pairs={{0,1},{1,0},{2,3},{3,2},{4,5},{5,4},{6,7},{7,6},{8,9},{9,8},{10,11... | collective-permute-start | bytes 1572872 | tf_op jit(solution)/shard_map/ppermute | solution.py:190
  177.6 3.4 %fusion = f32[256,2048]{1,0:T(8,128)S(1)} fusion(bf16[256,1024]{1,0:T(8,128)(2,1)S(1)} %fusion.8, bf16[1024,4096]{1,0:T(8,128)(2,1)} %param.16, s32[]{:T(128)S(6)} %select_n.96), kind=kOutput, calls=%fused_computation.4 | convolution fusion | flops 1073741824 | bytes 6815748 | tf_op jit(solution)/shard_map/dot_general | solution.py:187
  181.1 4.5 %fusion.3 = bf16[256,2048]{1,0:T(8,128)(2,1)} fusion(f32[256,2048]{1,0:T(8,128)S(1)} %fusion, bf16[256,1024]{1,0:T(8,128)(2,1)S(1)} %collective-permute-done.3, bf16[1024,2048]{1,0:T(8,128)(2,1)} %collective-permute-done.4, f32[2048]{0:T(1024)S(1)} %convert_element_type.63), kind=kOutput, calls=%fused_computation.8 | convolution fusion | flops 1075314688 | bytes 7872512 | tf_op jit(solution)/shard_map/dot_general | solution.py:191
  (48 shorter events, 5.5 us)
Async XLA Ops:
  0.0 2.7 %copy-start.5 = (s32[16]{0:T(128)S(1)}, s32[16]{0:T(128)}, u32[]{:S(2)}) copy-start(s32[16]{0:T(128)} %param.15) | copy-start | bytes 196
  5.2 3.5 %copy-start.3 = (s32[16,16]{1,0:T(8,128)S(1)}, s32[16,16]{1,0:T(8,128)}, u32[]{:S(2)}) copy-start(s32[16,16]{1,0:T(8,128)} %param.14) | copy-start | bytes 3076
  6.3 9.4 %copy-start = (bf16[32,8,8,128]{3,1,2,0:T(8,128)(2,1)}, bf16[32,8,8,128]{3,1,2,0:T(8,128)(2,1)S(1)}, u32[]{:S(2)}) copy-start(bf16[32,8,8,128]{3,1,2,0:T(8,128)(2,1)S(1)} %copy.51) | copy-start | bytes 1572868
  6.3 25.1 %collective-permute-start = (bf16[256,1024]{1,0:T(8,128)(2,1)S(1)}, bf16[256,1024]{1,0:T(8,128)(2,1)S(1)}, u32[]{:S(2)}, u32[]{:S(2)}) collective-permute-start(bf16[256,1024]{1,0:T(8,128)(2,1)S(1)} %bitcast.60), channel_id=1, source_target_pairs={{0,16},{16,0},{1,17},{17,1},{2,18},{18,2},{3,19},{19,3},{4,20},{20... | collective-permute-start | bytes 1572872 | tf_op jit(solution)/shard_map/ppermute | solution.py:153
  31.5 4.7 %copy-start.2 = (bf16[256,1024]{1,0:T(8,128)(2,1)}, bf16[256,1024]{1,0:T(8,128)(2,1)S(1)}, u32[]{:S(2)}) copy-start(bf16[256,1024]{1,0:T(8,128)(2,1)S(1)} %collective-permute-done.refs_0_) | copy-start | bytes 1572868
  31.5 56.1 %all-to-all-start.1 = ((bf16[8,2,128,1024]{3,2,1,0:T(8,128)(2,1)}), bf16[8,2,128,1024]{3,2,1,0:T(8,128)(2,1)}, u32[]{:S(2)}, u32[]{:S(2)}) async-start(bf16[8,2,128,1024]{3,2,1,0:T(8,128)(2,1)} %gather_fusion.1), calls=%async_computation.1 | async-start | bytes 8388608 | tf_op jit(solution)/shard_map/all_to_all | solution.py:157
  87.6 64.4 %all-to-all-start = ((bf16[8,2,128,1024]{3,2,1,0:T(8,128)(2,1)}), bf16[8,2,128,1024]{3,2,1,0:T(8,128)(2,1)}, u32[]{:S(2)}, u32[]{:S(2)}) async-start(bf16[8,2,128,1024]{3,2,1,0:T(8,128)(2,1)} %gather_fusion), calls=%async_computation | async-start | bytes 8388608 | tf_op jit(solution)/shard_map/all_to_all | solution.py:159
  97.1 84.0 %collective-permute-start.4 = (bf16[1024,2048]{1,0:T(8,128)(2,1)}, bf16[1024,2048]{1,0:T(8,128)(2,1)}, u32[]{:S(2)}, u32[]{:S(2)}) collective-permute-start(bf16[1024,2048]{1,0:T(8,128)(2,1)} %constant_dynamic-slice_fusion.2), channel_id=1, source_target_pairs={{0,1},{1,0},{2,3},{3,2},{4,5},{5,4},{6,7},{7,6},{8,9},{9,8},{10,11... | collective-permute-start | bytes 12582920 | tf_op jit(solution)/shard_map/ppermute | solution.py:142
  113.7 48.3 %collective-permute-start.1 = (f32[8,256,2]{1,0,2:T(8,128)S(1)}, f32[8,256,2]{1,0,2:T(8,128)S(1)}, u32[]{:S(2)}, u32[]{:S(2)}) collective-permute-start(f32[8,256,2]{1,0,2:T(8,128)S(1)} %pad_maximum_fusion.2), channel_id=1, source_target_pairs={{0,16},{16,0},{1,17},{17,1},{2,18},{18,2},{3,19},{19,3},{4,20},{20... | collective-permute-start | bytes 49160 | tf_op jit(solution)/shard_map/ppermute | solution.py:169
  116.7 54.8 %collective-permute-start.2 = (bf16[256,1024]{1,0:T(8,128)(2,1)}, bf16[256,1024]{1,0:T(8,128)(2,1)}, u32[]{:S(2)}, u32[]{:S(2)}) collective-permute-start(bf16[256,1024]{1,0:T(8,128)(2,1)} %get-tuple-element.21), channel_id=1, source_target_pairs={{0,16},{16,0},{1,17},{17,1},{2,18},{18,2},{3,19},{19,3},{4,20},{20... | collective-permute-start | bytes 1572872 | tf_op jit(solution)/shard_map/ppermute | solution.py:168
  165.4 7.1 %copy-start.1 = (f32[256,1024]{1,0:T(8,128)S(1)}, f32[256,1024]{1,0:T(8,128)}, u32[]{:S(2)}) copy-start(f32[256,1024]{1,0:T(8,128)} %get-tuple-element.14) | copy-start | bytes 3145732
  171.5 6.1 %copy-start.4 = (bf16[2048]{0:T(1024)(128)(2,1)S(1)}, bf16[2048]{0:T(1024)(128)(2,1)}, u32[]{:S(2)}) copy-start(bf16[2048]{0:T(1024)(128)(2,1)} %param.17) | copy-start | bytes 12292
  174.3 6.8 %collective-permute-start.3 = (bf16[256,1024]{1,0:T(8,128)(2,1)S(1)}, bf16[256,1024]{1,0:T(8,128)(2,1)S(1)}, u32[]{:S(2)}, u32[]{:S(2)}) collective-permute-start(bf16[256,1024]{1,0:T(8,128)(2,1)S(1)} %fusion.8), channel_id=1, source_target_pairs={{0,1},{1,0},{2,3},{3,2},{4,5},{5,4},{6,7},{7,6},{8,9},{9,8},{10,11... | collective-permute-start | bytes 1572872 | tf_op jit(solution)/shard_map/ppermute | solution.py:190

commit v6 on v3

--- a/solution.py
+++ b/solution.py
@@ -38,9 +38,9 @@
 
 def attention_kernel(*refs, with_local):
     if with_local:
-        q_ref, kl_ref, vl_ref, kp_ref, vp_ref, ok_ref, o_ref, m_ref, l_ref = refs
+        q_ref, kl_ref, vl_ref, kp_ref, vp_ref, ok_ref, bo_ref, bst_ref, o_ref = refs
     else:
-        q_ref, kp_ref, vp_ref, ok_ref, o_ref, m_ref, l_ref = refs
+        q_ref, kp_ref, vp_ref, ok_ref, o_ref, st_ref = refs
     score_scale = 1.0 / math.sqrt(HEAD_DIM)
     dims = (((1,), (1,)), ((), ()))
     q = q_ref[...]
@@ -65,12 +65,21 @@
         p_loc = jnp.exp(s_loc - m)
         l = l + jnp.sum(p_loc, axis=1, keepdims=True)
         acc = acc + jnp.dot(p_loc.astype(jnp.bfloat16), vl_ref[...], preferred_element_type=jnp.float32)
-    o_ref[...] = (acc / l).astype(o_ref.dtype)
-    m_ref[...] = m
-    l_ref[...] = l
-
-
-def attend(key_ok, query_rot, incoming, which, out_dtype, local=None):
+        stats = bst_ref[...]
+        back_max = stats[:, 0:1]
+        back_sum = stats[:, 1:2]
+        peak = jnp.maximum(m, back_max)
+        near_w = jnp.exp(m - peak)
+        back_w = jnp.exp(back_max - peak) * back_sum
+        merged = acc * near_w + bo_ref[...].astype(jnp.float32) * back_w
+        o_ref[...] = (merged / (l * near_w + back_w)).astype(o_ref.dtype)
+    else:
+        o_ref[...] = (acc / l).astype(o_ref.dtype)
+        st_ref[:, 0:1] = m
+        st_ref[:, 1:2] = l
+
+
+def attend(key_ok, query_rot, incoming, which, local=None, back=None):
     span, width = query_rot.shape
     head_count = width // HEAD_DIM
     block_count = incoming.shape[0]
@@ -81,23 +90,23 @@
         pl.BlockSpec((block_count, None, None, page_size, HEAD_DIM), lambda h: (0, which, 1, 0, h)),
         pl.BlockSpec((1, block_count * page_size), lambda h: (0, 0)),
     ]
-    stat_spec = pl.BlockSpec((None, span, 1), lambda h: (h, 0, 0))
+    stat_spec = pl.BlockSpec((None, span, 2), lambda h: (h, 0, 0))
+    out_shape = jax.ShapeDtypeStruct((span, width), jnp.bfloat16)
     if local is None:
         in_specs = [col_spec] + page_specs
         operands = (query_rot, incoming, incoming, key_ok)
+        out_specs = [col_spec, stat_spec]
+        out_shape = [out_shape, jax.ShapeDtypeStruct((head_count, span, 2), jnp.float32)]
     else:
-        in_specs = [col_spec, col_spec, col_spec] + page_specs
-        operands = (query_rot, local[0], local[1], incoming, incoming, key_ok)
+        in_specs = [col_spec, col_spec, col_spec] + page_specs + [col_spec, stat_spec]
+        operands = (query_rot, local[0], local[1], incoming, incoming, key_ok, back[0], back[1])
+        out_specs = col_spec
     return pl.pallas_call(
         partial(attention_kernel, with_local=local is not None),
         grid=(head_count,),
         in_specs=in_specs,
-        out_specs=[col_spec, stat_spec, stat_spec],
-        out_shape=[
-            jax.ShapeDtypeStruct((span, width), out_dtype),
-            jax.ShapeDtypeStruct((head_count, span, 1), jnp.float32),
-            jax.ShapeDtypeStruct((head_count, span, 1), jnp.float32),
-        ],
+        out_specs=out_specs,
+        out_shape=out_shape,
     )(*operands)
 
 
@@ -112,10 +121,6 @@
     nvalid = jnp.where(present, jnp.clip(length - slot_of * page_size, 0, page_size), 0)
     within = jnp.arange(page_size, dtype=jnp.int32)
     return (within[None, :] < nvalid[:, None]).astype(jnp.int32).reshape(1, source_count * page_size)
-
-
-def by_rows(stat):
-    return jnp.transpose(stat, (1, 0, 2))
 
 
 def on_device(new_queries, new_keys, new_values, kv_pages, page_table, cache_len, w_out, out_bias):
@@ -162,26 +167,12 @@
     ok_own = usable_keys(page_table, own_index, own_length, source_base, sub_count, page_count, page_size)
     ok_partner = usable_keys(page_table, partner, partner_length, source_base, sub_count, page_count, page_size)
 
-    far_out, far_max, far_sum = attend(ok_partner, partner_query, incoming, 1, jnp.bfloat16)
-    far_stats = jnp.concatenate([far_max, far_sum], axis=2)
+    far_out, far_stats = attend(ok_partner, partner_query, incoming, 1)
     back_out = lax.ppermute(far_out, "half", swap)
     back_stats = lax.ppermute(far_stats, "half", swap)
-    near_out, near_max, near_sum = attend(
-        ok_own, query_rot, incoming, 0, jnp.float32, local=(key_rot, new_values)
+    attended = attend(
+        ok_own, query_rot, incoming, 0, local=(key_rot, new_values), back=(back_out, back_stats)
     )
-
-    near_max = by_rows(near_max)
-    near_sum = by_rows(near_sum)
-    back_stats = by_rows(back_stats)
-    back_max = back_stats[:, :, 0:1]
-    back_sum = back_stats[:, :, 1:2]
-    peak = jnp.maximum(near_max, back_max)
-    near_w = jnp.exp(near_max - peak) * near_sum
-    back_w = jnp.exp(back_max - peak) * back_sum
-    near3 = near_out.reshape(span_len, head_count, HEAD_DIM)
-    back3 = back_out.astype(jnp.float32).reshape(span_len, head_count, HEAD_DIM)
-    merged = (near3 * near_w + back3 * back_w) / (near_w + back_w)
-    attended = merged.reshape(span_len, width).astype(jnp.bfloat16)
 
     summed = jnp.dot(attended, w_mine, preferred_element_type=jnp.float32)
     for shift in range(1, tp_count):

time: 182 us -> 191 us (1.049)
  waiting for transfers between devices: 100 us -> 120 us
  local copies, waits for them, and re-layouts: 27.6 us -> 20.9 us
  other arithmetic: 12 us -> 7.36 us
  Pallas kernels: 18.5 us -> 22.4 us
    ppermute x1, waiting for transfers between devices: 0.01 us -> 17.7 us  [on_device(): back_stats = lax.ppermute(far_stats, 'half', swap)]
    mul x4 -> x0, local copies, waits for them, and re-layouts: 5.14 us -> none  [on_device(): merged = (near3 * near_w + back3 * back_w) / (near_w + back_w)]
    pallas_call x2, Pallas kernels: 18.5 us -> 22.4 us  [attend(): pl.pallas_call(partial(attention_kernel, with_local=local is not None), g...]
    add x1 -> x0, other arithmetic: 3 us -> none  [on_device(): merged = (near3 * near_w + back3 * back_w) / (near_w + back_w)]
    ppermute x1, starting transfers between devices: 0.05 us -> 2.38 us  [on_device(): back_stats = lax.ppermute(far_stats, 'half', swap)]
    ppermute x1, starting transfers between devices: 2.35 us -> 0.07 us  [on_device(): back_out = lax.ppermute(far_out, 'half', swap)]
    div x2 -> x0, local copies, waits for them, and re-layouts: 1.93 us -> none  [on_device(): merged = (near3 * near_w + back3 * back_w) / (near_w + back_w)]
  transfers between devices with their start and end apart: 6 -> 6, of which waited for: 1 -> 3; matrix products, arithmetic and copies ran while one was open for 18% -> 9% of each run, Pallas kernels for 10% -> 12%
where the time goes in v6:
time: 191 us; the launch traced here: 190 us
  waiting for transfers between devices  120 us (63%)
  Pallas kernels  22.4 us (12%)
  local copies, waits for them, and re-layouts  20.9 us (11%)
  starting transfers between devices  11.2 us (6%)
  matrix products  7.92 us (4%)
  other arithmetic  7.36 us (4%)
    ppermute x1, waiting for transfers between devices, on_device(): partner_query = lax.ppermute(query_rot, 'half', swap)  100 us
    pallas_call x2, Pallas kernels, attend(): pl.pallas_call(partial(attention_kernel, with_local=local is not None), g...  22.4 us
    ppermute x1, waiting for transfers between devices, on_device(): back_stats = lax.ppermute(far_stats, 'half', swap)  17.7 us
    gather x1, local copies, waits for them, and re-layouts, on_device(): jnp.take(kv_pages, jnp.take(local_page, wanted), axis=0, mode='clip')  8.17 us
    all_to_all x1, starting transfers between devices, on_device(): lax.all_to_all(outgoing, 'sub', split_axis=0, concat_axis=0, tiled=True)  4.93 us
    dynamic_slice x1, local copies, waits for them, and re-layouts, on_device(): piece = lax.dynamic_slice_in_dim(w_out, target * out_cols, out_cols, axis=1)  4.81 us
    dot_general x1, matrix products, on_device(): summed = jnp.dot(attended, w_mine, preferred_element_type=jnp.float32)  4.48 us
  transfers between devices with their start and end apart: 6, of which 3 were waited for; matrix products, arithmetic and copies ran while one was open for 9% of the time, Pallas kernels for 12%

profile of v6, /device:TPU:11, one launch (start us, length us, event | category | flops | bytes accessed | tf_op | source)
XLA Modules:
  0.0 189.6 jit_solution(868812463835627112)
XLA Ops:
  0.2 0.8 select_reduce_fusion
  1.0 0.7 gather_fusion
  1.7 8.2 %gather_fusion.1 = bf16[16,2,128,1024]{3,2,1,0:T(8,128)(2,1)} fusion(bf16[16,2,128,1024]{3,2,1,0:T(8,128)(2,1)} %param.11, s32[1024]{0:T(1024)S(1)} %pad_clamp_fusion), kind=kCustom, calls=%fused_computation.1 | custom fusion | bytes 16777280 | tf_op jit(solution)/shard_map/jit(_take)/gather | solution.py:155
  9.9 4.9 %all-to-all-start = ((bf16[8,2,2,128,1024]{4,3,2,1,0:T(8,128)(2,1)}), bf16[8,2,2,128,1024]{4,3,2,1,0:T(8,128)(2,1)}, u32[]{:S(2)}, u32[]{:S(2)}) async-start(bf16[8,2,2,128,1024]{4,3,2,1,0:T(8,128)(2,1)} %bitcast.34), calls=%async_computation | async-start | bytes 16777216 | tf_op jit(solution)/shard_map/all_to_all | solution.py:157
  14.9 4.8 %constant_dynamic-slice_fusion.1 = bf16[1024,2048]{1,0:T(8,128)(2,1)} fusion(bf16[1024,4096]{1,0:T(8,128)(2,1)} %param.14, s32[]{:T(128)S(6)} %select_n.121), kind=kLoop, calls=%fused_computation.55 | loop fusion | bytes 8388612 | tf_op jit(solution)/shard_map/dynamic_slice | solution.py:145
  19.7 0.9 collective-permute-start.4
  20.6 0.2 slice.32
  21.0 0.7 fusion.24
  21.7 0.7 add_convert_fusion.2
  22.7 0.2 slice.35
  23.1 0.7 subtract_convert_fusion
  23.9 1.0 pad_maximum_fusion
  25.0 2.5 %collective-permute-start = (bf16[256,1024]{1,0:T(8,128)(2,1)S(1)}, bf16[256,1024]{1,0:T(8,128)(2,1)S(1)}, u32[]{:S(2)}, u32[]{:S(2)}) collective-permute-start(bf16[256,1024]{1,0:T(8,128)(2,1)S(1)} %bitcast.37), channel_id=1, source_target_pairs={{0,16},{16,0},{1,17},{17,1},{2,18},{18,2},{3,19},{19,3},{4,20},{20... | collective-permute-start | bytes 1572872 | tf_op jit(solution)/shard_map/ppermute | solution.py:164
  27.4 0.7 fusion.21
  28.2 0.2 compare_reduce_fusion
  28.5 1.3 clamp_select_fusion
  29.9 0.7 fusion.18
  30.5 100.2 %collective-permute-done.refs_0_ = bf16[256,1024]{1,0:T(8,128)(2,1)S(1)} collective-permute-done((bf16[256,1024]{1,0:T(8,128)(2,1)S(1)}, bf16[256,1024]{1,0:T(8,128)(2,1)S(1)}, u32[]{:S(2)}, u32[]{:S(2)}) %collective-permute-start) | collective-permute-done | bytes 524320 | tf_op jit(solution)/shard_map/ppermute | solution.py:164
  130.7 0.8 copy-done.1
  131.6 8.5 %shard_map.82 = (bf16[256,1024]{1,0:T(8,128)(2,1)}, f32[8,256,2]{2,1,0:T(8,128)}) custom-call(bf16[256,1024]{1,0:T(8,128)(2,1)} %copy-done.1, bf16[8,2,2,128,1024]{4,3,2,1,0:T(8,128)(2,1)} %all-to-all-done.refs_1_.refs_2_.refs_3_.refs_4_, bf16[8,2,2,128,1024]{4,3,2,1,0:T(8,128)(2,1)} %all-to-all-done.refs_1_.refs_2_.refs_3_.refs_4_, s32[1,1024]{1,0:T(1,128)} %bitcast.44), custom_call_target="tpu_custom_call" | custom-call | tf_op jit(solution)/shard_map/pallas_call | solution.py:104
  140.1 1.5 copy.18
  141.7 2.4 %collective-permute-start.2 = (f32[8,256,2]{1,0,2:T(8,128)S(1)}, f32[8,256,2]{1,0,2:T(8,128)S(1)}, u32[]{:S(2)}, u32[]{:S(2)}) collective-permute-start(f32[8,256,2]{1,0,2:T(8,128)S(1)} %copy.18), channel_id=1, source_target_pairs={{0,16},{16,0},{1,17},{17,1},{2,18},{18,2},{3,19},{19,3},{4,20},{20... | collective-permute-start | bytes 49160 | tf_op jit(solution)/shard_map/ppermute | solution.py:172
  144.1 0.7 fusion.17
  144.7 0.9 copy.26
  145.7 17.7 %collective-permute-done.2 = f32[8,256,2]{1,0,2:T(8,128)S(1)} collective-permute-done((f32[8,256,2]{1,0,2:T(8,128)S(1)}, f32[8,256,2]{1,0,2:T(8,128)S(1)}, u32[]{:S(2)}, u32[]{:S(2)}) %collective-permute-start.2) | collective-permute-done | bytes 16416 | tf_op jit(solution)/shard_map/ppermute | solution.py:172
  163.3 1.3 copy.19.refs_7_
  164.7 0.8 copy-done.3
  165.5 13.9 %shard_map.83 = bf16[256,1024]{1,0:T(8,128)(2,1)} custom-call(bf16[256,1024]{1,0:T(8,128)(2,1)} %bitcast.38, bf16[256,1024]{1,0:T(8,128)(2,1)} %bitcast.39, bf16[256,1024]{1,0:T(8,128)(2,1)} %refs_2_.1, bf16[8,2,2,128,1024]{4,3,2,1,0:T(8,128)(2,1)} %all-to-all-done.refs_1_.refs_2_.refs_3_.refs_4_, ...), custom_call_target="tpu_custom_call" | custom-call | tf_op jit(solution)/shard_map/pallas_call | solution.py:104
  179.4 0.5 collective-permute-start.3
  179.9 1.7 collective-permute-done.3
  181.6 3.4 %fusion.25 = f32[256,2048]{1,0:T(8,128)S(1)} fusion(bf16[256,1024]{1,0:T(8,128)(2,1)S(1)} %collective-permute-done.3, bf16[1024,2048]{1,0:T(8,128)(2,1)} %collective-permute-done.4), kind=kOutput, calls=%fused_computation.70 | convolution fusion | flops 1073741824 | bytes 6815744 | tf_op jit(solution)/shard_map/dot_general | solution.py:181
  185.1 4.5 %fusion.8 = bf16[256,2048]{1,0:T(8,128)(2,1)} fusion(f32[256,2048]{1,0:T(8,128)S(1)} %fusion.25, bf16[256,1024]{1,0:T(8,128)(2,1)S(1)} %copy-done.2, bf16[1024,4096]{1,0:T(8,128)(2,1)} %param.14, s32[]{:T(128)S(6)} %select_n.119, f32[2048]{0:T(1024)S(1)} %convert_element_type.55), kind=kOutput, calls=%fused_computation.6 | convolution fusion | flops 1075314688 | bytes 7872516 | tf_op jit(solution)/shard_map/dot_general | solution.py:177
  (38 shorter events, 1.3 us)
Async XLA Ops:
  9.9 120.8 %all-to-all-start = ((bf16[8,2,2,128,1024]{4,3,2,1,0:T(8,128)(2,1)}), bf16[8,2,2,128,1024]{4,3,2,1,0:T(8,128)(2,1)}, u32[]{:S(2)}, u32[]{:S(2)}) async-start(bf16[8,2,2,128,1024]{4,3,2,1,0:T(8,128)(2,1)} %bitcast.34), calls=%async_computation | async-start | bytes 16777216 | tf_op jit(solution)/shard_map/all_to_all | solution.py:157
  14.8 5.7 %copy-start.4 = (bf16[256,1024]{1,0:T(8,128)(2,1)S(1)}, bf16[256,1024]{1,0:T(8,128)(2,1)}, u32[]{:S(2)}) copy-start(bf16[256,1024]{1,0:T(8,128)(2,1)} %param.8) | copy-start | bytes 1572868
  14.8 6.0 %copy-start.5 = (bf16[256,1024]{1,0:T(8,128)(2,1)S(1)}, bf16[256,1024]{1,0:T(8,128)(2,1)}, u32[]{:S(2)}) copy-start(bf16[256,1024]{1,0:T(8,128)(2,1)} %param.9) | copy-start | bytes 1572868
  14.8 6.1 %copy-start.7 = (s32[16]{0:T(128)S(1)}, s32[16]{0:T(128)}, u32[]{:S(2)}) copy-start(s32[16]{0:T(128)} %param.13) | copy-start | bytes 196
  19.7 160.2 %collective-permute-start.4 = (bf16[1024,2048]{1,0:T(8,128)(2,1)}, bf16[1024,2048]{1,0:T(8,128)(2,1)}, u32[]{:S(2)}, u32[]{:S(2)}) collective-permute-start(bf16[1024,2048]{1,0:T(8,128)(2,1)} %constant_dynamic-slice_fusion.1), channel_id=1, source_target_pairs={{0,1},{1,0},{2,3},{3,2},{4,5},{5,4},{6,7},{7,6},{8,9},{9,8},{10,11... | collective-permute-start | bytes 12582920 | tf_op jit(solution)/shard_map/ppermute | solution.py:147
  24.9 115.1 %copy-start = (bf16[32,8,8,128]{3,1,2,0:T(8,128)(2,1)}, bf16[32,8,8,128]{3,1,2,0:T(8,128)(2,1)S(1)}, u32[]{:S(2)}) copy-start(bf16[32,8,8,128]{3,1,2,0:T(8,128)(2,1)S(1)} %copy.27) | copy-start | bytes 1572868
  25.0 105.7 %collective-permute-start = (bf16[256,1024]{1,0:T(8,128)(2,1)S(1)}, bf16[256,1024]{1,0:T(8,128)(2,1)S(1)}, u32[]{:S(2)}, u32[]{:S(2)}) collective-permute-start(bf16[256,1024]{1,0:T(8,128)(2,1)S(1)} %bitcast.37), channel_id=1, source_target_pairs={{0,16},{16,0},{1,17},{17,1},{2,18},{18,2},{3,19},{19,3},{4,20},{20... | collective-permute-start | bytes 1572872 | tf_op jit(solution)/shard_map/ppermute | solution.py:164
  130.7 0.8 copy-start.1
  140.1 24.6 %collective-permute-start.1 = (bf16[256,1024]{1,0:T(8,128)(2,1)}, bf16[256,1024]{1,0:T(8,128)(2,1)S(1)}, u32[]{:S(2)}, u32[]{:S(2)}) collective-permute-start(bf16[256,1024]{1,0:T(8,128)(2,1)} %get-tuple-element.7), channel_id=1, source_target_pairs={{0,16},{16,0},{1,17},{17,1},{2,18},{18,2},{3,19},{19,3},{4,20},{20... | collective-permute-start | bytes 1572872 | tf_op jit(solution)/shard_map/ppermute | solution.py:171
  141.7 21.7 %collective-permute-start.2 = (f32[8,256,2]{1,0,2:T(8,128)S(1)}, f32[8,256,2]{1,0,2:T(8,128)S(1)}, u32[]{:S(2)}, u32[]{:S(2)}) collective-permute-start(f32[8,256,2]{1,0,2:T(8,128)S(1)} %copy.18), channel_id=1, source_target_pairs={{0,16},{16,0},{1,17},{17,1},{2,18},{18,2},{3,19},{19,3},{4,20},{20... | collective-permute-start | bytes 49160 | tf_op jit(solution)/shard_map/ppermute | solution.py:172
  164.7 0.8 copy-start.3
  165.5 14.4 %copy-start.6 = (bf16[2048]{0:T(1024)(128)(2,1)S(1)}, bf16[2048]{0:T(1024)(128)(2,1)}, u32[]{:S(2)}) copy-start(bf16[2048]{0:T(1024)(128)(2,1)} %param.15) | copy-start | bytes 12292
  179.4 5.7 %copy-start.2 = (bf16[256,1024]{1,0:T(8,128)(2,1)S(1)}, bf16[256,1024]{1,0:T(8,128)(2,1)}, u32[]{:S(2)}) copy-start(bf16[256,1024]{1,0:T(8,128)(2,1)} %shard_map.83) | copy-start | bytes 1572868
  179.4 2.2 %collective-permute-start.3 = (bf16[256,1024]{1,0:T(8,128)(2,1)}, bf16[256,1024]{1,0:T(8,128)(2,1)S(1)}, u32[]{:S(2)}, u32[]{:S(2)}) collective-permute-start(bf16[256,1024]{1,0:T(8,128)(2,1)} %shard_map.83), channel_id=1, source_target_pairs={{0,1},{1,0},{2,3},{3,2},{4,5},{5,4},{6,7},{7,6},{8,9},{9,8},{10,11... | collective-permute-start | bytes 1572872 | tf_op jit(solution)/shard_map/ppermute | solution.py:180

commit v7 on v6

--- a/solution.py
+++ b/solution.py
@@ -38,7 +38,7 @@
 
 def attention_kernel(*refs, with_local):
     if with_local:
-        q_ref, kl_ref, vl_ref, kp_ref, vp_ref, ok_ref, bo_ref, bst_ref, o_ref = refs
+        q_ref, kl_ref, vl_ref, kp_ref, vp_ref, ok_ref, o_ref, st_ref = refs
     else:
         q_ref, kp_ref, vp_ref, ok_ref, o_ref, st_ref = refs
     score_scale = 1.0 / math.sqrt(HEAD_DIM)
@@ -65,21 +65,16 @@
         p_loc = jnp.exp(s_loc - m)
         l = l + jnp.sum(p_loc, axis=1, keepdims=True)
         acc = acc + jnp.dot(p_loc.astype(jnp.bfloat16), vl_ref[...], preferred_element_type=jnp.float32)
-        stats = bst_ref[...]
-        back_max = stats[:, 0:1]
-        back_sum = stats[:, 1:2]
-        peak = jnp.maximum(m, back_max)
-        near_w = jnp.exp(m - peak)
-        back_w = jnp.exp(back_max - peak) * back_sum
-        merged = acc * near_w + bo_ref[...].astype(jnp.float32) * back_w
-        o_ref[...] = (merged / (l * near_w + back_w)).astype(o_ref.dtype)
+        o_ref[...] = acc
+        st_ref[:, 0:1] = m
+        st_ref[:, 1:2] = l
     else:
         o_ref[...] = (acc / l).astype(o_ref.dtype)
         st_ref[:, 0:1] = m
         st_ref[:, 1:2] = l
 
 
-def attend(key_ok, query_rot, incoming, which, local=None, back=None):
+def attend(key_ok, query_rot, incoming, which, local=None):
     span, width = query_rot.shape
     head_count = width // HEAD_DIM
     block_count = incoming.shape[0]
@@ -91,16 +86,16 @@
         pl.BlockSpec((1, block_count * page_size), lambda h: (0, 0)),
     ]
     stat_spec = pl.BlockSpec((None, span, 2), lambda h: (h, 0, 0))
-    out_shape = jax.ShapeDtypeStruct((span, width), jnp.bfloat16)
+    stat_shape = jax.ShapeDtypeStruct((head_count, span, 2), jnp.float32)
+    out_specs = [col_spec, stat_spec]
     if local is None:
         in_specs = [col_spec] + page_specs
         operands = (query_rot, incoming, incoming, key_ok)
-        out_specs = [col_spec, stat_spec]
-        out_shape = [out_shape, jax.ShapeDtypeStruct((head_count, span, 2), jnp.float32)]
+        out_shape = [jax.ShapeDtypeStruct((span, width), jnp.bfloat16), stat_shape]
     else:
-        in_specs = [col_spec, col_spec, col_spec] + page_specs + [col_spec, stat_spec]
-        operands = (query_rot, local[0], local[1], incoming, incoming, key_ok, back[0], back[1])
-        out_specs = col_spec
+        in_specs = [col_spec, col_spec, col_spec] + page_specs
+        operands = (query_rot, local[0], local[1], incoming, incoming, key_ok)
+        out_shape = [jax.ShapeDtypeStruct((span, width), jnp.float32), stat_shape]
     return pl.pallas_call(
         partial(attention_kernel, with_local=local is not None),
         grid=(head_count,),
@@ -108,6 +103,33 @@
         out_specs=out_specs,
         out_shape=out_shape,
     )(*operands)
+
+
+def merge_kernel(na_ref, nst_ref, bo_ref, bst_ref, o_ref):
+    near = nst_ref[...]
+    back = bst_ref[...]
+    near_max = near[:, 0:1]
+    near_sum = near[:, 1:2]
+    back_max = back[:, 0:1]
+    back_sum = back[:, 1:2]
+    peak = jnp.maximum(near_max, back_max)
+    near_w = jnp.exp(near_max - peak)
+    back_w = jnp.exp(back_max - peak) * back_sum
+    merged = na_ref[...] * near_w + bo_ref[...].astype(jnp.float32) * back_w
+    o_ref[...] = (merged / (near_sum * near_w + back_w)).astype(o_ref.dtype)
+
+
+def merge(near_acc, near_stats, back_out, back_stats):
+    span, width = near_acc.shape
+    col_spec = pl.BlockSpec((span, HEAD_DIM), lambda h: (0, h))
+    stat_spec = pl.BlockSpec((None, span, 2), lambda h: (h, 0, 0))
+    return pl.pallas_call(
+        merge_kernel,
+        grid=(width // HEAD_DIM,),
+        in_specs=[col_spec, stat_spec, col_spec, stat_spec],
+        out_specs=col_spec,
+        out_shape=jax.ShapeDtypeStruct((span, width), jnp.bfloat16),
+    )(near_acc, near_stats, back_out, back_stats)
 
 
 def usable_keys(page_table, request, length, source_base, source_count, page_count, page_size):
@@ -170,9 +192,8 @@
     far_out, far_stats = attend(ok_partner, partner_query, incoming, 1)
     back_out = lax.ppermute(far_out, "half", swap)
     back_stats = lax.ppermute(far_stats, "half", swap)
-    attended = attend(
-        ok_own, query_rot, incoming, 0, local=(key_rot, new_values), back=(back_out, back_stats)
-    )
+    near_acc, near_stats = attend(ok_own, query_rot, incoming, 0, local=(key_rot, new_values))
+    attended = merge(near_acc, near_stats, back_out, back_stats)
 
     summed = jnp.dot(attended, w_mine, preferred_element_type=jnp.float32)
     for shift in range(1, tp_count):

time: 191 us -> 185 us (0.969)
  waiting for transfers between devices: 120 us -> 110 us
  Pallas kernels: 22.4 us -> 25.3 us
    ppermute x1, waiting for transfers between devices: 17.7 us -> 7.74 us  [on_device(): back_stats = lax.ppermute(far_stats, 'half', swap)]
    pallas_call x0 -> x1, Pallas kernels: none -> 6.9 us  [merge(): pl.pallas_call(merge_kernel, grid=(width // HEAD_DIM,), in_specs=[col_spe...]
    pallas_call x2, Pallas kernels: 22.4 us -> 18.4 us  [attend(): pl.pallas_call(partial(attention_kernel, with_local=local is not None), g...]
  transfers between devices with their start and end apart: 6 -> 6, of which waited for: 3 -> 3; matrix products, arithmetic and copies ran while one was open for 9% -> 9% of each run, Pallas kernels for 12% -> 14%
where the time goes in v7:
time: 185 us; the launch traced here: 182 us
  waiting for transfers between devices  110 us (59%)
  Pallas kernels  25.3 us (14%)
  local copies, waits for them, and re-layouts  20.7 us (11%)
  starting transfers between devices  11.2 us (6%)
  matrix products  7.92 us (4%)
  other arithmetic  7.2 us (4%)
    ppermute x1, waiting for transfers between devices, on_device(): partner_query = lax.ppermute(query_rot, 'half', swap)  100 us
    pallas_call x2, Pallas kernels, attend(): pl.pallas_call(partial(attention_kernel, with_local=local is not None), g...  18.4 us
    gather x1, local copies, waits for them, and re-layouts, on_device(): jnp.take(kv_pages, jnp.take(local_page, wanted), axis=0, mode='clip')  8.16 us
    ppermute x1, waiting for transfers between devices, on_device(): back_stats = lax.ppermute(far_stats, 'half', swap)  7.74 us
    pallas_call x1, Pallas kernels, merge(): pl.pallas_call(merge_kernel, grid=(width // HEAD_DIM,), in_specs=[col_spe...  6.9 us
    all_to_all x1, starting transfers between devices, on_device(): lax.all_to_all(outgoing, 'sub', split_axis=0, concat_axis=0, tiled=True)  4.92 us
    dynamic_slice x1, local copies, waits for them, and re-layouts, on_device(): piece = lax.dynamic_slice_in_dim(w_out, target * out_cols, out_cols, axis=1)  4.81 us
    dot_general x1, matrix products, on_device(): summed = jnp.dot(attended, w_mine, preferred_element_type=jnp.float32)  4.48 us
  transfers between devices with their start and end apart: 6, of which 3 were waited for; matrix products, arithmetic and copies ran while one was open for 9% of the time, Pallas kernels for 14%

profile of v7, /device:TPU:11, one launch (start us, length us, event | category | flops | bytes accessed | tf_op | source)
XLA Modules:
  0.0 182.5 jit_solution(13750794689548898171)
XLA Ops:
  0.2 0.8 select_reduce_fusion
  1.0 0.7 gather_fusion
  1.7 8.2 %gather_fusion.1 = bf16[16,2,128,1024]{3,2,1,0:T(8,128)(2,1)} fusion(bf16[16,2,128,1024]{3,2,1,0:T(8,128)(2,1)} %param.11, s32[1024]{0:T(1024)S(1)} %pad_clamp_fusion), kind=kCustom, calls=%fused_computation.1 | custom fusion | bytes 16777280 | tf_op jit(solution)/shard_map/jit(_take)/gather | solution.py:177
  9.9 4.9 %all-to-all-start = ((bf16[8,2,2,128,1024]{4,3,2,1,0:T(8,128)(2,1)}), bf16[8,2,2,128,1024]{4,3,2,1,0:T(8,128)(2,1)}, u32[]{:S(2)}, u32[]{:S(2)}) async-start(bf16[8,2,2,128,1024]{4,3,2,1,0:T(8,128)(2,1)} %bitcast.34), calls=%async_computation | async-start | bytes 16777216 | tf_op jit(solution)/shard_map/all_to_all | solution.py:179
  14.8 4.8 %constant_dynamic-slice_fusion.1 = bf16[1024,2048]{1,0:T(8,128)(2,1)} fusion(bf16[1024,4096]{1,0:T(8,128)(2,1)} %param.14, s32[]{:T(128)S(6)} %select_n.121), kind=kLoop, calls=%fused_computation.55 | loop fusion | bytes 8388612 | tf_op jit(solution)/shard_map/dynamic_slice | solution.py:167
  19.7 0.9 collective-permute-start.4
  20.6 0.2 slice.32
  21.0 0.6 fusion.24
  21.6 0.6 add_convert_fusion.2
  22.6 0.2 slice.35
  23.0 0.7 subtract_convert_fusion
  23.7 1.0 pad_maximum_fusion
  24.8 2.5 %collective-permute-start = (bf16[256,1024]{1,0:T(8,128)(2,1)S(1)}, bf16[256,1024]{1,0:T(8,128)(2,1)S(1)}, u32[]{:S(2)}, u32[]{:S(2)}) collective-permute-start(bf16[256,1024]{1,0:T(8,128)(2,1)S(1)} %bitcast.37), channel_id=1, source_target_pairs={{0,16},{16,0},{1,17},{17,1},{2,18},{18,2},{3,19},{19,3},{4,20},{20... | collective-permute-start | bytes 1572872 | tf_op jit(solution)/shard_map/ppermute | solution.py:186
  27.3 0.7 fusion.21
  28.4 1.3 clamp_select_fusion
  29.7 0.7 fusion.18
  30.3 100.4 %collective-permute-done.refs_0_ = bf16[256,1024]{1,0:T(8,128)(2,1)S(1)} collective-permute-done((bf16[256,1024]{1,0:T(8,128)(2,1)S(1)}, bf16[256,1024]{1,0:T(8,128)(2,1)S(1)}, u32[]{:S(2)}, u32[]{:S(2)}) %collective-permute-start) | collective-permute-done | bytes 524320 | tf_op jit(solution)/shard_map/ppermute | solution.py:186
  130.7 0.8 copy-done.1
  131.5 8.5 %shard_map.83 = (bf16[256,1024]{1,0:T(8,128)(2,1)}, f32[8,256,2]{2,1,0:T(8,128)}) custom-call(bf16[256,1024]{1,0:T(8,128)(2,1)} %copy-done.1, bf16[8,2,2,128,1024]{4,3,2,1,0:T(8,128)(2,1)} %all-to-all-done.refs_3_.refs_4_.refs_1_.refs_2_, bf16[8,2,2,128,1024]{4,3,2,1,0:T(8,128)(2,1)} %all-to-all-done.refs_3_.refs_4_.refs_1_.refs_2_, s32[1,1024]{1,0:T(1,128)} %bitcast.44), custom_call_target="tpu_custom_call" | custom-call | tf_op jit(solution)/shard_map/pallas_call | solution.py:99
  140.1 1.5 copy.18
  141.7 2.4 %collective-permute-start.2 = (f32[8,256,2]{1,0,2:T(8,128)S(1)}, f32[8,256,2]{1,0,2:T(8,128)S(1)}, u32[]{:S(2)}, u32[]{:S(2)}) collective-permute-start(f32[8,256,2]{1,0,2:T(8,128)S(1)} %copy.18), channel_id=1, source_target_pairs={{0,16},{16,0},{1,17},{17,1},{2,18},{18,2},{3,19},{19,3},{4,20},{20... | collective-permute-start | bytes 49160 | tf_op jit(solution)/shard_map/ppermute | solution.py:194
  144.1 0.7 fusion.17
  144.7 0.9 copy.26
  145.6 9.9 %shard_map.82 = (f32[256,1024]{1,0:T(8,128)}, f32[8,256,2]{2,1,0:T(8,128)}) custom-call(bf16[256,1024]{1,0:T(8,128)(2,1)} %bitcast.38, bf16[256,1024]{1,0:T(8,128)(2,1)} %bitcast.39, bf16[256,1024]{1,0:T(8,128)(2,1)} %refs_2_.1, bf16[8,2,2,128,1024]{4,3,2,1,0:T(8,128)(2,1)} %all-to-all-done.refs_3_.refs_4_.refs_1_.refs_2_, ...), custom_call_target="tpu_custom_call" | custom-call | tf_op jit(solution)/shard_map/pallas_call | solution.py:99
  155.6 7.7 %collective-permute-done.2 = f32[8,256,2]{1,0,2:T(8,128)S(1)} collective-permute-done((f32[8,256,2]{1,0,2:T(8,128)S(1)}, f32[8,256,2]{1,0,2:T(8,128)S(1)}, u32[]{:S(2)}, u32[]{:S(2)}) %collective-permute-start.2) | collective-permute-done | bytes 16416 | tf_op jit(solution)/shard_map/ppermute | solution.py:194
  163.3 1.3 copy.19.bst_ref
  164.6 0.8 copy-done.4
  165.4 6.9 %shard_map.84 = bf16[256,1024]{1,0:T(8,128)(2,1)} custom-call(f32[256,1024]{1,0:T(8,128)} %get-tuple-element.9.na_ref, f32[8,256,2]{2,1,0:T(8,128)} %get-tuple-element.10.nst_ref, bf16[256,1024]{1,0:T(8,128)(2,1)} %copy-done.4, f32[8,256,2]{2,1,0:T(8,128)} %copy.19.bst_ref), custom_call_target="tpu_custom_call" | custom-call | tf_op jit(solution)/shard_map/pallas_call | solution.py:126
  172.3 0.5 collective-permute-start.3
  172.8 1.7 collective-permute-done.3
  174.5 3.4 %fusion.25 = f32[256,2048]{1,0:T(8,128)S(1)} fusion(bf16[256,1024]{1,0:T(8,128)(2,1)S(1)} %collective-permute-done.3, bf16[1024,2048]{1,0:T(8,128)(2,1)} %collective-permute-done.4), kind=kOutput, calls=%fused_computation.70 | convolution fusion | flops 1073741824 | bytes 6815744 | tf_op jit(solution)/shard_map/dot_general | solution.py:202
  178.0 4.5 %fusion.8 = bf16[256,2048]{1,0:T(8,128)(2,1)} fusion(f32[256,2048]{1,0:T(8,128)S(1)} %fusion.25, bf16[256,1024]{1,0:T(8,128)(2,1)S(1)} %copy-done.5, bf16[1024,4096]{1,0:T(8,128)(2,1)} %param.14, s32[]{:T(128)S(6)} %select_n.119, f32[2048]{0:T(1024)S(1)} %convert_element_type.55), kind=kOutput, calls=%fused_computation.6 | convolution fusion | flops 1075314688 | bytes 7872516 | tf_op jit(solution)/shard_map/dot_general | solution.py:198
  (39 shorter events, 1.5 us)
Async XLA Ops:
  9.9 120.8 %all-to-all-start = ((bf16[8,2,2,128,1024]{4,3,2,1,0:T(8,128)(2,1)}), bf16[8,2,2,128,1024]{4,3,2,1,0:T(8,128)(2,1)}, u32[]{:S(2)}, u32[]{:S(2)}) async-start(bf16[8,2,2,128,1024]{4,3,2,1,0:T(8,128)(2,1)} %bitcast.34), calls=%async_computation | async-start | bytes 16777216 | tf_op jit(solution)/shard_map/all_to_all | solution.py:179
  14.8 5.7 %copy-start.2 = (bf16[256,1024]{1,0:T(8,128)(2,1)S(1)}, bf16[256,1024]{1,0:T(8,128)(2,1)}, u32[]{:S(2)}) copy-start(bf16[256,1024]{1,0:T(8,128)(2,1)} %param.8) | copy-start | bytes 1572868
  14.8 6.0 %copy-start.3 = (bf16[256,1024]{1,0:T(8,128)(2,1)S(1)}, bf16[256,1024]{1,0:T(8,128)(2,1)}, u32[]{:S(2)}) copy-start(bf16[256,1024]{1,0:T(8,128)(2,1)} %param.9) | copy-start | bytes 1572868
  14.8 6.1 %copy-start.7 = (s32[16]{0:T(128)S(1)}, s32[16]{0:T(128)}, u32[]{:S(2)}) copy-start(s32[16]{0:T(128)} %param.13) | copy-start | bytes 196
  19.7 153.1 %collective-permute-start.4 = (bf16[1024,2048]{1,0:T(8,128)(2,1)}, bf16[1024,2048]{1,0:T(8,128)(2,1)}, u32[]{:S(2)}, u32[]{:S(2)}) collective-permute-start(bf16[1024,2048]{1,0:T(8,128)(2,1)} %constant_dynamic-slice_fusion.1), channel_id=1, source_target_pairs={{0,1},{1,0},{2,3},{3,2},{4,5},{5,4},{6,7},{7,6},{8,9},{9,8},{10,11... | collective-permute-start | bytes 12582920 | tf_op jit(solution)/shard_map/ppermute | solution.py:169
  24.8 115.2 %copy-start = (bf16[32,8,8,128]{3,1,2,0:T(8,128)(2,1)}, bf16[32,8,8,128]{3,1,2,0:T(8,128)(2,1)S(1)}, u32[]{:S(2)}) copy-start(bf16[32,8,8,128]{3,1,2,0:T(8,128)(2,1)S(1)} %copy.27) | copy-start | bytes 1572868
  24.8 105.9 %collective-permute-start = (bf16[256,1024]{1,0:T(8,128)(2,1)S(1)}, bf16[256,1024]{1,0:T(8,128)(2,1)S(1)}, u32[]{:S(2)}, u32[]{:S(2)}) collective-permute-start(bf16[256,1024]{1,0:T(8,128)(2,1)S(1)} %bitcast.37), channel_id=1, source_target_pairs={{0,16},{16,0},{1,17},{17,1},{2,18},{18,2},{3,19},{19,3},{4,20},{20... | collective-permute-start | bytes 1572872 | tf_op jit(solution)/shard_map/ppermute | solution.py:186
  130.7 0.8 copy-start.1
  140.0 24.6 %collective-permute-start.1 = (bf16[256,1024]{1,0:T(8,128)(2,1)}, bf16[256,1024]{1,0:T(8,128)(2,1)S(1)}, u32[]{:S(2)}, u32[]{:S(2)}) collective-permute-start(bf16[256,1024]{1,0:T(8,128)(2,1)} %get-tuple-element.11), channel_id=1, source_target_pairs={{0,16},{16,0},{1,17},{17,1},{2,18},{18,2},{3,19},{19,3},{4,20},{20... | collective-permute-start | bytes 1572872 | tf_op jit(solution)/shard_map/ppermute | solution.py:193
  141.7 21.6 %collective-permute-start.2 = (f32[8,256,2]{1,0,2:T(8,128)S(1)}, f32[8,256,2]{1,0,2:T(8,128)S(1)}, u32[]{:S(2)}, u32[]{:S(2)}) collective-permute-start(f32[8,256,2]{1,0,2:T(8,128)S(1)} %copy.18), channel_id=1, source_target_pairs={{0,16},{16,0},{1,17},{17,1},{2,18},{18,2},{3,19},{19,3},{4,20},{20... | collective-permute-start | bytes 49160 | tf_op jit(solution)/shard_map/ppermute | solution.py:194
  155.6 17.2 %copy-start.6 = (bf16[2048]{0:T(1024)(128)(2,1)S(1)}, bf16[2048]{0:T(1024)(128)(2,1)}, u32[]{:S(2)}) copy-start(bf16[2048]{0:T(1024)(128)(2,1)} %param.15) | copy-start | bytes 12292
  164.6 0.8 copy-start.4
  172.3 5.7 %copy-start.5 = (bf16[256,1024]{1,0:T(8,128)(2,1)S(1)}, bf16[256,1024]{1,0:T(8,128)(2,1)}, u32[]{:S(2)}) copy-start(bf16[256,1024]{1,0:T(8,128)(2,1)} %shard_map.84) | copy-start | bytes 1572868
  172.3 2.2 %collective-permute-start.3 = (bf16[256,1024]{1,0:T(8,128)(2,1)}, bf16[256,1024]{1,0:T(8,128)(2,1)S(1)}, u32[]{:S(2)}, u32[]{:S(2)}) collective-permute-start(bf16[256,1024]{1,0:T(8,128)(2,1)} %shard_map.84), channel_id=1, source_target_pairs={{0,1},{1,0},{2,3},{3,2},{4,5},{5,4},{6,7},{7,6},{8,9},{9,8},{10,11... | collective-permute-start | bytes 1572872 | tf_op jit(solution)/shard_map/ppermute | solution.py:201

commit v8 on v5

--- a/solution.py
+++ b/solution.py
@@ -153,9 +153,9 @@
     partner_query = lax.ppermute(query_rot, "half", swap)
 
     far_pages = jnp.take(kv_pages, jnp.take(local_page, (1 - half) * sub_count + dest), axis=0, mode="clip")
-    partner_query, far_pages = lax.optimization_barrier((partner_query, far_pages))
     far_incoming = lax.all_to_all(far_pages, "sub", split_axis=0, concat_axis=0, tiled=True)
     near_pages = jnp.take(kv_pages, jnp.take(local_page, half * sub_count + dest), axis=0, mode="clip")
+    partner_query, near_pages = lax.optimization_barrier((partner_query, near_pages))
     near_incoming = lax.all_to_all(near_pages, "sub", split_axis=0, concat_axis=0, tiled=True)
     key_rot = rotate_rows(new_keys, positions)
 

time: 189 us -> 178 us (0.942)
  waiting for transfers between devices: 94.1 us -> 85.1 us
  local copies, waits for them, and re-layouts: 33.3 us -> 31.3 us
    all_to_all x1, waiting for transfers between devices: 44.6 us -> 0.01 us  [on_device(): lax.all_to_all(far_pages, 'sub', split_axis=0, concat_axis=0, tiled=True)]
    ppermute x1, waiting for transfers between devices: 15.8 us -> 51.4 us  [on_device(): partner_query = lax.ppermute(query_rot, 'half', swap)]
    all_to_all x1, waiting for transfers between devices: 33.8 us -> 6.96 us  [on_device(): lax.all_to_all(near_pages, 'sub', split_axis=0, concat_axis=0, tiled=True)]
    ppermute x1, waiting for transfers between devices: 0.01 us -> 26.7 us  [on_device(): back_stats = lax.ppermute(far_stats, 'half', swap)]
    ppermute x1, starting transfers between devices: 2.98 us -> 0.7 us  [on_device(): back_stats = lax.ppermute(far_stats, 'half', swap)]
    unnamed x16 -> x18, local copies, waits for them, and re-layouts: 3.27 us -> 1.2 us
  transfers between devices with their start and end apart: 7 -> 7, of which waited for: 3 -> 3; matrix products, arithmetic and copies ran while one was open for 22% -> 23% of each run, Pallas kernels for 10% -> 11%
where the time goes in v8:
time: 178 us; the launch traced here: 175 us
  waiting for transfers between devices  85.1 us (48%)
  local copies, waits for them, and re-layouts  31.3 us (18%)
  starting transfers between devices  19.4 us (11%)
  Pallas kernels  18.5 us (10%)
  other arithmetic  12.3 us (7%)
  matrix products  7.91 us (4%)
    ppermute x1, waiting for transfers between devices, on_device(): partner_query = lax.ppermute(query_rot, 'half', swap)  51.4 us
    ppermute x1, waiting for transfers between devices, on_device(): back_stats = lax.ppermute(far_stats, 'half', swap)  26.7 us
    pallas_call x2, Pallas kernels, attend(): pl.pallas_call(partial(attention_kernel, with_local=local is not None), g...  18.5 us
    all_to_all x1, waiting for transfers between devices, on_device(): lax.all_to_all(near_pages, 'sub', split_axis=0, concat_axis=0, tiled=True)  6.96 us
    gather x1, local copies, waits for them, and re-layouts, on_device(): jnp.take(kv_pages, jnp.take(local_page, (1 - half) * sub_count + dest), a...  6.15 us
    gather x1, local copies, waits for them, and re-layouts, on_device(): jnp.take(kv_pages, jnp.take(local_page, half * sub_count + dest), axis=0,...  6.12 us
    mul x4, local copies, waits for them, and re-layouts, on_device(): merged = (near3 * near_w + back3 * back_w) / (near_w + back_w)  5.14 us
    all_to_all x1, starting transfers between devices, on_device(): lax.all_to_all(near_pages, 'sub', split_axis=0, concat_axis=0, tiled=True)  5.03 us
  transfers between devices with their start and end apart: 7, of which 3 were waited for; matrix products, arithmetic and copies ran while one was open for 23% of the time, Pallas kernels for 11%

profile of v8, /device:TPU:11, one launch (start us, length us, event | category | flops | bytes accessed | tf_op | source)
XLA Modules:
  0.0 174.7 jit_solution(12164129277671514613)
XLA Ops:
  0.0 0.8 select_reduce_fusion
  1.5 6.1 %gather_fusion.1 = bf16[8,2,128,1024]{3,2,1,0:T(8,128)(2,1)} fusion(bf16[16,2,128,1024]{3,2,1,0:T(8,128)(2,1)} %param.13, s32[1024]{0:T(1024)S(1)} %pad_clamp_fusion), kind=kCustom, calls=%fused_computation.3 | custom fusion | bytes 8388640 | tf_op jit(solution)/shard_map/jit(_take)/gather | solution.py:155
  7.7 4.7 %all-to-all-start.1 = ((bf16[8,2,128,1024]{3,2,1,0:T(8,128)(2,1)}), bf16[8,2,128,1024]{3,2,1,0:T(8,128)(2,1)}, u32[]{:S(2)}, u32[]{:S(2)}) async-start(bf16[8,2,128,1024]{3,2,1,0:T(8,128)(2,1)} %gather_fusion.1), calls=%async_computation.1 | async-start | bytes 8388608 | tf_op jit(solution)/shard_map/all_to_all | solution.py:156
  12.4 0.7 fusion.24
  13.1 0.7 add_convert_fusion.2
  15.0 0.8 subtract_convert_fusion
  15.8 1.0 pad_maximum_fusion
  16.9 2.4 %collective-permute-start = (bf16[256,1024]{1,0:T(8,128)(2,1)S(1)}, bf16[256,1024]{1,0:T(8,128)(2,1)S(1)}, u32[]{:S(2)}, u32[]{:S(2)}) collective-permute-start(bf16[256,1024]{1,0:T(8,128)(2,1)S(1)} %bitcast.60), channel_id=1, source_target_pairs={{0,16},{16,0},{1,17},{17,1},{2,18},{18,2},{3,19},{19,3},{4,20},{20... | collective-permute-start | bytes 1572872 | tf_op jit(solution)/shard_map/ppermute | solution.py:153
  20.0 6.1 %gather_fusion = bf16[8,2,128,1024]{3,2,1,0:T(8,128)(2,1)} fusion(bf16[16,2,128,1024]{3,2,1,0:T(8,128)(2,1)} %param.13, s32[1024]{0:T(1024)S(1)} %pad_clamp_fusion.2), kind=kCustom, calls=%fused_computation.2 | custom fusion | bytes 8388640 | tf_op jit(solution)/shard_map/jit(_take)/gather | solution.py:157
  26.1 51.4 %collective-permute-done.refs_0_ = bf16[256,1024]{1,0:T(8,128)(2,1)S(1)} collective-permute-done((bf16[256,1024]{1,0:T(8,128)(2,1)S(1)}, bf16[256,1024]{1,0:T(8,128)(2,1)S(1)}, u32[]{:S(2)}, u32[]{:S(2)}) %collective-permute-start) | collective-permute-done | bytes 524320 | tf_op jit(solution)/shard_map/ppermute | solution.py:153
  77.4 5.0 %all-to-all-start = ((bf16[8,2,128,1024]{3,2,1,0:T(8,128)(2,1)}), bf16[8,2,128,1024]{3,2,1,0:T(8,128)(2,1)}, u32[]{:S(2)}, u32[]{:S(2)}) async-start(bf16[8,2,128,1024]{3,2,1,0:T(8,128)(2,1)} %gather_fusion), calls=%async_computation | async-start | bytes 8388608 | tf_op jit(solution)/shard_map/all_to_all | solution.py:159
  82.5 4.7 %constant_dynamic-slice_fusion.2 = bf16[1024,2048]{1,0:T(8,128)(2,1)} fusion(bf16[1024,4096]{1,0:T(8,128)(2,1)} %param.16, s32[]{:T(128)S(6)} %select_n.98), kind=kLoop, calls=%fused_computation.73 | loop fusion | bytes 8388612 | tf_op jit(solution)/shard_map/dynamic_slice | solution.py:140
  87.2 2.1 %collective-permute-start.4 = (bf16[1024,2048]{1,0:T(8,128)(2,1)}, bf16[1024,2048]{1,0:T(8,128)(2,1)}, u32[]{:S(2)}, u32[]{:S(2)}) collective-permute-start(bf16[1024,2048]{1,0:T(8,128)(2,1)} %constant_dynamic-slice_fusion.2), channel_id=1, source_target_pairs={{0,1},{1,0},{2,3},{3,2},{4,5},{5,4},{6,7},{7,6},{8,9},{9,8},{10,11... | collective-permute-start | bytes 12582920 | tf_op jit(solution)/shard_map/ppermute | solution.py:142
  89.3 0.7 fusion.19
  90.4 0.7 clamp_select_fusion.1
  92.4 8.6 %shard_map.83 = (bf16[256,1024]{1,0:T(8,128)(2,1)}, f32[8,256,1]{2,1,0:T(8,128)}, f32[8,256,1]{2,1,0:T(8,128)}) custom-call(bf16[256,1024]{1,0:T(8,128)(2,1)} %copy-done.2, bf16[8,2,128,1024]{3,2,1,0:T(8,128)(2,1)} %all-to-all-done.1.refs_1_.refs_2_, bf16[8,2,128,1024]{3,2,1,0:T(8,128)(2,1)} %all-to-all-done.1.refs_1_.refs_2_, s32[1,1024]{1,0:T(1,128)} %bitcast.71), custom_call_target="tpu_custom_call" | custom-call | tf_op jit(solution)/shard_map/pallas_call | solution.py:91
  101.0 1.5 copy.29
  102.5 1.6 copy.30
  104.1 0.7 collective-permute-start.1
  104.8 1.7 collective-permute-start.2
  107.1 0.9 copy.50
  108.0 26.7 %collective-permute-done.1 = f32[8,256,2]{1,0,2:T(8,128)S(1)} collective-permute-done((f32[8,256,2]{1,0,2:T(8,128)S(1)}, f32[8,256,2]{1,0,2:T(8,128)S(1)}, u32[]{:S(2)}, u32[]{:S(2)}) %collective-permute-start.1) | collective-permute-done | bytes 16416 | tf_op jit(solution)/shard_map/ppermute | solution.py:169
  135.1 7.0 %all-to-all-done.refs_3_.refs_4_ = bf16[8,2,128,1024]{3,2,1,0:T(8,128)(2,1)} async-done(((bf16[8,2,128,1024]{3,2,1,0:T(8,128)(2,1)}), bf16[8,2,128,1024]{3,2,1,0:T(8,128)(2,1)}, u32[]{:S(2)}, u32[]{:S(2)}) %all-to-all-start) | async-done | bytes 4194336 | tf_op jit(solution)/shard_map/all_to_all | solution.py:159
  142.1 9.9 %shard_map.82 = (f32[256,1024]{1,0:T(8,128)}, f32[8,256,1]{2,1,0:T(8,128)}, f32[8,256,1]{2,1,0:T(8,128)}) custom-call(bf16[256,1024]{1,0:T(8,128)(2,1)} %bitcast.61, bf16[256,1024]{1,0:T(8,128)(2,1)} %bitcast.62, bf16[256,1024]{1,0:T(8,128)(2,1)} %refs_2_.1, bf16[8,2,128,1024]{3,2,1,0:T(8,128)(2,1)} %all-to-all-done.refs_3_.refs_4_, ...), custom_call_target="tpu_custom_call" | custom-call | tf_op jit(solution)/shard_map/pallas_call | solution.py:91
  152.0 3.1 %fusion.21 = (f32[256,8,1]{2,0,1:T(8,128)S(1)}, f32[256,8,1]{2,0,1:T(8,128)S(1)}, f32[256,8,1]{2,0,1:T(8,128)}) fusion(f32[256,8,2]{2,0,1:T(8,128)S(1)} %bitcast.54, f32[8,256,1]{2,1,0:T(8,128)} %get-tuple-element.16, f32[8,256,1]{2,1,0:T(8,128)} %get-tuple-element.20), kind=kLoop, calls=%fused_computation.82 | loop fusion | flops 12288 | bytes 57344 | tf_op jit(solution)/shard_map/add | solution.py:184
  155.1 2.9 %copy.35 = f32[256,8,1]{1,0,2:T(8,128)S(1)} copy(f32[256,8,1]{2,0,1:T(8,128)} %get-tuple-element.28) | data formatting | bytes 16384 | tf_op jit(solution)/shard_map/mul | solution.py:184
  158.0 1.6 copy.36
  159.6 1.6 copy.37
  162.2 1.8 %fusion.8 = bf16[256,1024]{1,0:T(8,128)(2,1)S(1)} fusion(f32[32,8,8,128]{3,2,1,0:T(8,128)S(1)} %bitcast.59, f32[32,8,8,128]{3,2,1,0:T(8,128)S(1)} %bitcast.58, f32[256,1024]{1,0:T(8,128)S(1)} %copy-done.1, f32[32,8,8,128]{3,2,1,0:T(8,128)S(1)} %bitcast.57, bf16[256,1024]{1,0:T(8,128)(2,1)} %collective-permute-done.2), kind=kLoop, calls=%fused_computation.16 | loop fusion | flops 1572864 | bytes 5242880 | tf_op jit(solution)/shard_map/convert_element_type | solution.py:185
  164.0 2.8 %collective-permute-start.3 = (bf16[256,1024]{1,0:T(8,128)(2,1)S(1)}, bf16[256,1024]{1,0:T(8,128)(2,1)S(1)}, u32[]{:S(2)}, u32[]{:S(2)}) collective-permute-start(bf16[256,1024]{1,0:T(8,128)(2,1)S(1)} %fusion.8), channel_id=1, source_target_pairs={{0,1},{1,0},{2,3},{3,2},{4,5},{5,4},{6,7},{7,6},{8,9},{9,8},{10,11... | collective-permute-start | bytes 1572872 | tf_op jit(solution)/shard_map/ppermute | solution.py:190
  166.7 3.4 %fusion = f32[256,2048]{1,0:T(8,128)S(1)} fusion(bf16[256,1024]{1,0:T(8,128)(2,1)S(1)} %fusion.8, bf16[1024,4096]{1,0:T(8,128)(2,1)} %param.16, s32[]{:T(128)S(6)} %select_n.96), kind=kOutput, calls=%fused_computation.4 | convolution fusion | flops 1073741824 | bytes 6815748 | tf_op jit(solution)/shard_map/dot_general | solution.py:187
  170.2 4.5 %fusion.3 = bf16[256,2048]{1,0:T(8,128)(2,1)} fusion(f32[256,2048]{1,0:T(8,128)S(1)} %fusion, bf16[256,1024]{1,0:T(8,128)(2,1)S(1)} %collective-permute-done.3, bf16[1024,2048]{1,0:T(8,128)(2,1)} %collective-permute-done.4, f32[2048]{0:T(1024)S(1)} %convert_element_type.63), kind=kOutput, calls=%fused_computation.8 | convolution fusion | flops 1075314688 | bytes 7872512 | tf_op jit(solution)/shard_map/dot_general | solution.py:191
  (50 shorter events, 6.4 us)
Async XLA Ops:
  7.7 4.7 %copy-start.6 = (s32[16]{0:T(128)S(1)}, s32[16]{0:T(128)}, u32[]{:S(2)}) copy-start(s32[16]{0:T(128)} %param.15) | copy-start | bytes 196
  7.7 6.5 %copy-start.3 = (bf16[256,1024]{1,0:T(8,128)(2,1)S(1)}, bf16[256,1024]{1,0:T(8,128)(2,1)}, u32[]{:S(2)}) copy-start(bf16[256,1024]{1,0:T(8,128)(2,1)} %param.11) | copy-start | bytes 1572868
  7.7 6.6 %copy-start.4 = (bf16[256,1024]{1,0:T(8,128)(2,1)S(1)}, bf16[256,1024]{1,0:T(8,128)(2,1)}, u32[]{:S(2)}) copy-start(bf16[256,1024]{1,0:T(8,128)(2,1)} %param.10) | copy-start | bytes 1572868
  7.7 69.8 %all-to-all-start.1 = ((bf16[8,2,128,1024]{3,2,1,0:T(8,128)(2,1)}), bf16[8,2,128,1024]{3,2,1,0:T(8,128)(2,1)}, u32[]{:S(2)}, u32[]{:S(2)}) async-start(bf16[8,2,128,1024]{3,2,1,0:T(8,128)(2,1)} %gather_fusion.1), calls=%async_computation.1 | async-start | bytes 8388608 | tf_op jit(solution)/shard_map/all_to_all | solution.py:156
  16.9 9.2 %copy-start = (bf16[32,8,8,128]{3,1,2,0:T(8,128)(2,1)}, bf16[32,8,8,128]{3,1,2,0:T(8,128)(2,1)S(1)}, u32[]{:S(2)}) copy-start(bf16[32,8,8,128]{3,1,2,0:T(8,128)(2,1)S(1)} %copy.51) | copy-start | bytes 1572868
  16.9 60.6 %collective-permute-start = (bf16[256,1024]{1,0:T(8,128)(2,1)S(1)}, bf16[256,1024]{1,0:T(8,128)(2,1)S(1)}, u32[]{:S(2)}, u32[]{:S(2)}) collective-permute-start(bf16[256,1024]{1,0:T(8,128)(2,1)S(1)} %bitcast.60), channel_id=1, source_target_pairs={{0,16},{16,0},{1,17},{17,1},{2,18},{18,2},{3,19},{19,3},{4,20},{20... | collective-permute-start | bytes 1572872 | tf_op jit(solution)/shard_map/ppermute | solution.py:153
  77.4 5.0 %copy-start.2 = (bf16[256,1024]{1,0:T(8,128)(2,1)}, bf16[256,1024]{1,0:T(8,128)(2,1)S(1)}, u32[]{:S(2)}) copy-start(bf16[256,1024]{1,0:T(8,128)(2,1)S(1)} %collective-permute-done.refs_0_) | copy-start | bytes 1572868
  77.4 64.7 %all-to-all-start = ((bf16[8,2,128,1024]{3,2,1,0:T(8,128)(2,1)}), bf16[8,2,128,1024]{3,2,1,0:T(8,128)(2,1)}, u32[]{:S(2)}, u32[]{:S(2)}) async-start(bf16[8,2,128,1024]{3,2,1,0:T(8,128)(2,1)} %gather_fusion), calls=%async_computation | async-start | bytes 8388608 | tf_op jit(solution)/shard_map/all_to_all | solution.py:159
  87.2 83.0 %collective-permute-start.4 = (bf16[1024,2048]{1,0:T(8,128)(2,1)}, bf16[1024,2048]{1,0:T(8,128)(2,1)}, u32[]{:S(2)}, u32[]{:S(2)}) collective-permute-start(bf16[1024,2048]{1,0:T(8,128)(2,1)} %constant_dynamic-slice_fusion.2), channel_id=1, source_target_pairs={{0,1},{1,0},{2,3},{3,2},{4,5},{5,4},{6,7},{7,6},{8,9},{9,8},{10,11... | collective-permute-start | bytes 12582920 | tf_op jit(solution)/shard_map/ppermute | solution.py:142
  104.1 30.7 %collective-permute-start.1 = (f32[8,256,2]{1,0,2:T(8,128)S(1)}, f32[8,256,2]{1,0,2:T(8,128)S(1)}, u32[]{:S(2)}, u32[]{:S(2)}) collective-permute-start(f32[8,256,2]{1,0,2:T(8,128)S(1)} %pad_maximum_fusion.2), channel_id=1, source_target_pairs={{0,16},{16,0},{1,17},{17,1},{2,18},{18,2},{3,19},{19,3},{4,20},{20... | collective-permute-start | bytes 49160 | tf_op jit(solution)/shard_map/ppermute | solution.py:169
  104.8 56.4 %collective-permute-start.2 = (bf16[256,1024]{1,0:T(8,128)(2,1)}, bf16[256,1024]{1,0:T(8,128)(2,1)}, u32[]{:S(2)}, u32[]{:S(2)}) collective-permute-start(bf16[256,1024]{1,0:T(8,128)(2,1)} %get-tuple-element.21), channel_id=1, source_target_pairs={{0,16},{16,0},{1,17},{17,1},{2,18},{18,2},{3,19},{19,3},{4,20},{20... | collective-permute-start | bytes 1572872 | tf_op jit(solution)/shard_map/ppermute | solution.py:168
  155.1 7.1 %copy-start.1 = (f32[256,1024]{1,0:T(8,128)S(1)}, f32[256,1024]{1,0:T(8,128)}, u32[]{:S(2)}) copy-start(f32[256,1024]{1,0:T(8,128)} %get-tuple-element.15) | copy-start | bytes 3145732
  161.2 5.6 %copy-start.5 = (bf16[2048]{0:T(1024)(128)(2,1)S(1)}, bf16[2048]{0:T(1024)(128)(2,1)}, u32[]{:S(2)}) copy-start(bf16[2048]{0:T(1024)(128)(2,1)} %param.17) | copy-start | bytes 12292
  164.0 6.2 %collective-permute-start.3 = (bf16[256,1024]{1,0:T(8,128)(2,1)S(1)}, bf16[256,1024]{1,0:T(8,128)(2,1)S(1)}, u32[]{:S(2)}, u32[]{:S(2)}) collective-permute-start(bf16[256,1024]{1,0:T(8,128)(2,1)S(1)} %fusion.8), channel_id=1, source_target_pairs={{0,1},{1,0},{2,3},{3,2},{4,5},{5,4},{6,7},{7,6},{8,9},{9,8},{10,11... | collective-permute-start | bytes 1572872 | tf_op jit(solution)/shard_map/ppermute | solution.py:190

commit v9 on v6

--- a/solution.py
+++ b/solution.py
@@ -79,15 +79,15 @@
         st_ref[:, 1:2] = l
 
 
-def attend(key_ok, query_rot, incoming, which, local=None, back=None):
+def attend(key_ok, query_rot, incoming, local=None, back=None):
     span, width = query_rot.shape
     head_count = width // HEAD_DIM
     block_count = incoming.shape[0]
-    page_size = incoming.shape[3]
+    page_size = incoming.shape[2]
     col_spec = pl.BlockSpec((span, HEAD_DIM), lambda h: (0, h))
     page_specs = [
-        pl.BlockSpec((block_count, None, None, page_size, HEAD_DIM), lambda h: (0, which, 0, 0, h)),
-        pl.BlockSpec((block_count, None, None, page_size, HEAD_DIM), lambda h: (0, which, 1, 0, h)),
+        pl.BlockSpec((block_count, None, page_size, HEAD_DIM), lambda h: (0, 0, 0, h)),
+        pl.BlockSpec((block_count, None, page_size, HEAD_DIM), lambda h: (0, 1, 0, h)),
         pl.BlockSpec((1, block_count * page_size), lambda h: (0, 0)),
     ]
     stat_spec = pl.BlockSpec((None, span, 2), lambda h: (h, 0, 0))
@@ -151,27 +151,28 @@
     held_here = owners == own_index
     local_page = jnp.sum(jnp.where(held_here, page_table - own_index * page_count, 0), axis=1)
     dest = jnp.arange(sub_count, dtype=jnp.int32)
-    wanted = jnp.stack([half * sub_count + dest, (1 - half) * sub_count + dest], axis=1).reshape(-1)
-    outgoing = jnp.take(kv_pages, jnp.take(local_page, wanted), axis=0, mode="clip")
-    outgoing = outgoing.reshape((sub_count, 2) + kv_pages.shape[1:])
-    incoming = lax.all_to_all(outgoing, "sub", split_axis=0, concat_axis=0, tiled=True)
-
     own_length = lax.dynamic_index_in_dim(cache_len, own_index, 0, keepdims=False)
     partner_length = lax.dynamic_index_in_dim(cache_len, partner, 0, keepdims=False)
     positions = own_length + jnp.arange(span_len, dtype=jnp.int32)
     query_rot = rotate_rows(new_queries, positions)
+    partner_query = lax.ppermute(query_rot, "half", swap)
+
+    far_pages = jnp.take(kv_pages, jnp.take(local_page, (1 - half) * sub_count + dest), axis=0, mode="clip")
+    far_incoming = lax.all_to_all(far_pages, "sub", split_axis=0, concat_axis=0, tiled=True)
+    near_pages = jnp.take(kv_pages, jnp.take(local_page, half * sub_count + dest), axis=0, mode="clip")
+    partner_query, near_pages = lax.optimization_barrier((partner_query, near_pages))
+    near_incoming = lax.all_to_all(near_pages, "sub", split_axis=0, concat_axis=0, tiled=True)
     key_rot = rotate_rows(new_keys, positions)
-    partner_query = lax.ppermute(query_rot, "half", swap)
 
     source_base = half * sub_count
     ok_own = usable_keys(page_table, own_index, own_length, source_base, sub_count, page_count, page_size)
     ok_partner = usable_keys(page_table, partner, partner_length, source_base, sub_count, page_count, page_size)
 
-    far_out, far_stats = attend(ok_partner, partner_query, incoming, 1)
+    far_out, far_stats = attend(ok_partner, partner_query, far_incoming)
     back_out = lax.ppermute(far_out, "half", swap)
     back_stats = lax.ppermute(far_stats, "half", swap)
     attended = attend(
-        ok_own, query_rot, incoming, 0, local=(key_rot, new_values), back=(back_out, back_stats)
+        ok_own, query_rot, near_incoming, local=(key_rot, new_values), back=(back_out, back_stats)
     )
 
     summed = jnp.dot(attended, w_mine, preferred_element_type=jnp.float32)

time: 191 us -> 175 us (0.916)
  waiting for transfers between devices: 120 us -> 92.8 us
  starting transfers between devices: 11.2 us -> 19.1 us
  local copies, waits for them, and re-layouts: 20.9 us -> 24.5 us
    ppermute x1, waiting for transfers between devices: 100 us -> 51.3 us  [on_device(): partner_query = lax.ppermute(query_rot, 'half', swap)]
    ppermute x1, waiting for transfers between devices: 17.7 us -> 39.7 us  [on_device(): back_stats = lax.ppermute(far_stats, 'half', swap)]
    all_to_all x1 -> x2, starting transfers between devices: 4.93 us -> 9.79 us  [the longest x1 5.06 us: on_device(): lax.all_to_all(near_pages, 'sub', split_axis=0, concat_axis=0, tiled=True)]
    gather x2 -> x4, local copies, waits for them, and re-layouts: 8.83 us -> 13.6 us  [the longest x1 6.15 us: on_device(): jnp.take(kv_pages, jnp.take(local_page, (1 - half) * sub_count + dest), a...]
  transfers between devices with their start and end apart: 6 -> 7, of which waited for: 3 -> 3; matrix products, arithmetic and copies ran while one was open for 9% -> 13% of each run, Pallas kernels for 12% -> 13%
where the time goes in v9:
time: 175 us; the launch traced here: 174 us
  waiting for transfers between devices  92.8 us (53%)
  local copies, waits for them, and re-layouts  24.5 us (14%)
  Pallas kernels  22.4 us (13%)
  starting transfers between devices  19.1 us (11%)
  matrix products  7.93 us (5%)
  other arithmetic  7.47 us (4%)
    ppermute x1, waiting for transfers between devices, on_device(): partner_query = lax.ppermute(query_rot, 'half', swap)  51.3 us
    ppermute x1, waiting for transfers between devices, on_device(): back_stats = lax.ppermute(far_stats, 'half', swap)  39.7 us
    pallas_call x2, Pallas kernels, attend(): pl.pallas_call(partial(attention_kernel, with_local=local is not None), g...  22.4 us
    gather x1, local copies, waits for them, and re-layouts, on_device(): jnp.take(kv_pages, jnp.take(local_page, (1 - half) * sub_count + dest), a...  6.15 us
    gather x1, local copies, waits for them, and re-layouts, on_device(): jnp.take(kv_pages, jnp.take(local_page, half * sub_count + dest), axis=0,...  6.12 us
    all_to_all x1, starting transfers between devices, on_device(): lax.all_to_all(near_pages, 'sub', split_axis=0, concat_axis=0, tiled=True)  5.06 us
    dynamic_slice x1, local copies, waits for them, and re-layouts, on_device(): piece = lax.dynamic_slice_in_dim(w_out, target * out_cols, out_cols, axis=1)  4.73 us
    all_to_all x1, starting transfers between devices, on_device(): lax.all_to_all(far_pages, 'sub', split_axis=0, concat_axis=0, tiled=True)  4.73 us
  transfers between devices with their start and end apart: 7, of which 3 were waited for; matrix products, arithmetic and copies ran while one was open for 13% of the time, Pallas kernels for 13%

profile of v9, /device:TPU:11, one launch (start us, length us, event | category | flops | bytes accessed | tf_op | source)
XLA Modules:
  0.0 174.3 jit_solution(2460432000785569467)
XLA Ops:
  0.0 0.8 select_reduce_fusion
  0.8 0.6 gather_fusion.3
  1.5 6.2 %gather_fusion.1 = bf16[8,2,128,1024]{3,2,1,0:T(8,128)(2,1)} fusion(bf16[16,2,128,1024]{3,2,1,0:T(8,128)(2,1)} %param.13, s32[1024]{0:T(1024)S(1)} %pad_clamp_fusion), kind=kCustom, calls=%fused_computation.3 | custom fusion | bytes 8388640 | tf_op jit(solution)/shard_map/jit(_take)/gather | solution.py:160
  7.7 4.7 %all-to-all-start.1 = ((bf16[8,2,128,1024]{3,2,1,0:T(8,128)(2,1)}), bf16[8,2,128,1024]{3,2,1,0:T(8,128)(2,1)}, u32[]{:S(2)}, u32[]{:S(2)}) async-start(bf16[8,2,128,1024]{3,2,1,0:T(8,128)(2,1)} %gather_fusion.1), calls=%async_computation.1 | async-start | bytes 8388608 | tf_op jit(solution)/shard_map/all_to_all | solution.py:161
  12.4 0.7 fusion.22
  13.1 0.7 add_convert_fusion.2
  15.0 0.8 subtract_convert_fusion
  15.8 1.0 pad_maximum_fusion
  16.9 2.4 %collective-permute-start = (bf16[256,1024]{1,0:T(8,128)(2,1)S(1)}, bf16[256,1024]{1,0:T(8,128)(2,1)S(1)}, u32[]{:S(2)}, u32[]{:S(2)}) collective-permute-start(bf16[256,1024]{1,0:T(8,128)(2,1)S(1)} %bitcast.27), channel_id=1, source_target_pairs={{0,16},{16,0},{1,17},{17,1},{2,18},{18,2},{3,19},{19,3},{4,20},{20... | collective-permute-start | bytes 1572872 | tf_op jit(solution)/shard_map/ppermute | solution.py:158
  19.3 0.6 gather_fusion.2
  19.9 6.1 %gather_fusion = bf16[8,2,128,1024]{3,2,1,0:T(8,128)(2,1)} fusion(bf16[16,2,128,1024]{3,2,1,0:T(8,128)(2,1)} %param.13, s32[1024]{0:T(1024)S(1)} %pad_clamp_fusion.2), kind=kCustom, calls=%fused_computation.2 | custom fusion | bytes 8388640 | tf_op jit(solution)/shard_map/jit(_take)/gather | solution.py:162
  26.1 51.3 %collective-permute-done.refs_0_ = bf16[256,1024]{1,0:T(8,128)(2,1)S(1)} collective-permute-done((bf16[256,1024]{1,0:T(8,128)(2,1)S(1)}, bf16[256,1024]{1,0:T(8,128)(2,1)S(1)}, u32[]{:S(2)}, u32[]{:S(2)}) %collective-permute-start) | collective-permute-done | bytes 524320 | tf_op jit(solution)/shard_map/ppermute | solution.py:158
  77.4 5.1 %all-to-all-start = ((bf16[8,2,128,1024]{3,2,1,0:T(8,128)(2,1)}), bf16[8,2,128,1024]{3,2,1,0:T(8,128)(2,1)}, u32[]{:S(2)}, u32[]{:S(2)}) async-start(bf16[8,2,128,1024]{3,2,1,0:T(8,128)(2,1)} %gather_fusion), calls=%async_computation | async-start | bytes 8388608 | tf_op jit(solution)/shard_map/all_to_all | solution.py:164
  82.5 4.7 %constant_dynamic-slice_fusion.2 = bf16[1024,2048]{1,0:T(8,128)(2,1)} fusion(bf16[1024,4096]{1,0:T(8,128)(2,1)} %param.16, s32[]{:T(128)S(6)} %select_n.98), kind=kLoop, calls=%fused_computation.61 | loop fusion | bytes 8388612 | tf_op jit(solution)/shard_map/dynamic_slice | solution.py:145
  87.2 2.1 %collective-permute-start.4 = (bf16[1024,2048]{1,0:T(8,128)(2,1)}, bf16[1024,2048]{1,0:T(8,128)(2,1)}, u32[]{:S(2)}, u32[]{:S(2)}) collective-permute-start(bf16[1024,2048]{1,0:T(8,128)(2,1)} %constant_dynamic-slice_fusion.2), channel_id=1, source_target_pairs={{0,1},{1,0},{2,3},{3,2},{4,5},{5,4},{6,7},{7,6},{8,9},{9,8},{10,11... | collective-permute-start | bytes 12582920 | tf_op jit(solution)/shard_map/ppermute | solution.py:147
  89.3 0.7 fusion.20
  90.4 0.7 clamp_select_fusion
  91.1 0.7 fusion.18
  91.7 8.5 %shard_map.82 = (bf16[256,1024]{1,0:T(8,128)(2,1)}, f32[8,256,2]{2,1,0:T(8,128)}) custom-call(bf16[256,1024]{1,0:T(8,128)(2,1)} %copy-done.1, bf16[8,2,128,1024]{3,2,1,0:T(8,128)(2,1)} %all-to-all-done.1.refs_1_.refs_2_, bf16[8,2,128,1024]{3,2,1,0:T(8,128)(2,1)} %all-to-all-done.1.refs_1_.refs_2_, s32[1,1024]{1,0:T(1,128)} %bitcast.35), custom_call_target="tpu_custom_call" | custom-call | tf_op jit(solution)/shard_map/pallas_call | solution.py:104
  100.8 0.7 clamp_select_fusion.1
  101.5 1.5 copy.15
  103.1 1.8 %collective-permute-start.2 = (f32[8,256,2]{1,0,2:T(8,128)S(1)}, f32[8,256,2]{1,0,2:T(8,128)S(1)}, u32[]{:S(2)}, u32[]{:S(2)}) collective-permute-start(f32[8,256,2]{1,0,2:T(8,128)S(1)} %copy.15), channel_id=1, source_target_pairs={{0,16},{16,0},{1,17},{17,1},{2,18},{18,2},{3,19},{19,3},{4,20},{20... | collective-permute-start | bytes 49160 | tf_op jit(solution)/shard_map/ppermute | solution.py:173
  104.9 0.7 fusion.17
  105.6 0.9 copy.23
  106.4 39.7 %collective-permute-done.2 = f32[8,256,2]{1,0,2:T(8,128)S(1)} collective-permute-done((f32[8,256,2]{1,0,2:T(8,128)S(1)}, f32[8,256,2]{1,0,2:T(8,128)S(1)}, u32[]{:S(2)}, u32[]{:S(2)}) %collective-permute-start.2) | collective-permute-done | bytes 16416 | tf_op jit(solution)/shard_map/ppermute | solution.py:173
  146.1 1.3 copy.16.refs_7_
  147.5 0.8 copy-done.2
  148.3 13.9 %shard_map.83 = bf16[256,1024]{1,0:T(8,128)(2,1)} custom-call(bf16[256,1024]{1,0:T(8,128)(2,1)} %bitcast.28, bf16[256,1024]{1,0:T(8,128)(2,1)} %bitcast.29, bf16[256,1024]{1,0:T(8,128)(2,1)} %refs_2_.1, bf16[8,2,128,1024]{3,2,1,0:T(8,128)(2,1)} %all-to-all-done.refs_3_.refs_4_, bf16[8,2,128,1024]{3,2,1,0:T(8,128)(2,1)} %all-to-all-done.refs_3_.refs_4_, ...), custom_call_target="tpu_custom_call" | custom-call | tf_op jit(solution)/shard_map/pallas_call | solution.py:104
  162.2 2.4 %collective-permute-start.3 = (bf16[256,1024]{1,0:T(8,128)(2,1)}, bf16[256,1024]{1,0:T(8,128)(2,1)S(1)}, u32[]{:S(2)}, u32[]{:S(2)}) collective-permute-start(bf16[256,1024]{1,0:T(8,128)(2,1)} %shard_map.83), channel_id=1, source_target_pairs={{0,1},{1,0},{2,3},{3,2},{4,5},{5,4},{6,7},{7,6},{8,9},{9,8},{10,11... | collective-permute-start | bytes 1572872 | tf_op jit(solution)/shard_map/ppermute | solution.py:181
  164.6 1.7 collective-permute-done.3
  166.3 3.5 %fusion.23 = f32[256,2048]{1,0:T(8,128)S(1)} fusion(bf16[256,1024]{1,0:T(8,128)(2,1)S(1)} %collective-permute-done.3, bf16[1024,2048]{1,0:T(8,128)(2,1)} %collective-permute-done.4), kind=kOutput, calls=%fused_computation.71 | convolution fusion | flops 1073741824 | bytes 6815744 | tf_op jit(solution)/shard_map/dot_general | solution.py:182
  169.8 4.5 %fusion.8 = bf16[256,2048]{1,0:T(8,128)(2,1)} fusion(f32[256,2048]{1,0:T(8,128)S(1)} %fusion.23, bf16[256,1024]{1,0:T(8,128)(2,1)S(1)} %copy-done.3, bf16[1024,4096]{1,0:T(8,128)(2,1)} %param.16, s32[]{:T(128)S(6)} %select_n.96, f32[2048]{0:T(1024)S(1)} %convert_element_type.55), kind=kOutput, calls=%fused_computation.8 | convolution fusion | flops 1075314688 | bytes 7872516 | tf_op jit(solution)/shard_map/dot_general | solution.py:178
  (42 shorter events, 2.3 us)
Async XLA Ops:
  7.7 4.7 %copy-start.7 = (s32[16]{0:T(128)S(1)}, s32[16]{0:T(128)}, u32[]{:S(2)}) copy-start(s32[16]{0:T(128)} %param.15) | copy-start | bytes 196
  7.7 6.5 %copy-start.4 = (bf16[256,1024]{1,0:T(8,128)(2,1)S(1)}, bf16[256,1024]{1,0:T(8,128)(2,1)}, u32[]{:S(2)}) copy-start(bf16[256,1024]{1,0:T(8,128)(2,1)} %param.10) | copy-start | bytes 1572868
  7.7 6.6 %copy-start.5 = (bf16[256,1024]{1,0:T(8,128)(2,1)S(1)}, bf16[256,1024]{1,0:T(8,128)(2,1)}, u32[]{:S(2)}) copy-start(bf16[256,1024]{1,0:T(8,128)(2,1)} %param.11) | copy-start | bytes 1572868
  7.7 69.7 %all-to-all-start.1 = ((bf16[8,2,128,1024]{3,2,1,0:T(8,128)(2,1)}), bf16[8,2,128,1024]{3,2,1,0:T(8,128)(2,1)}, u32[]{:S(2)}, u32[]{:S(2)}) async-start(bf16[8,2,128,1024]{3,2,1,0:T(8,128)(2,1)} %gather_fusion.1), calls=%async_computation.1 | async-start | bytes 8388608 | tf_op jit(solution)/shard_map/all_to_all | solution.py:161
  16.9 9.2 %copy-start = (bf16[32,8,8,128]{3,1,2,0:T(8,128)(2,1)}, bf16[32,8,8,128]{3,1,2,0:T(8,128)(2,1)S(1)}, u32[]{:S(2)}) copy-start(bf16[32,8,8,128]{3,1,2,0:T(8,128)(2,1)S(1)} %copy.24) | copy-start | bytes 1572868
  16.9 60.5 %collective-permute-start = (bf16[256,1024]{1,0:T(8,128)(2,1)S(1)}, bf16[256,1024]{1,0:T(8,128)(2,1)S(1)}, u32[]{:S(2)}, u32[]{:S(2)}) collective-permute-start(bf16[256,1024]{1,0:T(8,128)(2,1)S(1)} %bitcast.27), channel_id=1, source_target_pairs={{0,16},{16,0},{1,17},{17,1},{2,18},{18,2},{3,19},{19,3},{4,20},{20... | collective-permute-start | bytes 1572872 | tf_op jit(solution)/shard_map/ppermute | solution.py:158
  77.4 5.1 %copy-start.1 = (bf16[256,1024]{1,0:T(8,128)(2,1)}, bf16[256,1024]{1,0:T(8,128)(2,1)S(1)}, u32[]{:S(2)}) copy-start(bf16[256,1024]{1,0:T(8,128)(2,1)S(1)} %collective-permute-done.refs_0_) | copy-start | bytes 1572868
  77.4 70.1 %all-to-all-start = ((bf16[8,2,128,1024]{3,2,1,0:T(8,128)(2,1)}), bf16[8,2,128,1024]{3,2,1,0:T(8,128)(2,1)}, u32[]{:S(2)}, u32[]{:S(2)}) async-start(bf16[8,2,128,1024]{3,2,1,0:T(8,128)(2,1)} %gather_fusion), calls=%async_computation | async-start | bytes 8388608 | tf_op jit(solution)/shard_map/all_to_all | solution.py:164
  87.2 77.4 %collective-permute-start.4 = (bf16[1024,2048]{1,0:T(8,128)(2,1)}, bf16[1024,2048]{1,0:T(8,128)(2,1)}, u32[]{:S(2)}, u32[]{:S(2)}) collective-permute-start(bf16[1024,2048]{1,0:T(8,128)(2,1)} %constant_dynamic-slice_fusion.2), channel_id=1, source_target_pairs={{0,1},{1,0},{2,3},{3,2},{4,5},{5,4},{6,7},{7,6},{8,9},{9,8},{10,11... | collective-permute-start | bytes 12582920 | tf_op jit(solution)/shard_map/ppermute | solution.py:147
  100.2 47.3 %collective-permute-start.1 = (bf16[256,1024]{1,0:T(8,128)(2,1)}, bf16[256,1024]{1,0:T(8,128)(2,1)S(1)}, u32[]{:S(2)}, u32[]{:S(2)}) collective-permute-start(bf16[256,1024]{1,0:T(8,128)(2,1)} %get-tuple-element.12), channel_id=1, source_target_pairs={{0,16},{16,0},{1,17},{17,1},{2,18},{18,2},{3,19},{19,3},{4,20},{20... | collective-permute-start | bytes 1572872 | tf_op jit(solution)/shard_map/ppermute | solution.py:172
  103.1 43.0 %collective-permute-start.2 = (f32[8,256,2]{1,0,2:T(8,128)S(1)}, f32[8,256,2]{1,0,2:T(8,128)S(1)}, u32[]{:S(2)}, u32[]{:S(2)}) collective-permute-start(f32[8,256,2]{1,0,2:T(8,128)S(1)} %copy.15), channel_id=1, source_target_pairs={{0,16},{16,0},{1,17},{17,1},{2,18},{18,2},{3,19},{19,3},{4,20},{20... | collective-permute-start | bytes 49160 | tf_op jit(solution)/shard_map/ppermute | solution.py:173
  147.5 0.8 copy-start.2
  148.3 16.3 %copy-start.6 = (bf16[2048]{0:T(1024)(128)(2,1)S(1)}, bf16[2048]{0:T(1024)(128)(2,1)}, u32[]{:S(2)}) copy-start(bf16[2048]{0:T(1024)(128)(2,1)} %param.17) | copy-start | bytes 12292
  162.2 7.6 %copy-start.3 = (bf16[256,1024]{1,0:T(8,128)(2,1)S(1)}, bf16[256,1024]{1,0:T(8,128)(2,1)}, u32[]{:S(2)}) copy-start(bf16[256,1024]{1,0:T(8,128)(2,1)} %shard_map.83) | copy-start | bytes 1572868
  162.2 4.1 %collective-permute-start.3 = (bf16[256,1024]{1,0:T(8,128)(2,1)}, bf16[256,1024]{1,0:T(8,128)(2,1)S(1)}, u32[]{:S(2)}, u32[]{:S(2)}) collective-permute-start(bf16[256,1024]{1,0:T(8,128)(2,1)} %shard_map.83), channel_id=1, source_target_pairs={{0,1},{1,0},{2,3},{3,2},{4,5},{5,4},{6,7},{7,6},{8,9},{9,8},{10,11... | collective-permute-start | bytes 1572872 | tf_op jit(solution)/shard_map/ppermute | solution.py:181

commit v10 on v9

--- a/solution.py
+++ b/solution.py
@@ -36,78 +36,116 @@
     return turned.reshape(row_count, -1).astype(jnp.bfloat16)
 
 
-def attention_kernel(*refs, with_local):
-    if with_local:
-        q_ref, kl_ref, vl_ref, kp_ref, vp_ref, ok_ref, bo_ref, bst_ref, o_ref = refs
-    else:
-        q_ref, kp_ref, vp_ref, ok_ref, o_ref, st_ref = refs
+SCORE_DIMS = (((1,), (1,)), ((), ()))
+
+
+def page_partial(q, kp_ref, vp_ref, ok_ref):
     score_scale = 1.0 / math.sqrt(HEAD_DIM)
-    dims = (((1,), (1,)), ((), ()))
-    q = q_ref[...]
-    span = q.shape[0]
     block_count, page_size, _ = kp_ref.shape
     keys_p = kp_ref[...].reshape(block_count * page_size, HEAD_DIM)
     values_p = vp_ref[...].reshape(block_count * page_size, HEAD_DIM)
-
-    s_pg = lax.dot_general(q, keys_p, dims, preferred_element_type=jnp.float32) * score_scale
-    s_pg = jnp.where(ok_ref[...] > 0, s_pg, NEG_FILL)
-    m = jnp.max(s_pg, axis=1, keepdims=True)
-    if with_local:
-        s_loc = lax.dot_general(q, kl_ref[...], dims, preferred_element_type=jnp.float32) * score_scale
-        row = lax.broadcasted_iota(jnp.int32, (span, span), 0)
-        col = lax.broadcasted_iota(jnp.int32, (span, span), 1)
-        s_loc = jnp.where(row >= col, s_loc, NEG_FILL)
-        m = jnp.maximum(m, jnp.max(s_loc, axis=1, keepdims=True))
-    p_pg = jnp.exp(s_pg - m)
-    l = jnp.sum(p_pg, axis=1, keepdims=True)
-    acc = jnp.dot(p_pg.astype(jnp.bfloat16), values_p, preferred_element_type=jnp.float32)
-    if with_local:
-        p_loc = jnp.exp(s_loc - m)
-        l = l + jnp.sum(p_loc, axis=1, keepdims=True)
-        acc = acc + jnp.dot(p_loc.astype(jnp.bfloat16), vl_ref[...], preferred_element_type=jnp.float32)
-        stats = bst_ref[...]
-        back_max = stats[:, 0:1]
-        back_sum = stats[:, 1:2]
-        peak = jnp.maximum(m, back_max)
-        near_w = jnp.exp(m - peak)
-        back_w = jnp.exp(back_max - peak) * back_sum
-        merged = acc * near_w + bo_ref[...].astype(jnp.float32) * back_w
-        o_ref[...] = (merged / (l * near_w + back_w)).astype(o_ref.dtype)
-    else:
-        o_ref[...] = (acc / l).astype(o_ref.dtype)
-        st_ref[:, 0:1] = m
-        st_ref[:, 1:2] = l
-
-
-def attend(key_ok, query_rot, incoming, local=None, back=None):
-    span, width = query_rot.shape
-    head_count = width // HEAD_DIM
-    block_count = incoming.shape[0]
-    page_size = incoming.shape[2]
+    s = lax.dot_general(q, keys_p, SCORE_DIMS, preferred_element_type=jnp.float32) * score_scale
+    s = jnp.where(ok_ref[...] > 0, s, NEG_FILL)
+    m = jnp.max(s, axis=1, keepdims=True)
+    p = jnp.exp(s - m)
+    l = jnp.sum(p, axis=1, keepdims=True)
+    acc = jnp.dot(p.astype(jnp.bfloat16), values_p, preferred_element_type=jnp.float32)
+    return m, l, acc
+
+
+def local_kernel(q_ref, kl_ref, vl_ref, acc_ref, st_ref):
+    score_scale = 1.0 / math.sqrt(HEAD_DIM)
+    q = q_ref[...]
+    span = q.shape[0]
+    s = lax.dot_general(q, kl_ref[...], SCORE_DIMS, preferred_element_type=jnp.float32) * score_scale
+    row = lax.broadcasted_iota(jnp.int32, (span, span), 0)
+    col = lax.broadcasted_iota(jnp.int32, (span, span), 1)
+    s = jnp.where(row >= col, s, NEG_FILL)
+    m = jnp.max(s, axis=1, keepdims=True)
+    p = jnp.exp(s - m)
+    acc_ref[...] = jnp.dot(p.astype(jnp.bfloat16), vl_ref[...], preferred_element_type=jnp.float32)
+    st_ref[:, 0:1] = m
+    st_ref[:, 1:2] = jnp.sum(p, axis=1, keepdims=True)
+
+
+def far_kernel(q_ref, kp_ref, vp_ref, ok_ref, o_ref, st_ref):
+    m, l, acc = page_partial(q_ref[...], kp_ref, vp_ref, ok_ref)
+    o_ref[...] = (acc / l).astype(o_ref.dtype)
+    st_ref[:, 0:1] = m
+    st_ref[:, 1:2] = l
+
+
+def near_kernel(q_ref, kp_ref, vp_ref, ok_ref, la_ref, lst_ref, bo_ref, bst_ref, o_ref):
+    m, l, acc = page_partial(q_ref[...], kp_ref, vp_ref, ok_ref)
+    local = lst_ref[...]
+    local_max = local[:, 0:1]
+    local_sum = local[:, 1:2]
+    back = bst_ref[...]
+    back_max = back[:, 0:1]
+    back_sum = back[:, 1:2]
+    peak = jnp.maximum(jnp.maximum(m, local_max), back_max)
+    page_w = jnp.exp(m - peak)
+    local_w = jnp.exp(local_max - peak)
+    back_w = jnp.exp(back_max - peak) * back_sum
+    merged = acc * page_w + la_ref[...] * local_w + bo_ref[...].astype(jnp.float32) * back_w
+    total = l * page_w + local_sum * local_w + back_w
+    o_ref[...] = (merged / total).astype(o_ref.dtype)
+
+
+def head_specs(span, block_count, page_size):
     col_spec = pl.BlockSpec((span, HEAD_DIM), lambda h: (0, h))
+    stat_spec = pl.BlockSpec((None, span, 2), lambda h: (h, 0, 0))
     page_specs = [
         pl.BlockSpec((block_count, None, page_size, HEAD_DIM), lambda h: (0, 0, 0, h)),
         pl.BlockSpec((block_count, None, page_size, HEAD_DIM), lambda h: (0, 1, 0, h)),
         pl.BlockSpec((1, block_count * page_size), lambda h: (0, 0)),
     ]
-    stat_spec = pl.BlockSpec((None, span, 2), lambda h: (h, 0, 0))
-    out_shape = jax.ShapeDtypeStruct((span, width), jnp.bfloat16)
-    if local is None:
-        in_specs = [col_spec] + page_specs
-        operands = (query_rot, incoming, incoming, key_ok)
-        out_specs = [col_spec, stat_spec]
-        out_shape = [out_shape, jax.ShapeDtypeStruct((head_count, span, 2), jnp.float32)]
-    else:
-        in_specs = [col_spec, col_spec, col_spec] + page_specs + [col_spec, stat_spec]
-        operands = (query_rot, local[0], local[1], incoming, incoming, key_ok, back[0], back[1])
-        out_specs = col_spec
+    return col_spec, stat_spec, page_specs
+
+
+def local_attend(query_rot, key_rot, values):
+    span, width = query_rot.shape
+    head_count = width // HEAD_DIM
+    col_spec, stat_spec, _ = head_specs(span, 1, 1)
     return pl.pallas_call(
-        partial(attention_kernel, with_local=local is not None),
+        local_kernel,
         grid=(head_count,),
-        in_specs=in_specs,
-        out_specs=out_specs,
-        out_shape=out_shape,
-    )(*operands)
+        in_specs=[col_spec, col_spec, col_spec],
+        out_specs=[col_spec, stat_spec],
+        out_shape=[
+            jax.ShapeDtypeStruct((span, width), jnp.float32),
+            jax.ShapeDtypeStruct((head_count, span, 2), jnp.float32),
+        ],
+    )(query_rot, key_rot, values)
+
+
+def far_attend(key_ok, query_rot, incoming):
+    span, width = query_rot.shape
+    head_count = width // HEAD_DIM
+    col_spec, stat_spec, page_specs = head_specs(span, incoming.shape[0], incoming.shape[2])
+    return pl.pallas_call(
+        far_kernel,
+        grid=(head_count,),
+        in_specs=[col_spec] + page_specs,
+        out_specs=[col_spec, stat_spec],
+        out_shape=[
+            jax.ShapeDtypeStruct((span, width), jnp.bfloat16),
+            jax.ShapeDtypeStruct((head_count, span, 2), jnp.float32),
+        ],
+    )(query_rot, incoming, incoming, key_ok)
+
+
+def near_attend(key_ok, query_rot, incoming, local_acc, local_stats, back_out, back_stats):
+    span, width = query_rot.shape
+    head_count = width // HEAD_DIM
+    col_spec, stat_spec, page_specs = head_specs(span, incoming.shape[0], incoming.shape[2])
+    return pl.pallas_call(
+        near_kernel,
+        grid=(head_count,),
+        in_specs=[col_spec] + page_specs + [col_spec, stat_spec, col_spec, stat_spec],
+        out_specs=col_spec,
+        out_shape=jax.ShapeDtypeStruct((span, width), jnp.bfloat16),
+    )(query_rot, incoming, incoming, key_ok, local_acc, local_stats, back_out, back_stats)
 
 
 def usable_keys(page_table, request, length, source_base, source_count, page_count, page_size):
@@ -168,11 +206,12 @@
     ok_own = usable_keys(page_table, own_index, own_length, source_base, sub_count, page_count, page_size)
     ok_partner = usable_keys(page_table, partner, partner_length, source_base, sub_count, page_count, page_size)
 
-    far_out, far_stats = attend(ok_partner, partner_query, far_incoming)
+    local_acc, local_stats = local_attend(query_rot, key_rot, new_values)
+    far_out, far_stats = far_attend(ok_partner, partner_query, far_incoming)
     back_out = lax.ppermute(far_out, "half", swap)
     back_stats = lax.ppermute(far_stats, "half", swap)
-    attended = attend(
-        ok_own, query_rot, near_incoming, local=(key_rot, new_values), back=(back_out, back_stats)
+    attended = near_attend(
+        ok_own, query_rot, near_incoming, local_acc, local_stats, back_out, back_stats
     )
 
     summed = jnp.dot(attended, w_mine, preferred_element_type=jnp.float32)

time: 175 us -> 173 us (0.989)
  waiting for transfers between devices: 92.8 us -> 86.3 us
  Pallas kernels: 22.4 us -> 26.7 us
    ppermute x1, waiting for transfers between devices: 39.7 us -> 33 us  [on_device(): back_stats = lax.ppermute(far_stats, 'half', swap)]
    pallas_call x2 -> x3, Pallas kernels: 22.4 us -> 26.7 us  [the longest x1 11.3 us: near_attend(): pl.pallas_call(near_kernel, grid=(head_count,), in_specs=[col_spec] + pag...]
  transfers between devices with their start and end apart: 7 -> 7, of which waited for: 3 -> 3; matrix products, arithmetic and copies ran while one was open for 13% -> 14% of each run, Pallas kernels for 13% -> 16%
where the time goes in v10:
time: 173 us; the launch traced here: 172 us
  waiting for transfers between devices  86.3 us (50%)
  Pallas kernels  26.7 us (15%)
  local copies, waits for them, and re-layouts  24.5 us (14%)
  starting transfers between devices  19 us (11%)
  matrix products  7.93 us (5%)
  other arithmetic  7.3 us (4%)
    ppermute x1, waiting for transfers between devices, on_device(): partner_query = lax.ppermute(query_rot, 'half', swap)  51.5 us
    ppermute x1, waiting for transfers between devices, on_device(): back_stats = lax.ppermute(far_stats, 'half', swap)  33 us
    pallas_call x1, Pallas kernels, near_attend(): pl.pallas_call(near_kernel, grid=(head_count,), in_specs=[col_spec] + pag...  11.3 us
    pallas_call x1, Pallas kernels, far_attend(): pl.pallas_call(far_kernel, grid=(head_count,), in_specs=[col_spec] + page...  8.5 us
    pallas_call x1, Pallas kernels, local_attend(): pl.pallas_call(local_kernel, grid=(head_count,), in_specs=[col_spec, col_...  6.82 us
    gather x1, local copies, waits for them, and re-layouts, on_device(): jnp.take(kv_pages, jnp.take(local_page, (1 - half) * sub_count + dest), a...  6.15 us
    gather x1, local copies, waits for them, and re-layouts, on_device(): jnp.take(kv_pages, jnp.take(local_page, half * sub_count + dest), axis=0,...  6.12 us
    all_to_all x1, starting transfers between devices, on_device(): lax.all_to_all(near_pages, 'sub', split_axis=0, concat_axis=0, tiled=True)  5.03 us
  transfers between devices with their start and end apart: 7, of which 3 were waited for; matrix products, arithmetic and copies ran while one was open for 14% of the time, Pallas kernels for 16%

profile of v10, /device:TPU:11, one launch (start us, length us, event | category | flops | bytes accessed | tf_op | source)
XLA Modules:
  0.0 171.8 jit_solution(17208984833449807285)
XLA Ops:
  0.0 0.8 select_reduce_fusion
  0.8 0.6 gather_fusion.3
  1.5 6.1 %gather_fusion.1 = bf16[8,2,128,1024]{3,2,1,0:T(8,128)(2,1)} fusion(bf16[16,2,128,1024]{3,2,1,0:T(8,128)(2,1)} %param.13, s32[1024]{0:T(1024)S(1)} %pad_clamp_fusion), kind=kCustom, calls=%fused_computation.3 | custom fusion | bytes 8388640 | tf_op jit(solution)/shard_map/jit(_take)/gather | solution.py:198
  7.7 4.7 %all-to-all-start.1 = ((bf16[8,2,128,1024]{3,2,1,0:T(8,128)(2,1)}), bf16[8,2,128,1024]{3,2,1,0:T(8,128)(2,1)}, u32[]{:S(2)}, u32[]{:S(2)}) async-start(bf16[8,2,128,1024]{3,2,1,0:T(8,128)(2,1)} %gather_fusion.1), calls=%async_computation.1 | async-start | bytes 8388608 | tf_op jit(solution)/shard_map/all_to_all | solution.py:199
  12.4 0.6 fusion.22
  14.8 0.8 subtract_convert_fusion
  15.7 1.0 pad_maximum_fusion
  16.7 2.4 %collective-permute-start = (bf16[256,1024]{1,0:T(8,128)(2,1)S(1)}, bf16[256,1024]{1,0:T(8,128)(2,1)S(1)}, u32[]{:S(2)}, u32[]{:S(2)}) collective-permute-start(bf16[256,1024]{1,0:T(8,128)(2,1)S(1)} %bitcast.25), channel_id=1, source_target_pairs={{0,16},{16,0},{1,17},{17,1},{2,18},{18,2},{3,19},{19,3},{4,20},{20... | collective-permute-start | bytes 1572872 | tf_op jit(solution)/shard_map/ppermute | solution.py:196
  19.1 0.6 gather_fusion.2
  19.8 6.1 %gather_fusion = bf16[8,2,128,1024]{3,2,1,0:T(8,128)(2,1)} fusion(bf16[16,2,128,1024]{3,2,1,0:T(8,128)(2,1)} %param.13, s32[1024]{0:T(1024)S(1)} %pad_clamp_fusion.2), kind=kCustom, calls=%fused_computation.2 | custom fusion | bytes 8388640 | tf_op jit(solution)/shard_map/jit(_take)/gather | solution.py:200
  25.9 51.5 %collective-permute-done.q_ref = bf16[256,1024]{1,0:T(8,128)(2,1)S(1)} collective-permute-done((bf16[256,1024]{1,0:T(8,128)(2,1)S(1)}, bf16[256,1024]{1,0:T(8,128)(2,1)S(1)}, u32[]{:S(2)}, u32[]{:S(2)}) %collective-permute-start) | collective-permute-done | bytes 524320 | tf_op jit(solution)/shard_map/ppermute | solution.py:196
  77.4 5.0 %all-to-all-start = ((bf16[8,2,128,1024]{3,2,1,0:T(8,128)(2,1)}), bf16[8,2,128,1024]{3,2,1,0:T(8,128)(2,1)}, u32[]{:S(2)}, u32[]{:S(2)}) async-start(bf16[8,2,128,1024]{3,2,1,0:T(8,128)(2,1)} %gather_fusion), calls=%async_computation | async-start | bytes 8388608 | tf_op jit(solution)/shard_map/all_to_all | solution.py:202
  82.5 4.7 %constant_dynamic-slice_fusion.2 = bf16[1024,2048]{1,0:T(8,128)(2,1)} fusion(bf16[1024,4096]{1,0:T(8,128)(2,1)} %param.16, s32[]{:T(128)S(6)} %select_n.98), kind=kLoop, calls=%fused_computation.61 | loop fusion | bytes 8388612 | tf_op jit(solution)/shard_map/dynamic_slice | solution.py:183
  87.2 2.1 %collective-permute-start.4 = (bf16[1024,2048]{1,0:T(8,128)(2,1)}, bf16[1024,2048]{1,0:T(8,128)(2,1)}, u32[]{:S(2)}, u32[]{:S(2)}) collective-permute-start(bf16[1024,2048]{1,0:T(8,128)(2,1)} %constant_dynamic-slice_fusion.2), channel_id=1, source_target_pairs={{0,1},{1,0},{2,3},{3,2},{4,5},{5,4},{6,7},{7,6},{8,9},{9,8},{10,11... | collective-permute-start | bytes 12582920 | tf_op jit(solution)/shard_map/ppermute | solution.py:185
  89.3 0.7 fusion.20
  90.4 0.7 clamp_select_fusion
  91.0 0.7 fusion.18
  91.7 8.5 %shard_map.83 = (bf16[256,1024]{1,0:T(8,128)(2,1)}, f32[8,256,2]{2,1,0:T(8,128)}) custom-call(bf16[256,1024]{1,0:T(8,128)(2,1)} %copy-done.1, bf16[8,2,128,1024]{3,2,1,0:T(8,128)(2,1)} %all-to-all-done.1.kp_ref.vp_ref, bf16[8,2,128,1024]{3,2,1,0:T(8,128)(2,1)} %all-to-all-done.1.kp_ref.vp_ref, s32[1,1024]{1,0:T(1,128)} %bitcast.36), custom_call_target="tpu_custom_call" | custom-call | tf_op jit(solution)/shard_map/pallas_call | solution.py:126
  100.2 0.7 collective-permute-start.1
  101.5 1.5 copy.15
  103.0 1.7 %collective-permute-start.2 = (f32[8,256,2]{1,0,2:T(8,128)S(1)}, f32[8,256,2]{1,0,2:T(8,128)S(1)}, u32[]{:S(2)}, u32[]{:S(2)}) collective-permute-start(f32[8,256,2]{1,0,2:T(8,128)S(1)} %copy.15), channel_id=1, source_target_pairs={{0,16},{16,0},{1,17},{17,1},{2,18},{18,2},{3,19},{19,3},{4,20},{20... | collective-permute-start | bytes 49160 | tf_op jit(solution)/shard_map/ppermute | solution.py:212
  104.8 0.7 fusion.17
  105.4 0.9 copy.23
  106.4 6.8 %shard_map.82 = (f32[256,1024]{1,0:T(8,128)}, f32[8,256,2]{2,1,0:T(8,128)}) custom-call(bf16[256,1024]{1,0:T(8,128)(2,1)} %bitcast.26, bf16[256,1024]{1,0:T(8,128)(2,1)} %bitcast.30, bf16[256,1024]{1,0:T(8,128)(2,1)} %vl_ref.1), custom_call_target="tpu_custom_call" | custom-call | tf_op jit(solution)/shard_map/pallas_call | solution.py:110
  113.2 33.0 %collective-permute-done.2 = f32[8,256,2]{1,0,2:T(8,128)S(1)} collective-permute-done((f32[8,256,2]{1,0,2:T(8,128)S(1)}, f32[8,256,2]{1,0,2:T(8,128)S(1)}, u32[]{:S(2)}, u32[]{:S(2)}) %collective-permute-start.2) | collective-permute-done | bytes 16416 | tf_op jit(solution)/shard_map/ppermute | solution.py:212
  146.2 1.4 copy.16.bst_ref
  147.6 0.8 copy-done.2
  148.4 11.3 %shard_map.84 = bf16[256,1024]{1,0:T(8,128)(2,1)} custom-call(bf16[256,1024]{1,0:T(8,128)(2,1)} %bitcast.27, bf16[8,2,128,1024]{3,2,1,0:T(8,128)(2,1)} %all-to-all-done.kp_ref.vp_ref, bf16[8,2,128,1024]{3,2,1,0:T(8,128)(2,1)} %all-to-all-done.kp_ref.vp_ref, s32[1,1024]{1,0:T(1,128)} %bitcast.35, f32[256,1024]{1,0:T(8,128)} %get-tuple-element.13.la_ref, ...), custom_call_target="tpu_custom_call" | custom-call | tf_op jit(solution)/shard_map/pallas_call | solution.py:142
  159.8 2.4 %collective-permute-start.3 = (bf16[256,1024]{1,0:T(8,128)(2,1)}, bf16[256,1024]{1,0:T(8,128)(2,1)S(1)}, u32[]{:S(2)}, u32[]{:S(2)}) collective-permute-start(bf16[256,1024]{1,0:T(8,128)(2,1)} %shard_map.84), channel_id=1, source_target_pairs={{0,1},{1,0},{2,3},{3,2},{4,5},{5,4},{6,7},{7,6},{8,9},{9,8},{10,11... | collective-permute-start | bytes 1572872 | tf_op jit(solution)/shard_map/ppermute | solution.py:220
  162.1 1.7 %collective-permute-done.3 = bf16[256,1024]{1,0:T(8,128)(2,1)S(1)} collective-permute-done((bf16[256,1024]{1,0:T(8,128)(2,1)}, bf16[256,1024]{1,0:T(8,128)(2,1)S(1)}, u32[]{:S(2)}, u32[]{:S(2)}) %collective-permute-start.3) | collective-permute-done | bytes 524320 | tf_op jit(solution)/shard_map/ppermute | solution.py:220
  163.9 3.5 %fusion.23 = f32[256,2048]{1,0:T(8,128)S(1)} fusion(bf16[256,1024]{1,0:T(8,128)(2,1)S(1)} %collective-permute-done.3, bf16[1024,2048]{1,0:T(8,128)(2,1)} %collective-permute-done.4), kind=kOutput, calls=%fused_computation.71 | convolution fusion | flops 1073741824 | bytes 6815744 | tf_op jit(solution)/shard_map/dot_general | solution.py:221
  167.3 4.5 %fusion.8 = bf16[256,2048]{1,0:T(8,128)(2,1)} fusion(f32[256,2048]{1,0:T(8,128)S(1)} %fusion.23, bf16[256,1024]{1,0:T(8,128)(2,1)S(1)} %copy-done.3, bf16[1024,4096]{1,0:T(8,128)(2,1)} %param.16, s32[]{:T(128)S(6)} %select_n.96, f32[2048]{0:T(1024)S(1)} %convert_element_type.55), kind=kOutput, calls=%fused_computation.8 | convolution fusion | flops 1075314688 | bytes 7872516 | tf_op jit(solution)/shard_map/dot_general | solution.py:217
  (43 shorter events, 2.9 us)
Async XLA Ops:
  7.7 4.7 %copy-start.7 = (s32[16]{0:T(128)S(1)}, s32[16]{0:T(128)}, u32[]{:S(2)}) copy-start(s32[16]{0:T(128)} %param.15) | copy-start | bytes 196
  7.7 6.3 %copy-start.4 = (bf16[256,1024]{1,0:T(8,128)(2,1)S(1)}, bf16[256,1024]{1,0:T(8,128)(2,1)}, u32[]{:S(2)}) copy-start(bf16[256,1024]{1,0:T(8,128)(2,1)} %param.10) | copy-start | bytes 1572868
  7.7 6.4 %copy-start.5 = (bf16[256,1024]{1,0:T(8,128)(2,1)S(1)}, bf16[256,1024]{1,0:T(8,128)(2,1)}, u32[]{:S(2)}) copy-start(bf16[256,1024]{1,0:T(8,128)(2,1)} %param.11) | copy-start | bytes 1572868
  7.7 69.8 %all-to-all-start.1 = ((bf16[8,2,128,1024]{3,2,1,0:T(8,128)(2,1)}), bf16[8,2,128,1024]{3,2,1,0:T(8,128)(2,1)}, u32[]{:S(2)}, u32[]{:S(2)}) async-start(bf16[8,2,128,1024]{3,2,1,0:T(8,128)(2,1)} %gather_fusion.1), calls=%async_computation.1 | async-start | bytes 8388608 | tf_op jit(solution)/shard_map/all_to_all | solution.py:199
  16.7 9.2 %copy-start = (bf16[32,8,8,128]{3,1,2,0:T(8,128)(2,1)}, bf16[32,8,8,128]{3,1,2,0:T(8,128)(2,1)S(1)}, u32[]{:S(2)}) copy-start(bf16[32,8,8,128]{3,1,2,0:T(8,128)(2,1)S(1)} %copy.24) | copy-start | bytes 1572868
  16.7 60.7 %collective-permute-start = (bf16[256,1024]{1,0:T(8,128)(2,1)S(1)}, bf16[256,1024]{1,0:T(8,128)(2,1)S(1)}, u32[]{:S(2)}, u32[]{:S(2)}) collective-permute-start(bf16[256,1024]{1,0:T(8,128)(2,1)S(1)} %bitcast.25), channel_id=1, source_target_pairs={{0,16},{16,0},{1,17},{17,1},{2,18},{18,2},{3,19},{19,3},{4,20},{20... | collective-permute-start | bytes 1572872 | tf_op jit(solution)/shard_map/ppermute | solution.py:196
  77.4 5.0 %copy-start.1 = (bf16[256,1024]{1,0:T(8,128)(2,1)}, bf16[256,1024]{1,0:T(8,128)(2,1)S(1)}, u32[]{:S(2)}) copy-start(bf16[256,1024]{1,0:T(8,128)(2,1)S(1)} %collective-permute-done.q_ref) | copy-start | bytes 1572868
  77.4 70.2 %all-to-all-start = ((bf16[8,2,128,1024]{3,2,1,0:T(8,128)(2,1)}), bf16[8,2,128,1024]{3,2,1,0:T(8,128)(2,1)}, u32[]{:S(2)}, u32[]{:S(2)}) async-start(bf16[8,2,128,1024]{3,2,1,0:T(8,128)(2,1)} %gather_fusion), calls=%async_computation | async-start | bytes 8388608 | tf_op jit(solution)/shard_map/all_to_all | solution.py:202
  87.2 74.9 %collective-permute-start.4 = (bf16[1024,2048]{1,0:T(8,128)(2,1)}, bf16[1024,2048]{1,0:T(8,128)(2,1)}, u32[]{:S(2)}, u32[]{:S(2)}) collective-permute-start(bf16[1024,2048]{1,0:T(8,128)(2,1)} %constant_dynamic-slice_fusion.2), channel_id=1, source_target_pairs={{0,1},{1,0},{2,3},{3,2},{4,5},{5,4},{6,7},{7,6},{8,9},{9,8},{10,11... | collective-permute-start | bytes 12582920 | tf_op jit(solution)/shard_map/ppermute | solution.py:185
  100.2 47.4 %collective-permute-start.1 = (bf16[256,1024]{1,0:T(8,128)(2,1)}, bf16[256,1024]{1,0:T(8,128)(2,1)S(1)}, u32[]{:S(2)}, u32[]{:S(2)}) collective-permute-start(bf16[256,1024]{1,0:T(8,128)(2,1)} %get-tuple-element.16), channel_id=1, source_target_pairs={{0,16},{16,0},{1,17},{17,1},{2,18},{18,2},{3,19},{19,3},{4,20},{20... | collective-permute-start | bytes 1572872 | tf_op jit(solution)/shard_map/ppermute | solution.py:211
  103.0 43.2 %collective-permute-start.2 = (f32[8,256,2]{1,0,2:T(8,128)S(1)}, f32[8,256,2]{1,0,2:T(8,128)S(1)}, u32[]{:S(2)}, u32[]{:S(2)}) collective-permute-start(f32[8,256,2]{1,0,2:T(8,128)S(1)} %copy.15), channel_id=1, source_target_pairs={{0,16},{16,0},{1,17},{17,1},{2,18},{18,2},{3,19},{19,3},{4,20},{20... | collective-permute-start | bytes 49160 | tf_op jit(solution)/shard_map/ppermute | solution.py:212
  147.6 0.8 copy-start.2
  148.4 13.7 %copy-start.6 = (bf16[2048]{0:T(1024)(128)(2,1)S(1)}, bf16[2048]{0:T(1024)(128)(2,1)}, u32[]{:S(2)}) copy-start(bf16[2048]{0:T(1024)(128)(2,1)} %param.17) | copy-start | bytes 12292
  159.8 7.6 %copy-start.3 = (bf16[256,1024]{1,0:T(8,128)(2,1)S(1)}, bf16[256,1024]{1,0:T(8,128)(2,1)}, u32[]{:S(2)}) copy-start(bf16[256,1024]{1,0:T(8,128)(2,1)} %shard_map.84) | copy-start | bytes 1572868
  159.8 4.1 %collective-permute-start.3 = (bf16[256,1024]{1,0:T(8,128)(2,1)}, bf16[256,1024]{1,0:T(8,128)(2,1)S(1)}, u32[]{:S(2)}, u32[]{:S(2)}) collective-permute-start(bf16[256,1024]{1,0:T(8,128)(2,1)} %shard_map.84), channel_id=1, source_target_pairs={{0,1},{1,0},{2,3},{3,2},{4,5},{5,4},{6,7},{7,6},{8,9},{9,8},{10,11... | collective-permute-start | bytes 1572872 | tf_op jit(solution)/shard_map/ppermute | solution.py:220

commit v11 on v10

--- a/solution.py
+++ b/solution.py
@@ -75,7 +75,7 @@
     st_ref[:, 1:2] = l
 
 
-def near_kernel(q_ref, kp_ref, vp_ref, ok_ref, la_ref, lst_ref, bo_ref, bst_ref, o_ref):
+def near_kernel(q_ref, kp_ref, vp_ref, ok_ref, la_ref, lst_ref, bo_ref, bst_ref, w_ref, o_ref, proj_ref):
     m, l, acc = page_partial(q_ref[...], kp_ref, vp_ref, ok_ref)
     local = lst_ref[...]
     local_max = local[:, 0:1]
@@ -89,7 +89,14 @@
     back_w = jnp.exp(back_max - peak) * back_sum
     merged = acc * page_w + la_ref[...] * local_w + bo_ref[...].astype(jnp.float32) * back_w
     total = l * page_w + local_sum * local_w + back_w
-    o_ref[...] = (merged / total).astype(o_ref.dtype)
+    attended = (merged / total).astype(o_ref.dtype)
+    o_ref[...] = attended
+
+    @pl.when(pl.program_id(0) == 0)
+    def _():
+        proj_ref[...] = jnp.zeros_like(proj_ref)
+
+    proj_ref[...] += jnp.dot(attended, w_ref[...], preferred_element_type=jnp.float32)
 
 
 def head_specs(span, block_count, page_size):
@@ -135,17 +142,23 @@
     )(query_rot, incoming, incoming, key_ok)
 
 
-def near_attend(key_ok, query_rot, incoming, local_acc, local_stats, back_out, back_stats):
+def near_attend(key_ok, query_rot, incoming, local_acc, local_stats, back_out, back_stats, w_rows):
     span, width = query_rot.shape
     head_count = width // HEAD_DIM
+    out_cols = w_rows.shape[1]
     col_spec, stat_spec, page_specs = head_specs(span, incoming.shape[0], incoming.shape[2])
+    w_spec = pl.BlockSpec((HEAD_DIM, out_cols), lambda h: (h, 0))
+    proj_spec = pl.BlockSpec((span, out_cols), lambda h: (0, 0))
     return pl.pallas_call(
         near_kernel,
         grid=(head_count,),
-        in_specs=[col_spec] + page_specs + [col_spec, stat_spec, col_spec, stat_spec],
-        out_specs=col_spec,
-        out_shape=jax.ShapeDtypeStruct((span, width), jnp.bfloat16),
-    )(query_rot, incoming, incoming, key_ok, local_acc, local_stats, back_out, back_stats)
+        in_specs=[col_spec] + page_specs + [col_spec, stat_spec, col_spec, stat_spec, w_spec],
+        out_specs=[col_spec, proj_spec],
+        out_shape=[
+            jax.ShapeDtypeStruct((span, width), jnp.bfloat16),
+            jax.ShapeDtypeStruct((span, out_cols), jnp.float32),
+        ],
+    )(query_rot, incoming, incoming, key_ok, local_acc, local_stats, back_out, back_stats, w_rows)
 
 
 def usable_keys(page_table, request, length, source_base, source_count, page_count, page_size):
@@ -210,11 +223,10 @@
     far_out, far_stats = far_attend(ok_partner, partner_query, far_incoming)
     back_out = lax.ppermute(far_out, "half", swap)
     back_stats = lax.ppermute(far_stats, "half", swap)
-    attended = near_attend(
-        ok_own, query_rot, near_incoming, local_acc, local_stats, back_out, back_stats
+    attended, summed = near_attend(
+        ok_own, query_rot, near_incoming, local_acc, local_stats, back_out, back_stats, w_mine
     )
 
-    summed = jnp.dot(attended, w_mine, preferred_element_type=jnp.float32)
     for shift in range(1, tp_count):
         perm = [(i, (i + shift) % tp_count) for i in range(tp_count)]
         other = lax.ppermute(attended, "tp", perm)

time: 173 us -> 174 us (level)
  matrix products: 7.93 us -> 3.46 us
  Pallas kernels: 26.7 us -> 30.9 us
  waiting for transfers between devices: 86.3 us -> 82.5 us
  local copies, waits for them, and re-layouts: 24.5 us -> 28.1 us
    dot_general x1 -> x0, matrix products: 4.47 us -> none  [on_device(): summed = jnp.dot(attended, w_mine, preferred_element_type=jnp.float32)]
    pallas_call x1, Pallas kernels: 11.3 us -> 15.6 us  [near_attend(): pl.pallas_call(near_kernel, grid=(head_count,), in_specs=[col_spec] + pag...]
    ppermute x1, waiting for transfers between devices: 33 us -> 29.3 us  [on_device(): back_stats = lax.ppermute(far_stats, 'half', swap)]
    dynamic_slice x1, local copies, waits for them, and re-layouts: 4.73 us -> 8.31 us  [on_device(): piece = lax.dynamic_slice_in_dim(w_out, target * out_cols, out_cols, axis=1)]
  transfers between devices with their start and end apart: 7 -> 7, of which waited for: 3 -> 3; matrix products, arithmetic and copies ran while one was open for 14% -> 16% of each run, Pallas kernels for 16% -> 18%
where the time goes in v11:
time: 174 us; the launch traced here: 173 us
  waiting for transfers between devices  82.5 us (47%)
  Pallas kernels  30.9 us (18%)
  local copies, waits for them, and re-layouts  28.1 us (16%)
  starting transfers between devices  19.1 us (11%)
  other arithmetic  8.7 us (5%)
  matrix products  3.46 us (2%)
    ppermute x1, waiting for transfers between devices, on_device(): partner_query = lax.ppermute(query_rot, 'half', swap)  51.4 us
    ppermute x1, waiting for transfers between devices, on_device(): back_stats = lax.ppermute(far_stats, 'half', swap)  29.3 us
    pallas_call x1, Pallas kernels, near_attend(): pl.pallas_call(near_kernel, grid=(head_count,), in_specs=[col_spec] + pag...  15.6 us
    pallas_call x1, Pallas kernels, far_attend(): pl.pallas_call(far_kernel, grid=(head_count,), in_specs=[col_spec] + page...  8.52 us
    dynamic_slice x1, local copies, waits for them, and re-layouts, on_device(): piece = lax.dynamic_slice_in_dim(w_out, target * out_cols, out_cols, axis=1)  8.31 us
    pallas_call x1, Pallas kernels, local_attend(): pl.pallas_call(local_kernel, grid=(head_count,), in_specs=[col_spec, col_...  6.82 us
    gather x1, local copies, waits for them, and re-layouts, on_device(): jnp.take(kv_pages, jnp.take(local_page, (1 - half) * sub_count + dest), a...  6.15 us
    gather x1, local copies, waits for them, and re-layouts, on_device(): jnp.take(kv_pages, jnp.take(local_page, half * sub_count + dest), axis=0,...  6.14 us
  transfers between devices with their start and end apart: 7, of which 3 were waited for; matrix products, arithmetic and copies ran while one was open for 16% of the time, Pallas kernels for 18%

profile of v11, /device:TPU:11, one launch (start us, length us, event | category | flops | bytes accessed | tf_op | source)
XLA Modules:
  0.0 173.0 jit_solution(15861958792835807879)
XLA Ops:
  0.0 0.8 select_reduce_fusion
  0.8 0.6 gather_fusion.3
  1.5 6.1 %gather_fusion.1 = bf16[8,2,128,1024]{3,2,1,0:T(8,128)(2,1)} fusion(bf16[16,2,128,1024]{3,2,1,0:T(8,128)(2,1)} %param.13, s32[1024]{0:T(1024)S(1)} %pad_clamp_fusion), kind=kCustom, calls=%fused_computation.3 | custom fusion | bytes 8388640 | tf_op jit(solution)/shard_map/jit(_take)/gather | solution.py:211
  7.7 4.7 %all-to-all-start.1 = ((bf16[8,2,128,1024]{3,2,1,0:T(8,128)(2,1)}), bf16[8,2,128,1024]{3,2,1,0:T(8,128)(2,1)}, u32[]{:S(2)}, u32[]{:S(2)}) async-start(bf16[8,2,128,1024]{3,2,1,0:T(8,128)(2,1)} %gather_fusion.1), calls=%async_computation.1 | async-start | bytes 8388608 | tf_op jit(solution)/shard_map/all_to_all | solution.py:212
  13.0 0.6 add_convert_fusion.3
  14.9 0.8 subtract_convert_fusion
  15.7 1.0 pad_maximum_fusion
  16.8 2.4 %collective-permute-start = (bf16[256,1024]{1,0:T(8,128)(2,1)S(1)}, bf16[256,1024]{1,0:T(8,128)(2,1)S(1)}, u32[]{:S(2)}, u32[]{:S(2)}) collective-permute-start(bf16[256,1024]{1,0:T(8,128)(2,1)S(1)} %bitcast.24), channel_id=1, source_target_pairs={{0,16},{16,0},{1,17},{17,1},{2,18},{18,2},{3,19},{19,3},{4,20},{20... | collective-permute-start | bytes 1572872 | tf_op jit(solution)/shard_map/ppermute | solution.py:209
  19.1 0.6 gather_fusion.2
  19.8 6.1 %gather_fusion = bf16[8,2,128,1024]{3,2,1,0:T(8,128)(2,1)} fusion(bf16[16,2,128,1024]{3,2,1,0:T(8,128)(2,1)} %param.13, s32[1024]{0:T(1024)S(1)} %pad_clamp_fusion.2), kind=kCustom, calls=%fused_computation.2 | custom fusion | bytes 8388640 | tf_op jit(solution)/shard_map/jit(_take)/gather | solution.py:213
  26.0 51.4 %collective-permute-done.q_ref = bf16[256,1024]{1,0:T(8,128)(2,1)S(1)} collective-permute-done((bf16[256,1024]{1,0:T(8,128)(2,1)S(1)}, bf16[256,1024]{1,0:T(8,128)(2,1)S(1)}, u32[]{:S(2)}, u32[]{:S(2)}) %collective-permute-start) | collective-permute-done | bytes 524320 | tf_op jit(solution)/shard_map/ppermute | solution.py:209
  77.4 5.1 %all-to-all-start = ((bf16[8,2,128,1024]{3,2,1,0:T(8,128)(2,1)}), bf16[8,2,128,1024]{3,2,1,0:T(8,128)(2,1)}, u32[]{:S(2)}, u32[]{:S(2)}) async-start(bf16[8,2,128,1024]{3,2,1,0:T(8,128)(2,1)} %gather_fusion), calls=%async_computation | async-start | bytes 8388608 | tf_op jit(solution)/shard_map/all_to_all | solution.py:215
  82.5 8.3 %constant_dynamic-slice_fusion.3 = (bf16[1024,2048]{1,0:T(8,128)(2,1)}, bf16[1024,2048]{1,0:T(8,128)(2,1)}) fusion(bf16[1024,4096]{1,0:T(8,128)(2,1)} %param.16, s32[]{:T(128)S(6)} %select_n.98, s32[]{:T(128)S(6)} %select_n.96), kind=kLoop, calls=%fused_computation.57 | loop fusion | bytes 16777224 | tf_op jit(solution)/shard_map/dynamic_slice | solution.py:196
  90.8 2.1 %collective-permute-start.4 = (bf16[1024,2048]{1,0:T(8,128)(2,1)}, bf16[1024,2048]{1,0:T(8,128)(2,1)}, u32[]{:S(2)}, u32[]{:S(2)}) collective-permute-start(bf16[1024,2048]{1,0:T(8,128)(2,1)} %get-tuple-element.26), channel_id=1, source_target_pairs={{0,1},{1,0},{2,3},{3,2},{4,5},{5,4},{6,7},{7,6},{8,9},{9,8},{10,11... | collective-permute-start | bytes 12582920 | tf_op jit(solution)/shard_map/ppermute | solution.py:198
  92.9 0.7 fusion.8
  94.0 0.7 clamp_select_fusion
  94.6 0.7 fusion.7
  95.3 8.5 %shard_map.83 = (bf16[256,1024]{1,0:T(8,128)(2,1)}, f32[8,256,2]{2,1,0:T(8,128)}) custom-call(bf16[256,1024]{1,0:T(8,128)(2,1)} %copy-done.2, bf16[8,2,128,1024]{3,2,1,0:T(8,128)(2,1)} %all-to-all-done.1.kp_ref.vp_ref, bf16[8,2,128,1024]{3,2,1,0:T(8,128)(2,1)} %all-to-all-done.1.kp_ref.vp_ref, s32[1,1024]{1,0:T(1,128)} %bitcast.35), custom_call_target="tpu_custom_call" | custom-call | tf_op jit(solution)/shard_map/pallas_call | solution.py:133
  104.4 0.6 clamp_select_fusion.1
  105.0 1.5 copy.15
  106.6 1.8 %collective-permute-start.2 = (f32[8,256,2]{1,0,2:T(8,128)S(1)}, f32[8,256,2]{1,0,2:T(8,128)S(1)}, u32[]{:S(2)}, u32[]{:S(2)}) collective-permute-start(f32[8,256,2]{1,0,2:T(8,128)S(1)} %copy.15), channel_id=1, source_target_pairs={{0,16},{16,0},{1,17},{17,1},{2,18},{18,2},{3,19},{19,3},{4,20},{20... | collective-permute-start | bytes 49160 | tf_op jit(solution)/shard_map/ppermute | solution.py:225
  108.4 0.7 fusion.6
  109.1 0.9 copy.23
  110.0 6.8 %shard_map.82 = (f32[256,1024]{1,0:T(8,128)}, f32[8,256,2]{2,1,0:T(8,128)}) custom-call(bf16[256,1024]{1,0:T(8,128)(2,1)} %bitcast.25, bf16[256,1024]{1,0:T(8,128)(2,1)} %bitcast.29, bf16[256,1024]{1,0:T(8,128)(2,1)} %vl_ref.1), custom_call_target="tpu_custom_call" | custom-call | tf_op jit(solution)/shard_map/pallas_call | solution.py:117
  116.8 29.3 %collective-permute-done.2 = f32[8,256,2]{1,0,2:T(8,128)S(1)} collective-permute-done((f32[8,256,2]{1,0,2:T(8,128)S(1)}, f32[8,256,2]{1,0,2:T(8,128)S(1)}, u32[]{:S(2)}, u32[]{:S(2)}) %collective-permute-start.2) | collective-permute-done | bytes 16416 | tf_op jit(solution)/shard_map/ppermute | solution.py:225
  146.1 1.4 copy.16.bst_ref
  147.5 0.8 copy-done.3
  148.3 15.6 %shard_map.84 = (bf16[256,1024]{1,0:T(8,128)(2,1)}, f32[256,2048]{1,0:T(8,128)}) custom-call(bf16[256,1024]{1,0:T(8,128)(2,1)} %bitcast.26, bf16[8,2,128,1024]{3,2,1,0:T(8,128)(2,1)} %all-to-all-done.kp_ref.vp_ref, bf16[8,2,128,1024]{3,2,1,0:T(8,128)(2,1)} %all-to-all-done.kp_ref.vp_ref, s32[1,1024]{1,0:T(1,128)} %bitcast.34, ...), custom_call_target="tpu_custom_call" | custom-call | tf_op jit(solution)/shard_map/pallas_call | solution.py:152
  163.9 2.5 %collective-permute-start.3 = (bf16[256,1024]{1,0:T(8,128)(2,1)}, bf16[256,1024]{1,0:T(8,128)(2,1)S(1)}, u32[]{:S(2)}, u32[]{:S(2)}) collective-permute-start(bf16[256,1024]{1,0:T(8,128)(2,1)} %get-tuple-element.21), channel_id=1, source_target_pairs={{0,1},{1,0},{2,3},{3,2},{4,5},{5,4},{6,7},{7,6},{8,9},{9,8},{10,11... | collective-permute-start | bytes 1572872 | tf_op jit(solution)/shard_map/ppermute | solution.py:232
  166.4 1.7 %collective-permute-done.3 = bf16[256,1024]{1,0:T(8,128)(2,1)S(1)} collective-permute-done((bf16[256,1024]{1,0:T(8,128)(2,1)}, bf16[256,1024]{1,0:T(8,128)(2,1)S(1)}, u32[]{:S(2)}, u32[]{:S(2)}) %collective-permute-start.3) | collective-permute-done | bytes 524320 | tf_op jit(solution)/shard_map/ppermute | solution.py:232
  168.1 3.5 %fusion.11 = f32[256,2048]{1,0:T(8,128)S(1)} fusion(bf16[256,1024]{1,0:T(8,128)(2,1)S(1)} %collective-permute-done.3, bf16[1024,2048]{1,0:T(8,128)(2,1)} %collective-permute-done.4), kind=kOutput, calls=%fused_computation.67 | convolution fusion | flops 1073741824 | bytes 6815744 | tf_op jit(solution)/shard_map/dot_general | solution.py:233
  171.6 1.4 add_convert_fusion
  (43 shorter events, 2.9 us)
Async XLA Ops:
  7.7 4.7 %copy-start.7 = (s32[16]{0:T(128)S(1)}, s32[16]{0:T(128)}, u32[]{:S(2)}) copy-start(s32[16]{0:T(128)} %param.15) | copy-start | bytes 196
  7.7 6.3 %copy-start.4 = (bf16[256,1024]{1,0:T(8,128)(2,1)S(1)}, bf16[256,1024]{1,0:T(8,128)(2,1)}, u32[]{:S(2)}) copy-start(bf16[256,1024]{1,0:T(8,128)(2,1)} %param.11) | copy-start | bytes 1572868
  7.7 6.5 %copy-start.5 = (bf16[256,1024]{1,0:T(8,128)(2,1)S(1)}, bf16[256,1024]{1,0:T(8,128)(2,1)}, u32[]{:S(2)}) copy-start(bf16[256,1024]{1,0:T(8,128)(2,1)} %param.10) | copy-start | bytes 1572868
  7.7 69.7 %all-to-all-start.1 = ((bf16[8,2,128,1024]{3,2,1,0:T(8,128)(2,1)}), bf16[8,2,128,1024]{3,2,1,0:T(8,128)(2,1)}, u32[]{:S(2)}, u32[]{:S(2)}) async-start(bf16[8,2,128,1024]{3,2,1,0:T(8,128)(2,1)} %gather_fusion.1), calls=%async_computation.1 | async-start | bytes 8388608 | tf_op jit(solution)/shard_map/all_to_all | solution.py:212
  16.7 9.2 %copy-start = (bf16[32,8,8,128]{3,1,2,0:T(8,128)(2,1)}, bf16[32,8,8,128]{3,1,2,0:T(8,128)(2,1)S(1)}, u32[]{:S(2)}) copy-start(bf16[32,8,8,128]{3,1,2,0:T(8,128)(2,1)S(1)} %copy.24) | copy-start | bytes 1572868
  16.8 60.6 %collective-permute-start = (bf16[256,1024]{1,0:T(8,128)(2,1)S(1)}, bf16[256,1024]{1,0:T(8,128)(2,1)S(1)}, u32[]{:S(2)}, u32[]{:S(2)}) collective-permute-start(bf16[256,1024]{1,0:T(8,128)(2,1)S(1)} %bitcast.24), channel_id=1, source_target_pairs={{0,16},{16,0},{1,17},{17,1},{2,18},{18,2},{3,19},{19,3},{4,20},{20... | collective-permute-start | bytes 1572872 | tf_op jit(solution)/shard_map/ppermute | solution.py:209
  77.4 5.1 %copy-start.2 = (bf16[256,1024]{1,0:T(8,128)(2,1)}, bf16[256,1024]{1,0:T(8,128)(2,1)S(1)}, u32[]{:S(2)}) copy-start(bf16[256,1024]{1,0:T(8,128)(2,1)S(1)} %collective-permute-done.q_ref) | copy-start | bytes 1572868
  77.4 70.1 %all-to-all-start = ((bf16[8,2,128,1024]{3,2,1,0:T(8,128)(2,1)}), bf16[8,2,128,1024]{3,2,1,0:T(8,128)(2,1)}, u32[]{:S(2)}, u32[]{:S(2)}) async-start(bf16[8,2,128,1024]{3,2,1,0:T(8,128)(2,1)} %gather_fusion), calls=%async_computation | async-start | bytes 8388608 | tf_op jit(solution)/shard_map/all_to_all | solution.py:215
  90.8 75.6 %collective-permute-start.4 = (bf16[1024,2048]{1,0:T(8,128)(2,1)}, bf16[1024,2048]{1,0:T(8,128)(2,1)}, u32[]{:S(2)}, u32[]{:S(2)}) collective-permute-start(bf16[1024,2048]{1,0:T(8,128)(2,1)} %get-tuple-element.26), channel_id=1, source_target_pairs={{0,1},{1,0},{2,3},{3,2},{4,5},{5,4},{6,7},{7,6},{8,9},{9,8},{10,11... | collective-permute-start | bytes 12582920 | tf_op jit(solution)/shard_map/ppermute | solution.py:198
  103.8 43.7 %collective-permute-start.1 = (bf16[256,1024]{1,0:T(8,128)(2,1)}, bf16[256,1024]{1,0:T(8,128)(2,1)S(1)}, u32[]{:S(2)}, u32[]{:S(2)}) collective-permute-start(bf16[256,1024]{1,0:T(8,128)(2,1)} %get-tuple-element.18), channel_id=1, source_target_pairs={{0,16},{16,0},{1,17},{17,1},{2,18},{18,2},{3,19},{19,3},{4,20},{20... | collective-permute-start | bytes 1572872 | tf_op jit(solution)/shard_map/ppermute | solution.py:224
  106.6 39.5 %collective-permute-start.2 = (f32[8,256,2]{1,0,2:T(8,128)S(1)}, f32[8,256,2]{1,0,2:T(8,128)S(1)}, u32[]{:S(2)}, u32[]{:S(2)}) collective-permute-start(f32[8,256,2]{1,0,2:T(8,128)S(1)} %copy.15), channel_id=1, source_target_pairs={{0,16},{16,0},{1,17},{17,1},{2,18},{18,2},{3,19},{19,3},{4,20},{20... | collective-permute-start | bytes 49160 | tf_op jit(solution)/shard_map/ppermute | solution.py:225
  147.5 0.8 copy-start.3
  148.3 18.1 %copy-start.6 = (bf16[2048]{0:T(1024)(128)(2,1)S(1)}, bf16[2048]{0:T(1024)(128)(2,1)}, u32[]{:S(2)}) copy-start(bf16[2048]{0:T(1024)(128)(2,1)} %param.17) | copy-start | bytes 12292
  163.9 7.7 %copy-start.1 = (f32[256,2048]{1,0:T(8,128)S(1)}, f32[256,2048]{1,0:T(8,128)}, u32[]{:S(2)}) copy-start(f32[256,2048]{1,0:T(8,128)} %get-tuple-element.20) | copy-start | bytes 6291460
  163.9 4.2 %collective-permute-start.3 = (bf16[256,1024]{1,0:T(8,128)(2,1)}, bf16[256,1024]{1,0:T(8,128)(2,1)S(1)}, u32[]{:S(2)}, u32[]{:S(2)}) collective-permute-start(bf16[256,1024]{1,0:T(8,128)(2,1)} %get-tuple-element.21), channel_id=1, source_target_pairs={{0,1},{1,0},{2,3},{3,2},{4,5},{5,4},{6,7},{7,6},{8,9},{9,8},{10,11... | collective-permute-start | bytes 1572872 | tf_op jit(solution)/shard_map/ppermute | solution.py:232

commit v12 on v10

--- a/solution.py
+++ b/solution.py
@@ -148,6 +148,30 @@
     )(query_rot, incoming, incoming, key_ok, local_acc, local_stats, back_out, back_stats)
 
 
+def projection_kernel(*refs):
+    count = (len(refs) - 2) // 2
+    total = refs[2 * count][...].astype(jnp.float32)
+    for j in range(count):
+        total = total + jnp.dot(refs[j][...], refs[count + j][...], preferred_element_type=jnp.float32)
+    refs[-1][...] = total.astype(refs[-1].dtype)
+
+
+def project(parts, weights, bias):
+    span, rows = parts[0].shape
+    out_cols = weights[0].shape[1]
+    block = 512 if out_cols % 512 == 0 else out_cols
+    a_spec = pl.BlockSpec((span, rows), lambda c: (0, 0))
+    w_spec = pl.BlockSpec((rows, block), lambda c: (0, c))
+    b_spec = pl.BlockSpec((1, block), lambda c: (0, c))
+    return pl.pallas_call(
+        projection_kernel,
+        grid=(out_cols // block,),
+        in_specs=[a_spec] * len(parts) + [w_spec] * len(weights) + [b_spec],
+        out_specs=pl.BlockSpec((span, block), lambda c: (0, c)),
+        out_shape=jax.ShapeDtypeStruct((span, out_cols), jnp.bfloat16),
+    )(*parts, *weights, bias.reshape(1, out_cols))
+
+
 def usable_keys(page_table, request, length, source_base, source_count, page_count, page_size):
     row = lax.dynamic_index_in_dim(page_table, request, 0, keepdims=False)
     row_owner = jnp.where(row >= 0, row // page_count, -1)
@@ -214,12 +238,11 @@
         ok_own, query_rot, near_incoming, local_acc, local_stats, back_out, back_stats
     )
 
-    summed = jnp.dot(attended, w_mine, preferred_element_type=jnp.float32)
+    parts = [attended]
     for shift in range(1, tp_count):
         perm = [(i, (i + shift) % tp_count) for i in range(tp_count)]
-        other = lax.ppermute(attended, "tp", perm)
-        summed = summed + jnp.dot(other, w_recv[shift - 1], preferred_element_type=jnp.float32)
-    return (summed + out_bias.astype(jnp.float32)).astype(jnp.bfloat16)
+        parts.append(lax.ppermute(attended, "tp", perm))
+    return project(parts, [w_mine] + w_recv, out_bias)
 
 
 def solution(mesh):

time: 173 us -> 173 us (level)
  matrix products: 7.93 us -> 0 us
  Pallas kernels: 26.7 us -> 33.5 us
  local copies, waits for them, and re-layouts: 24.5 us -> 29.6 us
  waiting for transfers between devices: 86.3 us -> 81.7 us
    dot_general x2 -> x0, matrix products: 7.93 us -> none  [the longest x1 4.47 us: on_device(): summed = jnp.dot(attended, w_mine, preferred_element_type=jnp.float32)]
    pallas_call x0 -> x1, Pallas kernels: none -> 6.86 us  [project(): pl.pallas_call(projection_kernel, grid=(out_cols // block,), in_specs=[a_...]
    ppermute x1, waiting for transfers between devices: 33 us -> 29.2 us  [on_device(): back_stats = lax.ppermute(far_stats, 'half', swap)]
    dynamic_slice x1, local copies, waits for them, and re-layouts: 4.73 us -> 8.35 us  [on_device(): piece = lax.dynamic_slice_in_dim(w_out, target * out_cols, out_cols, axis=1)]
  transfers between devices with their start and end apart: 7 -> 7, of which waited for: 3 -> 3; matrix products, arithmetic and copies ran while one was open for 14% -> 16% of each run, Pallas kernels for 16% -> 16%
where the time goes in v12:
time: 173 us; the launch traced here: 171 us
  waiting for transfers between devices  81.7 us (47%)
  Pallas kernels  33.5 us (19%)
  local copies, waits for them, and re-layouts  29.6 us (17%)
  starting transfers between devices  19.1 us (11%)
  other arithmetic  7.35 us (4%)
    ppermute x1, waiting for transfers between devices, on_device(): partner_query = lax.ppermute(query_rot, 'half', swap)  51.4 us
    ppermute x1, waiting for transfers between devices, on_device(): back_stats = lax.ppermute(far_stats, 'half', swap)  29.2 us
    pallas_call x1, Pallas kernels, near_attend(): pl.pallas_call(near_kernel, grid=(head_count,), in_specs=[col_spec] + pag...  11.3 us
    pallas_call x1, Pallas kernels, far_attend(): pl.pallas_call(far_kernel, grid=(head_count,), in_specs=[col_spec] + page...  8.51 us
    dynamic_slice x1, local copies, waits for them, and re-layouts, on_device(): piece = lax.dynamic_slice_in_dim(w_out, target * out_cols, out_cols, axis=1)  8.35 us
    pallas_call x1, Pallas kernels, project(): pl.pallas_call(projection_kernel, grid=(out_cols // block,), in_specs=[a_...  6.86 us
    pallas_call x1, Pallas kernels, local_attend(): pl.pallas_call(local_kernel, grid=(head_count,), in_specs=[col_spec, col_...  6.82 us
    gather x1, local copies, waits for them, and re-layouts, on_device(): jnp.take(kv_pages, jnp.take(local_page, (1 - half) * sub_count + dest), a...  6.14 us
  transfers between devices with their start and end apart: 7, of which 3 were waited for; matrix products, arithmetic and copies ran while one was open for 16% of the time, Pallas kernels for 16%

profile of v12, /device:TPU:11, one launch (start us, length us, event | category | flops | bytes accessed | tf_op | source)
XLA Modules:
  0.0 171.4 jit_solution(8170096159332315403)
XLA Ops:
  0.0 0.8 select_reduce_fusion
  0.8 0.6 gather_fusion.3
  1.5 6.1 %gather_fusion.1 = bf16[8,2,128,1024]{3,2,1,0:T(8,128)(2,1)} fusion(bf16[16,2,128,1024]{3,2,1,0:T(8,128)(2,1)} %param.13, s32[1024]{0:T(1024)S(1)} %pad_clamp_fusion), kind=kCustom, calls=%fused_computation.3 | custom fusion | bytes 8388640 | tf_op jit(solution)/shard_map/jit(_take)/gather | solution.py:222
  7.7 4.7 %all-to-all-start.1 = ((bf16[8,2,128,1024]{3,2,1,0:T(8,128)(2,1)}), bf16[8,2,128,1024]{3,2,1,0:T(8,128)(2,1)}, u32[]{:S(2)}, u32[]{:S(2)}) async-start(bf16[8,2,128,1024]{3,2,1,0:T(8,128)(2,1)} %gather_fusion.1), calls=%async_computation.1 | async-start | bytes 8388608 | tf_op jit(solution)/shard_map/all_to_all | solution.py:223
  12.4 0.7 fusion.10
  13.1 0.6 add_convert_fusion.2
  14.9 0.8 subtract_convert_fusion
  15.7 1.0 pad_maximum_fusion
  16.8 2.4 %collective-permute-start = (bf16[256,1024]{1,0:T(8,128)(2,1)S(1)}, bf16[256,1024]{1,0:T(8,128)(2,1)S(1)}, u32[]{:S(2)}, u32[]{:S(2)}) collective-permute-start(bf16[256,1024]{1,0:T(8,128)(2,1)S(1)} %bitcast.22), channel_id=1, source_target_pairs={{0,16},{16,0},{1,17},{17,1},{2,18},{18,2},{3,19},{19,3},{4,20},{20... | collective-permute-start | bytes 1572872 | tf_op jit(solution)/shard_map/ppermute | solution.py:220
  19.2 0.6 gather_fusion.2
  19.9 6.1 %gather_fusion = bf16[8,2,128,1024]{3,2,1,0:T(8,128)(2,1)} fusion(bf16[16,2,128,1024]{3,2,1,0:T(8,128)(2,1)} %param.13, s32[1024]{0:T(1024)S(1)} %pad_clamp_fusion.2), kind=kCustom, calls=%fused_computation.2 | custom fusion | bytes 8388640 | tf_op jit(solution)/shard_map/jit(_take)/gather | solution.py:224
  26.0 51.4 %collective-permute-done.q_ref = bf16[256,1024]{1,0:T(8,128)(2,1)S(1)} collective-permute-done((bf16[256,1024]{1,0:T(8,128)(2,1)S(1)}, bf16[256,1024]{1,0:T(8,128)(2,1)S(1)}, u32[]{:S(2)}, u32[]{:S(2)}) %collective-permute-start) | collective-permute-done | bytes 524320 | tf_op jit(solution)/shard_map/ppermute | solution.py:220
  77.4 5.1 %all-to-all-start = ((bf16[8,2,128,1024]{3,2,1,0:T(8,128)(2,1)}), bf16[8,2,128,1024]{3,2,1,0:T(8,128)(2,1)}, u32[]{:S(2)}, u32[]{:S(2)}) async-start(bf16[8,2,128,1024]{3,2,1,0:T(8,128)(2,1)} %gather_fusion), calls=%async_computation | async-start | bytes 8388608 | tf_op jit(solution)/shard_map/all_to_all | solution.py:226
  82.5 8.3 %constant_dynamic-slice_fusion.3 = (bf16[1024,2048]{1,0:T(8,128)(2,1)}, bf16[1024,2048]{1,0:T(8,128)(2,1)}) fusion(bf16[1024,4096]{1,0:T(8,128)(2,1)} %param.16, s32[]{:T(128)S(6)} %select_n.98, s32[]{:T(128)S(6)} %select_n.96), kind=kLoop, calls=%fused_computation.56 | loop fusion | bytes 16777224 | tf_op jit(solution)/shard_map/dynamic_slice | solution.py:207
  90.8 2.1 %collective-permute-start.4 = (bf16[1024,2048]{1,0:T(8,128)(2,1)}, bf16[1024,2048]{1,0:T(8,128)(2,1)}, u32[]{:S(2)}, u32[]{:S(2)}) collective-permute-start(bf16[1024,2048]{1,0:T(8,128)(2,1)} %get-tuple-element.22), channel_id=1, source_target_pairs={{0,1},{1,0},{2,3},{3,2},{4,5},{5,4},{6,7},{7,6},{8,9},{9,8},{10,11... | collective-permute-start | bytes 12582920 | tf_op jit(solution)/shard_map/ppermute | solution.py:209
  92.9 0.7 fusion.8
  94.0 0.7 clamp_select_fusion
  94.7 0.7 fusion.7
  95.3 8.5 %shard_map.83 = (bf16[256,1024]{1,0:T(8,128)(2,1)}, f32[8,256,2]{2,1,0:T(8,128)}) custom-call(bf16[256,1024]{1,0:T(8,128)(2,1)} %copy-done.1, bf16[8,2,128,1024]{3,2,1,0:T(8,128)(2,1)} %all-to-all-done.1.kp_ref.vp_ref, bf16[8,2,128,1024]{3,2,1,0:T(8,128)(2,1)} %all-to-all-done.1.kp_ref.vp_ref, s32[1,1024]{1,0:T(1,128)} %bitcast.33), custom_call_target="tpu_custom_call" | custom-call | tf_op jit(solution)/shard_map/pallas_call | solution.py:126
  105.0 1.5 copy.15
  106.6 1.9 %collective-permute-start.2 = (f32[8,256,2]{1,0,2:T(8,128)S(1)}, f32[8,256,2]{1,0,2:T(8,128)S(1)}, u32[]{:S(2)}, u32[]{:S(2)}) collective-permute-start(f32[8,256,2]{1,0,2:T(8,128)S(1)} %copy.15), channel_id=1, source_target_pairs={{0,16},{16,0},{1,17},{17,1},{2,18},{18,2},{3,19},{19,3},{4,20},{20... | collective-permute-start | bytes 49160 | tf_op jit(solution)/shard_map/ppermute | solution.py:236
  108.4 0.7 fusion.6
  109.1 0.9 copy.23
  110.0 6.8 %shard_map.82 = (f32[256,1024]{1,0:T(8,128)}, f32[8,256,2]{2,1,0:T(8,128)}) custom-call(bf16[256,1024]{1,0:T(8,128)(2,1)} %bitcast.23, bf16[256,1024]{1,0:T(8,128)(2,1)} %bitcast.27, bf16[256,1024]{1,0:T(8,128)(2,1)} %vl_ref.1), custom_call_target="tpu_custom_call" | custom-call | tf_op jit(solution)/shard_map/pallas_call | solution.py:110
  116.8 29.2 %collective-permute-done.2 = f32[8,256,2]{1,0,2:T(8,128)S(1)} collective-permute-done((f32[8,256,2]{1,0,2:T(8,128)S(1)}, f32[8,256,2]{1,0,2:T(8,128)S(1)}, u32[]{:S(2)}, u32[]{:S(2)}) %collective-permute-start.2) | collective-permute-done | bytes 16416 | tf_op jit(solution)/shard_map/ppermute | solution.py:236
  146.0 1.4 copy.16.bst_ref
  147.4 0.8 copy-done.2
  148.2 11.3 %shard_map.84.refs_0_ = bf16[256,1024]{1,0:T(8,128)(2,1)} custom-call(bf16[256,1024]{1,0:T(8,128)(2,1)} %bitcast.24, bf16[8,2,128,1024]{3,2,1,0:T(8,128)(2,1)} %all-to-all-done.kp_ref.vp_ref, bf16[8,2,128,1024]{3,2,1,0:T(8,128)(2,1)} %all-to-all-done.kp_ref.vp_ref, s32[1,1024]{1,0:T(1,128)} %bitcast.32, f32[256,1024]{1,0:T(8,128)} %get-tuple-element.13.la_ref, ...), custom_call_target="tpu_custom_call" | custom-call | tf_op jit(solution)/shard_map/pallas_call | solution.py:142
  159.5 2.4 %collective-permute-start.3 = (bf16[256,1024]{1,0:T(8,128)(2,1)}, bf16[256,1024]{1,0:T(8,128)(2,1)S(1)}, u32[]{:S(2)}, u32[]{:S(2)}) collective-permute-start(bf16[256,1024]{1,0:T(8,128)(2,1)} %shard_map.84.refs_0_), channel_id=1, source_target_pairs={{0,1},{1,0},{2,3},{3,2},{4,5},{5,4},{6,7},{7,6},{8,9},{9,8},{10,11... | collective-permute-start | bytes 1572872 | tf_op jit(solution)/shard_map/ppermute | solution.py:244
  162.6 1.1 collective-permute-done.3.refs_1_
  163.7 0.8 copy-done.3
  164.5 6.9 %shard_map.85 = bf16[256,2048]{1,0:T(8,128)(2,1)} custom-call(bf16[256,1024]{1,0:T(8,128)(2,1)} %shard_map.84.refs_0_, bf16[256,1024]{1,0:T(8,128)(2,1)} %copy-done.3, bf16[1024,2048]{1,0:T(8,128)(2,1)} %get-tuple-element.23.refs_2_, bf16[1024,2048]{1,0:T(8,128)(2,1)} %collective-permute-done.4.refs_3_, bf16[1,2048]{1,0:T(2,128)(2,1)} %reshape.161.refs_4_), custom_call_target="tpu_custom_call" | custom-call | tf_op jit(solution)/shard_map/pallas_call | solution.py:166
  (42 shorter events, 3.5 us)
Async XLA Ops:
  7.7 4.7 %copy-start.7 = (s32[16]{0:T(128)S(1)}, s32[16]{0:T(128)}, u32[]{:S(2)}) copy-start(s32[16]{0:T(128)} %param.15) | copy-start | bytes 196
  7.7 6.4 %copy-start.4 = (bf16[256,1024]{1,0:T(8,128)(2,1)S(1)}, bf16[256,1024]{1,0:T(8,128)(2,1)}, u32[]{:S(2)}) copy-start(bf16[256,1024]{1,0:T(8,128)(2,1)} %param.10) | copy-start | bytes 1572868
  7.7 6.5 %copy-start.5 = (bf16[256,1024]{1,0:T(8,128)(2,1)S(1)}, bf16[256,1024]{1,0:T(8,128)(2,1)}, u32[]{:S(2)}) copy-start(bf16[256,1024]{1,0:T(8,128)(2,1)} %param.11) | copy-start | bytes 1572868
  7.7 69.8 %all-to-all-start.1 = ((bf16[8,2,128,1024]{3,2,1,0:T(8,128)(2,1)}), bf16[8,2,128,1024]{3,2,1,0:T(8,128)(2,1)}, u32[]{:S(2)}, u32[]{:S(2)}) async-start(bf16[8,2,128,1024]{3,2,1,0:T(8,128)(2,1)} %gather_fusion.1), calls=%async_computation.1 | async-start | bytes 8388608 | tf_op jit(solution)/shard_map/all_to_all | solution.py:223
  16.8 9.2 %copy-start = (bf16[32,8,8,128]{3,1,2,0:T(8,128)(2,1)}, bf16[32,8,8,128]{3,1,2,0:T(8,128)(2,1)S(1)}, u32[]{:S(2)}) copy-start(bf16[32,8,8,128]{3,1,2,0:T(8,128)(2,1)S(1)} %copy.24) | copy-start | bytes 1572868
  16.8 60.6 %collective-permute-start = (bf16[256,1024]{1,0:T(8,128)(2,1)S(1)}, bf16[256,1024]{1,0:T(8,128)(2,1)S(1)}, u32[]{:S(2)}, u32[]{:S(2)}) collective-permute-start(bf16[256,1024]{1,0:T(8,128)(2,1)S(1)} %bitcast.22), channel_id=1, source_target_pairs={{0,16},{16,0},{1,17},{17,1},{2,18},{18,2},{3,19},{19,3},{4,20},{20... | collective-permute-start | bytes 1572872 | tf_op jit(solution)/shard_map/ppermute | solution.py:220
  77.4 5.1 %copy-start.1 = (bf16[256,1024]{1,0:T(8,128)(2,1)}, bf16[256,1024]{1,0:T(8,128)(2,1)S(1)}, u32[]{:S(2)}) copy-start(bf16[256,1024]{1,0:T(8,128)(2,1)S(1)} %collective-permute-done.q_ref) | copy-start | bytes 1572868
  77.4 70.0 %all-to-all-start = ((bf16[8,2,128,1024]{3,2,1,0:T(8,128)(2,1)}), bf16[8,2,128,1024]{3,2,1,0:T(8,128)(2,1)}, u32[]{:S(2)}, u32[]{:S(2)}) async-start(bf16[8,2,128,1024]{3,2,1,0:T(8,128)(2,1)} %gather_fusion), calls=%async_computation | async-start | bytes 8388608 | tf_op jit(solution)/shard_map/all_to_all | solution.py:226
  90.8 71.7 %collective-permute-start.4 = (bf16[1024,2048]{1,0:T(8,128)(2,1)}, bf16[1024,2048]{1,0:T(8,128)(2,1)}, u32[]{:S(2)}, u32[]{:S(2)}) collective-permute-start(bf16[1024,2048]{1,0:T(8,128)(2,1)} %get-tuple-element.22), channel_id=1, source_target_pairs={{0,1},{1,0},{2,3},{3,2},{4,5},{5,4},{6,7},{7,6},{8,9},{9,8},{10,11... | collective-permute-start | bytes 12582920 | tf_op jit(solution)/shard_map/ppermute | solution.py:209
  103.8 43.6 %collective-permute-start.1 = (bf16[256,1024]{1,0:T(8,128)(2,1)}, bf16[256,1024]{1,0:T(8,128)(2,1)S(1)}, u32[]{:S(2)}, u32[]{:S(2)}) collective-permute-start(bf16[256,1024]{1,0:T(8,128)(2,1)} %get-tuple-element.16), channel_id=1, source_target_pairs={{0,16},{16,0},{1,17},{17,1},{2,18},{18,2},{3,19},{19,3},{4,20},{20... | collective-permute-start | bytes 1572872 | tf_op jit(solution)/shard_map/ppermute | solution.py:235
  106.6 39.4 %collective-permute-start.2 = (f32[8,256,2]{1,0,2:T(8,128)S(1)}, f32[8,256,2]{1,0,2:T(8,128)S(1)}, u32[]{:S(2)}, u32[]{:S(2)}) collective-permute-start(f32[8,256,2]{1,0,2:T(8,128)S(1)} %copy.15), channel_id=1, source_target_pairs={{0,16},{16,0},{1,17},{17,1},{2,18},{18,2},{3,19},{19,3},{4,20},{20... | collective-permute-start | bytes 49160 | tf_op jit(solution)/shard_map/ppermute | solution.py:236
  147.4 0.8 copy-start.2
  148.2 13.8 %copy-start.6 = (bf16[2048]{0:T(1024)(128)(2,1)S(1)}, bf16[2048]{0:T(1024)(128)(2,1)}, u32[]{:S(2)}) copy-start(bf16[2048]{0:T(1024)(128)(2,1)} %param.17) | copy-start | bytes 12292
  159.5 4.2 %collective-permute-start.3 = (bf16[256,1024]{1,0:T(8,128)(2,1)}, bf16[256,1024]{1,0:T(8,128)(2,1)S(1)}, u32[]{:S(2)}, u32[]{:S(2)}) collective-permute-start(bf16[256,1024]{1,0:T(8,128)(2,1)} %shard_map.84.refs_0_), channel_id=1, source_target_pairs={{0,1},{1,0},{2,3},{3,2},{4,5},{5,4},{6,7},{7,6},{8,9},{9,8},{10,11... | collective-permute-start | bytes 1572872 | tf_op jit(solution)/shard_map/ppermute | solution.py:244
  163.7 0.8 copy-start.3

commit v13 on v12

--- a/solution.py
+++ b/solution.py
@@ -39,13 +39,39 @@
 SCORE_DIMS = (((1,), (1,)), ((), ()))
 
 
-def page_partial(q, kp_ref, vp_ref, ok_ref):
+def head_cols(ref, g):
+    return ref[..., g * HEAD_DIM:(g + 1) * HEAD_DIM]
+
+
+def local_kernel(q_ref, kl_ref, vl_ref, acc_ref, st_ref):
     score_scale = 1.0 / math.sqrt(HEAD_DIM)
+    for g in range(st_ref.shape[0]):
+        q = head_cols(q_ref, g)
+        span = q.shape[0]
+        s = lax.dot_general(q, head_cols(kl_ref, g), SCORE_DIMS, preferred_element_type=jnp.float32) * score_scale
+        row = lax.broadcasted_iota(jnp.int32, (span, span), 0)
+        col = lax.broadcasted_iota(jnp.int32, (span, span), 1)
+        s = jnp.where(row >= col, s, NEG_FILL)
+        m = jnp.max(s, axis=1, keepdims=True)
+        p = jnp.exp(s - m)
+        acc_ref[:, g * HEAD_DIM:(g + 1) * HEAD_DIM] = jnp.dot(
+            p.astype(jnp.bfloat16), head_cols(vl_ref, g), preferred_element_type=jnp.float32
+        )
+        st_ref[g, :, 0:1] = m
+        st_ref[g, :, 1:2] = jnp.sum(p, axis=1, keepdims=True)
+
+
+def head_pages(kp_ref, vp_ref, g):
     block_count, page_size, _ = kp_ref.shape
-    keys_p = kp_ref[...].reshape(block_count * page_size, HEAD_DIM)
-    values_p = vp_ref[...].reshape(block_count * page_size, HEAD_DIM)
+    keys = head_cols(kp_ref, g).reshape(block_count * page_size, HEAD_DIM)
+    values = head_cols(vp_ref, g).reshape(block_count * page_size, HEAD_DIM)
+    return keys, values
+
+
+def page_partial(q, keys_p, values_p, ok):
+    score_scale = 1.0 / math.sqrt(HEAD_DIM)
     s = lax.dot_general(q, keys_p, SCORE_DIMS, preferred_element_type=jnp.float32) * score_scale
-    s = jnp.where(ok_ref[...] > 0, s, NEG_FILL)
+    s = jnp.where(ok > 0, s, NEG_FILL)
     m = jnp.max(s, axis=1, keepdims=True)
     p = jnp.exp(s - m)
     l = jnp.sum(p, axis=1, keepdims=True)
@@ -53,51 +79,51 @@
     return m, l, acc
 
 
-def local_kernel(q_ref, kl_ref, vl_ref, acc_ref, st_ref):
-    score_scale = 1.0 / math.sqrt(HEAD_DIM)
-    q = q_ref[...]
-    span = q.shape[0]
-    s = lax.dot_general(q, kl_ref[...], SCORE_DIMS, preferred_element_type=jnp.float32) * score_scale
-    row = lax.broadcasted_iota(jnp.int32, (span, span), 0)
-    col = lax.broadcasted_iota(jnp.int32, (span, span), 1)
-    s = jnp.where(row >= col, s, NEG_FILL)
-    m = jnp.max(s, axis=1, keepdims=True)
-    p = jnp.exp(s - m)
-    acc_ref[...] = jnp.dot(p.astype(jnp.bfloat16), vl_ref[...], preferred_element_type=jnp.float32)
-    st_ref[:, 0:1] = m
-    st_ref[:, 1:2] = jnp.sum(p, axis=1, keepdims=True)
-
-
 def far_kernel(q_ref, kp_ref, vp_ref, ok_ref, o_ref, st_ref):
-    m, l, acc = page_partial(q_ref[...], kp_ref, vp_ref, ok_ref)
-    o_ref[...] = (acc / l).astype(o_ref.dtype)
-    st_ref[:, 0:1] = m
-    st_ref[:, 1:2] = l
+    ok = ok_ref[...]
+    for g in range(st_ref.shape[0]):
+        keys, values = head_pages(kp_ref, vp_ref, g)
+        m, l, acc = page_partial(head_cols(q_ref, g), keys, values, ok)
+        o_ref[:, g * HEAD_DIM:(g + 1) * HEAD_DIM] = (acc / l).astype(o_ref.dtype)
+        st_ref[g, :, 0:1] = m
+        st_ref[g, :, 1:2] = l
 
 
 def near_kernel(q_ref, kp_ref, vp_ref, ok_ref, la_ref, lst_ref, bo_ref, bst_ref, o_ref):
-    m, l, acc = page_partial(q_ref[...], kp_ref, vp_ref, ok_ref)
-    local = lst_ref[...]
-    local_max = local[:, 0:1]
-    local_sum = local[:, 1:2]
-    back = bst_ref[...]
-    back_max = back[:, 0:1]
-    back_sum = back[:, 1:2]
-    peak = jnp.maximum(jnp.maximum(m, local_max), back_max)
-    page_w = jnp.exp(m - peak)
-    local_w = jnp.exp(local_max - peak)
-    back_w = jnp.exp(back_max - peak) * back_sum
-    merged = acc * page_w + la_ref[...] * local_w + bo_ref[...].astype(jnp.float32) * back_w
-    total = l * page_w + local_sum * local_w + back_w
-    o_ref[...] = (merged / total).astype(o_ref.dtype)
-
-
-def head_specs(span, block_count, page_size):
-    col_spec = pl.BlockSpec((span, HEAD_DIM), lambda h: (0, h))
-    stat_spec = pl.BlockSpec((None, span, 2), lambda h: (h, 0, 0))
+    ok = ok_ref[...]
+    for g in range(lst_ref.shape[0]):
+        keys, values = head_pages(kp_ref, vp_ref, g)
+        m, l, acc = page_partial(head_cols(q_ref, g), keys, values, ok)
+        local = lst_ref[g]
+        local_max = local[:, 0:1]
+        local_sum = local[:, 1:2]
+        back = bst_ref[g]
+        back_max = back[:, 0:1]
+        back_sum = back[:, 1:2]
+        peak = jnp.maximum(jnp.maximum(m, local_max), back_max)
+        page_w = jnp.exp(m - peak)
+        local_w = jnp.exp(local_max - peak)
+        back_w = jnp.exp(back_max - peak) * back_sum
+        merged = (
+            acc * page_w
+            + head_cols(la_ref, g) * local_w
+            + head_cols(bo_ref, g).astype(jnp.float32) * back_w
+        )
+        total = l * page_w + local_sum * local_w + back_w
+        o_ref[:, g * HEAD_DIM:(g + 1) * HEAD_DIM] = (merged / total).astype(o_ref.dtype)
+
+
+def heads_per_step(head_count):
+    return 2 if head_count % 2 == 0 else 1
+
+
+def head_specs(span, block_count, page_size, group):
+    cols = group * HEAD_DIM
+    col_spec = pl.BlockSpec((span, cols), lambda h: (0, h))
+    stat_spec = pl.BlockSpec((group, span, 2), lambda h: (h, 0, 0))
     page_specs = [
-        pl.BlockSpec((block_count, None, page_size, HEAD_DIM), lambda h: (0, 0, 0, h)),
-        pl.BlockSpec((block_count, None, page_size, HEAD_DIM), lambda h: (0, 1, 0, h)),
+        pl.BlockSpec((block_count, None, page_size, cols), lambda h: (0, 0, 0, h)),
+        pl.BlockSpec((block_count, None, page_size, cols), lambda h: (0, 1, 0, h)),
         pl.BlockSpec((1, block_count * page_size), lambda h: (0, 0)),
     ]
     return col_spec, stat_spec, page_specs
@@ -106,10 +132,11 @@
 def local_attend(query_rot, key_rot, values):
     span, width = query_rot.shape
     head_count = width // HEAD_DIM
-    col_spec, stat_spec, _ = head_specs(span, 1, 1)
+    group = heads_per_step(head_count)
+    col_spec, stat_spec, _ = head_specs(span, 1, 1, group)
     return pl.pallas_call(
         local_kernel,
-        grid=(head_count,),
+        grid=(head_count // group,),
         in_specs=[col_spec, col_spec, col_spec],
         out_specs=[col_spec, stat_spec],
         out_shape=[
@@ -122,10 +149,11 @@
 def far_attend(key_ok, query_rot, incoming):
     span, width = query_rot.shape
     head_count = width // HEAD_DIM
-    col_spec, stat_spec, page_specs = head_specs(span, incoming.shape[0], incoming.shape[2])
+    group = heads_per_step(head_count)
+    col_spec, stat_spec, page_specs = head_specs(span, incoming.shape[0], incoming.shape[2], group)
     return pl.pallas_call(
         far_kernel,
-        grid=(head_count,),
+        grid=(head_count // group,),
         in_specs=[col_spec] + page_specs,
         out_specs=[col_spec, stat_spec],
         out_shape=[
@@ -138,10 +166,11 @@
 def near_attend(key_ok, query_rot, incoming, local_acc, local_stats, back_out, back_stats):
     span, width = query_rot.shape
     head_count = width // HEAD_DIM
-    col_spec, stat_spec, page_specs = head_specs(span, incoming.shape[0], incoming.shape[2])
+    group = heads_per_step(head_count)
+    col_spec, stat_spec, page_specs = head_specs(span, incoming.shape[0], incoming.shape[2], group)
     return pl.pallas_call(
         near_kernel,
-        grid=(head_count,),
+        grid=(head_count // group,),
         in_specs=[col_spec] + page_specs + [col_spec, stat_spec, col_spec, stat_spec],
         out_specs=col_spec,
         out_shape=jax.ShapeDtypeStruct((span, width), jnp.bfloat16),

time: 173 us -> 171 us (0.988)
  Pallas kernels: 33.5 us -> 29.2 us
  waiting for transfers between devices: 81.7 us -> 85.1 us
    pallas_call x3, Pallas kernels: 26.7 us -> 22.4 us  [the longest x1 10.5 us: near_attend(): pl.pallas_call(near_kernel, grid=(head_count // group,), in_specs=[col_sp...]
    ppermute x1, waiting for transfers between devices: 29.2 us -> 32.6 us  [on_device(): back_stats = lax.ppermute(far_stats, 'half', swap)]
  transfers between devices with their start and end apart: 7 -> 7, of which waited for: 3 -> 3; matrix products, arithmetic and copies ran while one was open for 16% -> 16% of each run, Pallas kernels for 16% -> 13%
where the time goes in v13:
time: 171 us
  waiting for transfers between devices  85.1 us (50%)
  local copies, waits for them, and re-layouts  29.6 us (17%)
  Pallas kernels  29.2 us (17%)
  starting transfers between devices  19.1 us (11%)
  other arithmetic  7.35 us (4%)
    ppermute x1, waiting for transfers between devices, on_device(): partner_query = lax.ppermute(query_rot, 'half', swap)  51.4 us
    ppermute x1, waiting for transfers between devices, on_device(): back_stats = lax.ppermute(far_stats, 'half', swap)  32.6 us
    pallas_call x1, Pallas kernels, near_attend(): pl.pallas_call(near_kernel, grid=(head_count // group,), in_specs=[col_sp...  10.5 us
    dynamic_slice x1, local copies, waits for them, and re-layouts, on_device(): piece = lax.dynamic_slice_in_dim(w_out, target * out_cols, out_cols, axis=1)  8.35 us
    pallas_call x1, Pallas kernels, project(): pl.pallas_call(projection_kernel, grid=(out_cols // block,), in_specs=[a_...  6.86 us
    pallas_call x1, Pallas kernels, far_attend(): pl.pallas_call(far_kernel, grid=(head_count // group,), in_specs=[col_spe...  6.81 us
    gather x1, local copies, waits for them, and re-layouts, on_device(): jnp.take(kv_pages, jnp.take(local_page, (1 - half) * sub_count + dest), a...  6.14 us
    gather x1, local copies, waits for them, and re-layouts, on_device(): jnp.take(kv_pages, jnp.take(local_page, half * sub_count + dest), axis=0,...  6.14 us
  transfers between devices with their start and end apart: 7, of which 3 were waited for; matrix products, arithmetic and copies ran while one was open for 16% of the time, Pallas kernels for 13%

profile of v13, /device:TPU:11, one launch (start us, length us, event | category | flops | bytes accessed | tf_op | source)
XLA Modules:
  0.0 170.5 jit_solution(2999575130710733312)
XLA Ops:
  0.0 0.8 select_reduce_fusion
  0.8 0.6 gather_fusion.3
  1.5 6.1 %gather_fusion.1 = bf16[8,2,128,1024]{3,2,1,0:T(8,128)(2,1)} fusion(bf16[16,2,128,1024]{3,2,1,0:T(8,128)(2,1)} %param.13, s32[1024]{0:T(1024)S(1)} %pad_clamp_fusion), kind=kCustom, calls=%fused_computation.3 | custom fusion | bytes 8388640 | tf_op jit(solution)/shard_map/jit(_take)/gather | solution.py:251
  7.7 4.7 %all-to-all-start.1 = ((bf16[8,2,128,1024]{3,2,1,0:T(8,128)(2,1)}), bf16[8,2,128,1024]{3,2,1,0:T(8,128)(2,1)}, u32[]{:S(2)}, u32[]{:S(2)}) async-start(bf16[8,2,128,1024]{3,2,1,0:T(8,128)(2,1)} %gather_fusion.1), calls=%async_computation.1 | async-start | bytes 8388608 | tf_op jit(solution)/shard_map/all_to_all | solution.py:252
  12.4 0.7 fusion.10
  13.1 0.6 add_convert_fusion.2
  14.9 0.8 subtract_convert_fusion
  15.7 1.0 pad_maximum_fusion
  16.8 2.4 %collective-permute-start = (bf16[256,1024]{1,0:T(8,128)(2,1)S(1)}, bf16[256,1024]{1,0:T(8,128)(2,1)S(1)}, u32[]{:S(2)}, u32[]{:S(2)}) collective-permute-start(bf16[256,1024]{1,0:T(8,128)(2,1)S(1)} %bitcast.22), channel_id=1, source_target_pairs={{0,16},{16,0},{1,17},{17,1},{2,18},{18,2},{3,19},{19,3},{4,20},{20... | collective-permute-start | bytes 1572872 | tf_op jit(solution)/shard_map/ppermute | solution.py:249
  19.2 0.6 gather_fusion.2
  19.9 6.1 %gather_fusion = bf16[8,2,128,1024]{3,2,1,0:T(8,128)(2,1)} fusion(bf16[16,2,128,1024]{3,2,1,0:T(8,128)(2,1)} %param.13, s32[1024]{0:T(1024)S(1)} %pad_clamp_fusion.2), kind=kCustom, calls=%fused_computation.2 | custom fusion | bytes 8388640 | tf_op jit(solution)/shard_map/jit(_take)/gather | solution.py:253
  26.0 51.4 %collective-permute-done.q_ref = bf16[256,1024]{1,0:T(8,128)(2,1)S(1)} collective-permute-done((bf16[256,1024]{1,0:T(8,128)(2,1)S(1)}, bf16[256,1024]{1,0:T(8,128)(2,1)S(1)}, u32[]{:S(2)}, u32[]{:S(2)}) %collective-permute-start) | collective-permute-done | bytes 524320 | tf_op jit(solution)/shard_map/ppermute | solution.py:249
  77.4 5.1 %all-to-all-start = ((bf16[8,2,128,1024]{3,2,1,0:T(8,128)(2,1)}), bf16[8,2,128,1024]{3,2,1,0:T(8,128)(2,1)}, u32[]{:S(2)}, u32[]{:S(2)}) async-start(bf16[8,2,128,1024]{3,2,1,0:T(8,128)(2,1)} %gather_fusion), calls=%async_computation | async-start | bytes 8388608 | tf_op jit(solution)/shard_map/all_to_all | solution.py:255
  82.5 8.3 %constant_dynamic-slice_fusion.3 = (bf16[1024,2048]{1,0:T(8,128)(2,1)}, bf16[1024,2048]{1,0:T(8,128)(2,1)}) fusion(bf16[1024,4096]{1,0:T(8,128)(2,1)} %param.16, s32[]{:T(128)S(6)} %select_n.98, s32[]{:T(128)S(6)} %select_n.96), kind=kLoop, calls=%fused_computation.56 | loop fusion | bytes 16777224 | tf_op jit(solution)/shard_map/dynamic_slice | solution.py:236
  90.8 2.1 %collective-permute-start.4 = (bf16[1024,2048]{1,0:T(8,128)(2,1)}, bf16[1024,2048]{1,0:T(8,128)(2,1)}, u32[]{:S(2)}, u32[]{:S(2)}) collective-permute-start(bf16[1024,2048]{1,0:T(8,128)(2,1)} %get-tuple-element.22), channel_id=1, source_target_pairs={{0,1},{1,0},{2,3},{3,2},{4,5},{5,4},{6,7},{7,6},{8,9},{9,8},{10,11... | collective-permute-start | bytes 12582920 | tf_op jit(solution)/shard_map/ppermute | solution.py:238
  92.9 0.7 fusion.8
  94.0 0.7 clamp_select_fusion
  94.7 0.7 fusion.7
  95.3 6.8 %shard_map.83 = (bf16[256,1024]{1,0:T(8,128)(2,1)}, f32[8,256,2]{2,1,0:T(8,128)}) custom-call(bf16[256,1024]{1,0:T(8,128)(2,1)} %copy-done.1, bf16[8,2,128,1024]{3,2,1,0:T(8,128)(2,1)} %all-to-all-done.1.kp_ref.vp_ref, bf16[8,2,128,1024]{3,2,1,0:T(8,128)(2,1)} %all-to-all-done.1.kp_ref.vp_ref, s32[1,1024]{1,0:T(1,128)} %bitcast.33), custom_call_target="tpu_custom_call" | custom-call | tf_op jit(solution)/shard_map/pallas_call | solution.py:154
  103.3 1.5 copy.15
  104.9 1.8 %collective-permute-start.2 = (f32[8,256,2]{1,0,2:T(8,128)S(1)}, f32[8,256,2]{1,0,2:T(8,128)S(1)}, u32[]{:S(2)}, u32[]{:S(2)}) collective-permute-start(f32[8,256,2]{1,0,2:T(8,128)S(1)} %copy.15), channel_id=1, source_target_pairs={{0,16},{16,0},{1,17},{17,1},{2,18},{18,2},{3,19},{19,3},{4,20},{20... | collective-permute-start | bytes 49160 | tf_op jit(solution)/shard_map/ppermute | solution.py:265
  106.7 0.7 fusion.6
  107.4 0.9 copy.23
  108.3 5.1 %shard_map.82 = (f32[256,1024]{1,0:T(8,128)}, f32[8,256,2]{2,1,0:T(8,128)}) custom-call(bf16[256,1024]{1,0:T(8,128)(2,1)} %bitcast.23, bf16[256,1024]{1,0:T(8,128)(2,1)} %bitcast.27, bf16[256,1024]{1,0:T(8,128)(2,1)} %vl_ref.1), custom_call_target="tpu_custom_call" | custom-call | tf_op jit(solution)/shard_map/pallas_call | solution.py:137
  113.4 32.6 %collective-permute-done.2 = f32[8,256,2]{1,0,2:T(8,128)S(1)} collective-permute-done((f32[8,256,2]{1,0,2:T(8,128)S(1)}, f32[8,256,2]{1,0,2:T(8,128)S(1)}, u32[]{:S(2)}, u32[]{:S(2)}) %collective-permute-start.2) | collective-permute-done | bytes 16416 | tf_op jit(solution)/shard_map/ppermute | solution.py:265
  146.0 1.4 copy.16.bst_ref
  147.4 0.8 copy-done.2
  148.2 10.5 %shard_map.84.refs_0_ = bf16[256,1024]{1,0:T(8,128)(2,1)} custom-call(bf16[256,1024]{1,0:T(8,128)(2,1)} %bitcast.24, bf16[8,2,128,1024]{3,2,1,0:T(8,128)(2,1)} %all-to-all-done.kp_ref.vp_ref, bf16[8,2,128,1024]{3,2,1,0:T(8,128)(2,1)} %all-to-all-done.kp_ref.vp_ref, s32[1,1024]{1,0:T(1,128)} %bitcast.32, f32[256,1024]{1,0:T(8,128)} %get-tuple-element.13.la_ref, ...), custom_call_target="tpu_custom_call" | custom-call | tf_op jit(solution)/shard_map/pallas_call | solution.py:171
  158.7 2.4 %collective-permute-start.3 = (bf16[256,1024]{1,0:T(8,128)(2,1)}, bf16[256,1024]{1,0:T(8,128)(2,1)S(1)}, u32[]{:S(2)}, u32[]{:S(2)}) collective-permute-start(bf16[256,1024]{1,0:T(8,128)(2,1)} %shard_map.84.refs_0_), channel_id=1, source_target_pairs={{0,1},{1,0},{2,3},{3,2},{4,5},{5,4},{6,7},{7,6},{8,9},{9,8},{10,11... | collective-permute-start | bytes 1572872 | tf_op jit(solution)/shard_map/ppermute | solution.py:273
  161.7 1.1 collective-permute-done.3.refs_1_
  162.8 0.8 copy-done.3
  163.7 6.9 %shard_map.85 = bf16[256,2048]{1,0:T(8,128)(2,1)} custom-call(bf16[256,1024]{1,0:T(8,128)(2,1)} %shard_map.84.refs_0_, bf16[256,1024]{1,0:T(8,128)(2,1)} %copy-done.3, bf16[1024,2048]{1,0:T(8,128)(2,1)} %get-tuple-element.23.refs_2_, bf16[1024,2048]{1,0:T(8,128)(2,1)} %collective-permute-done.4.refs_3_, bf16[1,2048]{1,0:T(2,128)(2,1)} %reshape.161.refs_4_), custom_call_target="tpu_custom_call" | custom-call | tf_op jit(solution)/shard_map/pallas_call | solution.py:195
  (42 shorter events, 3.5 us)
Async XLA Ops:
  7.7 4.7 %copy-start.7 = (s32[16]{0:T(128)S(1)}, s32[16]{0:T(128)}, u32[]{:S(2)}) copy-start(s32[16]{0:T(128)} %param.15) | copy-start | bytes 196
  7.7 6.4 %copy-start.4 = (bf16[256,1024]{1,0:T(8,128)(2,1)S(1)}, bf16[256,1024]{1,0:T(8,128)(2,1)}, u32[]{:S(2)}) copy-start(bf16[256,1024]{1,0:T(8,128)(2,1)} %param.10) | copy-start | bytes 1572868
  7.7 6.5 %copy-start.5 = (bf16[256,1024]{1,0:T(8,128)(2,1)S(1)}, bf16[256,1024]{1,0:T(8,128)(2,1)}, u32[]{:S(2)}) copy-start(bf16[256,1024]{1,0:T(8,128)(2,1)} %param.11) | copy-start | bytes 1572868
  7.7 69.8 %all-to-all-start.1 = ((bf16[8,2,128,1024]{3,2,1,0:T(8,128)(2,1)}), bf16[8,2,128,1024]{3,2,1,0:T(8,128)(2,1)}, u32[]{:S(2)}, u32[]{:S(2)}) async-start(bf16[8,2,128,1024]{3,2,1,0:T(8,128)(2,1)} %gather_fusion.1), calls=%async_computation.1 | async-start | bytes 8388608 | tf_op jit(solution)/shard_map/all_to_all | solution.py:252
  16.8 9.2 %copy-start = (bf16[32,8,8,128]{3,1,2,0:T(8,128)(2,1)}, bf16[32,8,8,128]{3,1,2,0:T(8,128)(2,1)S(1)}, u32[]{:S(2)}) copy-start(bf16[32,8,8,128]{3,1,2,0:T(8,128)(2,1)S(1)} %copy.24) | copy-start | bytes 1572868
  16.8 60.6 %collective-permute-start = (bf16[256,1024]{1,0:T(8,128)(2,1)S(1)}, bf16[256,1024]{1,0:T(8,128)(2,1)S(1)}, u32[]{:S(2)}, u32[]{:S(2)}) collective-permute-start(bf16[256,1024]{1,0:T(8,128)(2,1)S(1)} %bitcast.22), channel_id=1, source_target_pairs={{0,16},{16,0},{1,17},{17,1},{2,18},{18,2},{3,19},{19,3},{4,20},{20... | collective-permute-start | bytes 1572872 | tf_op jit(solution)/shard_map/ppermute | solution.py:249
  77.4 5.1 %copy-start.1 = (bf16[256,1024]{1,0:T(8,128)(2,1)}, bf16[256,1024]{1,0:T(8,128)(2,1)S(1)}, u32[]{:S(2)}) copy-start(bf16[256,1024]{1,0:T(8,128)(2,1)S(1)} %collective-permute-done.q_ref) | copy-start | bytes 1572868
  77.4 70.0 %all-to-all-start = ((bf16[8,2,128,1024]{3,2,1,0:T(8,128)(2,1)}), bf16[8,2,128,1024]{3,2,1,0:T(8,128)(2,1)}, u32[]{:S(2)}, u32[]{:S(2)}) async-start(bf16[8,2,128,1024]{3,2,1,0:T(8,128)(2,1)} %gather_fusion), calls=%async_computation | async-start | bytes 8388608 | tf_op jit(solution)/shard_map/all_to_all | solution.py:255
  90.8 70.9 %collective-permute-start.4 = (bf16[1024,2048]{1,0:T(8,128)(2,1)}, bf16[1024,2048]{1,0:T(8,128)(2,1)}, u32[]{:S(2)}, u32[]{:S(2)}) collective-permute-start(bf16[1024,2048]{1,0:T(8,128)(2,1)} %get-tuple-element.22), channel_id=1, source_target_pairs={{0,1},{1,0},{2,3},{3,2},{4,5},{5,4},{6,7},{7,6},{8,9},{9,8},{10,11... | collective-permute-start | bytes 12582920 | tf_op jit(solution)/shard_map/ppermute | solution.py:238
  102.1 45.3 %collective-permute-start.1 = (bf16[256,1024]{1,0:T(8,128)(2,1)}, bf16[256,1024]{1,0:T(8,128)(2,1)S(1)}, u32[]{:S(2)}, u32[]{:S(2)}) collective-permute-start(bf16[256,1024]{1,0:T(8,128)(2,1)} %get-tuple-element.16), channel_id=1, source_target_pairs={{0,16},{16,0},{1,17},{17,1},{2,18},{18,2},{3,19},{19,3},{4,20},{20... | collective-permute-start | bytes 1572872 | tf_op jit(solution)/shard_map/ppermute | solution.py:264
  104.9 41.1 %collective-permute-start.2 = (f32[8,256,2]{1,0,2:T(8,128)S(1)}, f32[8,256,2]{1,0,2:T(8,128)S(1)}, u32[]{:S(2)}, u32[]{:S(2)}) collective-permute-start(f32[8,256,2]{1,0,2:T(8,128)S(1)} %copy.15), channel_id=1, source_target_pairs={{0,16},{16,0},{1,17},{17,1},{2,18},{18,2},{3,19},{19,3},{4,20},{20... | collective-permute-start | bytes 49160 | tf_op jit(solution)/shard_map/ppermute | solution.py:265
  147.4 0.8 copy-start.2
  148.2 12.9 %copy-start.6 = (bf16[2048]{0:T(1024)(128)(2,1)S(1)}, bf16[2048]{0:T(1024)(128)(2,1)}, u32[]{:S(2)}) copy-start(bf16[2048]{0:T(1024)(128)(2,1)} %param.17) | copy-start | bytes 12292
  158.7 4.2 %collective-permute-start.3 = (bf16[256,1024]{1,0:T(8,128)(2,1)}, bf16[256,1024]{1,0:T(8,128)(2,1)S(1)}, u32[]{:S(2)}, u32[]{:S(2)}) collective-permute-start(bf16[256,1024]{1,0:T(8,128)(2,1)} %shard_map.84.refs_0_), channel_id=1, source_target_pairs={{0,1},{1,0},{2,3},{3,2},{4,5},{5,4},{6,7},{7,6},{8,9},{9,8},{10,11... | collective-permute-start | bytes 1572872 | tf_op jit(solution)/shard_map/ppermute | solution.py:273
  162.8 0.8 copy-start.3

commit v14 on v13

--- a/solution.py
+++ b/solution.py
@@ -163,17 +163,21 @@
     )(query_rot, incoming, incoming, key_ok)
 
 
-def near_attend(key_ok, query_rot, incoming, local_acc, local_stats, back_out, back_stats):
+def near_attend(key_ok, query_rot, incoming, local_acc, local_stats, back_out, back_stats, first_head):
     span, width = query_rot.shape
-    head_count = width // HEAD_DIM
+    head_count = incoming.shape[3] // HEAD_DIM
     group = heads_per_step(head_count)
-    col_spec, stat_spec, page_specs = head_specs(span, incoming.shape[0], incoming.shape[2], group)
+    base = first_head // group
+    cols = group * HEAD_DIM
+    _, _, page_specs = head_specs(span, incoming.shape[0], incoming.shape[2], group)
+    wide_spec = pl.BlockSpec((span, cols), lambda h: (0, h + base))
+    wide_stats = pl.BlockSpec((group, span, 2), lambda h: (h + base, 0, 0))
     return pl.pallas_call(
         near_kernel,
         grid=(head_count // group,),
-        in_specs=[col_spec] + page_specs + [col_spec, stat_spec, col_spec, stat_spec],
-        out_specs=col_spec,
-        out_shape=jax.ShapeDtypeStruct((span, width), jnp.bfloat16),
+        in_specs=[wide_spec] + page_specs + [wide_spec, wide_stats, wide_spec, wide_stats],
+        out_specs=pl.BlockSpec((span, cols), lambda h: (0, h)),
+        out_shape=jax.ShapeDtypeStruct((span, head_count * HEAD_DIM), jnp.bfloat16),
     )(query_rot, incoming, incoming, key_ok, local_acc, local_stats, back_out, back_stats)
 
 
@@ -251,8 +255,14 @@
     far_pages = jnp.take(kv_pages, jnp.take(local_page, (1 - half) * sub_count + dest), axis=0, mode="clip")
     far_incoming = lax.all_to_all(far_pages, "sub", split_axis=0, concat_axis=0, tiled=True)
     near_pages = jnp.take(kv_pages, jnp.take(local_page, half * sub_count + dest), axis=0, mode="clip")
-    partner_query, near_pages = lax.optimization_barrier((partner_query, near_pages))
-    near_incoming = lax.all_to_all(near_pages, "sub", split_axis=0, concat_axis=0, tiled=True)
+    split_heads = head_count // 2 if head_count % 2 == 0 else head_count
+    split_cols = split_heads * HEAD_DIM
+    near_first = near_pages[..., :split_cols]
+    near_rest = near_pages[..., split_cols:]
+    partner_query, near_first = lax.optimization_barrier((partner_query, near_first))
+    near_incoming = [lax.all_to_all(near_first, "sub", split_axis=0, concat_axis=0, tiled=True)]
+    if split_cols < width:
+        near_incoming.append(lax.all_to_all(near_rest, "sub", split_axis=0, concat_axis=0, tiled=True))
     key_rot = rotate_rows(new_keys, positions)
 
     source_base = half * sub_count
@@ -263,15 +273,18 @@
     far_out, far_stats = far_attend(ok_partner, partner_query, far_incoming)
     back_out = lax.ppermute(far_out, "half", swap)
     back_stats = lax.ppermute(far_stats, "half", swap)
-    attended = near_attend(
-        ok_own, query_rot, near_incoming, local_acc, local_stats, back_out, back_stats
-    )
-
-    parts = [attended]
+    attended = [
+        near_attend(ok_own, query_rot, part, local_acc, local_stats, back_out, back_stats, index * split_heads)
+        for index, part in enumerate(near_incoming)
+    ]
+    parts = list(attended)
     for shift in range(1, tp_count):
         perm = [(i, (i + shift) % tp_count) for i in range(tp_count)]
-        parts.append(lax.ppermute(attended, "tp", perm))
-    return project(parts, [w_mine] + w_recv, out_bias)
+        parts.extend(lax.ppermute(piece, "tp", perm) for piece in attended)
+    weights = []
+    for rows in [w_mine] + w_recv:
+        weights.extend(rows[index * split_cols:(index + 1) * split_cols] for index in range(len(attended)))
+    return project(parts, weights, out_bias)
 
 
 def solution(mesh):

time: 171 us -> 186 us (1.088)
  the two profiles are of different devices: /device:TPU:11 before, /device:TPU:0 now
where the time goes in v14:
time: 186 us; the launch traced here: 185 us
  waiting for transfers between devices  81.2 us (44%)
  local copies, waits for them, and re-layouts  41.6 us (22%)
  Pallas kernels  31.3 us (17%)
  starting transfers between devices  23.1 us (12%)
  other arithmetic  7.25 us (4%)
    ppermute x1, waiting for transfers between devices, on_device(): partner_query = lax.ppermute(query_rot, 'half', swap)  44.4 us
    all_to_all x1, waiting for transfers between devices, on_device(): lax.all_to_all(near_rest, 'sub', split_axis=0, concat_axis=0, tiled=True)  19.1 us
    pallas_call x2, Pallas kernels, near_attend(): pl.pallas_call(near_kernel, grid=(head_count // group,), in_specs=[wide_s...  12.6 us
    slice x2, local copies, waits for them, and re-layouts, on_device(): rows[index * split_cols:(index + 1) * split_cols]  9.68 us
    all_to_all x1, waiting for transfers between devices, on_device(): lax.all_to_all(far_pages, 'sub', split_axis=0, concat_axis=0, tiled=True)  9.28 us
    ppermute x1, waiting for transfers between devices, on_device(): back_stats = lax.ppermute(far_stats, 'half', swap)  8.45 us
    pallas_call x1, Pallas kernels, project(): pl.pallas_call(projection_kernel, grid=(out_cols // block,), in_specs=[a_...  6.84 us
    pallas_call x1, Pallas kernels, far_attend(): pl.pallas_call(far_kernel, grid=(head_count // group,), in_specs=[col_spe...  6.78 us
  transfers between devices with their start and end apart: 9, of which 4 were waited for; matrix products, arithmetic and copies ran while one was open for 18% of the time, Pallas kernels for 13%

profile of v14, /device:TPU:0, one launch (start us, length us, event | category | flops | bytes accessed | tf_op | source)
XLA Modules:
  0.0 184.7 jit_solution(4729298409981003932)
XLA Ops:
  0.0 0.8 select_reduce_fusion
  1.5 6.1 %gather_fusion = bf16[8,2,128,1024]{3,2,1,0:T(8,128)(2,1)} fusion(bf16[16,2,128,1024]{3,2,1,0:T(8,128)(2,1)} %param.13, s32[1024]{0:T(1024)S(1)} %pad_clamp_fusion.2), kind=kCustom, calls=%fused_computation.2 | custom fusion | bytes 8388640 | tf_op jit(solution)/shard_map/jit(_take)/gather | solution.py:257
  7.6 4.7 %fusion.12 = (bf16[8,2,128,512]{3,2,1,0:T(8,128)(2,1)}, bf16[8,2,128,512]{3,2,1,0:T(8,128)(2,1)}) fusion(bf16[8,2,128,1024]{3,2,1,0:T(8,128)(2,1)} %gather_fusion), kind=kLoop, calls=%fused_computation.67 | loop fusion | bytes 8388608 | tf_op jit(solution)/shard_map/slice | solution.py:261
  12.4 6.2 %all-to-all-start.2 = ((bf16[8,2,128,512]{3,2,1,0:T(8,128)(2,1)}), bf16[8,2,128,512]{3,2,1,0:T(8,128)(2,1)S(1)}, u32[]{:S(2)}, u32[]{:S(2)}) async-start(bf16[8,2,128,512]{3,2,1,0:T(8,128)(2,1)} %get-tuple-element.26), calls=%async_computation.2 | async-start | bytes 4194304 | tf_op jit(solution)/shard_map/all_to_all | solution.py:265
  19.2 6.2 %gather_fusion.1 = bf16[8,2,128,1024]{3,2,1,0:T(8,128)(2,1)} fusion(bf16[16,2,128,1024]{3,2,1,0:T(8,128)(2,1)} %param.13, s32[1024]{0:T(1024)S(1)} %pad_clamp_fusion), kind=kCustom, calls=%fused_computation.3 | custom fusion | bytes 8388640 | tf_op jit(solution)/shard_map/jit(_take)/gather | solution.py:255
  25.4 19.1 %all-to-all-done.2.kp_ref.vp_ref = bf16[8,2,128,512]{3,2,1,0:T(8,128)(2,1)S(1)} async-done(((bf16[8,2,128,512]{3,2,1,0:T(8,128)(2,1)}), bf16[8,2,128,512]{3,2,1,0:T(8,128)(2,1)S(1)}, u32[]{:S(2)}, u32[]{:S(2)}) %all-to-all-start.2) | async-done | bytes 2097184 | tf_op jit(solution)/shard_map/all_to_all | solution.py:265
  44.5 5.1 %all-to-all-start.1 = ((bf16[8,2,128,1024]{3,2,1,0:T(8,128)(2,1)}), bf16[8,2,128,1024]{3,2,1,0:T(8,128)(2,1)}, u32[]{:S(2)}, u32[]{:S(2)}) async-start(bf16[8,2,128,1024]{3,2,1,0:T(8,128)(2,1)} %gather_fusion.1), calls=%async_computation.1 | async-start | bytes 8388608 | tf_op jit(solution)/shard_map/all_to_all | solution.py:256
  52.1 0.7 subtract_convert_fusion
  52.8 1.0 pad_maximum_fusion
  53.9 2.7 %collective-permute-start = (bf16[256,1024]{1,0:T(8,128)(2,1)S(1)}, bf16[256,1024]{1,0:T(8,128)(2,1)S(1)}, u32[]{:S(2)}, u32[]{:S(2)}) collective-permute-start(bf16[256,1024]{1,0:T(8,128)(2,1)S(1)} %bitcast.22), channel_id=1, source_target_pairs={{0,16},{16,0},{1,17},{17,1},{2,18},{18,2},{3,19},{19,3},{4,20},{20... | collective-permute-start | bytes 1572872 | tf_op jit(solution)/shard_map/ppermute | solution.py:253
  56.6 4.8 %constant_dynamic-slice_fusion.1 = bf16[1024,2048]{1,0:T(8,128)(2,1)} fusion(bf16[1024,4096]{1,0:T(8,128)(2,1)} %param.16, s32[]{:T(128)S(6)} %select_n.98), kind=kLoop, calls=%fused_computation.54 | loop fusion | bytes 8388612 | tf_op jit(solution)/shard_map/dynamic_slice | solution.py:240
  61.3 44.4 %collective-permute-done.q_ref = bf16[256,1024]{1,0:T(8,128)(2,1)S(1)} collective-permute-done((bf16[256,1024]{1,0:T(8,128)(2,1)S(1)}, bf16[256,1024]{1,0:T(8,128)(2,1)S(1)}, u32[]{:S(2)}, u32[]{:S(2)}) %collective-permute-start) | collective-permute-done | bytes 524320 | tf_op jit(solution)/shard_map/ppermute | solution.py:253
  105.7 9.3 %all-to-all-done.1.kp_ref.vp_ref = bf16[8,2,128,1024]{3,2,1,0:T(8,128)(2,1)} async-done(((bf16[8,2,128,1024]{3,2,1,0:T(8,128)(2,1)}), bf16[8,2,128,1024]{3,2,1,0:T(8,128)(2,1)}, u32[]{:S(2)}, u32[]{:S(2)}) %all-to-all-start.1) | async-done | bytes 4194336 | tf_op jit(solution)/shard_map/all_to_all | solution.py:256
  115.0 5.8 %all-to-all-start = ((bf16[8,2,128,512]{3,2,1,0:T(8,128)(2,1)}), bf16[8,2,128,512]{3,2,1,0:T(8,128)(2,1)S(1)}, u32[]{:S(2)}, u32[]{:S(2)}) async-start(bf16[8,2,128,512]{3,2,1,0:T(8,128)(2,1)} %get-tuple-element.12), calls=%async_computation | async-start | bytes 4194304 | tf_op jit(solution)/shard_map/all_to_all | solution.py:263
  120.8 0.7 fusion.8
  122.5 0.7 clamp_select_fusion
  123.2 0.7 fusion.7
  123.8 6.8 %shard_map.83 = (bf16[256,1024]{1,0:T(8,128)(2,1)}, f32[8,256,2]{2,1,0:T(8,128)}) custom-call(bf16[256,1024]{1,0:T(8,128)(2,1)} %copy-done.4, bf16[8,2,128,1024]{3,2,1,0:T(8,128)(2,1)} %all-to-all-done.1.kp_ref.vp_ref, bf16[8,2,128,1024]{3,2,1,0:T(8,128)(2,1)} %all-to-all-done.1.kp_ref.vp_ref, s32[1,1024]{1,0:T(1,128)} %bitcast.35), custom_call_target="tpu_custom_call" | custom-call | tf_op jit(solution)/shard_map/pallas_call | solution.py:154
  130.6 4.9 %fusion.10 = (bf16[512,2048]{1,0:T(8,128)(2,1)}, bf16[512,2048]{1,0:T(8,128)(2,1)}) fusion(bf16[1024,4096]{1,0:T(8,128)(2,1)} %param.16, s32[]{:T(128)S(6)} %add.92, s32[]{:T(128)S(6)} %select_n.96), kind=kLoop, calls=%fused_computation.65 | loop fusion | bytes 8388616 | tf_op jit(solution)/shard_map/slice | solution.py:286
  135.5 1.5 copy.17
  137.1 2.9 %collective-permute-start.2 = (f32[8,256,2]{1,0,2:T(8,128)S(1)}, f32[8,256,2]{1,0,2:T(8,128)S(1)}, u32[]{:S(2)}, u32[]{:S(2)}) collective-permute-start(f32[8,256,2]{1,0,2:T(8,128)S(1)} %copy.17), channel_id=1, source_target_pairs={{0,16},{16,0},{1,17},{17,1},{2,18},{18,2},{3,19},{19,3},{4,20},{20... | collective-permute-start | bytes 49160 | tf_op jit(solution)/shard_map/ppermute | solution.py:275
  140.7 0.9 copy.26
  142.2 5.1 %shard_map.82 = (f32[256,1024]{1,0:T(8,128)}, f32[8,256,2]{2,1,0:T(8,128)}) custom-call(bf16[256,1024]{1,0:T(8,128)(2,1)} %bitcast.23, bf16[256,1024]{1,0:T(8,128)(2,1)} %bitcast.28, bf16[256,1024]{1,0:T(8,128)(2,1)} %vl_ref.1), custom_call_target="tpu_custom_call" | custom-call | tf_op jit(solution)/shard_map/pallas_call | solution.py:137
  147.3 8.4 %collective-permute-done.2 = f32[8,256,2]{1,0,2:T(8,128)S(1)} collective-permute-done((f32[8,256,2]{1,0,2:T(8,128)S(1)}, f32[8,256,2]{1,0,2:T(8,128)S(1)}, u32[]{:S(2)}, u32[]{:S(2)}) %collective-permute-start.2) | collective-permute-done | bytes 16416 | tf_op jit(solution)/shard_map/ppermute | solution.py:275
  155.7 1.4 copy.18.bst_ref
  157.1 0.8 copy-done.3
  157.9 6.3 %shard_map.85.refs_1_ = bf16[256,512]{1,0:T(8,128)(2,1)} custom-call(bf16[256,1024]{1,0:T(8,128)(2,1)} %bitcast.24, bf16[8,2,128,512]{3,2,1,0:T(8,128)(2,1)} %copy-done, bf16[8,2,128,512]{3,2,1,0:T(8,128)(2,1)} %copy-done, s32[1,1024]{1,0:T(1,128)} %bitcast.33, f32[256,1024]{1,0:T(8,128)} %get-tuple-element.13.la_ref, ...), custom_call_target="tpu_custom_call" | custom-call | tf_op jit(solution)/shard_map/pallas_call | solution.py:175
  164.2 1.3 copy-done.1
  165.5 6.3 %shard_map.84.refs_0_ = bf16[256,512]{1,0:T(8,128)(2,1)} custom-call(bf16[256,1024]{1,0:T(8,128)(2,1)} %bitcast.25, bf16[8,2,128,512]{3,2,1,0:T(8,128)(2,1)} %copy-done.1, bf16[8,2,128,512]{3,2,1,0:T(8,128)(2,1)} %copy-done.1, s32[1,1024]{1,0:T(1,128)} %bitcast.34, f32[256,1024]{1,0:T(8,128)} %get-tuple-element.13.la_ref, ...), custom_call_target="tpu_custom_call" | custom-call | tf_op jit(solution)/shard_map/pallas_call | solution.py:175
  172.3 4.8 %fusion.11 = (bf16[512,2048]{1,0:T(8,128)(2,1)}, bf16[512,2048]{1,0:T(8,128)(2,1)}) fusion(bf16[1024,2048]{1,0:T(8,128)(2,1)} %collective-permute-done.5), kind=kLoop, calls=%fused_computation.66 | loop fusion | bytes 8388608 | tf_op jit(solution)/shard_map/slice | solution.py:286
  177.1 0.7 copy-done.7
  177.9 6.8 %shard_map.86 = bf16[256,2048]{1,0:T(8,128)(2,1)} custom-call(bf16[256,512]{1,0:T(8,128)(2,1)} %shard_map.84.refs_0_, bf16[256,512]{1,0:T(8,128)(2,1)} %shard_map.85.refs_1_, bf16[256,512]{1,0:T(8,128)(2,1)} %copy-done.8, bf16[256,512]{1,0:T(8,128)(2,1)} %copy-done.7, bf16[512,2048]{1,0:T(8,128)(2,1)} %get-tuple-element.23.refs_4_, ...), custom_call_target="tpu_custom_call" | custom-call | tf_op jit(solution)/shard_map/pallas_call | solution.py:199
  (56 shorter events, 6.8 us)
Async XLA Ops:
  12.4 32.1 %all-to-all-start.2 = ((bf16[8,2,128,512]{3,2,1,0:T(8,128)(2,1)}), bf16[8,2,128,512]{3,2,1,0:T(8,128)(2,1)S(1)}, u32[]{:S(2)}, u32[]{:S(2)}) async-start(bf16[8,2,128,512]{3,2,1,0:T(8,128)(2,1)} %get-tuple-element.26), calls=%async_computation.2 | async-start | bytes 4194304 | tf_op jit(solution)/shard_map/all_to_all | solution.py:265
  25.4 24.2 %copy-start.10 = (s32[16]{0:T(128)S(1)}, s32[16]{0:T(128)}, u32[]{:S(2)}) copy-start(s32[16]{0:T(128)} %param.15) | copy-start | bytes 196
  25.4 25.8 %copy-start.5 = (bf16[256,1024]{1,0:T(8,128)(2,1)S(1)}, bf16[256,1024]{1,0:T(8,128)(2,1)}, u32[]{:S(2)}) copy-start(bf16[256,1024]{1,0:T(8,128)(2,1)} %param.11) | copy-start | bytes 1572868
  25.4 25.9 %copy-start.6 = (bf16[256,1024]{1,0:T(8,128)(2,1)S(1)}, bf16[256,1024]{1,0:T(8,128)(2,1)}, u32[]{:S(2)}) copy-start(bf16[256,1024]{1,0:T(8,128)(2,1)} %param.10) | copy-start | bytes 1572868
  44.5 5.1 %copy-start = (bf16[8,2,128,512]{3,2,1,0:T(8,128)(2,1)}, bf16[8,2,128,512]{3,2,1,0:T(8,128)(2,1)S(1)}, u32[]{:S(2)}) copy-start(bf16[8,2,128,512]{3,2,1,0:T(8,128)(2,1)S(1)} %all-to-all-done.2.kp_ref.vp_ref) | copy-start | bytes 6291460
  44.5 70.5 %all-to-all-start.1 = ((bf16[8,2,128,1024]{3,2,1,0:T(8,128)(2,1)}), bf16[8,2,128,1024]{3,2,1,0:T(8,128)(2,1)}, u32[]{:S(2)}, u32[]{:S(2)}) async-start(bf16[8,2,128,1024]{3,2,1,0:T(8,128)(2,1)} %gather_fusion.1), calls=%async_computation.1 | async-start | bytes 8388608 | tf_op jit(solution)/shard_map/all_to_all | solution.py:256
  53.9 7.4 %copy-start.2 = (bf16[32,8,8,128]{3,1,2,0:T(8,128)(2,1)}, bf16[32,8,8,128]{3,1,2,0:T(8,128)(2,1)S(1)}, u32[]{:S(2)}) copy-start(bf16[32,8,8,128]{3,1,2,0:T(8,128)(2,1)S(1)} %copy.27) | copy-start | bytes 1572868
  53.9 51.8 %collective-permute-start = (bf16[256,1024]{1,0:T(8,128)(2,1)S(1)}, bf16[256,1024]{1,0:T(8,128)(2,1)S(1)}, u32[]{:S(2)}, u32[]{:S(2)}) collective-permute-start(bf16[256,1024]{1,0:T(8,128)(2,1)S(1)} %bitcast.22), channel_id=1, source_target_pairs={{0,16},{16,0},{1,17},{17,1},{2,18},{18,2},{3,19},{19,3},{4,20},{20... | collective-permute-start | bytes 1572872 | tf_op jit(solution)/shard_map/ppermute | solution.py:253
  61.3 111.0 %collective-permute-start.5 = (bf16[1024,2048]{1,0:T(8,128)(2,1)}, bf16[1024,2048]{1,0:T(8,128)(2,1)}, u32[]{:S(2)}, u32[]{:S(2)}) collective-permute-start(bf16[1024,2048]{1,0:T(8,128)(2,1)} %constant_dynamic-slice_fusion.1), channel_id=1, source_target_pairs={{0,1},{1,0},{2,3},{3,2},{4,5},{5,4},{6,7},{7,6},{8,9},{9,8},{10,11... | collective-permute-start | bytes 12582920 | tf_op jit(solution)/shard_map/ppermute | solution.py:242
  105.7 9.3 %copy-start.4 = (bf16[256,1024]{1,0:T(8,128)(2,1)}, bf16[256,1024]{1,0:T(8,128)(2,1)S(1)}, u32[]{:S(2)}) copy-start(bf16[256,1024]{1,0:T(8,128)(2,1)S(1)} %collective-permute-done.q_ref) | copy-start | bytes 1572868
  115.0 49.2 %all-to-all-start = ((bf16[8,2,128,512]{3,2,1,0:T(8,128)(2,1)}), bf16[8,2,128,512]{3,2,1,0:T(8,128)(2,1)S(1)}, u32[]{:S(2)}, u32[]{:S(2)}) async-start(bf16[8,2,128,512]{3,2,1,0:T(8,128)(2,1)} %get-tuple-element.12), calls=%async_computation | async-start | bytes 4194304 | tf_op jit(solution)/shard_map/all_to_all | solution.py:263
  130.6 11.0 %copy-start.9 = (bf16[2048]{0:T(1024)(128)(2,1)S(1)}, bf16[2048]{0:T(1024)(128)(2,1)}, u32[]{:S(2)}) copy-start(bf16[2048]{0:T(1024)(128)(2,1)} %param.17) | copy-start | bytes 12292
  130.6 26.5 %collective-permute-start.1 = (bf16[256,1024]{1,0:T(8,128)(2,1)}, bf16[256,1024]{1,0:T(8,128)(2,1)S(1)}, u32[]{:S(2)}, u32[]{:S(2)}) collective-permute-start(bf16[256,1024]{1,0:T(8,128)(2,1)} %get-tuple-element.16), channel_id=1, source_target_pairs={{0,16},{16,0},{1,17},{17,1},{2,18},{18,2},{3,19},{19,3},{4,20},{20... | collective-permute-start | bytes 1572872 | tf_op jit(solution)/shard_map/ppermute | solution.py:274
  137.1 18.7 %collective-permute-start.2 = (f32[8,256,2]{1,0,2:T(8,128)S(1)}, f32[8,256,2]{1,0,2:T(8,128)S(1)}, u32[]{:S(2)}, u32[]{:S(2)}) collective-permute-start(f32[8,256,2]{1,0,2:T(8,128)S(1)} %copy.17), channel_id=1, source_target_pairs={{0,16},{16,0},{1,17},{17,1},{2,18},{18,2},{3,19},{19,3},{4,20},{20... | collective-permute-start | bytes 49160 | tf_op jit(solution)/shard_map/ppermute | solution.py:275
  157.1 0.8 copy-start.3
  164.2 12.9 %collective-permute-start.4 = (bf16[256,512]{1,0:T(8,128)(2,1)}, bf16[256,512]{1,0:T(8,128)(2,1)S(1)}, u32[]{:S(2)}, u32[]{:S(2)}) collective-permute-start(bf16[256,512]{1,0:T(8,128)(2,1)} %shard_map.85.refs_1_), channel_id=1, source_target_pairs={{0,1},{1,0},{2,3},{3,2},{4,5},{5,4},{6,7},{7,6},{8,9},{9,8},{10,11... | collective-permute-start | bytes 786440 | tf_op jit(solution)/shard_map/ppermute | solution.py:283
  164.2 1.3 copy-start.1
  171.8 5.3 %collective-permute-start.3 = (bf16[256,512]{1,0:T(8,128)(2,1)}, bf16[256,512]{1,0:T(8,128)(2,1)S(1)}, u32[]{:S(2)}, u32[]{:S(2)}) collective-permute-start(bf16[256,512]{1,0:T(8,128)(2,1)} %shard_map.84.refs_0_), channel_id=1, source_target_pairs={{0,1},{1,0},{2,3},{3,2},{4,5},{5,4},{6,7},{7,6},{8,9},{9,8},{10,11... | collective-permute-start | bytes 786440 | tf_op jit(solution)/shard_map/ppermute | solution.py:283
  177.1 0.7 copy-start.7
  177.1 0.8 copy-start.8

commit v15 on v13

--- a/solution.py
+++ b/solution.py
@@ -185,12 +185,21 @@
     refs[-1][...] = total.astype(refs[-1].dtype)
 
 
+def projection_block(out_cols):
+    return 512 if out_cols % 512 == 0 else out_cols
+
+
+def blocked(w, block):
+    rows, cols = w.shape
+    return jnp.transpose(w.reshape(rows, cols // block, block), (1, 0, 2))
+
+
 def project(parts, weights, bias):
     span, rows = parts[0].shape
-    out_cols = weights[0].shape[1]
-    block = 512 if out_cols % 512 == 0 else out_cols
+    block = weights[0].shape[2]
+    out_cols = weights[0].shape[0] * block
     a_spec = pl.BlockSpec((span, rows), lambda c: (0, 0))
-    w_spec = pl.BlockSpec((rows, block), lambda c: (0, c))
+    w_spec = pl.BlockSpec((None, rows, block), lambda c: (c, 0, 0))
     b_spec = pl.BlockSpec((1, block), lambda c: (0, c))
     return pl.pallas_call(
         projection_kernel,
@@ -235,8 +244,9 @@
         target = (tp_index + shift) % tp_count
         piece = lax.dynamic_slice_in_dim(w_out, target * out_cols, out_cols, axis=1)
         perm = [(i, (i + shift) % tp_count) for i in range(tp_count)]
-        w_recv.append(lax.ppermute(piece, "tp", perm))
+        w_recv.append(lax.ppermute(blocked(piece, projection_block(out_cols)), "tp", perm))
     w_mine = lax.dynamic_slice_in_dim(w_out, tp_index * out_cols, out_cols, axis=1)
+    w_mine = blocked(w_mine, projection_block(out_cols))
 
     owners = jnp.where(page_table >= 0, page_table // page_count, -1)
     held_here = owners == own_index

time: 171 us -> 183 us (1.070)
  local copies, waits for them, and re-layouts: 29.6 us -> 54.7 us
  waiting for transfers between devices: 85.1 us -> 71.4 us
    unnamed x20 -> x22, local copies, waits for them, and re-layouts: 2.86 us -> 15.5 us
    ppermute x1, waiting for transfers between devices: 32.6 us -> 20 us  [on_device(): back_stats = lax.ppermute(far_stats, 'half', swap)]
    reshape x0 -> x2, local copies, waits for them, and re-layouts: none -> 12.5 us  [blocked(): return jnp.transpose(w.reshape(rows, cols // block, block), (1, 0, 2))]
  transfers between devices with their start and end apart: 7 -> 7, of which waited for: 3 -> 2; matrix products, arithmetic and copies ran while one was open for 16% -> 29% of each run, Pallas kernels for 13% -> 12%
where the time goes in v15:
time: 183 us; the launch traced here: 182 us
  waiting for transfers between devices  71.4 us (39%)
  local copies, waits for them, and re-layouts  54.7 us (30%)
  Pallas kernels  29.2 us (16%)
  starting transfers between devices  19.1 us (10%)
  other arithmetic  7.35 us (4%)
    ppermute x1, waiting for transfers between devices, on_device(): partner_query = lax.ppermute(query_rot, 'half', swap)  51.4 us
    ppermute x1, waiting for transfers between devices, on_device(): back_stats = lax.ppermute(far_stats, 'half', swap)  20 us
    unnamed x22, local copies, waits for them, and re-layouts  15.5 us
    reshape x2, local copies, waits for them, and re-layouts, blocked(): return jnp.transpose(w.reshape(rows, cols // block, block), (1, 0, 2))  12.5 us
    pallas_call x1, Pallas kernels, near_attend(): pl.pallas_call(near_kernel, grid=(head_count // group,), in_specs=[col_sp...  10.5 us
    dynamic_slice x1, local copies, waits for them, and re-layouts, on_device(): piece = lax.dynamic_slice_in_dim(w_out, target * out_cols, out_cols, axis=1)  8.33 us
    pallas_call x1, Pallas kernels, project(): pl.pallas_call(projection_kernel, grid=(out_cols // block,), in_specs=[a_...  6.82 us
    pallas_call x1, Pallas kernels, far_attend(): pl.pallas_call(far_kernel, grid=(head_count // group,), in_specs=[col_spe...  6.78 us
  transfers between devices with their start and end apart: 7, of which 2 were waited for; matrix products, arithmetic and copies ran while one was open for 29% of the time, Pallas kernels for 12%

profile of v15, /device:TPU:11, one launch (start us, length us, event | category | flops | bytes accessed | tf_op | source)
XLA Modules:
  0.0 181.9 jit_solution(10194274819799148261)
XLA Ops:
  0.0 0.8 select_reduce_fusion
  1.5 6.1 %gather_fusion.1 = bf16[8,2,128,1024]{3,2,1,0:T(8,128)(2,1)} fusion(bf16[16,2,128,1024]{3,2,1,0:T(8,128)(2,1)} %param.13, s32[1024]{0:T(1024)S(1)} %pad_clamp_fusion), kind=kCustom, calls=%fused_computation.3 | custom fusion | bytes 8388640 | tf_op jit(solution)/shard_map/jit(_take)/gather | solution.py:261
  7.7 4.7 %all-to-all-start.1 = ((bf16[8,2,128,1024]{3,2,1,0:T(8,128)(2,1)}), bf16[8,2,128,1024]{3,2,1,0:T(8,128)(2,1)}, u32[]{:S(2)}, u32[]{:S(2)}) async-start(bf16[8,2,128,1024]{3,2,1,0:T(8,128)(2,1)} %gather_fusion.1), calls=%async_computation.1 | async-start | bytes 8388608 | tf_op jit(solution)/shard_map/all_to_all | solution.py:262
  12.4 0.7 fusion.10
  14.9 0.8 subtract_convert_fusion
  15.7 1.0 pad_maximum_fusion
  16.8 2.4 %collective-permute-start = (bf16[256,1024]{1,0:T(8,128)(2,1)S(1)}, bf16[256,1024]{1,0:T(8,128)(2,1)S(1)}, u32[]{:S(2)}, u32[]{:S(2)}) collective-permute-start(bf16[256,1024]{1,0:T(8,128)(2,1)S(1)} %bitcast.29), channel_id=1, source_target_pairs={{0,16},{16,0},{1,17},{17,1},{2,18},{18,2},{3,19},{19,3},{4,20},{20... | collective-permute-start | bytes 1572872 | tf_op jit(solution)/shard_map/ppermute | solution.py:259
  19.9 6.1 %gather_fusion = bf16[8,2,128,1024]{3,2,1,0:T(8,128)(2,1)} fusion(bf16[16,2,128,1024]{3,2,1,0:T(8,128)(2,1)} %param.13, s32[1024]{0:T(1024)S(1)} %pad_clamp_fusion.2), kind=kCustom, calls=%fused_computation.2 | custom fusion | bytes 8388640 | tf_op jit(solution)/shard_map/jit(_take)/gather | solution.py:263
  26.0 51.4 %collective-permute-done.q_ref = bf16[256,1024]{1,0:T(8,128)(2,1)S(1)} collective-permute-done((bf16[256,1024]{1,0:T(8,128)(2,1)S(1)}, bf16[256,1024]{1,0:T(8,128)(2,1)S(1)}, u32[]{:S(2)}, u32[]{:S(2)}) %collective-permute-start) | collective-permute-done | bytes 524320 | tf_op jit(solution)/shard_map/ppermute | solution.py:259
  77.4 5.1 %all-to-all-start = ((bf16[8,2,128,1024]{3,2,1,0:T(8,128)(2,1)}), bf16[8,2,128,1024]{3,2,1,0:T(8,128)(2,1)}, u32[]{:S(2)}, u32[]{:S(2)}) async-start(bf16[8,2,128,1024]{3,2,1,0:T(8,128)(2,1)} %gather_fusion), calls=%async_computation | async-start | bytes 8388608 | tf_op jit(solution)/shard_map/all_to_all | solution.py:265
  82.5 8.3 %constant_dynamic-slice_fusion.3 = (bf16[1024,2048]{1,0:T(8,128)(2,1)}, bf16[1024,2048]{1,0:T(8,128)(2,1)}) fusion(bf16[1024,4096]{1,0:T(8,128)(2,1)} %param.16, s32[]{:T(128)S(6)} %select_n.98, s32[]{:T(128)S(6)} %select_n.96), kind=kLoop, calls=%fused_computation.56 | loop fusion | bytes 16777224 | tf_op jit(solution)/shard_map/dynamic_slice | solution.py:245
  90.8 6.4 %copy.34 = bf16[1024,2048]{0,1:T(8,128)(2,1)} copy(bf16[1024,2048]{1,0:T(8,128)(2,1)} %get-tuple-element.22) | data formatting | bytes 8388608
  97.2 6.3 %copy.32 = bf16[1024,4,512]{2,0,1:T(8,128)(2,1)} copy(bf16[1024,4,512]{0,2,1:T(8,128)(2,1)} %bitcast.27) | data formatting | bytes 8388608 | tf_op jit(solution)/shard_map/reshape | solution.py:194
  103.4 2.1 %collective-permute-start.4 = (bf16[4,1024,512]{2,1,0:T(8,128)(2,1)}, bf16[4,1024,512]{2,1,0:T(8,128)(2,1)}, u32[]{:S(2)}, u32[]{:S(2)}) collective-permute-start(bf16[4,1024,512]{2,1,0:T(8,128)(2,1)} %bitcast.34), channel_id=1, source_target_pairs={{0,1},{1,0},{2,3},{3,2},{4,5},{5,4},{6,7},{7,6},{8,9},{9,8},{10,11... | collective-permute-start | bytes 12582920 | tf_op jit(solution)/shard_map/ppermute | solution.py:247
  105.5 0.7 fusion.8
  106.6 0.7 clamp_select_fusion
  107.3 0.7 fusion.7
  107.9 6.8 %shard_map.83 = (bf16[256,1024]{1,0:T(8,128)(2,1)}, f32[8,256,2]{2,1,0:T(8,128)}) custom-call(bf16[256,1024]{1,0:T(8,128)(2,1)} %copy-done.1, bf16[8,2,128,1024]{3,2,1,0:T(8,128)(2,1)} %all-to-all-done.1.kp_ref.vp_ref, bf16[8,2,128,1024]{3,2,1,0:T(8,128)(2,1)} %all-to-all-done.1.kp_ref.vp_ref, s32[1,1024]{1,0:T(1,128)} %bitcast.41), custom_call_target="tpu_custom_call" | custom-call | tf_op jit(solution)/shard_map/pallas_call | solution.py:154
  115.9 1.5 copy.27
  117.4 1.9 %collective-permute-start.2 = (f32[8,256,2]{1,0,2:T(8,128)S(1)}, f32[8,256,2]{1,0,2:T(8,128)S(1)}, u32[]{:S(2)}, u32[]{:S(2)}) collective-permute-start(f32[8,256,2]{1,0,2:T(8,128)S(1)} %copy.27), channel_id=1, source_target_pairs={{0,16},{16,0},{1,17},{17,1},{2,18},{18,2},{3,19},{19,3},{4,20},{20... | collective-permute-start | bytes 49160 | tf_op jit(solution)/shard_map/ppermute | solution.py:275
  119.3 0.7 fusion.6
  120.0 0.9 copy.41
  120.9 5.1 %shard_map.82 = (f32[256,1024]{1,0:T(8,128)}, f32[8,256,2]{2,1,0:T(8,128)}) custom-call(bf16[256,1024]{1,0:T(8,128)(2,1)} %bitcast.30, bf16[256,1024]{1,0:T(8,128)(2,1)} %bitcast.35, bf16[256,1024]{1,0:T(8,128)(2,1)} %vl_ref.1), custom_call_target="tpu_custom_call" | custom-call | tf_op jit(solution)/shard_map/pallas_call | solution.py:137
  126.0 20.0 %collective-permute-done.2 = f32[8,256,2]{1,0,2:T(8,128)S(1)} collective-permute-done((f32[8,256,2]{1,0,2:T(8,128)S(1)}, f32[8,256,2]{1,0,2:T(8,128)S(1)}, u32[]{:S(2)}, u32[]{:S(2)}) %collective-permute-start.2) | collective-permute-done | bytes 16416 | tf_op jit(solution)/shard_map/ppermute | solution.py:275
  146.0 1.4 copy.28.bst_ref
  147.4 0.8 copy-done.2
  148.2 10.5 %shard_map.84.refs_0_ = bf16[256,1024]{1,0:T(8,128)(2,1)} custom-call(bf16[256,1024]{1,0:T(8,128)(2,1)} %bitcast.31, bf16[8,2,128,1024]{3,2,1,0:T(8,128)(2,1)} %all-to-all-done.kp_ref.vp_ref, bf16[8,2,128,1024]{3,2,1,0:T(8,128)(2,1)} %all-to-all-done.kp_ref.vp_ref, s32[1,1024]{1,0:T(1,128)} %bitcast.40, f32[256,1024]{1,0:T(8,128)} %get-tuple-element.13.la_ref, ...), custom_call_target="tpu_custom_call" | custom-call | tf_op jit(solution)/shard_map/pallas_call | solution.py:171
  158.7 2.4 %collective-permute-start.3 = (bf16[256,1024]{1,0:T(8,128)(2,1)}, bf16[256,1024]{1,0:T(8,128)(2,1)S(1)}, u32[]{:S(2)}, u32[]{:S(2)}) collective-permute-start(bf16[256,1024]{1,0:T(8,128)(2,1)} %shard_map.84.refs_0_), channel_id=1, source_target_pairs={{0,1},{1,0},{2,3},{3,2},{4,5},{5,4},{6,7},{7,6},{8,9},{9,8},{10,11... | collective-permute-start | bytes 1572872 | tf_op jit(solution)/shard_map/ppermute | solution.py:283
  161.7 6.3 %copy.33 = bf16[1024,2048]{0,1:T(8,128)(2,1)} copy(bf16[1024,2048]{1,0:T(8,128)(2,1)} %get-tuple-element.23) | data formatting | bytes 8388608
  168.0 6.2 %copy.30 = bf16[1024,4,512]{2,0,1:T(8,128)(2,1)} copy(bf16[1024,4,512]{0,2,1:T(8,128)(2,1)} %bitcast.28) | data formatting | bytes 8388608 | tf_op jit(solution)/shard_map/reshape | solution.py:194
  174.3 0.8 copy-done.3
  175.0 6.8 %shard_map.85 = bf16[256,2048]{1,0:T(8,128)(2,1)} custom-call(bf16[256,1024]{1,0:T(8,128)(2,1)} %shard_map.84.refs_0_, bf16[256,1024]{1,0:T(8,128)(2,1)} %copy-done.3, bf16[4,1024,512]{2,1,0:T(8,128)(2,1)} %bitcast.26, bf16[4,1024,512]{2,1,0:T(8,128)(2,1)} %collective-permute-done.4.refs_3_, bf16[1,2048]{1,0:T(2,128)(2,1)} %reshape.169.refs_4_), custom_call_target="tpu_custom_call" | custom-call | tf_op jit(solution)/shard_map/pallas_call | solution.py:204
  (46 shorter events, 5.4 us)
Async XLA Ops:
  7.7 4.7 %copy-start.7 = (s32[16]{0:T(128)S(1)}, s32[16]{0:T(128)}, u32[]{:S(2)}) copy-start(s32[16]{0:T(128)} %param.15) | copy-start | bytes 196
  7.7 6.4 %copy-start.4 = (bf16[256,1024]{1,0:T(8,128)(2,1)S(1)}, bf16[256,1024]{1,0:T(8,128)(2,1)}, u32[]{:S(2)}) copy-start(bf16[256,1024]{1,0:T(8,128)(2,1)} %param.10) | copy-start | bytes 1572868
  7.7 6.5 %copy-start.5 = (bf16[256,1024]{1,0:T(8,128)(2,1)S(1)}, bf16[256,1024]{1,0:T(8,128)(2,1)}, u32[]{:S(2)}) copy-start(bf16[256,1024]{1,0:T(8,128)(2,1)} %param.11) | copy-start | bytes 1572868
  7.7 69.8 %all-to-all-start.1 = ((bf16[8,2,128,1024]{3,2,1,0:T(8,128)(2,1)}), bf16[8,2,128,1024]{3,2,1,0:T(8,128)(2,1)}, u32[]{:S(2)}, u32[]{:S(2)}) async-start(bf16[8,2,128,1024]{3,2,1,0:T(8,128)(2,1)} %gather_fusion.1), calls=%async_computation.1 | async-start | bytes 8388608 | tf_op jit(solution)/shard_map/all_to_all | solution.py:262
  16.8 9.2 %copy-start = (bf16[32,8,8,128]{3,1,2,0:T(8,128)(2,1)}, bf16[32,8,8,128]{3,1,2,0:T(8,128)(2,1)S(1)}, u32[]{:S(2)}) copy-start(bf16[32,8,8,128]{3,1,2,0:T(8,128)(2,1)S(1)} %copy.42) | copy-start | bytes 1572868
  16.8 60.6 %collective-permute-start = (bf16[256,1024]{1,0:T(8,128)(2,1)S(1)}, bf16[256,1024]{1,0:T(8,128)(2,1)S(1)}, u32[]{:S(2)}, u32[]{:S(2)}) collective-permute-start(bf16[256,1024]{1,0:T(8,128)(2,1)S(1)} %bitcast.29), channel_id=1, source_target_pairs={{0,16},{16,0},{1,17},{17,1},{2,18},{18,2},{3,19},{19,3},{4,20},{20... | collective-permute-start | bytes 1572872 | tf_op jit(solution)/shard_map/ppermute | solution.py:259
  77.4 5.1 %copy-start.1 = (bf16[256,1024]{1,0:T(8,128)(2,1)}, bf16[256,1024]{1,0:T(8,128)(2,1)S(1)}, u32[]{:S(2)}) copy-start(bf16[256,1024]{1,0:T(8,128)(2,1)S(1)} %collective-permute-done.q_ref) | copy-start | bytes 1572868
  77.4 70.0 %all-to-all-start = ((bf16[8,2,128,1024]{3,2,1,0:T(8,128)(2,1)}), bf16[8,2,128,1024]{3,2,1,0:T(8,128)(2,1)}, u32[]{:S(2)}, u32[]{:S(2)}) async-start(bf16[8,2,128,1024]{3,2,1,0:T(8,128)(2,1)} %gather_fusion), calls=%async_computation | async-start | bytes 8388608 | tf_op jit(solution)/shard_map/all_to_all | solution.py:265
  103.4 70.8 %collective-permute-start.4 = (bf16[4,1024,512]{2,1,0:T(8,128)(2,1)}, bf16[4,1024,512]{2,1,0:T(8,128)(2,1)}, u32[]{:S(2)}, u32[]{:S(2)}) collective-permute-start(bf16[4,1024,512]{2,1,0:T(8,128)(2,1)} %bitcast.34), channel_id=1, source_target_pairs={{0,1},{1,0},{2,3},{3,2},{4,5},{5,4},{6,7},{7,6},{8,9},{9,8},{10,11... | collective-permute-start | bytes 12582920 | tf_op jit(solution)/shard_map/ppermute | solution.py:247
  114.7 32.7 %collective-permute-start.1 = (bf16[256,1024]{1,0:T(8,128)(2,1)}, bf16[256,1024]{1,0:T(8,128)(2,1)S(1)}, u32[]{:S(2)}, u32[]{:S(2)}) collective-permute-start(bf16[256,1024]{1,0:T(8,128)(2,1)} %get-tuple-element.16), channel_id=1, source_target_pairs={{0,16},{16,0},{1,17},{17,1},{2,18},{18,2},{3,19},{19,3},{4,20},{20... | collective-permute-start | bytes 1572872 | tf_op jit(solution)/shard_map/ppermute | solution.py:274
  117.4 28.6 %collective-permute-start.2 = (f32[8,256,2]{1,0,2:T(8,128)S(1)}, f32[8,256,2]{1,0,2:T(8,128)S(1)}, u32[]{:S(2)}, u32[]{:S(2)}) collective-permute-start(f32[8,256,2]{1,0,2:T(8,128)S(1)} %copy.27), channel_id=1, source_target_pairs={{0,16},{16,0},{1,17},{17,1},{2,18},{18,2},{3,19},{19,3},{4,20},{20... | collective-permute-start | bytes 49160 | tf_op jit(solution)/shard_map/ppermute | solution.py:275
  147.4 0.8 copy-start.2
  148.2 12.9 %copy-start.6 = (bf16[2048]{0:T(1024)(128)(2,1)S(1)}, bf16[2048]{0:T(1024)(128)(2,1)}, u32[]{:S(2)}) copy-start(bf16[2048]{0:T(1024)(128)(2,1)} %param.17) | copy-start | bytes 12292
  158.7 15.6 %collective-permute-start.3 = (bf16[256,1024]{1,0:T(8,128)(2,1)}, bf16[256,1024]{1,0:T(8,128)(2,1)S(1)}, u32[]{:S(2)}, u32[]{:S(2)}) collective-permute-start(bf16[256,1024]{1,0:T(8,128)(2,1)} %shard_map.84.refs_0_), channel_id=1, source_target_pairs={{0,1},{1,0},{2,3},{3,2},{4,5},{5,4},{6,7},{7,6},{8,9},{9,8},{10,11... | collective-permute-start | bytes 1572872 | tf_op jit(solution)/shard_map/ppermute | solution.py:283
  174.3 0.8 copy-start.3

commit v16 on v13

--- a/solution.py
+++ b/solution.py
@@ -201,6 +201,33 @@
     )(*parts, *weights, bias.reshape(1, out_cols))
 
 
+def gather_kernel(ids_ref, src_ref, dst_ref, sems):
+    copies = [
+        pltpu.make_async_copy(src_ref.at[ids_ref[i]], dst_ref.at[i], sems.at[i])
+        for i in range(dst_ref.shape[0])
+    ]
+    for copy in copies:
+        copy.start()
+    for copy in copies:
+        copy.wait()
+
+
+def gather_pages(kv_pages, ids):
+    count = ids.shape[0]
+    ids = jnp.clip(ids, 0, kv_pages.shape[0] - 1).astype(jnp.int32)
+    return pl.pallas_call(
+        gather_kernel,
+        grid_spec=pltpu.PrefetchScalarGridSpec(
+            num_scalar_prefetch=1,
+            grid=(1,),
+            in_specs=[pl.BlockSpec(memory_space=pl.ANY)],
+            out_specs=pl.BlockSpec(memory_space=pl.ANY),
+            scratch_shapes=[pltpu.SemaphoreType.DMA((count,))],
+        ),
+        out_shape=jax.ShapeDtypeStruct((count,) + kv_pages.shape[1:], kv_pages.dtype),
+    )(ids, kv_pages)
+
+
 def usable_keys(page_table, request, length, source_base, source_count, page_count, page_size):
     row = lax.dynamic_index_in_dim(page_table, request, 0, keepdims=False)
     row_owner = jnp.where(row >= 0, row // page_count, -1)
@@ -248,9 +275,9 @@
     query_rot = rotate_rows(new_queries, positions)
     partner_query = lax.ppermute(query_rot, "half", swap)
 
-    far_pages = jnp.take(kv_pages, jnp.take(local_page, (1 - half) * sub_count + dest), axis=0, mode="clip")
+    far_pages = gather_pages(kv_pages, jnp.take(local_page, (1 - half) * sub_count + dest))
     far_incoming = lax.all_to_all(far_pages, "sub", split_axis=0, concat_axis=0, tiled=True)
-    near_pages = jnp.take(kv_pages, jnp.take(local_page, half * sub_count + dest), axis=0, mode="clip")
+    near_pages = gather_pages(kv_pages, jnp.take(local_page, half * sub_count + dest))
     partner_query, near_pages = lax.optimization_barrier((partner_query, near_pages))
     near_incoming = lax.all_to_all(near_pages, "sub", split_axis=0, concat_axis=0, tiled=True)
     key_rot = rotate_rows(new_keys, positions)

time: 171 us -> 366 us (2.14)
  Pallas kernels: 29.2 us -> 287 us
  waiting for transfers between devices: 85.1 us -> 32.6 us
  local copies, waits for them, and re-layouts: 29.6 us -> 18.1 us
    pallas_call x0 -> x2, Pallas kernels: none -> 258 us  [gather_pages(): pl.pallas_call(gather_kernel, grid_spec=pltpu.PrefetchScalarGridSpec(num_...]
    ppermute x1, waiting for transfers between devices: 51.4 us -> 0.01 us  [on_device(): partner_query = lax.ppermute(query_rot, 'half', swap)]
    gather x2 -> x0, local copies, waits for them, and re-layouts: 12.3 us -> none  [the longest x1 6.14 us: on_device(): jnp.take(kv_pages, jnp.take(local_page, (1 - half) * sub_count + dest), a...]
  transfers between devices with their start and end apart: 7 -> 7, of which waited for: 3 -> 2; matrix products, arithmetic and copies ran while one was open for 16% -> 6% of each run, Pallas kernels for 13% -> 41%
where the time goes in v16:
time: 366 us; the launch traced here: 365 us
  Pallas kernels  287 us (78%)
  waiting for transfers between devices  32.6 us (9%)
  starting transfers between devices  18.8 us (5%)
  local copies, waits for them, and re-layouts  18.1 us (5%)
  other arithmetic  8.38 us (2%)
    pallas_call x2, Pallas kernels, gather_pages(): pl.pallas_call(gather_kernel, grid_spec=pltpu.PrefetchScalarGridSpec(num_...  258 us
    ppermute x1, waiting for transfers between devices, on_device(): back_stats = lax.ppermute(far_stats, 'half', swap)  31.4 us
    pallas_call x1, Pallas kernels, near_attend(): pl.pallas_call(near_kernel, grid=(head_count // group,), in_specs=[col_sp...  10.5 us
    dynamic_slice x1, local copies, waits for them, and re-layouts, on_device(): piece = lax.dynamic_slice_in_dim(w_out, target * out_cols, out_cols, axis=1)  8.35 us
  transfers between devices with their start and end apart: 7, of which 2 were waited for; matrix products, arithmetic and copies ran while one was open for 6% of the time, Pallas kernels for 41%

profile of v16, /device:TPU:11, one launch (start us, length us, event | category | flops | bytes accessed | tf_op | source)
XLA Modules:
  0.0 365.0 jit_solution(1030271552024029342)
XLA Ops:
  0.0 0.8 select_reduce_fusion
  0.8 0.6 gather_fusion.1
  2.0 128.9 %shard_map.84 = bf16[8,2,128,1024]{3,2,1,0:T(8,128)(2,1)} custom-call(s32[8]{0:T(128)} %fusion.11.ids_ref, bf16[16,2,128,1024]{3,2,1,0:T(8,128)(2,1)} %src_ref.3), custom_call_target="tpu_custom_call" | custom-call | tf_op jit(solution)/shard_map/pallas_call | solution.py:218
  130.9 4.7 %all-to-all-start.1 = ((bf16[8,2,128,1024]{3,2,1,0:T(8,128)(2,1)}), bf16[8,2,128,1024]{3,2,1,0:T(8,128)(2,1)}, u32[]{:S(2)}, u32[]{:S(2)}) async-start(bf16[8,2,128,1024]{3,2,1,0:T(8,128)(2,1)} %shard_map.84), calls=%async_computation.1 | async-start | bytes 8388608 | tf_op jit(solution)/shard_map/all_to_all | solution.py:279
  135.7 0.7 fusion.12
  136.4 0.6 add_convert_fusion.2
  138.2 0.8 subtract_convert_fusion
  139.0 1.0 pad_maximum_fusion
  140.1 2.4 collective-permute-start
  142.5 0.6 gather_fusion
  143.7 128.9 %shard_map.82 = bf16[8,2,128,1024]{3,2,1,0:T(8,128)(2,1)} custom-call(s32[8]{0:T(128)} %fusion.10.ids_ref, bf16[16,2,128,1024]{3,2,1,0:T(8,128)(2,1)} %src_ref.3), custom_call_target="tpu_custom_call" | custom-call | tf_op jit(solution)/shard_map/pallas_call | solution.py:218
  272.6 0.8 copy-done.1
  273.4 4.6 %all-to-all-start = ((bf16[8,2,128,1024]{3,2,1,0:T(8,128)(2,1)}), bf16[8,2,128,1024]{3,2,1,0:T(8,128)(2,1)}, u32[]{:S(2)}, u32[]{:S(2)}) async-start(bf16[8,2,128,1024]{3,2,1,0:T(8,128)(2,1)} %shard_map.82), calls=%async_computation | async-start | bytes 8388608 | tf_op jit(solution)/shard_map/all_to_all | solution.py:282
  278.0 8.3 %constant_dynamic-slice_fusion.3 = (bf16[1024,2048]{1,0:T(8,128)(2,1)}, bf16[1024,2048]{1,0:T(8,128)(2,1)}) fusion(bf16[1024,4096]{1,0:T(8,128)(2,1)} %param.16, s32[]{:T(128)S(6)} %select_n.98, s32[]{:T(128)S(6)} %select_n.96), kind=kLoop, calls=%fused_computation.52 | loop fusion | bytes 16777224 | tf_op jit(solution)/shard_map/dynamic_slice | solution.py:263
  286.3 2.0 collective-permute-start.4
  288.4 0.7 fusion.8
  289.4 0.7 clamp_select_fusion
  290.1 0.7 fusion.7
  290.8 6.8 %shard_map.85 = (bf16[256,1024]{1,0:T(8,128)(2,1)}, f32[8,256,2]{2,1,0:T(8,128)}) custom-call(bf16[256,1024]{1,0:T(8,128)(2,1)} %copy-done.1, bf16[8,2,128,1024]{3,2,1,0:T(8,128)(2,1)} %all-to-all-done.1.kp_ref.vp_ref, bf16[8,2,128,1024]{3,2,1,0:T(8,128)(2,1)} %all-to-all-done.1.kp_ref.vp_ref, s32[1,1024]{1,0:T(1,128)} %bitcast.33), custom_call_target="tpu_custom_call" | custom-call | tf_op jit(solution)/shard_map/pallas_call | solution.py:154
  298.3 1.5 copy.15
  299.8 2.3 collective-permute-start.2
  302.2 0.7 fusion.6
  302.8 0.9 copy.23
  303.8 5.1 %shard_map.83 = (f32[256,1024]{1,0:T(8,128)}, f32[8,256,2]{2,1,0:T(8,128)}) custom-call(bf16[256,1024]{1,0:T(8,128)(2,1)} %bitcast.23, bf16[256,1024]{1,0:T(8,128)(2,1)} %bitcast.27, bf16[256,1024]{1,0:T(8,128)(2,1)} %vl_ref.1), custom_call_target="tpu_custom_call" | custom-call | tf_op jit(solution)/shard_map/pallas_call | solution.py:137
  308.9 31.4 %collective-permute-done.2 = f32[8,256,2]{1,0,2:T(8,128)S(1)} collective-permute-done((f32[8,256,2]{1,0,2:T(8,128)S(1)}, f32[8,256,2]{1,0,2:T(8,128)S(1)}, u32[]{:S(2)}, u32[]{:S(2)}) %collective-permute-start.2) | collective-permute-done | bytes 16416 | tf_op jit(solution)/shard_map/ppermute | solution.py:292
  340.3 1.4 copy.16.bst_ref
  341.7 0.8 copy-done.2
  342.5 10.5 %shard_map.86.refs_0_ = bf16[256,1024]{1,0:T(8,128)(2,1)} custom-call(bf16[256,1024]{1,0:T(8,128)(2,1)} %bitcast.24, bf16[8,2,128,1024]{3,2,1,0:T(8,128)(2,1)} %all-to-all-done.kp_ref.vp_ref, bf16[8,2,128,1024]{3,2,1,0:T(8,128)(2,1)} %all-to-all-done.kp_ref.vp_ref, s32[1,1024]{1,0:T(1,128)} %bitcast.32, f32[256,1024]{1,0:T(8,128)} %get-tuple-element.13.la_ref, ...), custom_call_target="tpu_custom_call" | custom-call | tf_op jit(solution)/shard_map/pallas_call | solution.py:171
  353.0 2.6 collective-permute-start.3
  356.2 1.1 collective-permute-done.3.refs_1_
  357.4 0.8 copy-done.3
  358.2 6.9 %shard_map.87 = bf16[256,2048]{1,0:T(8,128)(2,1)} custom-call(bf16[256,1024]{1,0:T(8,128)(2,1)} %shard_map.86.refs_0_, bf16[256,1024]{1,0:T(8,128)(2,1)} %copy-done.3, bf16[1024,2048]{1,0:T(8,128)(2,1)} %get-tuple-element.23.refs_2_, bf16[1024,2048]{1,0:T(8,128)(2,1)} %collective-permute-done.4.refs_3_, bf16[1,2048]{1,0:T(2,128)(2,1)} %reshape.161.refs_4_), custom_call_target="tpu_custom_call" | custom-call | tf_op jit(solution)/shard_map/pallas_call | solution.py:195
  (40 shorter events, 4.1 us)
Async XLA Ops:
  130.9 4.8 %copy-start.7 = (s32[16]{0:T(128)S(1)}, s32[16]{0:T(128)}, u32[]{:S(2)}) copy-start(s32[16]{0:T(128)} %param.15) | copy-start | bytes 196
  130.9 6.4 %copy-start.4 = (bf16[256,1024]{1,0:T(8,128)(2,1)S(1)}, bf16[256,1024]{1,0:T(8,128)(2,1)}, u32[]{:S(2)}) copy-start(bf16[256,1024]{1,0:T(8,128)(2,1)} %param.10) | copy-start | bytes 1572868
  130.9 6.5 %copy-start.5 = (bf16[256,1024]{1,0:T(8,128)(2,1)S(1)}, bf16[256,1024]{1,0:T(8,128)(2,1)}, u32[]{:S(2)}) copy-start(bf16[256,1024]{1,0:T(8,128)(2,1)} %param.11) | copy-start | bytes 1572868
  130.9 141.7 %all-to-all-start.1 = ((bf16[8,2,128,1024]{3,2,1,0:T(8,128)(2,1)}), bf16[8,2,128,1024]{3,2,1,0:T(8,128)(2,1)}, u32[]{:S(2)}, u32[]{:S(2)}) async-start(bf16[8,2,128,1024]{3,2,1,0:T(8,128)(2,1)} %shard_map.84), calls=%async_computation.1 | async-start | bytes 8388608 | tf_op jit(solution)/shard_map/all_to_all | solution.py:279
  140.1 132.5 %copy-start = (bf16[32,8,8,128]{3,1,2,0:T(8,128)(2,1)}, bf16[32,8,8,128]{3,1,2,0:T(8,128)(2,1)S(1)}, u32[]{:S(2)}) copy-start(bf16[32,8,8,128]{3,1,2,0:T(8,128)(2,1)S(1)} %copy.24) | copy-start | bytes 1572868
  140.1 132.5 %collective-permute-start = (bf16[256,1024]{1,0:T(8,128)(2,1)S(1)}, bf16[256,1024]{1,0:T(8,128)(2,1)S(1)}, u32[]{:S(2)}, u32[]{:S(2)}) collective-permute-start(bf16[256,1024]{1,0:T(8,128)(2,1)S(1)} %bitcast.22), channel_id=1, source_target_pairs={{0,16},{16,0},{1,17},{17,1},{2,18},{18,2},{3,19},{19,3},{4,20},{20... | collective-permute-start | bytes 1572872 | tf_op jit(solution)/shard_map/ppermute | solution.py:276
  272.6 0.8 copy-start.1
  273.4 68.3 %all-to-all-start = ((bf16[8,2,128,1024]{3,2,1,0:T(8,128)(2,1)}), bf16[8,2,128,1024]{3,2,1,0:T(8,128)(2,1)}, u32[]{:S(2)}, u32[]{:S(2)}) async-start(bf16[8,2,128,1024]{3,2,1,0:T(8,128)(2,1)} %shard_map.82), calls=%async_computation | async-start | bytes 8388608 | tf_op jit(solution)/shard_map/all_to_all | solution.py:282
  286.3 69.9 %collective-permute-start.4 = (bf16[1024,2048]{1,0:T(8,128)(2,1)}, bf16[1024,2048]{1,0:T(8,128)(2,1)}, u32[]{:S(2)}, u32[]{:S(2)}) collective-permute-start(bf16[1024,2048]{1,0:T(8,128)(2,1)} %get-tuple-element.22), channel_id=1, source_target_pairs={{0,1},{1,0},{2,3},{3,2},{4,5},{5,4},{6,7},{7,6},{8,9},{9,8},{10,11... | collective-permute-start | bytes 12582920 | tf_op jit(solution)/shard_map/ppermute | solution.py:265
  297.6 44.1 %collective-permute-start.1 = (bf16[256,1024]{1,0:T(8,128)(2,1)}, bf16[256,1024]{1,0:T(8,128)(2,1)S(1)}, u32[]{:S(2)}, u32[]{:S(2)}) collective-permute-start(bf16[256,1024]{1,0:T(8,128)(2,1)} %get-tuple-element.16), channel_id=1, source_target_pairs={{0,16},{16,0},{1,17},{17,1},{2,18},{18,2},{3,19},{19,3},{4,20},{20... | collective-permute-start | bytes 1572872 | tf_op jit(solution)/shard_map/ppermute | solution.py:291
  299.8 40.5 %collective-permute-start.2 = (f32[8,256,2]{1,0,2:T(8,128)S(1)}, f32[8,256,2]{1,0,2:T(8,128)S(1)}, u32[]{:S(2)}, u32[]{:S(2)}) collective-permute-start(f32[8,256,2]{1,0,2:T(8,128)S(1)} %copy.15), channel_id=1, source_target_pairs={{0,16},{16,0},{1,17},{17,1},{2,18},{18,2},{3,19},{19,3},{4,20},{20... | collective-permute-start | bytes 49160 | tf_op jit(solution)/shard_map/ppermute | solution.py:292
  341.7 0.8 copy-start.2
  342.5 13.1 %copy-start.6 = (bf16[2048]{0:T(1024)(128)(2,1)S(1)}, bf16[2048]{0:T(1024)(128)(2,1)}, u32[]{:S(2)}) copy-start(bf16[2048]{0:T(1024)(128)(2,1)} %param.17) | copy-start | bytes 12292
  353.0 4.4 %collective-permute-start.3 = (bf16[256,1024]{1,0:T(8,128)(2,1)}, bf16[256,1024]{1,0:T(8,128)(2,1)S(1)}, u32[]{:S(2)}, u32[]{:S(2)}) collective-permute-start(bf16[256,1024]{1,0:T(8,128)(2,1)} %shard_map.86.refs_0_), channel_id=1, source_target_pairs={{0,1},{1,0},{2,3},{3,2},{4,5},{5,4},{6,7},{7,6},{8,9},{9,8},{10,11... | collective-permute-start | bytes 1572872 | tf_op jit(solution)/shard_map/ppermute | solution.py:300
  357.3 0.8 copy-start.3

commit v17 on v13

--- a/solution.py
+++ b/solution.py
@@ -188,7 +188,7 @@
 def project(parts, weights, bias):
     span, rows = parts[0].shape
     out_cols = weights[0].shape[1]
-    block = 512 if out_cols % 512 == 0 else out_cols
+    block = 1024 if out_cols % 1024 == 0 else out_cols
     a_spec = pl.BlockSpec((span, rows), lambda c: (0, 0))
     w_spec = pl.BlockSpec((rows, block), lambda c: (0, c))
     b_spec = pl.BlockSpec((1, block), lambda c: (0, c))

time: 171 us -> 171 us (level)
  no operation moved by 1% of the time
where the time goes in v17:
time: 171 us; the launch traced here: 170 us
  waiting for transfers between devices  85.1 us (50%)
  local copies, waits for them, and re-layouts  29.6 us (17%)
  Pallas kernels  28.8 us (17%)
  starting transfers between devices  19.1 us (11%)
  other arithmetic  7.35 us (4%)
    ppermute x1, waiting for transfers between devices, on_device(): partner_query = lax.ppermute(query_rot, 'half', swap)  51.4 us
    ppermute x1, waiting for transfers between devices, on_device(): back_stats = lax.ppermute(far_stats, 'half', swap)  32.6 us
    pallas_call x1, Pallas kernels, near_attend(): pl.pallas_call(near_kernel, grid=(head_count // group,), in_specs=[col_sp...  10.5 us
    dynamic_slice x1, local copies, waits for them, and re-layouts, on_device(): piece = lax.dynamic_slice_in_dim(w_out, target * out_cols, out_cols, axis=1)  8.35 us
    pallas_call x1, Pallas kernels, far_attend(): pl.pallas_call(far_kernel, grid=(head_count // group,), in_specs=[col_spe...  6.81 us
    pallas_call x1, Pallas kernels, project(): pl.pallas_call(projection_kernel, grid=(out_cols // block,), in_specs=[a_...  6.39 us
    gather x1, local copies, waits for them, and re-layouts, on_device(): jnp.take(kv_pages, jnp.take(local_page, (1 - half) * sub_count + dest), a...  6.14 us
    gather x1, local copies, waits for them, and re-layouts, on_device(): jnp.take(kv_pages, jnp.take(local_page, half * sub_count + dest), axis=0,...  6.14 us
  transfers between devices with their start and end apart: 7, of which 3 were waited for; matrix products, arithmetic and copies ran while one was open for 16% of the time, Pallas kernels for 13%

profile of v17, /device:TPU:11, one launch (start us, length us, event | category | flops | bytes accessed | tf_op | source)
XLA Modules:
  0.0 170.1 jit_solution(8329125315480127680)
XLA Ops:
  0.0 0.8 select_reduce_fusion
  0.8 0.6 gather_fusion.3
  1.5 6.1 %gather_fusion.1 = bf16[8,2,128,1024]{3,2,1,0:T(8,128)(2,1)} fusion(bf16[16,2,128,1024]{3,2,1,0:T(8,128)(2,1)} %param.13, s32[1024]{0:T(1024)S(1)} %pad_clamp_fusion), kind=kCustom, calls=%fused_computation.3 | custom fusion | bytes 8388640 | tf_op jit(solution)/shard_map/jit(_take)/gather | solution.py:251
  7.7 4.7 %all-to-all-start.1 = ((bf16[8,2,128,1024]{3,2,1,0:T(8,128)(2,1)}), bf16[8,2,128,1024]{3,2,1,0:T(8,128)(2,1)}, u32[]{:S(2)}, u32[]{:S(2)}) async-start(bf16[8,2,128,1024]{3,2,1,0:T(8,128)(2,1)} %gather_fusion.1), calls=%async_computation.1 | async-start | bytes 8388608 | tf_op jit(solution)/shard_map/all_to_all | solution.py:252
  12.4 0.7 fusion.10
  13.1 0.6 add_convert_fusion.2
  14.9 0.8 subtract_convert_fusion
  15.7 1.0 pad_maximum_fusion
  16.8 2.4 %collective-permute-start = (bf16[256,1024]{1,0:T(8,128)(2,1)S(1)}, bf16[256,1024]{1,0:T(8,128)(2,1)S(1)}, u32[]{:S(2)}, u32[]{:S(2)}) collective-permute-start(bf16[256,1024]{1,0:T(8,128)(2,1)S(1)} %bitcast.22), channel_id=1, source_target_pairs={{0,16},{16,0},{1,17},{17,1},{2,18},{18,2},{3,19},{19,3},{4,20},{20... | collective-permute-start | bytes 1572872 | tf_op jit(solution)/shard_map/ppermute | solution.py:249
  19.2 0.6 gather_fusion.2
  19.9 6.1 %gather_fusion = bf16[8,2,128,1024]{3,2,1,0:T(8,128)(2,1)} fusion(bf16[16,2,128,1024]{3,2,1,0:T(8,128)(2,1)} %param.13, s32[1024]{0:T(1024)S(1)} %pad_clamp_fusion.2), kind=kCustom, calls=%fused_computation.2 | custom fusion | bytes 8388640 | tf_op jit(solution)/shard_map/jit(_take)/gather | solution.py:253
  26.0 51.4 %collective-permute-done.q_ref = bf16[256,1024]{1,0:T(8,128)(2,1)S(1)} collective-permute-done((bf16[256,1024]{1,0:T(8,128)(2,1)S(1)}, bf16[256,1024]{1,0:T(8,128)(2,1)S(1)}, u32[]{:S(2)}, u32[]{:S(2)}) %collective-permute-start) | collective-permute-done | bytes 524320 | tf_op jit(solution)/shard_map/ppermute | solution.py:249
  77.4 5.1 %all-to-all-start = ((bf16[8,2,128,1024]{3,2,1,0:T(8,128)(2,1)}), bf16[8,2,128,1024]{3,2,1,0:T(8,128)(2,1)}, u32[]{:S(2)}, u32[]{:S(2)}) async-start(bf16[8,2,128,1024]{3,2,1,0:T(8,128)(2,1)} %gather_fusion), calls=%async_computation | async-start | bytes 8388608 | tf_op jit(solution)/shard_map/all_to_all | solution.py:255
  82.5 8.3 %constant_dynamic-slice_fusion.3 = (bf16[1024,2048]{1,0:T(8,128)(2,1)}, bf16[1024,2048]{1,0:T(8,128)(2,1)}) fusion(bf16[1024,4096]{1,0:T(8,128)(2,1)} %param.16, s32[]{:T(128)S(6)} %select_n.98, s32[]{:T(128)S(6)} %select_n.96), kind=kLoop, calls=%fused_computation.56 | loop fusion | bytes 16777224 | tf_op jit(solution)/shard_map/dynamic_slice | solution.py:236
  90.8 2.1 %collective-permute-start.4 = (bf16[1024,2048]{1,0:T(8,128)(2,1)}, bf16[1024,2048]{1,0:T(8,128)(2,1)}, u32[]{:S(2)}, u32[]{:S(2)}) collective-permute-start(bf16[1024,2048]{1,0:T(8,128)(2,1)} %get-tuple-element.22), channel_id=1, source_target_pairs={{0,1},{1,0},{2,3},{3,2},{4,5},{5,4},{6,7},{7,6},{8,9},{9,8},{10,11... | collective-permute-start | bytes 12582920 | tf_op jit(solution)/shard_map/ppermute | solution.py:238
  92.9 0.7 fusion.8
  94.0 0.7 clamp_select_fusion
  94.7 0.7 fusion.7
  95.3 6.8 %shard_map.83 = (bf16[256,1024]{1,0:T(8,128)(2,1)}, f32[8,256,2]{2,1,0:T(8,128)}) custom-call(bf16[256,1024]{1,0:T(8,128)(2,1)} %copy-done.1, bf16[8,2,128,1024]{3,2,1,0:T(8,128)(2,1)} %all-to-all-done.1.kp_ref.vp_ref, bf16[8,2,128,1024]{3,2,1,0:T(8,128)(2,1)} %all-to-all-done.1.kp_ref.vp_ref, s32[1,1024]{1,0:T(1,128)} %bitcast.33), custom_call_target="tpu_custom_call" | custom-call | tf_op jit(solution)/shard_map/pallas_call | solution.py:154
  103.3 1.5 copy.15
  104.9 1.8 %collective-permute-start.2 = (f32[8,256,2]{1,0,2:T(8,128)S(1)}, f32[8,256,2]{1,0,2:T(8,128)S(1)}, u32[]{:S(2)}, u32[]{:S(2)}) collective-permute-start(f32[8,256,2]{1,0,2:T(8,128)S(1)} %copy.15), channel_id=1, source_target_pairs={{0,16},{16,0},{1,17},{17,1},{2,18},{18,2},{3,19},{19,3},{4,20},{20... | collective-permute-start | bytes 49160 | tf_op jit(solution)/shard_map/ppermute | solution.py:265
  106.7 0.7 fusion.6
  107.4 0.9 copy.23
  108.3 5.1 %shard_map.82 = (f32[256,1024]{1,0:T(8,128)}, f32[8,256,2]{2,1,0:T(8,128)}) custom-call(bf16[256,1024]{1,0:T(8,128)(2,1)} %bitcast.23, bf16[256,1024]{1,0:T(8,128)(2,1)} %bitcast.27, bf16[256,1024]{1,0:T(8,128)(2,1)} %vl_ref.1), custom_call_target="tpu_custom_call" | custom-call | tf_op jit(solution)/shard_map/pallas_call | solution.py:137
  113.4 32.6 %collective-permute-done.2 = f32[8,256,2]{1,0,2:T(8,128)S(1)} collective-permute-done((f32[8,256,2]{1,0,2:T(8,128)S(1)}, f32[8,256,2]{1,0,2:T(8,128)S(1)}, u32[]{:S(2)}, u32[]{:S(2)}) %collective-permute-start.2) | collective-permute-done | bytes 16416 | tf_op jit(solution)/shard_map/ppermute | solution.py:265
  146.0 1.4 copy.16.bst_ref
  147.4 0.8 copy-done.2
  148.2 10.5 %shard_map.84.refs_0_ = bf16[256,1024]{1,0:T(8,128)(2,1)} custom-call(bf16[256,1024]{1,0:T(8,128)(2,1)} %bitcast.24, bf16[8,2,128,1024]{3,2,1,0:T(8,128)(2,1)} %all-to-all-done.kp_ref.vp_ref, bf16[8,2,128,1024]{3,2,1,0:T(8,128)(2,1)} %all-to-all-done.kp_ref.vp_ref, s32[1,1024]{1,0:T(1,128)} %bitcast.32, f32[256,1024]{1,0:T(8,128)} %get-tuple-element.13.la_ref, ...), custom_call_target="tpu_custom_call" | custom-call | tf_op jit(solution)/shard_map/pallas_call | solution.py:171
  158.7 2.4 %collective-permute-start.3 = (bf16[256,1024]{1,0:T(8,128)(2,1)}, bf16[256,1024]{1,0:T(8,128)(2,1)S(1)}, u32[]{:S(2)}, u32[]{:S(2)}) collective-permute-start(bf16[256,1024]{1,0:T(8,128)(2,1)} %shard_map.84.refs_0_), channel_id=1, source_target_pairs={{0,1},{1,0},{2,3},{3,2},{4,5},{5,4},{6,7},{7,6},{8,9},{9,8},{10,11... | collective-permute-start | bytes 1572872 | tf_op jit(solution)/shard_map/ppermute | solution.py:273
  161.7 1.1 collective-permute-done.3.refs_1_
  162.8 0.8 copy-done.3
  163.7 6.4 %shard_map.85 = bf16[256,2048]{1,0:T(8,128)(2,1)} custom-call(bf16[256,1024]{1,0:T(8,128)(2,1)} %shard_map.84.refs_0_, bf16[256,1024]{1,0:T(8,128)(2,1)} %copy-done.3, bf16[1024,2048]{1,0:T(8,128)(2,1)} %get-tuple-element.23.refs_2_, bf16[1024,2048]{1,0:T(8,128)(2,1)} %collective-permute-done.4.refs_3_, bf16[1,2048]{1,0:T(2,128)(2,1)} %reshape.161.refs_4_), custom_call_target="tpu_custom_call" | custom-call | tf_op jit(solution)/shard_map/pallas_call | solution.py:195
  (42 shorter events, 3.5 us)
Async XLA Ops:
  7.7 4.7 %copy-start.7 = (s32[16]{0:T(128)S(1)}, s32[16]{0:T(128)}, u32[]{:S(2)}) copy-start(s32[16]{0:T(128)} %param.15) | copy-start | bytes 196
  7.7 6.4 %copy-start.4 = (bf16[256,1024]{1,0:T(8,128)(2,1)S(1)}, bf16[256,1024]{1,0:T(8,128)(2,1)}, u32[]{:S(2)}) copy-start(bf16[256,1024]{1,0:T(8,128)(2,1)} %param.10) | copy-start | bytes 1572868
  7.7 6.5 %copy-start.5 = (bf16[256,1024]{1,0:T(8,128)(2,1)S(1)}, bf16[256,1024]{1,0:T(8,128)(2,1)}, u32[]{:S(2)}) copy-start(bf16[256,1024]{1,0:T(8,128)(2,1)} %param.11) | copy-start | bytes 1572868
  7.7 69.8 %all-to-all-start.1 = ((bf16[8,2,128,1024]{3,2,1,0:T(8,128)(2,1)}), bf16[8,2,128,1024]{3,2,1,0:T(8,128)(2,1)}, u32[]{:S(2)}, u32[]{:S(2)}) async-start(bf16[8,2,128,1024]{3,2,1,0:T(8,128)(2,1)} %gather_fusion.1), calls=%async_computation.1 | async-start | bytes 8388608 | tf_op jit(solution)/shard_map/all_to_all | solution.py:252
  16.8 9.2 %copy-start = (bf16[32,8,8,128]{3,1,2,0:T(8,128)(2,1)}, bf16[32,8,8,128]{3,1,2,0:T(8,128)(2,1)S(1)}, u32[]{:S(2)}) copy-start(bf16[32,8,8,128]{3,1,2,0:T(8,128)(2,1)S(1)} %copy.24) | copy-start | bytes 1572868
  16.8 60.6 %collective-permute-start = (bf16[256,1024]{1,0:T(8,128)(2,1)S(1)}, bf16[256,1024]{1,0:T(8,128)(2,1)S(1)}, u32[]{:S(2)}, u32[]{:S(2)}) collective-permute-start(bf16[256,1024]{1,0:T(8,128)(2,1)S(1)} %bitcast.22), channel_id=1, source_target_pairs={{0,16},{16,0},{1,17},{17,1},{2,18},{18,2},{3,19},{19,3},{4,20},{20... | collective-permute-start | bytes 1572872 | tf_op jit(solution)/shard_map/ppermute | solution.py:249
  77.4 5.1 %copy-start.1 = (bf16[256,1024]{1,0:T(8,128)(2,1)}, bf16[256,1024]{1,0:T(8,128)(2,1)S(1)}, u32[]{:S(2)}) copy-start(bf16[256,1024]{1,0:T(8,128)(2,1)S(1)} %collective-permute-done.q_ref) | copy-start | bytes 1572868
  77.4 70.0 %all-to-all-start = ((bf16[8,2,128,1024]{3,2,1,0:T(8,128)(2,1)}), bf16[8,2,128,1024]{3,2,1,0:T(8,128)(2,1)}, u32[]{:S(2)}, u32[]{:S(2)}) async-start(bf16[8,2,128,1024]{3,2,1,0:T(8,128)(2,1)} %gather_fusion), calls=%async_computation | async-start | bytes 8388608 | tf_op jit(solution)/shard_map/all_to_all | solution.py:255
  90.8 70.9 %collective-permute-start.4 = (bf16[1024,2048]{1,0:T(8,128)(2,1)}, bf16[1024,2048]{1,0:T(8,128)(2,1)}, u32[]{:S(2)}, u32[]{:S(2)}) collective-permute-start(bf16[1024,2048]{1,0:T(8,128)(2,1)} %get-tuple-element.22), channel_id=1, source_target_pairs={{0,1},{1,0},{2,3},{3,2},{4,5},{5,4},{6,7},{7,6},{8,9},{9,8},{10,11... | collective-permute-start | bytes 12582920 | tf_op jit(solution)/shard_map/ppermute | solution.py:238
  102.1 45.3 %collective-permute-start.1 = (bf16[256,1024]{1,0:T(8,128)(2,1)}, bf16[256,1024]{1,0:T(8,128)(2,1)S(1)}, u32[]{:S(2)}, u32[]{:S(2)}) collective-permute-start(bf16[256,1024]{1,0:T(8,128)(2,1)} %get-tuple-element.16), channel_id=1, source_target_pairs={{0,16},{16,0},{1,17},{17,1},{2,18},{18,2},{3,19},{19,3},{4,20},{20... | collective-permute-start | bytes 1572872 | tf_op jit(solution)/shard_map/ppermute | solution.py:264
  104.9 41.1 %collective-permute-start.2 = (f32[8,256,2]{1,0,2:T(8,128)S(1)}, f32[8,256,2]{1,0,2:T(8,128)S(1)}, u32[]{:S(2)}, u32[]{:S(2)}) collective-permute-start(f32[8,256,2]{1,0,2:T(8,128)S(1)} %copy.15), channel_id=1, source_target_pairs={{0,16},{16,0},{1,17},{17,1},{2,18},{18,2},{3,19},{19,3},{4,20},{20... | collective-permute-start | bytes 49160 | tf_op jit(solution)/shard_map/ppermute | solution.py:265
  147.4 0.8 copy-start.2
  148.2 12.9 %copy-start.6 = (bf16[2048]{0:T(1024)(128)(2,1)S(1)}, bf16[2048]{0:T(1024)(128)(2,1)}, u32[]{:S(2)}) copy-start(bf16[2048]{0:T(1024)(128)(2,1)} %param.17) | copy-start | bytes 12292
  158.7 4.2 %collective-permute-start.3 = (bf16[256,1024]{1,0:T(8,128)(2,1)}, bf16[256,1024]{1,0:T(8,128)(2,1)S(1)}, u32[]{:S(2)}, u32[]{:S(2)}) collective-permute-start(bf16[256,1024]{1,0:T(8,128)(2,1)} %shard_map.84.refs_0_), channel_id=1, source_target_pairs={{0,1},{1,0},{2,3},{3,2},{4,5},{5,4},{6,7},{7,6},{8,9},{9,8},{10,11... | collective-permute-start | bytes 1572872 | tf_op jit(solution)/shard_map/ppermute | solution.py:273
  162.8 0.8 copy-start.3

commit v18 on v17

--- a/solution.py
+++ b/solution.py
@@ -114,7 +114,10 @@
 
 
 def heads_per_step(head_count):
-    return 2 if head_count % 2 == 0 else 1
+    for group in (4, 2):
+        if head_count % group == 0:
+            return group
+    return 1
 
 
 def head_specs(span, block_count, page_size, group):

time: 171 us -> 171 us (level)
  transfers between devices with their start and end apart: 7 -> 7, of which waited for: 3 -> 3; matrix products, arithmetic and copies ran while one was open for 16% -> 16% of each run, Pallas kernels for 13% -> 12%
where the time goes in v18:
time: 171 us; the launch traced here: 170 us
  waiting for transfers between devices  86.6 us (51%)
  local copies, waits for them, and re-layouts  29.6 us (17%)
  Pallas kernels  27.4 us (16%)
  starting transfers between devices  19.1 us (11%)
  other arithmetic  7.35 us (4%)
    ppermute x1, waiting for transfers between devices, on_device(): partner_query = lax.ppermute(query_rot, 'half', swap)  51.4 us
    ppermute x1, waiting for transfers between devices, on_device(): back_stats = lax.ppermute(far_stats, 'half', swap)  34.1 us
    pallas_call x1, Pallas kernels, near_attend(): pl.pallas_call(near_kernel, grid=(head_count // group,), in_specs=[col_sp...  10.5 us
    dynamic_slice x1, local copies, waits for them, and re-layouts, on_device(): piece = lax.dynamic_slice_in_dim(w_out, target * out_cols, out_cols, axis=1)  8.35 us
    pallas_call x1, Pallas kernels, far_attend(): pl.pallas_call(far_kernel, grid=(head_count // group,), in_specs=[col_spe...  6.75 us
    pallas_call x1, Pallas kernels, project(): pl.pallas_call(projection_kernel, grid=(out_cols // block,), in_specs=[a_...  6.39 us
    gather x1, local copies, waits for them, and re-layouts, on_device(): jnp.take(kv_pages, jnp.take(local_page, (1 - half) * sub_count + dest), a...  6.14 us
    gather x1, local copies, waits for them, and re-layouts, on_device(): jnp.take(kv_pages, jnp.take(local_page, half * sub_count + dest), axis=0,...  6.14 us
  transfers between devices with their start and end apart: 7, of which 3 were waited for; matrix products, arithmetic and copies ran while one was open for 16% of the time, Pallas kernels for 12%

profile of v18, /device:TPU:11, one launch (start us, length us, event | category | flops | bytes accessed | tf_op | source)
XLA Modules:
  0.0 170.2 jit_solution(16618784563045932796)
XLA Ops:
  0.0 0.8 select_reduce_fusion
  0.8 0.6 gather_fusion.3
  1.5 6.1 %gather_fusion.1 = bf16[8,2,128,1024]{3,2,1,0:T(8,128)(2,1)} fusion(bf16[16,2,128,1024]{3,2,1,0:T(8,128)(2,1)} %param.13, s32[1024]{0:T(1024)S(1)} %pad_clamp_fusion), kind=kCustom, calls=%fused_computation.3 | custom fusion | bytes 8388640 | tf_op jit(solution)/shard_map/jit(_take)/gather | solution.py:254
  7.7 4.7 %all-to-all-start.1 = ((bf16[8,2,128,1024]{3,2,1,0:T(8,128)(2,1)}), bf16[8,2,128,1024]{3,2,1,0:T(8,128)(2,1)}, u32[]{:S(2)}, u32[]{:S(2)}) async-start(bf16[8,2,128,1024]{3,2,1,0:T(8,128)(2,1)} %gather_fusion.1), calls=%async_computation.1 | async-start | bytes 8388608 | tf_op jit(solution)/shard_map/all_to_all | solution.py:255
  12.4 0.7 fusion.10
  13.1 0.6 add_convert_fusion.2
  14.9 0.8 subtract_convert_fusion
  15.7 1.0 pad_maximum_fusion
  16.8 2.4 %collective-permute-start = (bf16[256,1024]{1,0:T(8,128)(2,1)S(1)}, bf16[256,1024]{1,0:T(8,128)(2,1)S(1)}, u32[]{:S(2)}, u32[]{:S(2)}) collective-permute-start(bf16[256,1024]{1,0:T(8,128)(2,1)S(1)} %bitcast.22), channel_id=1, source_target_pairs={{0,16},{16,0},{1,17},{17,1},{2,18},{18,2},{3,19},{19,3},{4,20},{20... | collective-permute-start | bytes 1572872 | tf_op jit(solution)/shard_map/ppermute | solution.py:252
  19.2 0.6 gather_fusion.2
  19.9 6.1 %gather_fusion = bf16[8,2,128,1024]{3,2,1,0:T(8,128)(2,1)} fusion(bf16[16,2,128,1024]{3,2,1,0:T(8,128)(2,1)} %param.13, s32[1024]{0:T(1024)S(1)} %pad_clamp_fusion.2), kind=kCustom, calls=%fused_computation.2 | custom fusion | bytes 8388640 | tf_op jit(solution)/shard_map/jit(_take)/gather | solution.py:256
  26.0 51.4 %collective-permute-done.q_ref = bf16[256,1024]{1,0:T(8,128)(2,1)S(1)} collective-permute-done((bf16[256,1024]{1,0:T(8,128)(2,1)S(1)}, bf16[256,1024]{1,0:T(8,128)(2,1)S(1)}, u32[]{:S(2)}, u32[]{:S(2)}) %collective-permute-start) | collective-permute-done | bytes 524320 | tf_op jit(solution)/shard_map/ppermute | solution.py:252
  77.4 5.1 %all-to-all-start = ((bf16[8,2,128,1024]{3,2,1,0:T(8,128)(2,1)}), bf16[8,2,128,1024]{3,2,1,0:T(8,128)(2,1)}, u32[]{:S(2)}, u32[]{:S(2)}) async-start(bf16[8,2,128,1024]{3,2,1,0:T(8,128)(2,1)} %gather_fusion), calls=%async_computation | async-start | bytes 8388608 | tf_op jit(solution)/shard_map/all_to_all | solution.py:258
  82.5 8.3 %constant_dynamic-slice_fusion.3 = (bf16[1024,2048]{1,0:T(8,128)(2,1)}, bf16[1024,2048]{1,0:T(8,128)(2,1)}) fusion(bf16[1024,4096]{1,0:T(8,128)(2,1)} %param.16, s32[]{:T(128)S(6)} %select_n.98, s32[]{:T(128)S(6)} %select_n.96), kind=kLoop, calls=%fused_computation.56 | loop fusion | bytes 16777224 | tf_op jit(solution)/shard_map/dynamic_slice | solution.py:239
  90.8 2.1 %collective-permute-start.4 = (bf16[1024,2048]{1,0:T(8,128)(2,1)}, bf16[1024,2048]{1,0:T(8,128)(2,1)}, u32[]{:S(2)}, u32[]{:S(2)}) collective-permute-start(bf16[1024,2048]{1,0:T(8,128)(2,1)} %get-tuple-element.22), channel_id=1, source_target_pairs={{0,1},{1,0},{2,3},{3,2},{4,5},{5,4},{6,7},{7,6},{8,9},{9,8},{10,11... | collective-permute-start | bytes 12582920 | tf_op jit(solution)/shard_map/ppermute | solution.py:241
  92.9 0.7 fusion.8
  94.0 0.7 clamp_select_fusion
  94.7 0.7 fusion.7
  95.3 6.8 %shard_map.83 = (bf16[256,1024]{1,0:T(8,128)(2,1)}, f32[8,256,2]{2,1,0:T(8,128)}) custom-call(bf16[256,1024]{1,0:T(8,128)(2,1)} %copy-done.1, bf16[8,2,128,1024]{3,2,1,0:T(8,128)(2,1)} %all-to-all-done.1.kp_ref.vp_ref, bf16[8,2,128,1024]{3,2,1,0:T(8,128)(2,1)} %all-to-all-done.1.kp_ref.vp_ref, s32[1,1024]{1,0:T(1,128)} %bitcast.33), custom_call_target="tpu_custom_call" | custom-call | tf_op jit(solution)/shard_map/pallas_call | solution.py:157
  103.3 1.5 copy.15
  104.8 1.8 %collective-permute-start.2 = (f32[8,256,2]{1,0,2:T(8,128)S(1)}, f32[8,256,2]{1,0,2:T(8,128)S(1)}, u32[]{:S(2)}, u32[]{:S(2)}) collective-permute-start(f32[8,256,2]{1,0,2:T(8,128)S(1)} %copy.15), channel_id=1, source_target_pairs={{0,16},{16,0},{1,17},{17,1},{2,18},{18,2},{3,19},{19,3},{4,20},{20... | collective-permute-start | bytes 49160 | tf_op jit(solution)/shard_map/ppermute | solution.py:268
  106.7 0.7 fusion.6
  107.3 0.9 copy.23
  108.3 3.8 %shard_map.82 = (f32[256,1024]{1,0:T(8,128)}, f32[8,256,2]{2,1,0:T(8,128)}) custom-call(bf16[256,1024]{1,0:T(8,128)(2,1)} %bitcast.23, bf16[256,1024]{1,0:T(8,128)(2,1)} %bitcast.27, bf16[256,1024]{1,0:T(8,128)(2,1)} %vl_ref.1), custom_call_target="tpu_custom_call" | custom-call | tf_op jit(solution)/shard_map/pallas_call | solution.py:140
  112.0 34.1 %collective-permute-done.2 = f32[8,256,2]{1,0,2:T(8,128)S(1)} collective-permute-done((f32[8,256,2]{1,0,2:T(8,128)S(1)}, f32[8,256,2]{1,0,2:T(8,128)S(1)}, u32[]{:S(2)}, u32[]{:S(2)}) %collective-permute-start.2) | collective-permute-done | bytes 16416 | tf_op jit(solution)/shard_map/ppermute | solution.py:268
  146.1 1.4 copy.16.bst_ref
  147.5 0.8 copy-done.2
  148.3 10.5 %shard_map.84.refs_0_ = bf16[256,1024]{1,0:T(8,128)(2,1)} custom-call(bf16[256,1024]{1,0:T(8,128)(2,1)} %bitcast.24, bf16[8,2,128,1024]{3,2,1,0:T(8,128)(2,1)} %all-to-all-done.kp_ref.vp_ref, bf16[8,2,128,1024]{3,2,1,0:T(8,128)(2,1)} %all-to-all-done.kp_ref.vp_ref, s32[1,1024]{1,0:T(1,128)} %bitcast.32, f32[256,1024]{1,0:T(8,128)} %get-tuple-element.13.la_ref, ...), custom_call_target="tpu_custom_call" | custom-call | tf_op jit(solution)/shard_map/pallas_call | solution.py:174
  158.8 2.4 %collective-permute-start.3 = (bf16[256,1024]{1,0:T(8,128)(2,1)}, bf16[256,1024]{1,0:T(8,128)(2,1)S(1)}, u32[]{:S(2)}, u32[]{:S(2)}) collective-permute-start(bf16[256,1024]{1,0:T(8,128)(2,1)} %shard_map.84.refs_0_), channel_id=1, source_target_pairs={{0,1},{1,0},{2,3},{3,2},{4,5},{5,4},{6,7},{7,6},{8,9},{9,8},{10,11... | collective-permute-start | bytes 1572872 | tf_op jit(solution)/shard_map/ppermute | solution.py:276
  161.8 1.1 collective-permute-done.3.refs_1_
  162.9 0.8 copy-done.3
  163.8 6.4 %shard_map.85 = bf16[256,2048]{1,0:T(8,128)(2,1)} custom-call(bf16[256,1024]{1,0:T(8,128)(2,1)} %shard_map.84.refs_0_, bf16[256,1024]{1,0:T(8,128)(2,1)} %copy-done.3, bf16[1024,2048]{1,0:T(8,128)(2,1)} %get-tuple-element.23.refs_2_, bf16[1024,2048]{1,0:T(8,128)(2,1)} %collective-permute-done.4.refs_3_, bf16[1,2048]{1,0:T(2,128)(2,1)} %reshape.161.refs_4_), custom_call_target="tpu_custom_call" | custom-call | tf_op jit(solution)/shard_map/pallas_call | solution.py:198
  (42 shorter events, 3.5 us)
Async XLA Ops:
  7.7 4.7 %copy-start.7 = (s32[16]{0:T(128)S(1)}, s32[16]{0:T(128)}, u32[]{:S(2)}) copy-start(s32[16]{0:T(128)} %param.15) | copy-start | bytes 196
  7.7 6.4 %copy-start.4 = (bf16[256,1024]{1,0:T(8,128)(2,1)S(1)}, bf16[256,1024]{1,0:T(8,128)(2,1)}, u32[]{:S(2)}) copy-start(bf16[256,1024]{1,0:T(8,128)(2,1)} %param.10) | copy-start | bytes 1572868
  7.7 6.5 %copy-start.5 = (bf16[256,1024]{1,0:T(8,128)(2,1)S(1)}, bf16[256,1024]{1,0:T(8,128)(2,1)}, u32[]{:S(2)}) copy-start(bf16[256,1024]{1,0:T(8,128)(2,1)} %param.11) | copy-start | bytes 1572868
  7.7 69.8 %all-to-all-start.1 = ((bf16[8,2,128,1024]{3,2,1,0:T(8,128)(2,1)}), bf16[8,2,128,1024]{3,2,1,0:T(8,128)(2,1)}, u32[]{:S(2)}, u32[]{:S(2)}) async-start(bf16[8,2,128,1024]{3,2,1,0:T(8,128)(2,1)} %gather_fusion.1), calls=%async_computation.1 | async-start | bytes 8388608 | tf_op jit(solution)/shard_map/all_to_all | solution.py:255
  16.8 9.2 %copy-start = (bf16[32,8,8,128]{3,1,2,0:T(8,128)(2,1)}, bf16[32,8,8,128]{3,1,2,0:T(8,128)(2,1)S(1)}, u32[]{:S(2)}) copy-start(bf16[32,8,8,128]{3,1,2,0:T(8,128)(2,1)S(1)} %copy.24) | copy-start | bytes 1572868
  16.8 60.6 %collective-permute-start = (bf16[256,1024]{1,0:T(8,128)(2,1)S(1)}, bf16[256,1024]{1,0:T(8,128)(2,1)S(1)}, u32[]{:S(2)}, u32[]{:S(2)}) collective-permute-start(bf16[256,1024]{1,0:T(8,128)(2,1)S(1)} %bitcast.22), channel_id=1, source_target_pairs={{0,16},{16,0},{1,17},{17,1},{2,18},{18,2},{3,19},{19,3},{4,20},{20... | collective-permute-start | bytes 1572872 | tf_op jit(solution)/shard_map/ppermute | solution.py:252
  77.4 5.1 %copy-start.1 = (bf16[256,1024]{1,0:T(8,128)(2,1)}, bf16[256,1024]{1,0:T(8,128)(2,1)S(1)}, u32[]{:S(2)}) copy-start(bf16[256,1024]{1,0:T(8,128)(2,1)S(1)} %collective-permute-done.q_ref) | copy-start | bytes 1572868
  77.4 70.1 %all-to-all-start = ((bf16[8,2,128,1024]{3,2,1,0:T(8,128)(2,1)}), bf16[8,2,128,1024]{3,2,1,0:T(8,128)(2,1)}, u32[]{:S(2)}, u32[]{:S(2)}) async-start(bf16[8,2,128,1024]{3,2,1,0:T(8,128)(2,1)} %gather_fusion), calls=%async_computation | async-start | bytes 8388608 | tf_op jit(solution)/shard_map/all_to_all | solution.py:258
  90.8 71.0 %collective-permute-start.4 = (bf16[1024,2048]{1,0:T(8,128)(2,1)}, bf16[1024,2048]{1,0:T(8,128)(2,1)}, u32[]{:S(2)}, u32[]{:S(2)}) collective-permute-start(bf16[1024,2048]{1,0:T(8,128)(2,1)} %get-tuple-element.22), channel_id=1, source_target_pairs={{0,1},{1,0},{2,3},{3,2},{4,5},{5,4},{6,7},{7,6},{8,9},{9,8},{10,11... | collective-permute-start | bytes 12582920 | tf_op jit(solution)/shard_map/ppermute | solution.py:241
  102.1 45.4 %collective-permute-start.1 = (bf16[256,1024]{1,0:T(8,128)(2,1)}, bf16[256,1024]{1,0:T(8,128)(2,1)S(1)}, u32[]{:S(2)}, u32[]{:S(2)}) collective-permute-start(bf16[256,1024]{1,0:T(8,128)(2,1)} %get-tuple-element.16), channel_id=1, source_target_pairs={{0,16},{16,0},{1,17},{17,1},{2,18},{18,2},{3,19},{19,3},{4,20},{20... | collective-permute-start | bytes 1572872 | tf_op jit(solution)/shard_map/ppermute | solution.py:267
  104.8 41.3 %collective-permute-start.2 = (f32[8,256,2]{1,0,2:T(8,128)S(1)}, f32[8,256,2]{1,0,2:T(8,128)S(1)}, u32[]{:S(2)}, u32[]{:S(2)}) collective-permute-start(f32[8,256,2]{1,0,2:T(8,128)S(1)} %copy.15), channel_id=1, source_target_pairs={{0,16},{16,0},{1,17},{17,1},{2,18},{18,2},{3,19},{19,3},{4,20},{20... | collective-permute-start | bytes 49160 | tf_op jit(solution)/shard_map/ppermute | solution.py:268
  147.5 0.8 copy-start.2
  148.3 12.9 %copy-start.6 = (bf16[2048]{0:T(1024)(128)(2,1)S(1)}, bf16[2048]{0:T(1024)(128)(2,1)}, u32[]{:S(2)}) copy-start(bf16[2048]{0:T(1024)(128)(2,1)} %param.17) | copy-start | bytes 12292
  158.8 4.2 %collective-permute-start.3 = (bf16[256,1024]{1,0:T(8,128)(2,1)}, bf16[256,1024]{1,0:T(8,128)(2,1)S(1)}, u32[]{:S(2)}, u32[]{:S(2)}) collective-permute-start(bf16[256,1024]{1,0:T(8,128)(2,1)} %shard_map.84.refs_0_), channel_id=1, source_target_pairs={{0,1},{1,0},{2,3},{3,2},{4,5},{5,4},{6,7},{7,6},{8,9},{9,8},{10,11... | collective-permute-start | bytes 1572872 | tf_op jit(solution)/shard_map/ppermute | solution.py:276
  162.9 0.8 copy-start.3

commit v19 on v18

--- a/solution.py
+++ b/solution.py
@@ -204,6 +204,13 @@
     )(*parts, *weights, bias.reshape(1, out_cols))
 
 
+def pick_pages(kv_pages, ids):
+    ids = jnp.clip(ids, 0, kv_pages.shape[0] - 1)
+    return jnp.stack(
+        [lax.dynamic_index_in_dim(kv_pages, ids[i], 0, keepdims=False) for i in range(ids.shape[0])]
+    )
+
+
 def usable_keys(page_table, request, length, source_base, source_count, page_count, page_size):
     row = lax.dynamic_index_in_dim(page_table, request, 0, keepdims=False)
     row_owner = jnp.where(row >= 0, row // page_count, -1)
@@ -251,9 +258,9 @@
     query_rot = rotate_rows(new_queries, positions)
     partner_query = lax.ppermute(query_rot, "half", swap)
 
-    far_pages = jnp.take(kv_pages, jnp.take(local_page, (1 - half) * sub_count + dest), axis=0, mode="clip")
+    far_pages = pick_pages(kv_pages, jnp.take(local_page, (1 - half) * sub_count + dest))
     far_incoming = lax.all_to_all(far_pages, "sub", split_axis=0, concat_axis=0, tiled=True)
-    near_pages = jnp.take(kv_pages, jnp.take(local_page, half * sub_count + dest), axis=0, mode="clip")
+    near_pages = pick_pages(kv_pages, jnp.take(local_page, half * sub_count + dest))
     partner_query, near_pages = lax.optimization_barrier((partner_query, near_pages))
     near_incoming = lax.all_to_all(near_pages, "sub", split_axis=0, concat_axis=0, tiled=True)
     key_rot = rotate_rows(new_keys, positions)

time: 171 us -> 207 us (1.21)
  between operations: 0.15 us -> 30.4 us
  waiting for transfers between devices: 86.6 us -> 93.2 us
    gather x2 -> x0, local copies, waits for them, and re-layouts: 12.3 us -> none  [the longest x1 6.14 us: on_device(): jnp.take(kv_pages, jnp.take(local_page, (1 - half) * sub_count + dest), a...]
    unnamed x20 -> x33, local copies, waits for them, and re-layouts: 2.86 us -> 13.3 us
    ppermute x1, waiting for transfers between devices: 51.4 us -> 58.4 us  [on_device(): partner_query = lax.ppermute(query_rot, 'half', swap)]
  transfers between devices with their start and end apart: 7 -> 7, of which waited for: 3 -> 3; matrix products, arithmetic and copies ran while one was open for 16% -> 10% of each run, Pallas kernels for 12% -> 10%
where the time goes in v19:
time: 207 us; the launch traced here: 206 us
  waiting for transfers between devices  93.2 us (45%)
  between operations  30.4 us (15%)
  local copies, waits for them, and re-layouts  29.1 us (14%)
  Pallas kernels  27.4 us (13%)
  starting transfers between devices  18.8 us (9%)
  other arithmetic  7.22 us (3%)
    ppermute x1, waiting for transfers between devices, on_device(): partner_query = lax.ppermute(query_rot, 'half', swap)  58.4 us
    ppermute x1, waiting for transfers between devices, on_device(): back_stats = lax.ppermute(far_stats, 'half', swap)  33.6 us
    unnamed x33, local copies, waits for them, and re-layouts  13.3 us
    pallas_call x1, Pallas kernels, near_attend(): pl.pallas_call(near_kernel, grid=(head_count // group,), in_specs=[col_sp...  10.5 us
    dynamic_slice x1, local copies, waits for them, and re-layouts, on_device(): piece = lax.dynamic_slice_in_dim(w_out, target * out_cols, out_cols, axis=1)  8.39 us
    pallas_call x1, Pallas kernels, far_attend(): pl.pallas_call(far_kernel, grid=(head_count // group,), in_specs=[col_spe...  6.75 us
    pallas_call x1, Pallas kernels, project(): pl.pallas_call(projection_kernel, grid=(out_cols // block,), in_specs=[a_...  6.39 us
    all_to_all x1, starting transfers between devices, on_device(): lax.all_to_all(far_pages, 'sub', split_axis=0, concat_axis=0, tiled=True)  4.73 us
  transfers between devices with their start and end apart: 7, of which 3 were waited for; matrix products, arithmetic and copies ran while one was open for 10% of the time, Pallas kernels for 10%

profile of v19, /device:TPU:11, one launch (start us, length us, event | category | flops | bytes accessed | tf_op | source)
XLA Modules:
  0.0 206.0 jit_solution(5119869657278872686)
XLA Ops:
  0.0 0.8 select_reduce_fusion
  1.5 0.7 fusion.14
  4.2 0.7 fusion.13
  33.7 1.4 dynamic-slice_dynamic-update-slice_fusion.7
  35.1 1.5 dynamic-slice_dynamic-update-slice_fusion.6
  36.6 1.3 dynamic-slice_dynamic-update-slice_fusion.5
  38.0 1.3 dynamic-slice_dynamic-update-slice_fusion.4
  39.6 1.9 copy-done.1
  41.5 1.9 copy-done.2
  43.5 4.7 %all-to-all-start.1 = ((bf16[8,2,128,1024]{3,2,1,0:T(8,128)(2,1)}), bf16[8,2,128,1024]{3,2,1,0:T(8,128)(2,1)}, u32[]{:S(2)}, u32[]{:S(2)}) async-start(bf16[8,2,128,1024]{3,2,1,0:T(8,128)(2,1)} %copy-done.1), calls=%async_computation.1 | async-start | bytes 8388608 | tf_op jit(solution)/shard_map/all_to_all | solution.py:262
  50.6 0.7 subtract_convert_fusion
  51.4 1.0 pad_maximum_fusion
  52.5 2.4 %collective-permute-start = (bf16[256,1024]{1,0:T(8,128)(2,1)S(1)}, bf16[256,1024]{1,0:T(8,128)(2,1)S(1)}, u32[]{:S(2)}, u32[]{:S(2)}) collective-permute-start(bf16[256,1024]{1,0:T(8,128)(2,1)S(1)} %bitcast.38), channel_id=1, source_target_pairs={{0,16},{16,0},{1,17},{17,1},{2,18},{18,2},{3,19},{19,3},{4,20},{20... | collective-permute-start | bytes 1572872 | tf_op jit(solution)/shard_map/ppermute | solution.py:259
  54.8 58.4 %collective-permute-done.q_ref = bf16[256,1024]{1,0:T(8,128)(2,1)S(1)} collective-permute-done((bf16[256,1024]{1,0:T(8,128)(2,1)S(1)}, bf16[256,1024]{1,0:T(8,128)(2,1)S(1)}, u32[]{:S(2)}, u32[]{:S(2)}) %collective-permute-start) | collective-permute-done | bytes 524320 | tf_op jit(solution)/shard_map/ppermute | solution.py:259
  113.2 0.8 copy-done.4
  114.0 4.7 %all-to-all-start = ((bf16[8,2,128,1024]{3,2,1,0:T(8,128)(2,1)}), bf16[8,2,128,1024]{3,2,1,0:T(8,128)(2,1)}, u32[]{:S(2)}, u32[]{:S(2)}) async-start(bf16[8,2,128,1024]{3,2,1,0:T(8,128)(2,1)} %copy-done.2), calls=%async_computation | async-start | bytes 8388608 | tf_op jit(solution)/shard_map/all_to_all | solution.py:265
  118.7 8.4 %constant_dynamic-slice_fusion = (bf16[1024,2048]{1,0:T(8,128)(2,1)}, bf16[1024,2048]{1,0:T(8,128)(2,1)}) fusion(bf16[1024,4096]{1,0:T(8,128)(2,1)} %param.16, s32[]{:T(128)S(6)} %select_n.163, s32[]{:T(128)S(6)} %select_n.161), kind=kLoop, calls=%fused_computation.42 | loop fusion | bytes 16777224 | tf_op jit(solution)/shard_map/dynamic_slice | solution.py:246
  127.1 2.2 %collective-permute-start.4 = (bf16[1024,2048]{1,0:T(8,128)(2,1)}, bf16[1024,2048]{1,0:T(8,128)(2,1)}, u32[]{:S(2)}, u32[]{:S(2)}) collective-permute-start(bf16[1024,2048]{1,0:T(8,128)(2,1)} %get-tuple-element.22), channel_id=1, source_target_pairs={{0,1},{1,0},{2,3},{3,2},{4,5},{5,4},{6,7},{7,6},{8,9},{9,8},{10,11... | collective-permute-start | bytes 12582920 | tf_op jit(solution)/shard_map/ppermute | solution.py:248
  129.3 0.7 fusion.9
  131.7 6.7 %shard_map.83 = (bf16[256,1024]{1,0:T(8,128)(2,1)}, f32[8,256,2]{2,1,0:T(8,128)}) custom-call(bf16[256,1024]{1,0:T(8,128)(2,1)} %copy-done.4, bf16[8,2,128,1024]{3,2,1,0:T(8,128)(2,1)} %all-to-all-done.1.kp_ref.vp_ref, bf16[8,2,128,1024]{3,2,1,0:T(8,128)(2,1)} %all-to-all-done.1.kp_ref.vp_ref, s32[1,1024]{1,0:T(1,128)} %bitcast.49), custom_call_target="tpu_custom_call" | custom-call | tf_op jit(solution)/shard_map/pallas_call | solution.py:157
  139.1 1.5 copy.15
  140.7 2.4 %collective-permute-start.2 = (f32[8,256,2]{1,0,2:T(8,128)S(1)}, f32[8,256,2]{1,0,2:T(8,128)S(1)}, u32[]{:S(2)}, u32[]{:S(2)}) collective-permute-start(f32[8,256,2]{1,0,2:T(8,128)S(1)} %copy.15), channel_id=1, source_target_pairs={{0,16},{16,0},{1,17},{17,1},{2,18},{18,2},{3,19},{19,3},{4,20},{20... | collective-permute-start | bytes 49160 | tf_op jit(solution)/shard_map/ppermute | solution.py:275
  143.7 0.9 copy.23
  144.6 3.8 %shard_map.82 = (f32[256,1024]{1,0:T(8,128)}, f32[8,256,2]{2,1,0:T(8,128)}) custom-call(bf16[256,1024]{1,0:T(8,128)(2,1)} %bitcast.39, bf16[256,1024]{1,0:T(8,128)(2,1)} %bitcast.43, bf16[256,1024]{1,0:T(8,128)(2,1)} %vl_ref.1), custom_call_target="tpu_custom_call" | custom-call | tf_op jit(solution)/shard_map/pallas_call | solution.py:140
  148.4 33.6 %collective-permute-done.2 = f32[8,256,2]{1,0,2:T(8,128)S(1)} collective-permute-done((f32[8,256,2]{1,0,2:T(8,128)S(1)}, f32[8,256,2]{1,0,2:T(8,128)S(1)}, u32[]{:S(2)}, u32[]{:S(2)}) %collective-permute-start.2) | collective-permute-done | bytes 16416 | tf_op jit(solution)/shard_map/ppermute | solution.py:275
  182.0 1.4 copy.16.bst_ref
  183.4 0.8 copy-done.5
  184.2 10.5 %shard_map.84.refs_0_ = bf16[256,1024]{1,0:T(8,128)(2,1)} custom-call(bf16[256,1024]{1,0:T(8,128)(2,1)} %bitcast.40, bf16[8,2,128,1024]{3,2,1,0:T(8,128)(2,1)} %all-to-all-done.kp_ref.vp_ref, bf16[8,2,128,1024]{3,2,1,0:T(8,128)(2,1)} %all-to-all-done.kp_ref.vp_ref, s32[1,1024]{1,0:T(1,128)} %bitcast.48, f32[256,1024]{1,0:T(8,128)} %get-tuple-element.13.la_ref, ...), custom_call_target="tpu_custom_call" | custom-call | tf_op jit(solution)/shard_map/pallas_call | solution.py:174
  194.7 2.4 %collective-permute-start.3 = (bf16[256,1024]{1,0:T(8,128)(2,1)}, bf16[256,1024]{1,0:T(8,128)(2,1)S(1)}, u32[]{:S(2)}, u32[]{:S(2)}) collective-permute-start(bf16[256,1024]{1,0:T(8,128)(2,1)} %shard_map.84.refs_0_), channel_id=1, source_target_pairs={{0,1},{1,0},{2,3},{3,2},{4,5},{5,4},{6,7},{7,6},{8,9},{9,8},{10,11... | collective-permute-start | bytes 1572872 | tf_op jit(solution)/shard_map/ppermute | solution.py:283
  197.7 1.1 collective-permute-done.3.refs_1_
  198.8 0.9 copy-done.6
  199.7 6.4 %shard_map.85 = bf16[256,2048]{1,0:T(8,128)(2,1)} custom-call(bf16[256,1024]{1,0:T(8,128)(2,1)} %shard_map.84.refs_0_, bf16[256,1024]{1,0:T(8,128)(2,1)} %copy-done.6, bf16[1024,2048]{1,0:T(8,128)(2,1)} %get-tuple-element.23.refs_2_, bf16[1024,2048]{1,0:T(8,128)(2,1)} %collective-permute-done.4.refs_3_, bf16[1,2048]{1,0:T(2,128)(2,1)} %reshape.161.refs_4_), custom_call_target="tpu_custom_call" | custom-call | tf_op jit(solution)/shard_map/pallas_call | solution.py:198
  (54 shorter events, 7.8 us)
Async XLA Ops:
  33.7 5.6 %copy-start = (bf16[16,2,128,1024]{3,2,1,0:T(8,128)(2,1)S(1)}, bf16[16,2,128,1024]{3,2,1,0:T(8,128)(2,1)}, u32[]{:S(2)}) copy-start(bf16[16,2,128,1024]{3,2,1,0:T(8,128)(2,1)} %param.13) | copy-start | bytes 25165828
  39.6 1.9 copy-start.1
  41.5 1.9 copy-start.2
  43.5 4.7 %copy-start.10 = (s32[16]{0:T(128)S(1)}, s32[16]{0:T(128)}, u32[]{:S(2)}) copy-start(s32[16]{0:T(128)} %param.15) | copy-start | bytes 196
  43.5 6.3 %copy-start.7 = (bf16[256,1024]{1,0:T(8,128)(2,1)S(1)}, bf16[256,1024]{1,0:T(8,128)(2,1)}, u32[]{:S(2)}) copy-start(bf16[256,1024]{1,0:T(8,128)(2,1)} %param.11) | copy-start | bytes 1572868
  43.5 6.4 %copy-start.8 = (bf16[256,1024]{1,0:T(8,128)(2,1)S(1)}, bf16[256,1024]{1,0:T(8,128)(2,1)}, u32[]{:S(2)}) copy-start(bf16[256,1024]{1,0:T(8,128)(2,1)} %param.10) | copy-start | bytes 1572868
  43.5 69.8 %all-to-all-start.1 = ((bf16[8,2,128,1024]{3,2,1,0:T(8,128)(2,1)}), bf16[8,2,128,1024]{3,2,1,0:T(8,128)(2,1)}, u32[]{:S(2)}, u32[]{:S(2)}) async-start(bf16[8,2,128,1024]{3,2,1,0:T(8,128)(2,1)} %copy-done.1), calls=%async_computation.1 | async-start | bytes 8388608 | tf_op jit(solution)/shard_map/all_to_all | solution.py:262
  52.4 60.8 %copy-start.3 = (bf16[32,8,8,128]{3,1,2,0:T(8,128)(2,1)}, bf16[32,8,8,128]{3,1,2,0:T(8,128)(2,1)S(1)}, u32[]{:S(2)}) copy-start(bf16[32,8,8,128]{3,1,2,0:T(8,128)(2,1)S(1)} %copy.24) | copy-start | bytes 1572868
  52.5 60.8 %collective-permute-start = (bf16[256,1024]{1,0:T(8,128)(2,1)S(1)}, bf16[256,1024]{1,0:T(8,128)(2,1)S(1)}, u32[]{:S(2)}, u32[]{:S(2)}) collective-permute-start(bf16[256,1024]{1,0:T(8,128)(2,1)S(1)} %bitcast.38), channel_id=1, source_target_pairs={{0,16},{16,0},{1,17},{17,1},{2,18},{18,2},{3,19},{19,3},{4,20},{20... | collective-permute-start | bytes 1572872 | tf_op jit(solution)/shard_map/ppermute | solution.py:259
  113.2 0.8 copy-start.4
  114.0 69.4 %all-to-all-start = ((bf16[8,2,128,1024]{3,2,1,0:T(8,128)(2,1)}), bf16[8,2,128,1024]{3,2,1,0:T(8,128)(2,1)}, u32[]{:S(2)}, u32[]{:S(2)}) async-start(bf16[8,2,128,1024]{3,2,1,0:T(8,128)(2,1)} %copy-done.2), calls=%async_computation | async-start | bytes 8388608 | tf_op jit(solution)/shard_map/all_to_all | solution.py:265
  127.1 70.6 %collective-permute-start.4 = (bf16[1024,2048]{1,0:T(8,128)(2,1)}, bf16[1024,2048]{1,0:T(8,128)(2,1)}, u32[]{:S(2)}, u32[]{:S(2)}) collective-permute-start(bf16[1024,2048]{1,0:T(8,128)(2,1)} %get-tuple-element.22), channel_id=1, source_target_pairs={{0,1},{1,0},{2,3},{3,2},{4,5},{5,4},{6,7},{7,6},{8,9},{9,8},{10,11... | collective-permute-start | bytes 12582920 | tf_op jit(solution)/shard_map/ppermute | solution.py:248
  138.5 44.9 %collective-permute-start.1 = (bf16[256,1024]{1,0:T(8,128)(2,1)}, bf16[256,1024]{1,0:T(8,128)(2,1)S(1)}, u32[]{:S(2)}, u32[]{:S(2)}) collective-permute-start(bf16[256,1024]{1,0:T(8,128)(2,1)} %get-tuple-element.16), channel_id=1, source_target_pairs={{0,16},{16,0},{1,17},{17,1},{2,18},{18,2},{3,19},{19,3},{4,20},{20... | collective-permute-start | bytes 1572872 | tf_op jit(solution)/shard_map/ppermute | solution.py:274
  140.7 41.3 %collective-permute-start.2 = (f32[8,256,2]{1,0,2:T(8,128)S(1)}, f32[8,256,2]{1,0,2:T(8,128)S(1)}, u32[]{:S(2)}, u32[]{:S(2)}) collective-permute-start(f32[8,256,2]{1,0,2:T(8,128)S(1)} %copy.15), channel_id=1, source_target_pairs={{0,16},{16,0},{1,17},{17,1},{2,18},{18,2},{3,19},{19,3},{4,20},{20... | collective-permute-start | bytes 49160 | tf_op jit(solution)/shard_map/ppermute | solution.py:275
  183.4 0.8 copy-start.5
  184.2 12.9 %copy-start.9 = (bf16[2048]{0:T(1024)(128)(2,1)S(1)}, bf16[2048]{0:T(1024)(128)(2,1)}, u32[]{:S(2)}) copy-start(bf16[2048]{0:T(1024)(128)(2,1)} %param.17) | copy-start | bytes 12292
  194.7 4.1 %collective-permute-start.3 = (bf16[256,1024]{1,0:T(8,128)(2,1)}, bf16[256,1024]{1,0:T(8,128)(2,1)S(1)}, u32[]{:S(2)}, u32[]{:S(2)}) collective-permute-start(bf16[256,1024]{1,0:T(8,128)(2,1)} %shard_map.84.refs_0_), channel_id=1, source_target_pairs={{0,1},{1,0},{2,3},{3,2},{4,5},{5,4},{6,7},{7,6},{8,9},{9,8},{10,11... | collective-permute-start | bytes 1572872 | tf_op jit(solution)/shard_map/ppermute | solution.py:283
  198.8 0.9 copy-start.6

commit v20 on v18

--- a/solution.py
+++ b/solution.py
@@ -180,28 +180,27 @@
     )(query_rot, incoming, incoming, key_ok, local_acc, local_stats, back_out, back_stats)
 
 
-def projection_kernel(*refs):
-    count = (len(refs) - 2) // 2
+def projection_kernel(*refs, count):
     total = refs[2 * count][...].astype(jnp.float32)
     for j in range(count):
         total = total + jnp.dot(refs[j][...], refs[count + j][...], preferred_element_type=jnp.float32)
     refs[-1][...] = total.astype(refs[-1].dtype)
 
 
-def project(parts, weights, bias):
+def project(parts, weights, base, out_dtype):
     span, rows = parts[0].shape
     out_cols = weights[0].shape[1]
     block = 1024 if out_cols % 1024 == 0 else out_cols
     a_spec = pl.BlockSpec((span, rows), lambda c: (0, 0))
     w_spec = pl.BlockSpec((rows, block), lambda c: (0, c))
-    b_spec = pl.BlockSpec((1, block), lambda c: (0, c))
+    base_spec = pl.BlockSpec((base.shape[0], block), lambda c: (0, c))
     return pl.pallas_call(
-        projection_kernel,
+        partial(projection_kernel, count=len(parts)),
         grid=(out_cols // block,),
-        in_specs=[a_spec] * len(parts) + [w_spec] * len(weights) + [b_spec],
+        in_specs=[a_spec] * len(parts) + [w_spec] * len(weights) + [base_spec],
         out_specs=pl.BlockSpec((span, block), lambda c: (0, c)),
-        out_shape=jax.ShapeDtypeStruct((span, out_cols), jnp.bfloat16),
-    )(*parts, *weights, bias.reshape(1, out_cols))
+        out_shape=jax.ShapeDtypeStruct((span, out_cols), out_dtype),
+    )(*parts, *weights, base)
 
 
 def usable_keys(page_table, request, length, source_base, source_count, page_count, page_size):
@@ -274,7 +273,8 @@
     for shift in range(1, tp_count):
         perm = [(i, (i + shift) % tp_count) for i in range(tp_count)]
         parts.append(lax.ppermute(attended, "tp", perm))
-    return project(parts, [w_mine] + w_recv, out_bias)
+    local_sum = project([attended], [w_mine], out_bias.reshape(1, -1), jnp.float32)
+    return project(parts[1:], w_recv, local_sum, jnp.bfloat16)
 
 
 def solution(mesh):

time: 171 us -> 173 us (1.012)
  Pallas kernels: 27.4 us -> 30.6 us
    pallas_call x1 -> x2, Pallas kernels: 6.39 us -> 9.6 us  [project(): pl.pallas_call(partial(projection_kernel, count=len(parts)), grid=(out_co...]
  transfers between devices with their start and end apart: 7 -> 7, of which waited for: 3 -> 2; matrix products, arithmetic and copies ran while one was open for 16% -> 16% of each run, Pallas kernels for 12% -> 15%
where the time goes in v20:
time: 173 us; the launch traced here: 172 us
  waiting for transfers between devices  85.4 us (49%)
  Pallas kernels  30.6 us (18%)
  local copies, waits for them, and re-layouts  29.6 us (17%)
  starting transfers between devices  19.1 us (11%)
  other arithmetic  7.35 us (4%)
    ppermute x1, waiting for transfers between devices, on_device(): partner_query = lax.ppermute(query_rot, 'half', swap)  51.4 us
    ppermute x1, waiting for transfers between devices, on_device(): back_stats = lax.ppermute(far_stats, 'half', swap)  34 us
    pallas_call x1, Pallas kernels, near_attend(): pl.pallas_call(near_kernel, grid=(head_count // group,), in_specs=[col_sp...  10.5 us
    pallas_call x2, Pallas kernels, project(): pl.pallas_call(partial(projection_kernel, count=len(parts)), grid=(out_co...  9.6 us
    dynamic_slice x1, local copies, waits for them, and re-layouts, on_device(): lax.dynamic_slice_in_dim(w_out, tp_index * out_cols, out_cols, axis=1)  8.4 us
    pallas_call x1, Pallas kernels, far_attend(): pl.pallas_call(far_kernel, grid=(head_count // group,), in_specs=[col_spe...  6.75 us
    gather x1, local copies, waits for them, and re-layouts, on_device(): jnp.take(kv_pages, jnp.take(local_page, (1 - half) * sub_count + dest), a...  6.14 us
    gather x1, local copies, waits for them, and re-layouts, on_device(): jnp.take(kv_pages, jnp.take(local_page, half * sub_count + dest), axis=0,...  6.14 us
  transfers between devices with their start and end apart: 7, of which 2 were waited for; matrix products, arithmetic and copies ran while one was open for 16% of the time, Pallas kernels for 15%

profile of v20, /device:TPU:11, one launch (start us, length us, event | category | flops | bytes accessed | tf_op | source)
XLA Modules:
  0.0 172.2 jit_solution(14701620482402498257)
XLA Ops:
  0.0 0.8 select_reduce_fusion
  0.8 0.6 gather_fusion.3
  1.5 6.1 %gather_fusion.1 = bf16[8,2,128,1024]{3,2,1,0:T(8,128)(2,1)} fusion(bf16[16,2,128,1024]{3,2,1,0:T(8,128)(2,1)} %param.13, s32[1024]{0:T(1024)S(1)} %pad_clamp_fusion), kind=kCustom, calls=%fused_computation.3 | custom fusion | bytes 8388640 | tf_op jit(solution)/shard_map/jit(_take)/gather | solution.py:253
  7.7 4.7 %all-to-all-start.1 = ((bf16[8,2,128,1024]{3,2,1,0:T(8,128)(2,1)}), bf16[8,2,128,1024]{3,2,1,0:T(8,128)(2,1)}, u32[]{:S(2)}, u32[]{:S(2)}) async-start(bf16[8,2,128,1024]{3,2,1,0:T(8,128)(2,1)} %gather_fusion.1), calls=%async_computation.1 | async-start | bytes 8388608 | tf_op jit(solution)/shard_map/all_to_all | solution.py:254
  12.4 0.7 fusion.10
  13.1 0.6 add_convert_fusion.2
  14.9 0.8 subtract_convert_fusion
  15.7 1.0 pad_maximum_fusion
  16.8 2.4 %collective-permute-start = (bf16[256,1024]{1,0:T(8,128)(2,1)S(1)}, bf16[256,1024]{1,0:T(8,128)(2,1)S(1)}, u32[]{:S(2)}, u32[]{:S(2)}) collective-permute-start(bf16[256,1024]{1,0:T(8,128)(2,1)S(1)} %bitcast.22), channel_id=1, source_target_pairs={{0,16},{16,0},{1,17},{17,1},{2,18},{18,2},{3,19},{19,3},{4,20},{20... | collective-permute-start | bytes 1572872 | tf_op jit(solution)/shard_map/ppermute | solution.py:251
  19.2 0.6 gather_fusion.2
  19.9 6.1 %gather_fusion = bf16[8,2,128,1024]{3,2,1,0:T(8,128)(2,1)} fusion(bf16[16,2,128,1024]{3,2,1,0:T(8,128)(2,1)} %param.13, s32[1024]{0:T(1024)S(1)} %pad_clamp_fusion.2), kind=kCustom, calls=%fused_computation.2 | custom fusion | bytes 8388640 | tf_op jit(solution)/shard_map/jit(_take)/gather | solution.py:255
  26.0 51.4 %collective-permute-done.q_ref = bf16[256,1024]{1,0:T(8,128)(2,1)S(1)} collective-permute-done((bf16[256,1024]{1,0:T(8,128)(2,1)S(1)}, bf16[256,1024]{1,0:T(8,128)(2,1)S(1)}, u32[]{:S(2)}, u32[]{:S(2)}) %collective-permute-start) | collective-permute-done | bytes 524320 | tf_op jit(solution)/shard_map/ppermute | solution.py:251
  77.4 5.1 %all-to-all-start = ((bf16[8,2,128,1024]{3,2,1,0:T(8,128)(2,1)}), bf16[8,2,128,1024]{3,2,1,0:T(8,128)(2,1)}, u32[]{:S(2)}, u32[]{:S(2)}) async-start(bf16[8,2,128,1024]{3,2,1,0:T(8,128)(2,1)} %gather_fusion), calls=%async_computation | async-start | bytes 8388608 | tf_op jit(solution)/shard_map/all_to_all | solution.py:257
  82.5 8.4 %constant_dynamic-slice_fusion.3 = (bf16[1024,2048]{1,0:T(8,128)(2,1)}, bf16[1024,2048]{1,0:T(8,128)(2,1)}) fusion(bf16[1024,4096]{1,0:T(8,128)(2,1)} %param.16, s32[]{:T(128)S(6)} %select_n.98, s32[]{:T(128)S(6)} %select_n.97), kind=kLoop, calls=%fused_computation.56 | loop fusion | bytes 16777224 | tf_op jit(solution)/shard_map/dynamic_slice | solution.py:241
  90.9 2.1 %collective-permute-start.4 = (bf16[1024,2048]{1,0:T(8,128)(2,1)}, bf16[1024,2048]{1,0:T(8,128)(2,1)}, u32[]{:S(2)}, u32[]{:S(2)}) collective-permute-start(bf16[1024,2048]{1,0:T(8,128)(2,1)} %get-tuple-element.23), channel_id=1, source_target_pairs={{0,1},{1,0},{2,3},{3,2},{4,5},{5,4},{6,7},{7,6},{8,9},{9,8},{10,11... | collective-permute-start | bytes 12582920 | tf_op jit(solution)/shard_map/ppermute | solution.py:240
  93.0 0.7 fusion.8
  94.0 0.7 clamp_select_fusion
  94.7 0.7 fusion.7
  95.4 6.8 %shard_map.83 = (bf16[256,1024]{1,0:T(8,128)(2,1)}, f32[8,256,2]{2,1,0:T(8,128)}) custom-call(bf16[256,1024]{1,0:T(8,128)(2,1)} %copy-done.1, bf16[8,2,128,1024]{3,2,1,0:T(8,128)(2,1)} %all-to-all-done.1.kp_ref.vp_ref, bf16[8,2,128,1024]{3,2,1,0:T(8,128)(2,1)} %all-to-all-done.1.kp_ref.vp_ref, s32[1,1024]{1,0:T(1,128)} %bitcast.33), custom_call_target="tpu_custom_call" | custom-call | tf_op jit(solution)/shard_map/pallas_call | solution.py:157
  103.3 1.5 copy.15
  104.9 1.8 %collective-permute-start.2 = (f32[8,256,2]{1,0,2:T(8,128)S(1)}, f32[8,256,2]{1,0,2:T(8,128)S(1)}, u32[]{:S(2)}, u32[]{:S(2)}) collective-permute-start(f32[8,256,2]{1,0,2:T(8,128)S(1)} %copy.15), channel_id=1, source_target_pairs={{0,16},{16,0},{1,17},{17,1},{2,18},{18,2},{3,19},{19,3},{4,20},{20... | collective-permute-start | bytes 49160 | tf_op jit(solution)/shard_map/ppermute | solution.py:267
  106.7 0.7 fusion.6
  107.4 0.9 copy.23
  108.3 3.8 %shard_map.82 = (f32[256,1024]{1,0:T(8,128)}, f32[8,256,2]{2,1,0:T(8,128)}) custom-call(bf16[256,1024]{1,0:T(8,128)(2,1)} %bitcast.23, bf16[256,1024]{1,0:T(8,128)(2,1)} %bitcast.27, bf16[256,1024]{1,0:T(8,128)(2,1)} %vl_ref.1), custom_call_target="tpu_custom_call" | custom-call | tf_op jit(solution)/shard_map/pallas_call | solution.py:140
  112.1 34.0 %collective-permute-done.2 = f32[8,256,2]{1,0,2:T(8,128)S(1)} collective-permute-done((f32[8,256,2]{1,0,2:T(8,128)S(1)}, f32[8,256,2]{1,0,2:T(8,128)S(1)}, u32[]{:S(2)}, u32[]{:S(2)}) %collective-permute-start.2) | collective-permute-done | bytes 16416 | tf_op jit(solution)/shard_map/ppermute | solution.py:267
  146.1 1.4 copy.16.bst_ref
  147.5 0.8 copy-done.2
  148.3 10.5 %shard_map.84.refs_0_ = bf16[256,1024]{1,0:T(8,128)(2,1)} custom-call(bf16[256,1024]{1,0:T(8,128)(2,1)} %bitcast.24, bf16[8,2,128,1024]{3,2,1,0:T(8,128)(2,1)} %all-to-all-done.kp_ref.vp_ref, bf16[8,2,128,1024]{3,2,1,0:T(8,128)(2,1)} %all-to-all-done.kp_ref.vp_ref, s32[1,1024]{1,0:T(1,128)} %bitcast.32, f32[256,1024]{1,0:T(8,128)} %get-tuple-element.13.la_ref, ...), custom_call_target="tpu_custom_call" | custom-call | tf_op jit(solution)/shard_map/pallas_call | solution.py:174
  158.8 2.4 %collective-permute-start.3 = (bf16[256,1024]{1,0:T(8,128)(2,1)}, bf16[256,1024]{1,0:T(8,128)(2,1)S(1)}, u32[]{:S(2)}, u32[]{:S(2)}) collective-permute-start(bf16[256,1024]{1,0:T(8,128)(2,1)} %shard_map.84.refs_0_), channel_id=1, source_target_pairs={{0,1},{1,0},{2,3},{3,2},{4,5},{5,4},{6,7},{7,6},{8,9},{9,8},{10,11... | collective-permute-start | bytes 1572872 | tf_op jit(solution)/shard_map/ppermute | solution.py:275
  161.8 4.7 %shard_map.85.refs_2_ = f32[256,2048]{1,0:T(8,128)} custom-call(bf16[256,1024]{1,0:T(8,128)(2,1)} %shard_map.84.refs_0_, bf16[1024,2048]{1,0:T(8,128)(2,1)} %get-tuple-element.22.refs_1_, bf16[1,2048]{1,0:T(2,128)(2,1)} %reshape.161.refs_2_), custom_call_target="tpu_custom_call" | custom-call | tf_op jit(solution)/shard_map/pallas_call | solution.py:197
  166.6 0.8 copy-done.5
  167.3 4.9 %shard_map.86 = bf16[256,2048]{1,0:T(8,128)(2,1)} custom-call(bf16[256,1024]{1,0:T(8,128)(2,1)} %copy-done.5, bf16[1024,2048]{1,0:T(8,128)(2,1)} %collective-permute-done.4.refs_1_, f32[256,2048]{1,0:T(8,128)} %shard_map.85.refs_2_), custom_call_target="tpu_custom_call" | custom-call | tf_op jit(solution)/shard_map/pallas_call | solution.py:197
  (43 shorter events, 3.5 us)
Async XLA Ops:
  7.7 4.7 %copy-start.7 = (s32[16]{0:T(128)S(1)}, s32[16]{0:T(128)}, u32[]{:S(2)}) copy-start(s32[16]{0:T(128)} %param.15) | copy-start | bytes 196
  7.7 6.4 %copy-start.3 = (bf16[256,1024]{1,0:T(8,128)(2,1)S(1)}, bf16[256,1024]{1,0:T(8,128)(2,1)}, u32[]{:S(2)}) copy-start(bf16[256,1024]{1,0:T(8,128)(2,1)} %param.10) | copy-start | bytes 1572868
  7.7 6.5 %copy-start.4 = (bf16[256,1024]{1,0:T(8,128)(2,1)S(1)}, bf16[256,1024]{1,0:T(8,128)(2,1)}, u32[]{:S(2)}) copy-start(bf16[256,1024]{1,0:T(8,128)(2,1)} %param.11) | copy-start | bytes 1572868
  7.7 69.8 %all-to-all-start.1 = ((bf16[8,2,128,1024]{3,2,1,0:T(8,128)(2,1)}), bf16[8,2,128,1024]{3,2,1,0:T(8,128)(2,1)}, u32[]{:S(2)}, u32[]{:S(2)}) async-start(bf16[8,2,128,1024]{3,2,1,0:T(8,128)(2,1)} %gather_fusion.1), calls=%async_computation.1 | async-start | bytes 8388608 | tf_op jit(solution)/shard_map/all_to_all | solution.py:254
  16.8 9.2 %copy-start = (bf16[32,8,8,128]{3,1,2,0:T(8,128)(2,1)}, bf16[32,8,8,128]{3,1,2,0:T(8,128)(2,1)S(1)}, u32[]{:S(2)}) copy-start(bf16[32,8,8,128]{3,1,2,0:T(8,128)(2,1)S(1)} %copy.24) | copy-start | bytes 1572868
  16.8 60.6 %collective-permute-start = (bf16[256,1024]{1,0:T(8,128)(2,1)S(1)}, bf16[256,1024]{1,0:T(8,128)(2,1)S(1)}, u32[]{:S(2)}, u32[]{:S(2)}) collective-permute-start(bf16[256,1024]{1,0:T(8,128)(2,1)S(1)} %bitcast.22), channel_id=1, source_target_pairs={{0,16},{16,0},{1,17},{17,1},{2,18},{18,2},{3,19},{19,3},{4,20},{20... | collective-permute-start | bytes 1572872 | tf_op jit(solution)/shard_map/ppermute | solution.py:251
  77.4 5.1 %copy-start.1 = (bf16[256,1024]{1,0:T(8,128)(2,1)}, bf16[256,1024]{1,0:T(8,128)(2,1)S(1)}, u32[]{:S(2)}) copy-start(bf16[256,1024]{1,0:T(8,128)(2,1)S(1)} %collective-permute-done.q_ref) | copy-start | bytes 1572868
  77.4 70.1 %all-to-all-start = ((bf16[8,2,128,1024]{3,2,1,0:T(8,128)(2,1)}), bf16[8,2,128,1024]{3,2,1,0:T(8,128)(2,1)}, u32[]{:S(2)}, u32[]{:S(2)}) async-start(bf16[8,2,128,1024]{3,2,1,0:T(8,128)(2,1)} %gather_fusion), calls=%async_computation | async-start | bytes 8388608 | tf_op jit(solution)/shard_map/all_to_all | solution.py:257
  90.9 75.7 %collective-permute-start.4 = (bf16[1024,2048]{1,0:T(8,128)(2,1)}, bf16[1024,2048]{1,0:T(8,128)(2,1)}, u32[]{:S(2)}, u32[]{:S(2)}) collective-permute-start(bf16[1024,2048]{1,0:T(8,128)(2,1)} %get-tuple-element.23), channel_id=1, source_target_pairs={{0,1},{1,0},{2,3},{3,2},{4,5},{5,4},{6,7},{7,6},{8,9},{9,8},{10,11... | collective-permute-start | bytes 12582920 | tf_op jit(solution)/shard_map/ppermute | solution.py:240
  102.1 45.4 %collective-permute-start.1 = (bf16[256,1024]{1,0:T(8,128)(2,1)}, bf16[256,1024]{1,0:T(8,128)(2,1)S(1)}, u32[]{:S(2)}, u32[]{:S(2)}) collective-permute-start(bf16[256,1024]{1,0:T(8,128)(2,1)} %get-tuple-element.16), channel_id=1, source_target_pairs={{0,16},{16,0},{1,17},{17,1},{2,18},{18,2},{3,19},{19,3},{4,20},{20... | collective-permute-start | bytes 1572872 | tf_op jit(solution)/shard_map/ppermute | solution.py:266
  104.9 41.2 %collective-permute-start.2 = (f32[8,256,2]{1,0,2:T(8,128)S(1)}, f32[8,256,2]{1,0,2:T(8,128)S(1)}, u32[]{:S(2)}, u32[]{:S(2)}) collective-permute-start(f32[8,256,2]{1,0,2:T(8,128)S(1)} %copy.15), channel_id=1, source_target_pairs={{0,16},{16,0},{1,17},{17,1},{2,18},{18,2},{3,19},{19,3},{4,20},{20... | collective-permute-start | bytes 49160 | tf_op jit(solution)/shard_map/ppermute | solution.py:267
  147.5 0.8 copy-start.2
  148.3 12.9 %copy-start.6 = (bf16[2048]{0:T(1024)(128)(2,1)S(1)}, bf16[2048]{0:T(1024)(128)(2,1)}, u32[]{:S(2)}) copy-start(bf16[2048]{0:T(1024)(128)(2,1)} %param.17) | copy-start | bytes 12292
  158.8 7.8 %collective-permute-start.3 = (bf16[256,1024]{1,0:T(8,128)(2,1)}, bf16[256,1024]{1,0:T(8,128)(2,1)S(1)}, u32[]{:S(2)}, u32[]{:S(2)}) collective-permute-start(bf16[256,1024]{1,0:T(8,128)(2,1)} %shard_map.84.refs_0_), channel_id=1, source_target_pairs={{0,1},{1,0},{2,3},{3,2},{4,5},{5,4},{6,7},{7,6},{8,9},{9,8},{10,11... | collective-permute-start | bytes 1572872 | tf_op jit(solution)/shard_map/ppermute | solution.py:275
  166.6 0.8 copy-start.5

commit v21 on v18

--- a/solution.py
+++ b/solution.py
@@ -70,8 +70,7 @@
 
 def page_partial(q, keys_p, values_p, ok):
     score_scale = 1.0 / math.sqrt(HEAD_DIM)
-    s = lax.dot_general(q, keys_p, SCORE_DIMS, preferred_element_type=jnp.float32) * score_scale
-    s = jnp.where(ok > 0, s, NEG_FILL)
+    s = lax.dot_general(q, keys_p, SCORE_DIMS, preferred_element_type=jnp.float32) * score_scale + ok
     m = jnp.max(s, axis=1, keepdims=True)
     p = jnp.exp(s - m)
     l = jnp.sum(p, axis=1, keepdims=True)
@@ -214,7 +213,8 @@
     slot_of = jnp.sum(jnp.where(matches, slot_ids[None, :], 0), axis=1)
     nvalid = jnp.where(present, jnp.clip(length - slot_of * page_size, 0, page_size), 0)
     within = jnp.arange(page_size, dtype=jnp.int32)
-    return (within[None, :] < nvalid[:, None]).astype(jnp.int32).reshape(1, source_count * page_size)
+    usable = within[None, :] < nvalid[:, None]
+    return jnp.where(usable, 0.0, NEG_FILL).astype(jnp.float32).reshape(1, source_count * page_size)
 
 
 def on_device(new_queries, new_keys, new_values, kv_pages, page_table, cache_len, w_out, out_bias):

time: 171 us -> 171 us (level)
  no operation moved by 1% of the time
where the time goes in v21:
time: 171 us; the launch traced here: 170 us
  waiting for transfers between devices  86.5 us (51%)
  local copies, waits for them, and re-layouts  29.6 us (17%)
  Pallas kernels  27.4 us (16%)
  starting transfers between devices  19.1 us (11%)
  other arithmetic  7.35 us (4%)
    ppermute x1, waiting for transfers between devices, on_device(): partner_query = lax.ppermute(query_rot, 'half', swap)  51.4 us
    ppermute x1, waiting for transfers between devices, on_device(): back_stats = lax.ppermute(far_stats, 'half', swap)  34 us
    pallas_call x1, Pallas kernels, near_attend(): pl.pallas_call(near_kernel, grid=(head_count // group,), in_specs=[col_sp...  10.4 us
    dynamic_slice x1, local copies, waits for them, and re-layouts, on_device(): piece = lax.dynamic_slice_in_dim(w_out, target * out_cols, out_cols, axis=1)  8.35 us
    pallas_call x1, Pallas kernels, far_attend(): pl.pallas_call(far_kernel, grid=(head_count // group,), in_specs=[col_spe...  6.84 us
    pallas_call x1, Pallas kernels, project(): pl.pallas_call(projection_kernel, grid=(out_cols // block,), in_specs=[a_...  6.39 us
    gather x1, local copies, waits for them, and re-layouts, on_device(): jnp.take(kv_pages, jnp.take(local_page, (1 - half) * sub_count + dest), a...  6.14 us
    gather x1, local copies, waits for them, and re-layouts, on_device(): jnp.take(kv_pages, jnp.take(local_page, half * sub_count + dest), axis=0,...  6.14 us
  transfers between devices with their start and end apart: 7, of which 3 were waited for; matrix products, arithmetic and copies ran while one was open for 16% of the time, Pallas kernels for 12%

profile of v21, /device:TPU:11, one launch (start us, length us, event | category | flops | bytes accessed | tf_op | source)
XLA Modules:
  0.0 170.1 jit_solution(6328578411027468533)
XLA Ops:
  0.0 0.8 select_reduce_fusion
  0.8 0.6 gather_fusion.3
  1.5 6.1 %gather_fusion.1 = bf16[8,2,128,1024]{3,2,1,0:T(8,128)(2,1)} fusion(bf16[16,2,128,1024]{3,2,1,0:T(8,128)(2,1)} %param.13, s32[1024]{0:T(1024)S(1)} %pad_clamp_fusion), kind=kCustom, calls=%fused_computation.3 | custom fusion | bytes 8388640 | tf_op jit(solution)/shard_map/jit(_take)/gather | solution.py:254
  7.7 4.7 %all-to-all-start.1 = ((bf16[8,2,128,1024]{3,2,1,0:T(8,128)(2,1)}), bf16[8,2,128,1024]{3,2,1,0:T(8,128)(2,1)}, u32[]{:S(2)}, u32[]{:S(2)}) async-start(bf16[8,2,128,1024]{3,2,1,0:T(8,128)(2,1)} %gather_fusion.1), calls=%async_computation.1 | async-start | bytes 8388608 | tf_op jit(solution)/shard_map/all_to_all | solution.py:255
  12.4 0.7 fusion.10
  13.1 0.6 add_convert_fusion.2
  14.9 0.8 subtract_convert_fusion
  15.7 1.0 pad_maximum_fusion
  16.8 2.4 %collective-permute-start = (bf16[256,1024]{1,0:T(8,128)(2,1)S(1)}, bf16[256,1024]{1,0:T(8,128)(2,1)S(1)}, u32[]{:S(2)}, u32[]{:S(2)}) collective-permute-start(bf16[256,1024]{1,0:T(8,128)(2,1)S(1)} %bitcast.22), channel_id=1, source_target_pairs={{0,16},{16,0},{1,17},{17,1},{2,18},{18,2},{3,19},{19,3},{4,20},{20... | collective-permute-start | bytes 1572872 | tf_op jit(solution)/shard_map/ppermute | solution.py:252
  19.2 0.6 gather_fusion.2
  19.9 6.1 %gather_fusion = bf16[8,2,128,1024]{3,2,1,0:T(8,128)(2,1)} fusion(bf16[16,2,128,1024]{3,2,1,0:T(8,128)(2,1)} %param.13, s32[1024]{0:T(1024)S(1)} %pad_clamp_fusion.2), kind=kCustom, calls=%fused_computation.2 | custom fusion | bytes 8388640 | tf_op jit(solution)/shard_map/jit(_take)/gather | solution.py:256
  26.0 51.4 %collective-permute-done.q_ref = bf16[256,1024]{1,0:T(8,128)(2,1)S(1)} collective-permute-done((bf16[256,1024]{1,0:T(8,128)(2,1)S(1)}, bf16[256,1024]{1,0:T(8,128)(2,1)S(1)}, u32[]{:S(2)}, u32[]{:S(2)}) %collective-permute-start) | collective-permute-done | bytes 524320 | tf_op jit(solution)/shard_map/ppermute | solution.py:252
  77.4 5.1 %all-to-all-start = ((bf16[8,2,128,1024]{3,2,1,0:T(8,128)(2,1)}), bf16[8,2,128,1024]{3,2,1,0:T(8,128)(2,1)}, u32[]{:S(2)}, u32[]{:S(2)}) async-start(bf16[8,2,128,1024]{3,2,1,0:T(8,128)(2,1)} %gather_fusion), calls=%async_computation | async-start | bytes 8388608 | tf_op jit(solution)/shard_map/all_to_all | solution.py:258
  82.5 8.3 %constant_dynamic-slice_fusion.3 = (bf16[1024,2048]{1,0:T(8,128)(2,1)}, bf16[1024,2048]{1,0:T(8,128)(2,1)}) fusion(bf16[1024,4096]{1,0:T(8,128)(2,1)} %param.16, s32[]{:T(128)S(6)} %select_n.129, s32[]{:T(128)S(6)} %select_n.127), kind=kLoop, calls=%fused_computation.56 | loop fusion | bytes 16777224 | tf_op jit(solution)/shard_map/dynamic_slice | solution.py:239
  90.8 2.1 %collective-permute-start.4 = (bf16[1024,2048]{1,0:T(8,128)(2,1)}, bf16[1024,2048]{1,0:T(8,128)(2,1)}, u32[]{:S(2)}, u32[]{:S(2)}) collective-permute-start(bf16[1024,2048]{1,0:T(8,128)(2,1)} %get-tuple-element.22), channel_id=1, source_target_pairs={{0,1},{1,0},{2,3},{3,2},{4,5},{5,4},{6,7},{7,6},{8,9},{9,8},{10,11... | collective-permute-start | bytes 12582920 | tf_op jit(solution)/shard_map/ppermute | solution.py:241
  92.9 0.7 fusion.8
  94.0 0.7 clamp_select_fusion
  94.7 0.7 fusion.7
  95.3 6.8 %shard_map.83 = (bf16[256,1024]{1,0:T(8,128)(2,1)}, f32[8,256,2]{2,1,0:T(8,128)}) custom-call(bf16[256,1024]{1,0:T(8,128)(2,1)} %copy-done.1, bf16[8,2,128,1024]{3,2,1,0:T(8,128)(2,1)} %all-to-all-done.1.kp_ref.vp_ref, bf16[8,2,128,1024]{3,2,1,0:T(8,128)(2,1)} %all-to-all-done.1.kp_ref.vp_ref, f32[1,1024]{1,0:T(1,128)} %bitcast.33), custom_call_target="tpu_custom_call" | custom-call | tf_op jit(solution)/shard_map/pallas_call | solution.py:156
  103.4 1.5 copy.15
  104.9 1.9 %collective-permute-start.2 = (f32[8,256,2]{1,0,2:T(8,128)S(1)}, f32[8,256,2]{1,0,2:T(8,128)S(1)}, u32[]{:S(2)}, u32[]{:S(2)}) collective-permute-start(f32[8,256,2]{1,0,2:T(8,128)S(1)} %copy.15), channel_id=1, source_target_pairs={{0,16},{16,0},{1,17},{17,1},{2,18},{18,2},{3,19},{19,3},{4,20},{20... | collective-permute-start | bytes 49160 | tf_op jit(solution)/shard_map/ppermute | solution.py:268
  106.8 0.7 fusion.6
  107.4 0.9 copy.23
  108.4 3.8 %shard_map.82 = (f32[256,1024]{1,0:T(8,128)}, f32[8,256,2]{2,1,0:T(8,128)}) custom-call(bf16[256,1024]{1,0:T(8,128)(2,1)} %bitcast.23, bf16[256,1024]{1,0:T(8,128)(2,1)} %bitcast.27, bf16[256,1024]{1,0:T(8,128)(2,1)} %vl_ref.1), custom_call_target="tpu_custom_call" | custom-call | tf_op jit(solution)/shard_map/pallas_call | solution.py:139
  112.1 34.0 %collective-permute-done.2 = f32[8,256,2]{1,0,2:T(8,128)S(1)} collective-permute-done((f32[8,256,2]{1,0,2:T(8,128)S(1)}, f32[8,256,2]{1,0,2:T(8,128)S(1)}, u32[]{:S(2)}, u32[]{:S(2)}) %collective-permute-start.2) | collective-permute-done | bytes 16416 | tf_op jit(solution)/shard_map/ppermute | solution.py:268
  146.1 1.4 copy.16.bst_ref
  147.5 0.8 copy-done.2
  148.3 10.4 %shard_map.84.refs_0_ = bf16[256,1024]{1,0:T(8,128)(2,1)} custom-call(bf16[256,1024]{1,0:T(8,128)(2,1)} %bitcast.24, bf16[8,2,128,1024]{3,2,1,0:T(8,128)(2,1)} %all-to-all-done.kp_ref.vp_ref, bf16[8,2,128,1024]{3,2,1,0:T(8,128)(2,1)} %all-to-all-done.kp_ref.vp_ref, f32[1,1024]{1,0:T(1,128)} %bitcast.32, f32[256,1024]{1,0:T(8,128)} %get-tuple-element.13.la_ref, ...), custom_call_target="tpu_custom_call" | custom-call | tf_op jit(solution)/shard_map/pallas_call | solution.py:173
  158.7 2.4 %collective-permute-start.3 = (bf16[256,1024]{1,0:T(8,128)(2,1)}, bf16[256,1024]{1,0:T(8,128)(2,1)S(1)}, u32[]{:S(2)}, u32[]{:S(2)}) collective-permute-start(bf16[256,1024]{1,0:T(8,128)(2,1)} %shard_map.84.refs_0_), channel_id=1, source_target_pairs={{0,1},{1,0},{2,3},{3,2},{4,5},{5,4},{6,7},{7,6},{8,9},{9,8},{10,11... | collective-permute-start | bytes 1572872 | tf_op jit(solution)/shard_map/ppermute | solution.py:276
  161.7 1.1 collective-permute-done.3.refs_1_
  162.9 0.8 copy-done.3
  163.7 6.4 %shard_map.85 = bf16[256,2048]{1,0:T(8,128)(2,1)} custom-call(bf16[256,1024]{1,0:T(8,128)(2,1)} %shard_map.84.refs_0_, bf16[256,1024]{1,0:T(8,128)(2,1)} %copy-done.3, bf16[1024,2048]{1,0:T(8,128)(2,1)} %get-tuple-element.23.refs_2_, bf16[1024,2048]{1,0:T(8,128)(2,1)} %collective-permute-done.4.refs_3_, bf16[1,2048]{1,0:T(2,128)(2,1)} %reshape.163.refs_4_), custom_call_target="tpu_custom_call" | custom-call | tf_op jit(solution)/shard_map/pallas_call | solution.py:197
  (42 shorter events, 3.5 us)
Async XLA Ops:
  7.7 4.7 %copy-start.7 = (s32[16]{0:T(128)S(1)}, s32[16]{0:T(128)}, u32[]{:S(2)}) copy-start(s32[16]{0:T(128)} %param.15) | copy-start | bytes 196
  7.7 6.4 %copy-start.4 = (bf16[256,1024]{1,0:T(8,128)(2,1)S(1)}, bf16[256,1024]{1,0:T(8,128)(2,1)}, u32[]{:S(2)}) copy-start(bf16[256,1024]{1,0:T(8,128)(2,1)} %param.10) | copy-start | bytes 1572868
  7.7 6.5 %copy-start.5 = (bf16[256,1024]{1,0:T(8,128)(2,1)S(1)}, bf16[256,1024]{1,0:T(8,128)(2,1)}, u32[]{:S(2)}) copy-start(bf16[256,1024]{1,0:T(8,128)(2,1)} %param.11) | copy-start | bytes 1572868
  7.7 69.8 %all-to-all-start.1 = ((bf16[8,2,128,1024]{3,2,1,0:T(8,128)(2,1)}), bf16[8,2,128,1024]{3,2,1,0:T(8,128)(2,1)}, u32[]{:S(2)}, u32[]{:S(2)}) async-start(bf16[8,2,128,1024]{3,2,1,0:T(8,128)(2,1)} %gather_fusion.1), calls=%async_computation.1 | async-start | bytes 8388608 | tf_op jit(solution)/shard_map/all_to_all | solution.py:255
  16.8 9.2 %copy-start = (bf16[32,8,8,128]{3,1,2,0:T(8,128)(2,1)}, bf16[32,8,8,128]{3,1,2,0:T(8,128)(2,1)S(1)}, u32[]{:S(2)}) copy-start(bf16[32,8,8,128]{3,1,2,0:T(8,128)(2,1)S(1)} %copy.24) | copy-start | bytes 1572868
  16.8 60.6 %collective-permute-start = (bf16[256,1024]{1,0:T(8,128)(2,1)S(1)}, bf16[256,1024]{1,0:T(8,128)(2,1)S(1)}, u32[]{:S(2)}, u32[]{:S(2)}) collective-permute-start(bf16[256,1024]{1,0:T(8,128)(2,1)S(1)} %bitcast.22), channel_id=1, source_target_pairs={{0,16},{16,0},{1,17},{17,1},{2,18},{18,2},{3,19},{19,3},{4,20},{20... | collective-permute-start | bytes 1572872 | tf_op jit(solution)/shard_map/ppermute | solution.py:252
  77.4 5.1 %copy-start.1 = (bf16[256,1024]{1,0:T(8,128)(2,1)}, bf16[256,1024]{1,0:T(8,128)(2,1)S(1)}, u32[]{:S(2)}) copy-start(bf16[256,1024]{1,0:T(8,128)(2,1)S(1)} %collective-permute-done.q_ref) | copy-start | bytes 1572868
  77.4 70.1 %all-to-all-start = ((bf16[8,2,128,1024]{3,2,1,0:T(8,128)(2,1)}), bf16[8,2,128,1024]{3,2,1,0:T(8,128)(2,1)}, u32[]{:S(2)}, u32[]{:S(2)}) async-start(bf16[8,2,128,1024]{3,2,1,0:T(8,128)(2,1)} %gather_fusion), calls=%async_computation | async-start | bytes 8388608 | tf_op jit(solution)/shard_map/all_to_all | solution.py:258
  90.8 70.9 %collective-permute-start.4 = (bf16[1024,2048]{1,0:T(8,128)(2,1)}, bf16[1024,2048]{1,0:T(8,128)(2,1)}, u32[]{:S(2)}, u32[]{:S(2)}) collective-permute-start(bf16[1024,2048]{1,0:T(8,128)(2,1)} %get-tuple-element.22), channel_id=1, source_target_pairs={{0,1},{1,0},{2,3},{3,2},{4,5},{5,4},{6,7},{7,6},{8,9},{9,8},{10,11... | collective-permute-start | bytes 12582920 | tf_op jit(solution)/shard_map/ppermute | solution.py:241
  102.2 45.3 %collective-permute-start.1 = (bf16[256,1024]{1,0:T(8,128)(2,1)}, bf16[256,1024]{1,0:T(8,128)(2,1)S(1)}, u32[]{:S(2)}, u32[]{:S(2)}) collective-permute-start(bf16[256,1024]{1,0:T(8,128)(2,1)} %get-tuple-element.16), channel_id=1, source_target_pairs={{0,16},{16,0},{1,17},{17,1},{2,18},{18,2},{3,19},{19,3},{4,20},{20... | collective-permute-start | bytes 1572872 | tf_op jit(solution)/shard_map/ppermute | solution.py:267
  104.9 41.2 %collective-permute-start.2 = (f32[8,256,2]{1,0,2:T(8,128)S(1)}, f32[8,256,2]{1,0,2:T(8,128)S(1)}, u32[]{:S(2)}, u32[]{:S(2)}) collective-permute-start(f32[8,256,2]{1,0,2:T(8,128)S(1)} %copy.15), channel_id=1, source_target_pairs={{0,16},{16,0},{1,17},{17,1},{2,18},{18,2},{3,19},{19,3},{4,20},{20... | collective-permute-start | bytes 49160 | tf_op jit(solution)/shard_map/ppermute | solution.py:268
  147.5 0.8 copy-start.2
  148.3 12.8 %copy-start.6 = (bf16[2048]{0:T(1024)(128)(2,1)S(1)}, bf16[2048]{0:T(1024)(128)(2,1)}, u32[]{:S(2)}) copy-start(bf16[2048]{0:T(1024)(128)(2,1)} %param.17) | copy-start | bytes 12292
  158.7 4.2 %collective-permute-start.3 = (bf16[256,1024]{1,0:T(8,128)(2,1)}, bf16[256,1024]{1,0:T(8,128)(2,1)S(1)}, u32[]{:S(2)}, u32[]{:S(2)}) collective-permute-start(bf16[256,1024]{1,0:T(8,128)(2,1)} %shard_map.84.refs_0_), channel_id=1, source_target_pairs={{0,1},{1,0},{2,3},{3,2},{4,5},{5,4},{6,7},{7,6},{8,9},{9,8},{10,11... | collective-permute-start | bytes 1572872 | tf_op jit(solution)/shard_map/ppermute | solution.py:276
  162.9 0.8 copy-start.3

commit v22 on v21

--- a/solution.py
+++ b/solution.py
@@ -80,25 +80,29 @@
 
 def far_kernel(q_ref, kp_ref, vp_ref, ok_ref, o_ref, st_ref):
     ok = ok_ref[...]
-    for g in range(st_ref.shape[0]):
+    span = q_ref.shape[0]
+    lane = lax.broadcasted_iota(jnp.int32, (span, HEAD_DIM), 1)
+    packed = jnp.zeros((span, HEAD_DIM), jnp.float32)
+    for g in range(st_ref.shape[0] // 2):
         keys, values = head_pages(kp_ref, vp_ref, g)
         m, l, acc = page_partial(head_cols(q_ref, g), keys, values, ok)
         o_ref[:, g * HEAD_DIM:(g + 1) * HEAD_DIM] = (acc / l).astype(o_ref.dtype)
-        st_ref[g, :, 0:1] = m
-        st_ref[g, :, 1:2] = l
+        packed = jnp.where(lane == 2 * g, m, jnp.where(lane == 2 * g + 1, l, packed))
+    st_ref[...] = packed.T[: st_ref.shape[0]]
 
 
 def near_kernel(q_ref, kp_ref, vp_ref, ok_ref, la_ref, lst_ref, bo_ref, bst_ref, o_ref):
     ok = ok_ref[...]
+    rows, span = bst_ref.shape
+    back = jnp.concatenate([bst_ref[...], jnp.zeros((HEAD_DIM - rows, span), jnp.float32)], axis=0).T
     for g in range(lst_ref.shape[0]):
         keys, values = head_pages(kp_ref, vp_ref, g)
         m, l, acc = page_partial(head_cols(q_ref, g), keys, values, ok)
         local = lst_ref[g]
         local_max = local[:, 0:1]
         local_sum = local[:, 1:2]
-        back = bst_ref[g]
-        back_max = back[:, 0:1]
-        back_sum = back[:, 1:2]
+        back_max = back[:, 2 * g:2 * g + 1]
+        back_sum = back[:, 2 * g + 1:2 * g + 2]
         peak = jnp.maximum(jnp.maximum(m, local_max), back_max)
         page_w = jnp.exp(m - peak)
         local_w = jnp.exp(local_max - peak)
@@ -157,10 +161,10 @@
         far_kernel,
         grid=(head_count // group,),
         in_specs=[col_spec] + page_specs,
-        out_specs=[col_spec, stat_spec],
+        out_specs=[col_spec, pl.BlockSpec((2 * group, span), lambda h: (h, 0))],
         out_shape=[
             jax.ShapeDtypeStruct((span, width), jnp.bfloat16),
-            jax.ShapeDtypeStruct((head_count, span, 2), jnp.float32),
+            jax.ShapeDtypeStruct((2 * head_count, span), jnp.float32),
         ],
     )(query_rot, incoming, incoming, key_ok)
 
@@ -173,7 +177,9 @@
     return pl.pallas_call(
         near_kernel,
         grid=(head_count // group,),
-        in_specs=[col_spec] + page_specs + [col_spec, stat_spec, col_spec, stat_spec],
+        in_specs=[col_spec] + page_specs + [
+            col_spec, stat_spec, col_spec, pl.BlockSpec((2 * group, span), lambda h: (h, 0))
+        ],
         out_specs=col_spec,
         out_shape=jax.ShapeDtypeStruct((span, width), jnp.bfloat16),
     )(query_rot, incoming, incoming, key_ok, local_acc, local_stats, back_out, back_stats)

time: 171 us -> 170 us (level)
  local copies, waits for them, and re-layouts: 29.6 us -> 26.7 us
    ppermute x1, waiting for transfers between devices: 34 us -> 35.8 us  [on_device(): back_stats = lax.ppermute(far_stats, 'half', swap)]
  transfers between devices with their start and end apart: 7 -> 7, of which waited for: 3 -> 3; matrix products, arithmetic and copies ran while one was open for 16% -> 15% of each run, Pallas kernels for 12% -> 13%
where the time goes in v22:
time: 170 us; the launch traced here: 169 us
  waiting for transfers between devices  88.2 us (52%)
  Pallas kernels  27.9 us (16%)
  local copies, waits for them, and re-layouts  26.7 us (16%)
  starting transfers between devices  19.1 us (11%)
  other arithmetic  7.35 us (4%)
    ppermute x1, waiting for transfers between devices, on_device(): partner_query = lax.ppermute(query_rot, 'half', swap)  51.3 us
    ppermute x1, waiting for transfers between devices, on_device(): back_stats = lax.ppermute(far_stats, 'half', swap)  35.8 us
    pallas_call x1, Pallas kernels, near_attend(): pl.pallas_call(near_kernel, grid=(head_count // group,), in_specs=[col_sp...  11 us
    dynamic_slice x1, local copies, waits for them, and re-layouts, on_device(): piece = lax.dynamic_slice_in_dim(w_out, target * out_cols, out_cols, axis=1)  8.34 us
    pallas_call x1, Pallas kernels, far_attend(): pl.pallas_call(far_kernel, grid=(head_count // group,), in_specs=[col_spe...  6.73 us
    pallas_call x1, Pallas kernels, project(): pl.pallas_call(projection_kernel, grid=(out_cols // block,), in_specs=[a_...  6.39 us
    gather x1, local copies, waits for them, and re-layouts, on_device(): jnp.take(kv_pages, jnp.take(local_page, (1 - half) * sub_count + dest), a...  6.15 us
    gather x1, local copies, waits for them, and re-layouts, on_device(): jnp.take(kv_pages, jnp.take(local_page, half * sub_count + dest), axis=0,...  6.14 us
  transfers between devices with their start and end apart: 7, of which 3 were waited for; matrix products, arithmetic and copies ran while one was open for 15% of the time, Pallas kernels for 13%

profile of v22, /device:TPU:11, one launch (start us, length us, event | category | flops | bytes accessed | tf_op | source)
XLA Modules:
  0.0 169.4 jit_solution(5105360548301016835)
XLA Ops:
  0.0 0.8 select_reduce_fusion
  0.8 0.6 gather_fusion.3
  1.5 6.1 %gather_fusion.1 = bf16[8,2,128,1024]{3,2,1,0:T(8,128)(2,1)} fusion(bf16[16,2,128,1024]{3,2,1,0:T(8,128)(2,1)} %param.13, s32[1024]{0:T(1024)S(1)} %pad_clamp_fusion), kind=kCustom, calls=%fused_computation.3 | custom fusion | bytes 8388640 | tf_op jit(solution)/shard_map/jit(_take)/gather | solution.py:260
  7.7 4.7 %all-to-all-start.1 = ((bf16[8,2,128,1024]{3,2,1,0:T(8,128)(2,1)}), bf16[8,2,128,1024]{3,2,1,0:T(8,128)(2,1)}, u32[]{:S(2)}, u32[]{:S(2)}) async-start(bf16[8,2,128,1024]{3,2,1,0:T(8,128)(2,1)} %gather_fusion.1), calls=%async_computation.1 | async-start | bytes 8388608 | tf_op jit(solution)/shard_map/all_to_all | solution.py:261
  12.4 0.7 fusion.10
  13.1 0.7 add_convert_fusion.2
  15.0 0.8 subtract_convert_fusion
  15.8 1.0 pad_maximum_fusion
  16.9 2.4 %collective-permute-start = (bf16[256,1024]{1,0:T(8,128)(2,1)S(1)}, bf16[256,1024]{1,0:T(8,128)(2,1)S(1)}, u32[]{:S(2)}, u32[]{:S(2)}) collective-permute-start(bf16[256,1024]{1,0:T(8,128)(2,1)S(1)} %bitcast.22), channel_id=1, source_target_pairs={{0,16},{16,0},{1,17},{17,1},{2,18},{18,2},{3,19},{19,3},{4,20},{20... | collective-permute-start | bytes 1572872 | tf_op jit(solution)/shard_map/ppermute | solution.py:258
  19.3 0.6 gather_fusion.2
  19.9 6.1 %gather_fusion = bf16[8,2,128,1024]{3,2,1,0:T(8,128)(2,1)} fusion(bf16[16,2,128,1024]{3,2,1,0:T(8,128)(2,1)} %param.13, s32[1024]{0:T(1024)S(1)} %pad_clamp_fusion.2), kind=kCustom, calls=%fused_computation.2 | custom fusion | bytes 8388640 | tf_op jit(solution)/shard_map/jit(_take)/gather | solution.py:262
  26.1 51.3 %collective-permute-done.q_ref = bf16[256,1024]{1,0:T(8,128)(2,1)S(1)} collective-permute-done((bf16[256,1024]{1,0:T(8,128)(2,1)S(1)}, bf16[256,1024]{1,0:T(8,128)(2,1)S(1)}, u32[]{:S(2)}, u32[]{:S(2)}) %collective-permute-start) | collective-permute-done | bytes 524320 | tf_op jit(solution)/shard_map/ppermute | solution.py:258
  77.4 5.1 %all-to-all-start = ((bf16[8,2,128,1024]{3,2,1,0:T(8,128)(2,1)}), bf16[8,2,128,1024]{3,2,1,0:T(8,128)(2,1)}, u32[]{:S(2)}, u32[]{:S(2)}) async-start(bf16[8,2,128,1024]{3,2,1,0:T(8,128)(2,1)} %gather_fusion), calls=%async_computation | async-start | bytes 8388608 | tf_op jit(solution)/shard_map/all_to_all | solution.py:264
  82.5 8.3 %constant_dynamic-slice_fusion.3 = (bf16[1024,2048]{1,0:T(8,128)(2,1)}, bf16[1024,2048]{1,0:T(8,128)(2,1)}) fusion(bf16[1024,4096]{1,0:T(8,128)(2,1)} %param.16, s32[]{:T(128)S(6)} %select_n.129, s32[]{:T(128)S(6)} %select_n.127), kind=kLoop, calls=%fused_computation.56 | loop fusion | bytes 16777224 | tf_op jit(solution)/shard_map/dynamic_slice | solution.py:245
  90.8 2.1 %collective-permute-start.4 = (bf16[1024,2048]{1,0:T(8,128)(2,1)}, bf16[1024,2048]{1,0:T(8,128)(2,1)}, u32[]{:S(2)}, u32[]{:S(2)}) collective-permute-start(bf16[1024,2048]{1,0:T(8,128)(2,1)} %get-tuple-element.22), channel_id=1, source_target_pairs={{0,1},{1,0},{2,3},{3,2},{4,5},{5,4},{6,7},{7,6},{8,9},{9,8},{10,11... | collective-permute-start | bytes 12582920 | tf_op jit(solution)/shard_map/ppermute | solution.py:247
  92.9 0.7 fusion.8
  94.6 0.7 fusion.7
  95.2 6.7 %shard_map.83 = (bf16[256,1024]{1,0:T(8,128)(2,1)}, f32[16,256]{1,0:T(8,128)}) custom-call(bf16[256,1024]{1,0:T(8,128)(2,1)} %copy-done.1, bf16[8,2,128,1024]{3,2,1,0:T(8,128)(2,1)} %all-to-all-done.1.kp_ref.vp_ref, bf16[8,2,128,1024]{3,2,1,0:T(8,128)(2,1)} %all-to-all-done.1.kp_ref.vp_ref, f32[1,1024]{1,0:T(1,128)} %bitcast.33), custom_call_target="tpu_custom_call" | custom-call | tf_op jit(solution)/shard_map/pallas_call | solution.py:160
  102.0 0.6 collective-permute-start.1
  102.5 0.7 clamp_select_fusion.1
  103.2 1.8 %collective-permute-start.2 = (f32[16,256]{1,0:T(8,128)}, f32[16,256]{1,0:T(8,128)S(1)}, u32[]{:S(2)}, u32[]{:S(2)}) collective-permute-start(f32[16,256]{1,0:T(8,128)} %get-tuple-element.17), channel_id=1, source_target_pairs={{0,16},{16,0},{1,17},{17,1},{2,18},{18,2},{3,19},{19,3},{4,20},{20... | collective-permute-start | bytes 49160 | tf_op jit(solution)/shard_map/ppermute | solution.py:274
  105.1 0.7 fusion.6
  105.7 0.9 copy.17
  106.7 3.8 %shard_map.82 = (f32[256,1024]{1,0:T(8,128)}, f32[8,256,2]{2,1,0:T(8,128)}) custom-call(bf16[256,1024]{1,0:T(8,128)(2,1)} %bitcast.23, bf16[256,1024]{1,0:T(8,128)(2,1)} %bitcast.27, bf16[256,1024]{1,0:T(8,128)(2,1)} %vl_ref.1), custom_call_target="tpu_custom_call" | custom-call | tf_op jit(solution)/shard_map/pallas_call | solution.py:143
  110.4 35.8 %collective-permute-done.2.bst_ref = f32[16,256]{1,0:T(8,128)S(1)} collective-permute-done((f32[16,256]{1,0:T(8,128)}, f32[16,256]{1,0:T(8,128)S(1)}, u32[]{:S(2)}, u32[]{:S(2)}) %collective-permute-start.2) | collective-permute-done | bytes 16416 | tf_op jit(solution)/shard_map/ppermute | solution.py:274
  146.2 0.6 copy-done.6
  147.0 11.0 %shard_map.84.refs_0_ = bf16[256,1024]{1,0:T(8,128)(2,1)} custom-call(bf16[256,1024]{1,0:T(8,128)(2,1)} %bitcast.24, bf16[8,2,128,1024]{3,2,1,0:T(8,128)(2,1)} %all-to-all-done.kp_ref.vp_ref, bf16[8,2,128,1024]{3,2,1,0:T(8,128)(2,1)} %all-to-all-done.kp_ref.vp_ref, f32[1,1024]{1,0:T(1,128)} %bitcast.32, f32[256,1024]{1,0:T(8,128)} %get-tuple-element.13.la_ref, ...), custom_call_target="tpu_custom_call" | custom-call | tf_op jit(solution)/shard_map/pallas_call | solution.py:177
  158.1 2.4 %collective-permute-start.3 = (bf16[256,1024]{1,0:T(8,128)(2,1)}, bf16[256,1024]{1,0:T(8,128)(2,1)S(1)}, u32[]{:S(2)}, u32[]{:S(2)}) collective-permute-start(bf16[256,1024]{1,0:T(8,128)(2,1)} %shard_map.84.refs_0_), channel_id=1, source_target_pairs={{0,1},{1,0},{2,3},{3,2},{4,5},{5,4},{6,7},{7,6},{8,9},{9,8},{10,11... | collective-permute-start | bytes 1572872 | tf_op jit(solution)/shard_map/ppermute | solution.py:282
  160.5 0.6 reshape.163.refs_4_
  161.1 1.1 collective-permute-done.3.refs_1_
  162.2 0.8 copy-done.3
  163.0 6.4 %shard_map.85 = bf16[256,2048]{1,0:T(8,128)(2,1)} custom-call(bf16[256,1024]{1,0:T(8,128)(2,1)} %shard_map.84.refs_0_, bf16[256,1024]{1,0:T(8,128)(2,1)} %copy-done.3, bf16[1024,2048]{1,0:T(8,128)(2,1)} %get-tuple-element.23.refs_2_, bf16[1024,2048]{1,0:T(8,128)(2,1)} %collective-permute-done.4.refs_3_, bf16[1,2048]{1,0:T(2,128)(2,1)} %reshape.163.refs_4_), custom_call_target="tpu_custom_call" | custom-call | tf_op jit(solution)/shard_map/pallas_call | solution.py:203
  (42 shorter events, 2.5 us)
Async XLA Ops:
  7.7 4.7 %copy-start.8 = (s32[16]{0:T(128)S(1)}, s32[16]{0:T(128)}, u32[]{:S(2)}) copy-start(s32[16]{0:T(128)} %param.15) | copy-start | bytes 196
  7.7 6.5 %copy-start.4 = (bf16[256,1024]{1,0:T(8,128)(2,1)S(1)}, bf16[256,1024]{1,0:T(8,128)(2,1)}, u32[]{:S(2)}) copy-start(bf16[256,1024]{1,0:T(8,128)(2,1)} %param.10) | copy-start | bytes 1572868
  7.7 6.6 %copy-start.5 = (bf16[256,1024]{1,0:T(8,128)(2,1)S(1)}, bf16[256,1024]{1,0:T(8,128)(2,1)}, u32[]{:S(2)}) copy-start(bf16[256,1024]{1,0:T(8,128)(2,1)} %param.11) | copy-start | bytes 1572868
  7.7 69.7 %all-to-all-start.1 = ((bf16[8,2,128,1024]{3,2,1,0:T(8,128)(2,1)}), bf16[8,2,128,1024]{3,2,1,0:T(8,128)(2,1)}, u32[]{:S(2)}, u32[]{:S(2)}) async-start(bf16[8,2,128,1024]{3,2,1,0:T(8,128)(2,1)} %gather_fusion.1), calls=%async_computation.1 | async-start | bytes 8388608 | tf_op jit(solution)/shard_map/all_to_all | solution.py:261
  16.9 9.2 %copy-start = (bf16[32,8,8,128]{3,1,2,0:T(8,128)(2,1)}, bf16[32,8,8,128]{3,1,2,0:T(8,128)(2,1)S(1)}, u32[]{:S(2)}) copy-start(bf16[32,8,8,128]{3,1,2,0:T(8,128)(2,1)S(1)} %copy.18) | copy-start | bytes 1572868
  16.9 60.5 %collective-permute-start = (bf16[256,1024]{1,0:T(8,128)(2,1)S(1)}, bf16[256,1024]{1,0:T(8,128)(2,1)S(1)}, u32[]{:S(2)}, u32[]{:S(2)}) collective-permute-start(bf16[256,1024]{1,0:T(8,128)(2,1)S(1)} %bitcast.22), channel_id=1, source_target_pairs={{0,16},{16,0},{1,17},{17,1},{2,18},{18,2},{3,19},{19,3},{4,20},{20... | collective-permute-start | bytes 1572872 | tf_op jit(solution)/shard_map/ppermute | solution.py:258
  77.4 5.1 %copy-start.1 = (bf16[256,1024]{1,0:T(8,128)(2,1)}, bf16[256,1024]{1,0:T(8,128)(2,1)S(1)}, u32[]{:S(2)}) copy-start(bf16[256,1024]{1,0:T(8,128)(2,1)S(1)} %collective-permute-done.q_ref) | copy-start | bytes 1572868
  77.4 68.8 %all-to-all-start = ((bf16[8,2,128,1024]{3,2,1,0:T(8,128)(2,1)}), bf16[8,2,128,1024]{3,2,1,0:T(8,128)(2,1)}, u32[]{:S(2)}, u32[]{:S(2)}) async-start(bf16[8,2,128,1024]{3,2,1,0:T(8,128)(2,1)} %gather_fusion), calls=%async_computation | async-start | bytes 8388608 | tf_op jit(solution)/shard_map/all_to_all | solution.py:264
  90.8 70.3 %collective-permute-start.4 = (bf16[1024,2048]{1,0:T(8,128)(2,1)}, bf16[1024,2048]{1,0:T(8,128)(2,1)}, u32[]{:S(2)}, u32[]{:S(2)}) collective-permute-start(bf16[1024,2048]{1,0:T(8,128)(2,1)} %get-tuple-element.22), channel_id=1, source_target_pairs={{0,1},{1,0},{2,3},{3,2},{4,5},{5,4},{6,7},{7,6},{8,9},{9,8},{10,11... | collective-permute-start | bytes 12582920 | tf_op jit(solution)/shard_map/ppermute | solution.py:247
  102.0 44.3 %collective-permute-start.1 = (bf16[256,1024]{1,0:T(8,128)(2,1)}, bf16[256,1024]{1,0:T(8,128)(2,1)S(1)}, u32[]{:S(2)}, u32[]{:S(2)}) collective-permute-start(bf16[256,1024]{1,0:T(8,128)(2,1)} %get-tuple-element.16), channel_id=1, source_target_pairs={{0,16},{16,0},{1,17},{17,1},{2,18},{18,2},{3,19},{19,3},{4,20},{20... | collective-permute-start | bytes 1572872 | tf_op jit(solution)/shard_map/ppermute | solution.py:273
  103.2 43.0 %collective-permute-start.2 = (f32[16,256]{1,0:T(8,128)}, f32[16,256]{1,0:T(8,128)S(1)}, u32[]{:S(2)}, u32[]{:S(2)}) collective-permute-start(f32[16,256]{1,0:T(8,128)} %get-tuple-element.17), channel_id=1, source_target_pairs={{0,16},{16,0},{1,17},{17,1},{2,18},{18,2},{3,19},{19,3},{4,20},{20... | collective-permute-start | bytes 49160 | tf_op jit(solution)/shard_map/ppermute | solution.py:274
  146.2 0.6 copy-start.6
  146.2 0.8 copy-start.2
  147.0 13.4 %copy-start.7 = (bf16[2048]{0:T(1024)(128)(2,1)S(1)}, bf16[2048]{0:T(1024)(128)(2,1)}, u32[]{:S(2)}) copy-start(bf16[2048]{0:T(1024)(128)(2,1)} %param.17) | copy-start | bytes 12292
  158.1 4.1 %collective-permute-start.3 = (bf16[256,1024]{1,0:T(8,128)(2,1)}, bf16[256,1024]{1,0:T(8,128)(2,1)S(1)}, u32[]{:S(2)}, u32[]{:S(2)}) collective-permute-start(bf16[256,1024]{1,0:T(8,128)(2,1)} %shard_map.84.refs_0_), channel_id=1, source_target_pairs={{0,1},{1,0},{2,3},{3,2},{4,5},{5,4},{6,7},{7,6},{8,9},{9,8},{10,11... | collective-permute-start | bytes 1572872 | tf_op jit(solution)/shard_map/ppermute | solution.py:282
  162.2 0.8 copy-start.3

commit v23 on v22

--- a/solution.py
+++ b/solution.py
@@ -45,9 +45,11 @@
 
 def local_kernel(q_ref, kl_ref, vl_ref, acc_ref, st_ref):
     score_scale = 1.0 / math.sqrt(HEAD_DIM)
-    for g in range(st_ref.shape[0]):
+    span = q_ref.shape[0]
+    lane = lax.broadcasted_iota(jnp.int32, (span, HEAD_DIM), 1)
+    packed = jnp.zeros((span, HEAD_DIM), jnp.float32)
+    for g in range(st_ref.shape[0] // 2):
         q = head_cols(q_ref, g)
-        span = q.shape[0]
         s = lax.dot_general(q, head_cols(kl_ref, g), SCORE_DIMS, preferred_element_type=jnp.float32) * score_scale
         row = lax.broadcasted_iota(jnp.int32, (span, span), 0)
         col = lax.broadcasted_iota(jnp.int32, (span, span), 1)
@@ -57,8 +59,8 @@
         acc_ref[:, g * HEAD_DIM:(g + 1) * HEAD_DIM] = jnp.dot(
             p.astype(jnp.bfloat16), head_cols(vl_ref, g), preferred_element_type=jnp.float32
         )
-        st_ref[g, :, 0:1] = m
-        st_ref[g, :, 1:2] = jnp.sum(p, axis=1, keepdims=True)
+        packed = jnp.where(lane == 2 * g, m, jnp.where(lane == 2 * g + 1, jnp.sum(p, axis=1, keepdims=True), packed))
+    st_ref[...] = packed.T[: st_ref.shape[0]]
 
 
 def head_pages(kp_ref, vp_ref, g):
@@ -95,12 +97,12 @@
     ok = ok_ref[...]
     rows, span = bst_ref.shape
     back = jnp.concatenate([bst_ref[...], jnp.zeros((HEAD_DIM - rows, span), jnp.float32)], axis=0).T
-    for g in range(lst_ref.shape[0]):
+    local = jnp.concatenate([lst_ref[...], jnp.zeros((HEAD_DIM - rows, span), jnp.float32)], axis=0).T
+    for g in range(rows // 2):
         keys, values = head_pages(kp_ref, vp_ref, g)
         m, l, acc = page_partial(head_cols(q_ref, g), keys, values, ok)
-        local = lst_ref[g]
-        local_max = local[:, 0:1]
-        local_sum = local[:, 1:2]
+        local_max = local[:, 2 * g:2 * g + 1]
+        local_sum = local[:, 2 * g + 1:2 * g + 2]
         back_max = back[:, 2 * g:2 * g + 1]
         back_sum = back[:, 2 * g + 1:2 * g + 2]
         peak = jnp.maximum(jnp.maximum(m, local_max), back_max)
@@ -144,10 +146,10 @@
         local_kernel,
         grid=(head_count // group,),
         in_specs=[col_spec, col_spec, col_spec],
-        out_specs=[col_spec, stat_spec],
+        out_specs=[col_spec, pl.BlockSpec((2 * group, span), lambda h: (h, 0))],
         out_shape=[
             jax.ShapeDtypeStruct((span, width), jnp.float32),
-            jax.ShapeDtypeStruct((head_count, span, 2), jnp.float32),
+            jax.ShapeDtypeStruct((2 * head_count, span), jnp.float32),
         ],
     )(query_rot, key_rot, values)
 
@@ -174,11 +176,12 @@
     head_count = width // HEAD_DIM
     group = heads_per_step(head_count)
     col_spec, stat_spec, page_specs = head_specs(span, incoming.shape[0], incoming.shape[2], group)
+    row_stats = pl.BlockSpec((2 * group, span), lambda h: (h, 0))
     return pl.pallas_call(
         near_kernel,
         grid=(head_count // group,),
         in_specs=[col_spec] + page_specs + [
-            col_spec, stat_spec, col_spec, pl.BlockSpec((2 * group, span), lambda h: (h, 0))
+            col_spec, row_stats, col_spec, row_stats
         ],
         out_specs=col_spec,
         out_shape=jax.ShapeDtypeStruct((span, width), jnp.bfloat16),

time: 170 us -> 169 us (level)
  transfers between devices with their start and end apart: 7 -> 7, of which waited for: 3 -> 3; matrix products, arithmetic and copies ran while one was open for 15% -> 15% of each run, Pallas kernels for 13% -> 12%
where the time goes in v23:
time: 169 us
  waiting for transfers between devices  88.4 us (52%)
  Pallas kernels  27 us (16%)
  local copies, waits for them, and re-layouts  26.6 us (16%)
  starting transfers between devices  19.1 us (11%)
  other arithmetic  7.36 us (4%)
    ppermute x1, waiting for transfers between devices, on_device(): partner_query = lax.ppermute(query_rot, 'half', swap)  51.3 us
    ppermute x1, waiting for transfers between devices, on_device(): back_stats = lax.ppermute(far_stats, 'half', swap)  36 us
    pallas_call x1, Pallas kernels, near_attend(): pl.pallas_call(near_kernel, grid=(head_count // group,), in_specs=[col_sp...  10.3 us
    dynamic_slice x1, local copies, waits for them, and re-layouts, on_device(): piece = lax.dynamic_slice_in_dim(w_out, target * out_cols, out_cols, axis=1)  8.34 us
    pallas_call x1, Pallas kernels, far_attend(): pl.pallas_call(far_kernel, grid=(head_count // group,), in_specs=[col_spe...  6.73 us
    pallas_call x1, Pallas kernels, project(): pl.pallas_call(projection_kernel, grid=(out_cols // block,), in_specs=[a_...  6.39 us
    gather x1, local copies, waits for them, and re-layouts, on_device(): jnp.take(kv_pages, jnp.take(local_page, (1 - half) * sub_count + dest), a...  6.15 us
    gather x1, local copies, waits for them, and re-layouts, on_device(): jnp.take(kv_pages, jnp.take(local_page, half * sub_count + dest), axis=0,...  6.14 us
  transfers between devices with their start and end apart: 7, of which 3 were waited for; matrix products, arithmetic and copies ran while one was open for 15% of the time, Pallas kernels for 12%

profile of v23, /device:TPU:11, one launch (start us, length us, event | category | flops | bytes accessed | tf_op | source)
XLA Modules:
  0.0 168.6 jit_solution(10805391148054006635)
XLA Ops:
  0.0 0.8 select_reduce_fusion
  0.8 0.6 gather_fusion.3
  1.5 6.1 %gather_fusion.1 = bf16[8,2,128,1024]{3,2,1,0:T(8,128)(2,1)} fusion(bf16[16,2,128,1024]{3,2,1,0:T(8,128)(2,1)} %param.13, s32[1024]{0:T(1024)S(1)} %pad_clamp_fusion), kind=kCustom, calls=%fused_computation.3 | custom fusion | bytes 8388640 | tf_op jit(solution)/shard_map/jit(_take)/gather | solution.py:263
  7.7 4.7 %all-to-all-start.1 = ((bf16[8,2,128,1024]{3,2,1,0:T(8,128)(2,1)}), bf16[8,2,128,1024]{3,2,1,0:T(8,128)(2,1)}, u32[]{:S(2)}, u32[]{:S(2)}) async-start(bf16[8,2,128,1024]{3,2,1,0:T(8,128)(2,1)} %gather_fusion.1), calls=%async_computation.1 | async-start | bytes 8388608 | tf_op jit(solution)/shard_map/all_to_all | solution.py:264
  12.4 0.7 fusion.10
  13.1 0.7 add_convert_fusion.2
  15.0 0.8 subtract_convert_fusion
  15.8 1.0 pad_maximum_fusion
  16.9 2.4 %collective-permute-start = (bf16[256,1024]{1,0:T(8,128)(2,1)S(1)}, bf16[256,1024]{1,0:T(8,128)(2,1)S(1)}, u32[]{:S(2)}, u32[]{:S(2)}) collective-permute-start(bf16[256,1024]{1,0:T(8,128)(2,1)S(1)} %bitcast.22), channel_id=1, source_target_pairs={{0,16},{16,0},{1,17},{17,1},{2,18},{18,2},{3,19},{19,3},{4,20},{20... | collective-permute-start | bytes 1572872 | tf_op jit(solution)/shard_map/ppermute | solution.py:261
  19.3 0.6 gather_fusion.2
  19.9 6.1 %gather_fusion = bf16[8,2,128,1024]{3,2,1,0:T(8,128)(2,1)} fusion(bf16[16,2,128,1024]{3,2,1,0:T(8,128)(2,1)} %param.13, s32[1024]{0:T(1024)S(1)} %pad_clamp_fusion.2), kind=kCustom, calls=%fused_computation.2 | custom fusion | bytes 8388640 | tf_op jit(solution)/shard_map/jit(_take)/gather | solution.py:265
  26.1 51.3 %collective-permute-done.q_ref = bf16[256,1024]{1,0:T(8,128)(2,1)S(1)} collective-permute-done((bf16[256,1024]{1,0:T(8,128)(2,1)S(1)}, bf16[256,1024]{1,0:T(8,128)(2,1)S(1)}, u32[]{:S(2)}, u32[]{:S(2)}) %collective-permute-start) | collective-permute-done | bytes 524320 | tf_op jit(solution)/shard_map/ppermute | solution.py:261
  77.4 5.1 %all-to-all-start = ((bf16[8,2,128,1024]{3,2,1,0:T(8,128)(2,1)}), bf16[8,2,128,1024]{3,2,1,0:T(8,128)(2,1)}, u32[]{:S(2)}, u32[]{:S(2)}) async-start(bf16[8,2,128,1024]{3,2,1,0:T(8,128)(2,1)} %gather_fusion), calls=%async_computation | async-start | bytes 8388608 | tf_op jit(solution)/shard_map/all_to_all | solution.py:267
  82.5 8.3 %constant_dynamic-slice_fusion.3 = (bf16[1024,2048]{1,0:T(8,128)(2,1)}, bf16[1024,2048]{1,0:T(8,128)(2,1)}) fusion(bf16[1024,4096]{1,0:T(8,128)(2,1)} %param.16, s32[]{:T(128)S(6)} %select_n.129, s32[]{:T(128)S(6)} %select_n.127), kind=kLoop, calls=%fused_computation.56 | loop fusion | bytes 16777224 | tf_op jit(solution)/shard_map/dynamic_slice | solution.py:248
  90.8 2.1 %collective-permute-start.4 = (bf16[1024,2048]{1,0:T(8,128)(2,1)}, bf16[1024,2048]{1,0:T(8,128)(2,1)}, u32[]{:S(2)}, u32[]{:S(2)}) collective-permute-start(bf16[1024,2048]{1,0:T(8,128)(2,1)} %get-tuple-element.22), channel_id=1, source_target_pairs={{0,1},{1,0},{2,3},{3,2},{4,5},{5,4},{6,7},{7,6},{8,9},{9,8},{10,11... | collective-permute-start | bytes 12582920 | tf_op jit(solution)/shard_map/ppermute | solution.py:250
  92.9 0.7 fusion.8
  94.6 0.7 fusion.7
  95.2 6.7 %shard_map.83 = (bf16[256,1024]{1,0:T(8,128)(2,1)}, f32[16,256]{1,0:T(8,128)}) custom-call(bf16[256,1024]{1,0:T(8,128)(2,1)} %copy-done.1, bf16[8,2,128,1024]{3,2,1,0:T(8,128)(2,1)} %all-to-all-done.1.kp_ref.vp_ref, bf16[8,2,128,1024]{3,2,1,0:T(8,128)(2,1)} %all-to-all-done.1.kp_ref.vp_ref, f32[1,1024]{1,0:T(1,128)} %bitcast.33), custom_call_target="tpu_custom_call" | custom-call | tf_op jit(solution)/shard_map/pallas_call | solution.py:162
  102.0 0.6 collective-permute-start.1
  102.5 0.7 clamp_select_fusion.1
  103.2 1.8 %collective-permute-start.2 = (f32[16,256]{1,0:T(8,128)}, f32[16,256]{1,0:T(8,128)S(1)}, u32[]{:S(2)}, u32[]{:S(2)}) collective-permute-start(f32[16,256]{1,0:T(8,128)} %get-tuple-element.17), channel_id=1, source_target_pairs={{0,16},{16,0},{1,17},{17,1},{2,18},{18,2},{3,19},{19,3},{4,20},{20... | collective-permute-start | bytes 49160 | tf_op jit(solution)/shard_map/ppermute | solution.py:277
  105.1 0.7 fusion.6
  105.7 0.9 copy.17
  106.6 3.6 %shard_map.82 = (f32[256,1024]{1,0:T(8,128)}, f32[16,256]{1,0:T(8,128)}) custom-call(bf16[256,1024]{1,0:T(8,128)(2,1)} %bitcast.23, bf16[256,1024]{1,0:T(8,128)(2,1)} %bitcast.27, bf16[256,1024]{1,0:T(8,128)(2,1)} %vl_ref.1), custom_call_target="tpu_custom_call" | custom-call | tf_op jit(solution)/shard_map/pallas_call | solution.py:145
  110.2 36.0 %collective-permute-done.2.bst_ref = f32[16,256]{1,0:T(8,128)S(1)} collective-permute-done((f32[16,256]{1,0:T(8,128)}, f32[16,256]{1,0:T(8,128)S(1)}, u32[]{:S(2)}, u32[]{:S(2)}) %collective-permute-start.2) | collective-permute-done | bytes 16416 | tf_op jit(solution)/shard_map/ppermute | solution.py:277
  146.2 0.6 copy-done.6
  147.0 10.3 %shard_map.84.refs_0_ = bf16[256,1024]{1,0:T(8,128)(2,1)} custom-call(bf16[256,1024]{1,0:T(8,128)(2,1)} %bitcast.24, bf16[8,2,128,1024]{3,2,1,0:T(8,128)(2,1)} %all-to-all-done.kp_ref.vp_ref, bf16[8,2,128,1024]{3,2,1,0:T(8,128)(2,1)} %all-to-all-done.kp_ref.vp_ref, f32[1,1024]{1,0:T(1,128)} %bitcast.32, f32[256,1024]{1,0:T(8,128)} %get-tuple-element.13.la_ref, ...), custom_call_target="tpu_custom_call" | custom-call | tf_op jit(solution)/shard_map/pallas_call | solution.py:180
  157.3 2.4 %collective-permute-start.3 = (bf16[256,1024]{1,0:T(8,128)(2,1)}, bf16[256,1024]{1,0:T(8,128)(2,1)S(1)}, u32[]{:S(2)}, u32[]{:S(2)}) collective-permute-start(bf16[256,1024]{1,0:T(8,128)(2,1)} %shard_map.84.refs_0_), channel_id=1, source_target_pairs={{0,1},{1,0},{2,3},{3,2},{4,5},{5,4},{6,7},{7,6},{8,9},{9,8},{10,11... | collective-permute-start | bytes 1572872 | tf_op jit(solution)/shard_map/ppermute | solution.py:285
  159.7 0.6 reshape.163.refs_4_
  160.3 1.1 collective-permute-done.3.refs_1_
  161.4 0.8 copy-done.3
  162.2 6.4 %shard_map.85 = bf16[256,2048]{1,0:T(8,128)(2,1)} custom-call(bf16[256,1024]{1,0:T(8,128)(2,1)} %shard_map.84.refs_0_, bf16[256,1024]{1,0:T(8,128)(2,1)} %copy-done.3, bf16[1024,2048]{1,0:T(8,128)(2,1)} %get-tuple-element.23.refs_2_, bf16[1024,2048]{1,0:T(8,128)(2,1)} %collective-permute-done.4.refs_3_, bf16[1,2048]{1,0:T(2,128)(2,1)} %reshape.163.refs_4_), custom_call_target="tpu_custom_call" | custom-call | tf_op jit(solution)/shard_map/pallas_call | solution.py:206
  (42 shorter events, 2.5 us)
Async XLA Ops:
  7.7 4.7 %copy-start.8 = (s32[16]{0:T(128)S(1)}, s32[16]{0:T(128)}, u32[]{:S(2)}) copy-start(s32[16]{0:T(128)} %param.15) | copy-start | bytes 196
  7.7 6.5 %copy-start.4 = (bf16[256,1024]{1,0:T(8,128)(2,1)S(1)}, bf16[256,1024]{1,0:T(8,128)(2,1)}, u32[]{:S(2)}) copy-start(bf16[256,1024]{1,0:T(8,128)(2,1)} %param.10) | copy-start | bytes 1572868
  7.7 6.6 %copy-start.5 = (bf16[256,1024]{1,0:T(8,128)(2,1)S(1)}, bf16[256,1024]{1,0:T(8,128)(2,1)}, u32[]{:S(2)}) copy-start(bf16[256,1024]{1,0:T(8,128)(2,1)} %param.11) | copy-start | bytes 1572868
  7.7 69.7 %all-to-all-start.1 = ((bf16[8,2,128,1024]{3,2,1,0:T(8,128)(2,1)}), bf16[8,2,128,1024]{3,2,1,0:T(8,128)(2,1)}, u32[]{:S(2)}, u32[]{:S(2)}) async-start(bf16[8,2,128,1024]{3,2,1,0:T(8,128)(2,1)} %gather_fusion.1), calls=%async_computation.1 | async-start | bytes 8388608 | tf_op jit(solution)/shard_map/all_to_all | solution.py:264
  16.9 9.2 %copy-start = (bf16[32,8,8,128]{3,1,2,0:T(8,128)(2,1)}, bf16[32,8,8,128]{3,1,2,0:T(8,128)(2,1)S(1)}, u32[]{:S(2)}) copy-start(bf16[32,8,8,128]{3,1,2,0:T(8,128)(2,1)S(1)} %copy.18) | copy-start | bytes 1572868
  16.9 60.5 %collective-permute-start = (bf16[256,1024]{1,0:T(8,128)(2,1)S(1)}, bf16[256,1024]{1,0:T(8,128)(2,1)S(1)}, u32[]{:S(2)}, u32[]{:S(2)}) collective-permute-start(bf16[256,1024]{1,0:T(8,128)(2,1)S(1)} %bitcast.22), channel_id=1, source_target_pairs={{0,16},{16,0},{1,17},{17,1},{2,18},{18,2},{3,19},{19,3},{4,20},{20... | collective-permute-start | bytes 1572872 | tf_op jit(solution)/shard_map/ppermute | solution.py:261
  77.4 5.1 %copy-start.1 = (bf16[256,1024]{1,0:T(8,128)(2,1)}, bf16[256,1024]{1,0:T(8,128)(2,1)S(1)}, u32[]{:S(2)}) copy-start(bf16[256,1024]{1,0:T(8,128)(2,1)S(1)} %collective-permute-done.q_ref) | copy-start | bytes 1572868
  77.4 68.8 %all-to-all-start = ((bf16[8,2,128,1024]{3,2,1,0:T(8,128)(2,1)}), bf16[8,2,128,1024]{3,2,1,0:T(8,128)(2,1)}, u32[]{:S(2)}, u32[]{:S(2)}) async-start(bf16[8,2,128,1024]{3,2,1,0:T(8,128)(2,1)} %gather_fusion), calls=%async_computation | async-start | bytes 8388608 | tf_op jit(solution)/shard_map/all_to_all | solution.py:267
  90.8 69.5 %collective-permute-start.4 = (bf16[1024,2048]{1,0:T(8,128)(2,1)}, bf16[1024,2048]{1,0:T(8,128)(2,1)}, u32[]{:S(2)}, u32[]{:S(2)}) collective-permute-start(bf16[1024,2048]{1,0:T(8,128)(2,1)} %get-tuple-element.22), channel_id=1, source_target_pairs={{0,1},{1,0},{2,3},{3,2},{4,5},{5,4},{6,7},{7,6},{8,9},{9,8},{10,11... | collective-permute-start | bytes 12582920 | tf_op jit(solution)/shard_map/ppermute | solution.py:250
  102.0 44.3 %collective-permute-start.1 = (bf16[256,1024]{1,0:T(8,128)(2,1)}, bf16[256,1024]{1,0:T(8,128)(2,1)S(1)}, u32[]{:S(2)}, u32[]{:S(2)}) collective-permute-start(bf16[256,1024]{1,0:T(8,128)(2,1)} %get-tuple-element.16), channel_id=1, source_target_pairs={{0,16},{16,0},{1,17},{17,1},{2,18},{18,2},{3,19},{19,3},{4,20},{20... | collective-permute-start | bytes 1572872 | tf_op jit(solution)/shard_map/ppermute | solution.py:276
  103.2 43.0 %collective-permute-start.2 = (f32[16,256]{1,0:T(8,128)}, f32[16,256]{1,0:T(8,128)S(1)}, u32[]{:S(2)}, u32[]{:S(2)}) collective-permute-start(f32[16,256]{1,0:T(8,128)} %get-tuple-element.17), channel_id=1, source_target_pairs={{0,16},{16,0},{1,17},{17,1},{2,18},{18,2},{3,19},{19,3},{4,20},{20... | collective-permute-start | bytes 49160 | tf_op jit(solution)/shard_map/ppermute | solution.py:277
  146.2 0.6 copy-start.6
  146.2 0.8 copy-start.2
  147.0 12.6 %copy-start.7 = (bf16[2048]{0:T(1024)(128)(2,1)S(1)}, bf16[2048]{0:T(1024)(128)(2,1)}, u32[]{:S(2)}) copy-start(bf16[2048]{0:T(1024)(128)(2,1)} %param.17) | copy-start | bytes 12292
  157.3 4.1 %collective-permute-start.3 = (bf16[256,1024]{1,0:T(8,128)(2,1)}, bf16[256,1024]{1,0:T(8,128)(2,1)S(1)}, u32[]{:S(2)}, u32[]{:S(2)}) collective-permute-start(bf16[256,1024]{1,0:T(8,128)(2,1)} %shard_map.84.refs_0_), channel_id=1, source_target_pairs={{0,1},{1,0},{2,3},{3,2},{4,5},{5,4},{6,7},{7,6},{8,9},{9,8},{10,11... | collective-permute-start | bytes 1572872 | tf_op jit(solution)/shard_map/ppermute | solution.py:285
  161.4 0.8 copy-start.3

commit v24 on v23

--- a/solution.py
+++ b/solution.py
@@ -115,7 +115,7 @@
             + head_cols(bo_ref, g).astype(jnp.float32) * back_w
         )
         total = l * page_w + local_sum * local_w + back_w
-        o_ref[:, g * HEAD_DIM:(g + 1) * HEAD_DIM] = (merged / total).astype(o_ref.dtype)
+        o_ref[:, g * HEAD_DIM:(g + 1) * HEAD_DIM] = (merged * (1.0 / total)).astype(o_ref.dtype)
 
 
 def heads_per_step(head_count):

time: 169 us -> 169 us (level)
  no operation moved by 1% of the time
where the time goes in v24:
time: 169 us
  waiting for transfers between devices  88.4 us (52%)
  Pallas kernels  27 us (16%)
  local copies, waits for them, and re-layouts  26.6 us (16%)
  starting transfers between devices  19.1 us (11%)
  other arithmetic  7.36 us (4%)
    ppermute x1, waiting for transfers between devices, on_device(): partner_query = lax.ppermute(query_rot, 'half', swap)  51.3 us
    ppermute x1, waiting for transfers between devices, on_device(): back_stats = lax.ppermute(far_stats, 'half', swap)  36 us
    pallas_call x1, Pallas kernels, near_attend(): pl.pallas_call(near_kernel, grid=(head_count // group,), in_specs=[col_sp...  10.3 us
    dynamic_slice x1, local copies, waits for them, and re-layouts, on_device(): piece = lax.dynamic_slice_in_dim(w_out, target * out_cols, out_cols, axis=1)  8.34 us
    pallas_call x1, Pallas kernels, far_attend(): pl.pallas_call(far_kernel, grid=(head_count // group,), in_specs=[col_spe...  6.73 us
    pallas_call x1, Pallas kernels, project(): pl.pallas_call(projection_kernel, grid=(out_cols // block,), in_specs=[a_...  6.39 us
    gather x1, local copies, waits for them, and re-layouts, on_device(): jnp.take(kv_pages, jnp.take(local_page, (1 - half) * sub_count + dest), a...  6.15 us
    gather x1, local copies, waits for them, and re-layouts, on_device(): jnp.take(kv_pages, jnp.take(local_page, half * sub_count + dest), axis=0,...  6.14 us
  transfers between devices with their start and end apart: 7, of which 3 were waited for; matrix products, arithmetic and copies ran while one was open for 15% of the time, Pallas kernels for 12%

profile of v24, /device:TPU:11, one launch (start us, length us, event | category | flops | bytes accessed | tf_op | source)
XLA Modules:
  0.0 168.7 jit_solution(2308434933054868083)
XLA Ops:
  0.0 0.8 select_reduce_fusion
  0.8 0.6 gather_fusion.3
  1.5 6.1 %gather_fusion.1 = bf16[8,2,128,1024]{3,2,1,0:T(8,128)(2,1)} fusion(bf16[16,2,128,1024]{3,2,1,0:T(8,128)(2,1)} %param.13, s32[1024]{0:T(1024)S(1)} %pad_clamp_fusion), kind=kCustom, calls=%fused_computation.3 | custom fusion | bytes 8388640 | tf_op jit(solution)/shard_map/jit(_take)/gather | solution.py:263
  7.7 4.7 %all-to-all-start.1 = ((bf16[8,2,128,1024]{3,2,1,0:T(8,128)(2,1)}), bf16[8,2,128,1024]{3,2,1,0:T(8,128)(2,1)}, u32[]{:S(2)}, u32[]{:S(2)}) async-start(bf16[8,2,128,1024]{3,2,1,0:T(8,128)(2,1)} %gather_fusion.1), calls=%async_computation.1 | async-start | bytes 8388608 | tf_op jit(solution)/shard_map/all_to_all | solution.py:264
  12.4 0.7 fusion.10
  13.1 0.7 add_convert_fusion.2
  15.0 0.8 subtract_convert_fusion
  15.8 1.0 pad_maximum_fusion
  16.9 2.4 %collective-permute-start = (bf16[256,1024]{1,0:T(8,128)(2,1)S(1)}, bf16[256,1024]{1,0:T(8,128)(2,1)S(1)}, u32[]{:S(2)}, u32[]{:S(2)}) collective-permute-start(bf16[256,1024]{1,0:T(8,128)(2,1)S(1)} %bitcast.22), channel_id=1, source_target_pairs={{0,16},{16,0},{1,17},{17,1},{2,18},{18,2},{3,19},{19,3},{4,20},{20... | collective-permute-start | bytes 1572872 | tf_op jit(solution)/shard_map/ppermute | solution.py:261
  19.3 0.6 gather_fusion.2
  19.9 6.1 %gather_fusion = bf16[8,2,128,1024]{3,2,1,0:T(8,128)(2,1)} fusion(bf16[16,2,128,1024]{3,2,1,0:T(8,128)(2,1)} %param.13, s32[1024]{0:T(1024)S(1)} %pad_clamp_fusion.2), kind=kCustom, calls=%fused_computation.2 | custom fusion | bytes 8388640 | tf_op jit(solution)/shard_map/jit(_take)/gather | solution.py:265
  26.1 51.3 %collective-permute-done.q_ref = bf16[256,1024]{1,0:T(8,128)(2,1)S(1)} collective-permute-done((bf16[256,1024]{1,0:T(8,128)(2,1)S(1)}, bf16[256,1024]{1,0:T(8,128)(2,1)S(1)}, u32[]{:S(2)}, u32[]{:S(2)}) %collective-permute-start) | collective-permute-done | bytes 524320 | tf_op jit(solution)/shard_map/ppermute | solution.py:261
  77.4 5.1 %all-to-all-start = ((bf16[8,2,128,1024]{3,2,1,0:T(8,128)(2,1)}), bf16[8,2,128,1024]{3,2,1,0:T(8,128)(2,1)}, u32[]{:S(2)}, u32[]{:S(2)}) async-start(bf16[8,2,128,1024]{3,2,1,0:T(8,128)(2,1)} %gather_fusion), calls=%async_computation | async-start | bytes 8388608 | tf_op jit(solution)/shard_map/all_to_all | solution.py:267
  82.5 8.3 %constant_dynamic-slice_fusion.3 = (bf16[1024,2048]{1,0:T(8,128)(2,1)}, bf16[1024,2048]{1,0:T(8,128)(2,1)}) fusion(bf16[1024,4096]{1,0:T(8,128)(2,1)} %param.16, s32[]{:T(128)S(6)} %select_n.129, s32[]{:T(128)S(6)} %select_n.127), kind=kLoop, calls=%fused_computation.56 | loop fusion | bytes 16777224 | tf_op jit(solution)/shard_map/dynamic_slice | solution.py:248
  90.8 2.1 %collective-permute-start.4 = (bf16[1024,2048]{1,0:T(8,128)(2,1)}, bf16[1024,2048]{1,0:T(8,128)(2,1)}, u32[]{:S(2)}, u32[]{:S(2)}) collective-permute-start(bf16[1024,2048]{1,0:T(8,128)(2,1)} %get-tuple-element.22), channel_id=1, source_target_pairs={{0,1},{1,0},{2,3},{3,2},{4,5},{5,4},{6,7},{7,6},{8,9},{9,8},{10,11... | collective-permute-start | bytes 12582920 | tf_op jit(solution)/shard_map/ppermute | solution.py:250
  92.9 0.7 fusion.8
  94.6 0.7 fusion.7
  95.2 6.7 %shard_map.83 = (bf16[256,1024]{1,0:T(8,128)(2,1)}, f32[16,256]{1,0:T(8,128)}) custom-call(bf16[256,1024]{1,0:T(8,128)(2,1)} %copy-done.1, bf16[8,2,128,1024]{3,2,1,0:T(8,128)(2,1)} %all-to-all-done.1.kp_ref.vp_ref, bf16[8,2,128,1024]{3,2,1,0:T(8,128)(2,1)} %all-to-all-done.1.kp_ref.vp_ref, f32[1,1024]{1,0:T(1,128)} %bitcast.33), custom_call_target="tpu_custom_call" | custom-call | tf_op jit(solution)/shard_map/pallas_call | solution.py:162
  102.0 0.6 collective-permute-start.1
  102.5 0.7 clamp_select_fusion.1
  103.2 1.8 %collective-permute-start.2 = (f32[16,256]{1,0:T(8,128)}, f32[16,256]{1,0:T(8,128)S(1)}, u32[]{:S(2)}, u32[]{:S(2)}) collective-permute-start(f32[16,256]{1,0:T(8,128)} %get-tuple-element.17), channel_id=1, source_target_pairs={{0,16},{16,0},{1,17},{17,1},{2,18},{18,2},{3,19},{19,3},{4,20},{20... | collective-permute-start | bytes 49160 | tf_op jit(solution)/shard_map/ppermute | solution.py:277
  105.1 0.7 fusion.6
  105.7 0.9 copy.17
  106.6 3.6 %shard_map.82 = (f32[256,1024]{1,0:T(8,128)}, f32[16,256]{1,0:T(8,128)}) custom-call(bf16[256,1024]{1,0:T(8,128)(2,1)} %bitcast.23, bf16[256,1024]{1,0:T(8,128)(2,1)} %bitcast.27, bf16[256,1024]{1,0:T(8,128)(2,1)} %vl_ref.1), custom_call_target="tpu_custom_call" | custom-call | tf_op jit(solution)/shard_map/pallas_call | solution.py:145
  110.2 36.0 %collective-permute-done.2.bst_ref = f32[16,256]{1,0:T(8,128)S(1)} collective-permute-done((f32[16,256]{1,0:T(8,128)}, f32[16,256]{1,0:T(8,128)S(1)}, u32[]{:S(2)}, u32[]{:S(2)}) %collective-permute-start.2) | collective-permute-done | bytes 16416 | tf_op jit(solution)/shard_map/ppermute | solution.py:277
  146.2 0.6 copy-done.6
  147.0 10.3 %shard_map.84.refs_0_ = bf16[256,1024]{1,0:T(8,128)(2,1)} custom-call(bf16[256,1024]{1,0:T(8,128)(2,1)} %bitcast.24, bf16[8,2,128,1024]{3,2,1,0:T(8,128)(2,1)} %all-to-all-done.kp_ref.vp_ref, bf16[8,2,128,1024]{3,2,1,0:T(8,128)(2,1)} %all-to-all-done.kp_ref.vp_ref, f32[1,1024]{1,0:T(1,128)} %bitcast.32, f32[256,1024]{1,0:T(8,128)} %get-tuple-element.13.la_ref, ...), custom_call_target="tpu_custom_call" | custom-call | tf_op jit(solution)/shard_map/pallas_call | solution.py:180
  157.3 2.4 %collective-permute-start.3 = (bf16[256,1024]{1,0:T(8,128)(2,1)}, bf16[256,1024]{1,0:T(8,128)(2,1)S(1)}, u32[]{:S(2)}, u32[]{:S(2)}) collective-permute-start(bf16[256,1024]{1,0:T(8,128)(2,1)} %shard_map.84.refs_0_), channel_id=1, source_target_pairs={{0,1},{1,0},{2,3},{3,2},{4,5},{5,4},{6,7},{7,6},{8,9},{9,8},{10,11... | collective-permute-start | bytes 1572872 | tf_op jit(solution)/shard_map/ppermute | solution.py:285
  159.7 0.6 reshape.163.refs_4_
  160.3 1.1 collective-permute-done.3.refs_1_
  161.5 0.8 copy-done.3
  162.3 6.4 %shard_map.85 = bf16[256,2048]{1,0:T(8,128)(2,1)} custom-call(bf16[256,1024]{1,0:T(8,128)(2,1)} %shard_map.84.refs_0_, bf16[256,1024]{1,0:T(8,128)(2,1)} %copy-done.3, bf16[1024,2048]{1,0:T(8,128)(2,1)} %get-tuple-element.23.refs_2_, bf16[1024,2048]{1,0:T(8,128)(2,1)} %collective-permute-done.4.refs_3_, bf16[1,2048]{1,0:T(2,128)(2,1)} %reshape.163.refs_4_), custom_call_target="tpu_custom_call" | custom-call | tf_op jit(solution)/shard_map/pallas_call | solution.py:206
  (42 shorter events, 2.5 us)
Async XLA Ops:
  7.7 4.7 %copy-start.8 = (s32[16]{0:T(128)S(1)}, s32[16]{0:T(128)}, u32[]{:S(2)}) copy-start(s32[16]{0:T(128)} %param.15) | copy-start | bytes 196
  7.7 6.5 %copy-start.4 = (bf16[256,1024]{1,0:T(8,128)(2,1)S(1)}, bf16[256,1024]{1,0:T(8,128)(2,1)}, u32[]{:S(2)}) copy-start(bf16[256,1024]{1,0:T(8,128)(2,1)} %param.10) | copy-start | bytes 1572868
  7.7 6.6 %copy-start.5 = (bf16[256,1024]{1,0:T(8,128)(2,1)S(1)}, bf16[256,1024]{1,0:T(8,128)(2,1)}, u32[]{:S(2)}) copy-start(bf16[256,1024]{1,0:T(8,128)(2,1)} %param.11) | copy-start | bytes 1572868
  7.7 69.7 %all-to-all-start.1 = ((bf16[8,2,128,1024]{3,2,1,0:T(8,128)(2,1)}), bf16[8,2,128,1024]{3,2,1,0:T(8,128)(2,1)}, u32[]{:S(2)}, u32[]{:S(2)}) async-start(bf16[8,2,128,1024]{3,2,1,0:T(8,128)(2,1)} %gather_fusion.1), calls=%async_computation.1 | async-start | bytes 8388608 | tf_op jit(solution)/shard_map/all_to_all | solution.py:264
  16.9 9.2 %copy-start = (bf16[32,8,8,128]{3,1,2,0:T(8,128)(2,1)}, bf16[32,8,8,128]{3,1,2,0:T(8,128)(2,1)S(1)}, u32[]{:S(2)}) copy-start(bf16[32,8,8,128]{3,1,2,0:T(8,128)(2,1)S(1)} %copy.18) | copy-start | bytes 1572868
  16.9 60.5 %collective-permute-start = (bf16[256,1024]{1,0:T(8,128)(2,1)S(1)}, bf16[256,1024]{1,0:T(8,128)(2,1)S(1)}, u32[]{:S(2)}, u32[]{:S(2)}) collective-permute-start(bf16[256,1024]{1,0:T(8,128)(2,1)S(1)} %bitcast.22), channel_id=1, source_target_pairs={{0,16},{16,0},{1,17},{17,1},{2,18},{18,2},{3,19},{19,3},{4,20},{20... | collective-permute-start | bytes 1572872 | tf_op jit(solution)/shard_map/ppermute | solution.py:261
  77.4 5.1 %copy-start.1 = (bf16[256,1024]{1,0:T(8,128)(2,1)}, bf16[256,1024]{1,0:T(8,128)(2,1)S(1)}, u32[]{:S(2)}) copy-start(bf16[256,1024]{1,0:T(8,128)(2,1)S(1)} %collective-permute-done.q_ref) | copy-start | bytes 1572868
  77.4 68.8 %all-to-all-start = ((bf16[8,2,128,1024]{3,2,1,0:T(8,128)(2,1)}), bf16[8,2,128,1024]{3,2,1,0:T(8,128)(2,1)}, u32[]{:S(2)}, u32[]{:S(2)}) async-start(bf16[8,2,128,1024]{3,2,1,0:T(8,128)(2,1)} %gather_fusion), calls=%async_computation | async-start | bytes 8388608 | tf_op jit(solution)/shard_map/all_to_all | solution.py:267
  90.8 69.5 %collective-permute-start.4 = (bf16[1024,2048]{1,0:T(8,128)(2,1)}, bf16[1024,2048]{1,0:T(8,128)(2,1)}, u32[]{:S(2)}, u32[]{:S(2)}) collective-permute-start(bf16[1024,2048]{1,0:T(8,128)(2,1)} %get-tuple-element.22), channel_id=1, source_target_pairs={{0,1},{1,0},{2,3},{3,2},{4,5},{5,4},{6,7},{7,6},{8,9},{9,8},{10,11... | collective-permute-start | bytes 12582920 | tf_op jit(solution)/shard_map/ppermute | solution.py:250
  102.0 44.3 %collective-permute-start.1 = (bf16[256,1024]{1,0:T(8,128)(2,1)}, bf16[256,1024]{1,0:T(8,128)(2,1)S(1)}, u32[]{:S(2)}, u32[]{:S(2)}) collective-permute-start(bf16[256,1024]{1,0:T(8,128)(2,1)} %get-tuple-element.16), channel_id=1, source_target_pairs={{0,16},{16,0},{1,17},{17,1},{2,18},{18,2},{3,19},{19,3},{4,20},{20... | collective-permute-start | bytes 1572872 | tf_op jit(solution)/shard_map/ppermute | solution.py:276
  103.2 43.0 %collective-permute-start.2 = (f32[16,256]{1,0:T(8,128)}, f32[16,256]{1,0:T(8,128)S(1)}, u32[]{:S(2)}, u32[]{:S(2)}) collective-permute-start(f32[16,256]{1,0:T(8,128)} %get-tuple-element.17), channel_id=1, source_target_pairs={{0,16},{16,0},{1,17},{17,1},{2,18},{18,2},{3,19},{19,3},{4,20},{20... | collective-permute-start | bytes 49160 | tf_op jit(solution)/shard_map/ppermute | solution.py:277
  146.2 0.6 copy-start.6
  146.2 0.8 copy-start.2
  147.0 12.7 %copy-start.7 = (bf16[2048]{0:T(1024)(128)(2,1)S(1)}, bf16[2048]{0:T(1024)(128)(2,1)}, u32[]{:S(2)}) copy-start(bf16[2048]{0:T(1024)(128)(2,1)} %param.17) | copy-start | bytes 12292
  157.3 4.1 %collective-permute-start.3 = (bf16[256,1024]{1,0:T(8,128)(2,1)}, bf16[256,1024]{1,0:T(8,128)(2,1)S(1)}, u32[]{:S(2)}, u32[]{:S(2)}) collective-permute-start(bf16[256,1024]{1,0:T(8,128)(2,1)} %shard_map.84.refs_0_), channel_id=1, source_target_pairs={{0,1},{1,0},{2,3},{3,2},{4,5},{5,4},{6,7},{7,6},{8,9},{9,8},{10,11... | collective-permute-start | bytes 1572872 | tf_op jit(solution)/shard_map/ppermute | solution.py:285
  161.5 0.8 copy-start.3
